TPU v7x, 256 devices: a whole 4x4x8 slice. The times are simulated.
256 devices in a mesh: dp: 32 (over x, z), segment: 2 (over core), rows: 4 (over y).
Axes of the slice: x: 4, y: 4, z: 8, core: 2. Of those that a mesh axis runs over, the one named last changes fastest.
Arguments:
- block_input: bfloat16 [32, 16, 32, 416], P('dp', 'rows'), may hold values from -6 to 6
- saved_maps: bfloat16 [2, 32, 16, 32, 2496], P('segment', 'dp', 'rows'), may hold values from -6 to 6
- grad_p5: bfloat16 [32, 16, 32, 384], P('dp', 'rows'), may hold values from -6 to 6
- grad_p6: bfloat16 [32, 8, 16, 384], P('dp', 'rows'), may hold values from -12 to 12
- grad_p7: bfloat16 [32, 4, 8, 384], P('dp', 'rows'), may hold values from -16 to 16
- lateral: bfloat16 [416, 384], replicated, may hold values from -0.3125 to 0.3125
- stacked: bfloat16 [2, 1038336], P('segment', ('dp', 'rows')), may hold values from -0.3125 to 0.3125
- kernel: bfloat16 [25, 2496], replicated, may hold values from -1.75 to 1.75
- se_reduce: bfloat16 [2496, 104], replicated, may hold values from -0.3125 to 0.3125
- se_expand: bfloat16 [104, 2496], replicated, may hold values from -1.25 to 1.25
Outputs:
- grad_inputs: bfloat16 [2, 32, 16, 32, 416], P('segment', 'dp', 'rows')
- param_grads: float32 [2, 1038336], P('segment', ('dp', 'rows'))
All inputs are finite; a program needn't handle non-finite values.
Results may differ from a plain program's by a relative error of at most 0.0059.
Values may be sent and summed in bfloat16 or wider, within the bound.
No kernel may reach another device: no remote copies, remote signals or barrier semaphores. Data moves between devices by JAX's collectives and lax.ppermute only.
A program may use at most 64 MiB of HBM per device.

v0:
```python
import jax
import jax.numpy as jnp
from jax import lax
from jax.sharding import PartitionSpec as P


def extended_2(block, sides, width):
    for axis, dim in sides:
        count = lax.axis_size(axis)
        forward = [(i, i + 1) for i in range(count - 1)]
        backward = [(target, source) for source, target in forward]
        low = lax.ppermute(
            lax.slice_in_dim(block, block.shape[dim] - width, None, axis=dim), axis, forward
        )
        high = lax.ppermute(lax.slice_in_dim(block, 0, width, axis=dim), axis, backward)
        block = jnp.concatenate([low, block, high], axis=dim)
    return block


def passed_along(array, axis, by):
    length = lax.axis_size(axis)
    pairs = [(i, i + by) for i in range(length) if 0 <= i + by < length]
    return lax.ppermute(array, axis, pairs)


def flat_bits():
    rows_bits = lax.axis_size("rows").bit_length() - 1
    dp_bits = lax.axis_size("dp").bit_length() - 1
    return [("rows", k) for k in range(rows_bits)] + [("dp", k) for k in range(dp_bits)]


def swap_pairs(axis, j):
    return [(i, i ^ (1 << j)) for i in range(lax.axis_size(axis))]


def gather_chunks(piece, order):
    bits = flat_bits()
    buf = piece
    lead = []
    for axis, j in order:
        recv = lax.ppermute(buf, axis, swap_pairs(axis, j))
        high = (lax.axis_index(axis) >> j) & 1
        buf = jnp.stack([jnp.where(high == 0, buf, recv), jnp.where(high == 0, recv, buf)])
        lead.insert(0, bits.index((axis, j)))
    count = len(bits)
    perm = [lead.index(k) for k in reversed(range(count))] + [count, count + 1]
    return jnp.transpose(buf, perm).reshape((2**count,) + piece.shape)


def gather_streams(piece, orders, cuts):
    parts = jnp.split(piece, cuts, axis=-1)
    done = [gather_chunks(part, order) for part, order in zip(parts, orders)]
    return jnp.concatenate(done, axis=-1).reshape(-1)


def scatter_chunks(full, order):
    bits = flat_bits()
    count = len(bits)
    buf = full.reshape((2,) * count + full.shape[1:])
    live = list(reversed(range(count)))
    for axis, j in order:
        at = live.index(bits.index((axis, j)))
        high = (lax.axis_index(axis) >> j) & 1
        mine = lax.dynamic_index_in_dim(buf, high, at, keepdims=False)
        other = lax.dynamic_index_in_dim(buf, 1 - high, at, keepdims=False)
        buf = mine + lax.ppermute(other, axis, swap_pairs(axis, j))
        live.pop(at)
    return buf


def scatter_streams(full, orders, cuts):
    parts = jnp.split(full, cuts, axis=-1)
    done = [scatter_chunks(part, order) for part, order in zip(parts, orders)]
    return jnp.concatenate(done, axis=-1).reshape(-1)


def rows_sum(values):
    for j in range(lax.axis_size("rows").bit_length() - 1):
        values = tuple(v + lax.ppermute(v, "rows", swap_pairs("rows", j)) for v in values)
    return values


GATHER_ORDERS = (
    [("dp", 2), ("dp", 4), ("dp", 1), ("rows", 1), ("dp", 3), ("dp", 0), ("rows", 0)],
    [("dp", 4), ("rows", 1), ("dp", 2), ("dp", 1), ("rows", 0), ("dp", 3), ("dp", 0)],
)
SCATTER_ORDERS = tuple(order[::-1] for order in GATHER_ORDERS)


def up_two(v):
    return jnp.repeat(jnp.repeat(v, 2, axis=0), 2, axis=1)


def silu_slope(v):
    sig = jax.nn.sigmoid(v)
    return sig * (1.0 + v * (1.0 - sig))


def depth_forward(padded, taps, rows, cols):
    total = jnp.zeros((rows, cols, taps.shape[1]), jnp.float32)
    for p in range(5):
        for q in range(5):
            total = total + taps[5 * p + q] * padded[p : p + rows, q : q + cols].astype(jnp.float32)
    return total


def depth_backward(padded, taps, rows, cols):
    total = jnp.zeros((rows, cols, taps.shape[1]), jnp.float32)
    for p in range(5):
        for q in range(5):
            total = total + taps[5 * p + q] * padded[
                4 - p : 4 - p + rows, 4 - q : 4 - q + cols
            ].astype(jnp.float32)
    return total


def margin(values):
    extended = extended_2(values, (("rows", 0),), 2)
    return jnp.pad(extended, ((0, 0), (2, 2), (0, 0)))


def squeeze_gate(pool_total, grad_total, cells, reduce_w, expand_w):
    pooled = pool_total / cells
    z1 = jnp.dot(pooled, reduce_w, precision=lax.Precision.HIGHEST)
    z2 = jnp.dot(jax.nn.silu(z1), expand_w, precision=lax.Precision.HIGHEST)
    gate = jax.nn.sigmoid(z2)
    dz2 = grad_total * gate * (1.0 - gate)
    dz1 = jnp.dot(dz2, expand_w.T, precision=lax.Precision.HIGHEST) * silu_slope(z1)
    dpool = jnp.dot(dz1, reduce_w.T, precision=lax.Precision.HIGHEST)
    return (gate, dpool)


def body(
    block_input,
    saved_maps,
    grad_p5,
    grad_p6,
    grad_p7,
    lateral,
    stacked,
    kernel,
    se_reduce,
    se_expand,
):
    rows_here = block_input.shape[1]
    cols = block_input.shape[2]
    cin = block_input.shape[3]
    wide = saved_maps.shape[-1]
    cells_here = rows_here * cols
    row_count = lax.axis_size("rows")
    cells = cells_here * row_count
    images = block_input.shape[0] * lax.axis_size("dp")
    flat = gather_streams(stacked[0].reshape(16, -1), GATHER_ORDERS, [254])
    weight = flat.reshape(cin, wide)
    segment = lax.axis_index("segment")
    held = saved_maps[0, 0]
    image = block_input[0]
    taps = kernel.astype(jnp.float32)
    reduce_w = se_reduce.astype(jnp.float32)
    expand_w = se_expand.astype(jnp.float32)

    def rise_branch():
        return jax.nn.silu(held.astype(jnp.float32)).astype(jnp.bfloat16)

    def rise_still():
        return jnp.zeros((rows_here, cols, wide), jnp.bfloat16)

    expanded = lax.cond(segment == 1, rise_branch, rise_still)
    padded_e = margin(expanded)

    def pool_branch():
        dwo = depth_forward(padded_e, taps, rows_here, cols)
        act = jax.nn.silu(dwo)
        return (dwo, act, jnp.sum(act, axis=(0, 1)))

    def still_branch():
        return (
            jnp.zeros((rows_here, cols, wide), jnp.float32),
            jnp.zeros((rows_here, cols, wide), jnp.float32),
            jnp.zeros((wide,), jnp.float32),
        )

    dwo, act, pool_part = lax.cond(segment == 1, pool_branch, still_branch)

    def head_branch():
        inner = grad_p6[0].astype(jnp.float32) + up_two(grad_p7[0].astype(jnp.float32)) / 4.0
        g = (grad_p5[0].astype(jnp.float32) + up_two(inner) / 4.0).astype(jnp.bfloat16)
        grad_out = jnp.dot(
            g.reshape(cells_here, -1), lateral.T, preferred_element_type=jnp.float32
        ).astype(jnp.bfloat16)
        grad_proj = jnp.dot(grad_out, weight, preferred_element_type=jnp.float32).astype(
            jnp.bfloat16
        )
        term = jnp.dot(
            grad_out.T, held.reshape(cells_here, wide), preferred_element_type=jnp.float32
        )
        return (
            grad_out.reshape(rows_here, cols, cin),
            grad_proj.reshape(rows_here, cols, wide),
            term,
        )

    def head_still():
        return (
            jnp.zeros((rows_here, cols, cin), jnp.bfloat16),
            jnp.zeros((rows_here, cols, wide), jnp.bfloat16),
            jnp.zeros((cin, wide), jnp.float32),
        )

    grad_top, grad_proj, head_term = lax.cond(segment == 0, head_branch, head_still)
    shards = lax.axis_size("dp") * row_count
    chunk = cin * wide // shards

    def spread(term):
        flat_term = (term / images).reshape(shards, 8, -1)
        return scatter_streams(flat_term, SCATTER_ORDERS, [512])

    def spread_still(term):
        return jnp.zeros((chunk,), jnp.float32)

    sent_top, sent_mid = passed_along((grad_top, grad_proj), "segment", 1)
    sent_top, sent_mid, head_term = lax.optimization_barrier((sent_top, sent_mid, head_term))
    head_share = lax.cond(segment == 0, spread, spread_still, head_term)
    head_share, sent_top, sent_mid, act = lax.optimization_barrier(
        (head_share, sent_top, sent_mid, act)
    )
    grad_part = jnp.sum(sent_mid.astype(jnp.float32) * act, axis=(0, 1))
    pool_total, grad_total = rows_sum((pool_part, grad_part))

    def gate_branch():
        gate, dpool = squeeze_gate(pool_total, grad_total, cells, reduce_w, expand_w)
        return ((sent_mid.astype(jnp.float32) * gate + dpool / cells) * silu_slope(dwo)).astype(
            jnp.bfloat16
        )

    def quiet_branch():
        return jnp.zeros((rows_here, cols, wide), jnp.bfloat16)

    grad_dw = lax.cond(segment == 1, gate_branch, quiet_branch)
    padded_grad = margin(grad_dw)

    def tail_branch():
        grad_e = depth_backward(padded_grad, taps, rows_here, cols)
        grad_pre = (
            (grad_e * silu_slope(held.astype(jnp.float32)))
            .astype(jnp.bfloat16)
            .reshape(cells_here, wide)
        )
        term = jnp.dot(
            image.reshape(cells_here, cin).T, grad_pre, preferred_element_type=jnp.float32
        )
        back = jnp.dot(grad_pre, weight.T, preferred_element_type=jnp.float32)
        grad_x = (sent_top.reshape(cells_here, cin).astype(jnp.float32) + back).astype(jnp.bfloat16)
        return (grad_x.reshape(rows_here, cols, cin), spread(term))

    def head_keep():
        return (grad_top, head_share)

    grad_here, share = lax.cond(segment == 1, tail_branch, head_keep)
    return (grad_here[None, None], share[None])


def solution(mesh):
    in_specs = (
        P("dp", "rows", None, None),
        P("segment", "dp", "rows", None, None),
        P("dp", "rows", None, None),
        P("dp", "rows", None, None),
        P("dp", "rows", None, None),
        P(),
        P("segment", ("dp", "rows")),
        P(),
        P(),
        P(),
    )
    out_specs = (P("segment", "dp", "rows", None, None), P("segment", ("dp", "rows")))
    return jax.shard_map(body, mesh=mesh, in_specs=in_specs, out_specs=out_specs, check_vma=False)
```

profile of v0, /device:TPU:8, one launch (start us, length us, event | category | flops | bytes accessed | tf_op | source)
XLA Modules:
  0.0 220.4 jit_solution(10481075343046653425)
XLA Ops:
  1.7 3.0 %collective-permute-start.35 = (bf16[16,253]{1,0:T(8,128)(2,1)S(1)}, bf16[16,253]{1,0:T(8,128)(2,1)S(1)}, u32[]{:S(2)}, u32[]{:S(2)}) collective-permute-start(bf16[16,253]{1,0:T(8,128)(2,1)S(1)} %split.25), channel_id=1, source_target_pairs={{0,128},{8,136},{16,144},{24,152},{32,160},{40,168},{48,176},{56,1... | collective-permute-start | bytes 24296 | tf_op jit(solution)/shard_map/ppermute | solution.py:41
  4.7 7.2 %collective-permute-start.28 = (bf16[16,254]{1,0:T(8,128)(2,1)S(1)}, bf16[16,254]{1,0:T(8,128)(2,1)S(1)}, u32[]{:S(2)}, u32[]{:S(2)}) collective-permute-start(bf16[16,254]{1,0:T(8,128)(2,1)S(1)} %split.24), channel_id=1, source_target_pairs={{0,32},{8,40},{16,48},{24,56},{32,0},{40,8},{48,16},{56,24},{64,96... | collective-permute-start | bytes 24392 | tf_op jit(solution)/shard_map/ppermute | solution.py:41
  12.1 2.4 %collective-permute-start.36 = (bf16[2,16,253]{2,1,0:T(8,128)(2,1)S(1)}, bf16[2,16,253]{2,1,0:T(8,128)(2,1)S(1)}, u32[]{:S(2)}, u32[]{:S(2)}) collective-permute-start(bf16[2,16,253]{2,1,0:T(8,128)(2,1)S(1)} %pad_maximum_fusion.16), channel_id=1, source_target_pairs={{0,2},{1,3},{2,0},{3,1},{4,6},{5,7},{6,4},{7,5},{8,10},{9,11},{10,... | collective-permute-start | bytes 48584 | tf_op jit(solution)/shard_map/ppermute | solution.py:41
  15.1 2.3 %collective-permute-done.36 = bf16[2,16,253]{2,1,0:T(8,128)(2,1)S(1)} collective-permute-done((bf16[2,16,253]{2,1,0:T(8,128)(2,1)S(1)}, bf16[2,16,253]{2,1,0:T(8,128)(2,1)S(1)}, u32[]{:S(2)}, u32[]{:S(2)}) %collective-permute-start.36) | collective-permute-done | bytes 16224 | tf_op jit(solution)/shard_map/ppermute | solution.py:41
  17.4 2.8 %collective-permute-start.37 = (bf16[2,2,16,253]{3,2,1,0:T(8,128)(2,1)S(1)}, bf16[2,2,16,253]{3,2,1,0:T(8,128)(2,1)S(1)}, u32[]{:S(2)}, u32[]{:S(2)}) collective-permute-start(bf16[2,2,16,253]{3,2,1,0:T(8,128)(2,1)S(1)} %pad_maximum_fusion.14), channel_id=1, source_target_pairs={{0,32},{8,40},{16,48},{24,56},{32,0},{40,8},{48,16},{56,24},{64,96... | collective-permute-start | bytes 97160 | tf_op jit(solution)/shard_map/ppermute | solution.py:41
  21.8 3.8 %collective-permute-done.37 = bf16[2,2,16,253]{3,2,1,0:T(8,128)(2,1)S(1)} collective-permute-done((bf16[2,2,16,253]{3,2,1,0:T(8,128)(2,1)S(1)}, bf16[2,2,16,253]{3,2,1,0:T(8,128)(2,1)S(1)}, u32[]{:S(2)}, u32[]{:S(2)}) %collective-permute-start.37) | collective-permute-done | bytes 32416 | tf_op jit(solution)/shard_map/ppermute | solution.py:41
  27.1 2.4 %collective-permute-start.31 = (bf16[2,2,2,16,254]{4,3,2,1,0:T(8,128)(2,1)S(1)}, bf16[2,2,2,16,254]{4,3,2,1,0:T(8,128)(2,1)S(1)}, u32[]{:S(2)}, u32[]{:S(2)}) collective-permute-start(bf16[2,2,2,16,254]{4,3,2,1,0:T(8,128)(2,1)S(1)} %pad_maximum_fusion.11), channel_id=1, source_target_pairs={{0,2},{1,3},{2,0},{3,1},{4,6},{5,7},{6,4},{7,5},{8,10},{9,11},{10,... | collective-permute-start | bytes 195080 | tf_op jit(solution)/shard_map/ppermute | solution.py:41
  29.5 2.1 collective-permute-done.38
  34.1 2.5 %collective-permute-done.39 = bf16[2,2,2,2,16,253]{5,4,3,2,1,0:T(8,128)(2,1)S(1)} collective-permute-done((bf16[2,2,2,2,16,253]{5,4,3,2,1,0:T(8,128)(2,1)S(1)}, bf16[2,2,2,2,16,253]{5,4,3,2,1,0:T(8,128)(2,1)S(1)}, u32[]{:S(2)}, u32[]{:S(2)}) %collective-permute-start.39) | collective-permute-done | bytes 129568 | tf_op jit(solution)/shard_map/ppermute | solution.py:41
  37.4 2.5 %collective-permute-done.32 = bf16[2,2,2,2,16,254]{5,4,3,2,1,0:T(8,128)(2,1)S(1)} collective-permute-done((bf16[2,2,2,2,16,254]{5,4,3,2,1,0:T(8,128)(2,1)S(1)}, bf16[2,2,2,2,16,254]{5,4,3,2,1,0:T(8,128)(2,1)S(1)}, u32[]{:S(2)}, u32[]{:S(2)}) %collective-permute-start.32) | collective-permute-done | bytes 130080 | tf_op jit(solution)/shard_map/ppermute | solution.py:41
  40.1 3.2 %collective-permute-done.40 = bf16[2,2,2,2,2,16,253]{6,5,4,3,2,1,0:T(8,128)(2,1)S(1)} collective-permute-done((bf16[2,2,2,2,2,16,253]{6,5,4,3,2,1,0:T(8,128)(2,1)S(1)}, bf16[2,2,2,2,2,16,253]{6,5,4,3,2,1,0:T(8,128)(2,1)S(1)}, u32[]{:S(2)}, u32[]{:S(2)}) %collective-permute-start.40) | collective-permute-done | bytes 259104 | tf_op jit(solution)/shard_map/ppermute | solution.py:41
  43.8 5.5 %collective-permute-done.33 = bf16[2,2,2,2,2,16,254]{6,5,4,3,2,1,0:T(8,128)(2,1)S(1)} collective-permute-done((bf16[2,2,2,2,2,16,254]{6,5,4,3,2,1,0:T(8,128)(2,1)S(1)}, bf16[2,2,2,2,2,16,254]{6,5,4,3,2,1,0:T(8,128)(2,1)S(1)}, u32[]{:S(2)}, u32[]{:S(2)}) %collective-permute-start.33) | collective-permute-done | bytes 260128 | tf_op jit(solution)/shard_map/ppermute | solution.py:41
  51.6 3.6 %collective-permute-start.45 = (bf16[2,32,2496]{2,1,0:T(8,128)(2,1)}, bf16[2,32,2496]{2,1,0:T(8,128)(2,1)}, u32[]{:S(2)}, u32[]{:S(2)}) collective-permute-start(bf16[2,32,2496]{2,1,0:T(8,128)(2,1)} %get-tuple-element.197), channel_id=1, source_target_pairs={{1,0},{2,1},{3,2},{5,4},{6,5},{7,6},{9,8},{10,9},{11,10},{13,12},{... | collective-permute-start | bytes 958472 | tf_op jit(solution)/shard_map/ppermute | solution.py:15
  55.2 16.0 %collective-permute-start.44 = (bf16[2,32,2496]{2,1,0:T(8,128)(2,1)}, bf16[2,32,2496]{2,1,0:T(8,128)(2,1)}, u32[]{:S(2)}, u32[]{:S(2)}) collective-permute-start(bf16[2,32,2496]{2,1,0:T(8,128)(2,1)} %get-tuple-element.196), channel_id=1, source_target_pairs={{0,1},{1,2},{2,3},{4,5},{5,6},{6,7},{8,9},{9,10},{10,11},{12,13},{... | collective-permute-start | bytes 958472 | tf_op jit(solution)/shard_map/ppermute | solution.py:12
  75.1 2.2 %pad_maximum_fusion.2 = bf16[128,16,507]{2,1,0:T(8,128)(2,1)} fusion(bf16[128,16,253]{2,1,0:T(8,128)(2,1)S(1)} %bitcast.256, bf16[128,16,254]{2,1,0:T(8,128)(2,1)S(1)} %bitcast.257), kind=kLoop, calls=%fused_computation.195 | loop fusion | flops 4153344 | bytes 4153344 | tf_op jit(solution)/shard_map/concatenate | solution.py:53
  77.4 5.3 %reshape_reshape.3 = bf16[416,2496]{1,0:T(8,128)(2,1)S(1)} reshape(bf16[128,16,507]{2,1,0:T(8,128)(2,1)} %pad_maximum_fusion.2) | data formatting | bytes 4153344 | tf_op jit(solution)/shard_map/reshape;reshape | solution.py:154
  82.7 9.6 %conditional.6 = (bf16[4,32,416]{2,1,0:T(8,128)(2,1)}, bf16[4,32,2496]{2,1,0:T(8,128)(2,1)}, f32[416,2496]{1,0:T(8,128)S(1)}) conditional(s32[]{:T(128)} %convert_element_type.233, () %tuple.55, (bf16[1,4,32,384]{3,2,1,0:T(8,128)(2,1)}, bf16[1,2,16,384]{3,2,1,0:T(8,128)(2,1)S(1)}, bf16[1,1,8,384]{3,2,1,0:T(8,128)(2,1)S(1)}, ...), branch_computations={%region_0.1_spmd, %region_1.2_spmd} | conditional | flops 573085696 | bytes 10971160 | solution.py:210
  87.5 2.0 convolution_convert_fusion
  89.4 2.2 copy.45
  92.3 2.2 %collective-permute-start.43 = (bf16[4,32,2496]{2,1,0:T(8,128)(2,1)}, bf16[4,32,2496]{2,1,0:T(8,128)(2,1)}, u32[]{:S(2)}, u32[]{:S(2)}) collective-permute-start(bf16[4,32,2496]{2,1,0:T(8,128)(2,1)} %get-tuple-element.109), channel_id=1, source_target_pairs={{0,4},{1,5},{2,6},{3,7},{8,12},{9,13},{10,14},{11,15},{16,20},{17,... | collective-permute-start | bytes 1916936 | tf_op jit(solution)/shard_map/ppermute | solution.py:23
  95.5 1.9 collective-permute-start.42
  100.1 2.0 collective-permute-start.46
  102.1 91.8 %conditional.7 = (f32[8112]{0:T(1024)S(1)}) conditional(s32[]{:T(128)} %convert_element_type.233, () %tuple.57, f32[416,2496]{1,0:T(8,128)} %copy-done), branch_computations={%region_2.3_spmd, %region_3.4_spmd} | conditional | flops 2076740 | bytes 83029064 | solution.py:223
  102.1 4.5 %broadcast_multiply_fusion = f32[416,2496]{1,0:T(8,128)} fusion(f32[416,2496]{1,0:T(8,128)} %param.3), kind=kLoop, calls=%fused_computation.7 | loop fusion | flops 1038336 | bytes 8306688 | tf_op jit(solution)/shard_map/cond/branch_1_fun/div | solution.py:215
  106.6 7.2 %reshape.115 = f32[128,8,1014]{2,1,0:T(8,128)} reshape(f32[416,2496]{1,0:T(8,128)} %broadcast_multiply_fusion) | data formatting | bytes 8306688 | tf_op jit(solution)/shard_map/cond/branch_1_fun/reshape | solution.py:215
  113.8 3.1 %split.21 = f32[128,8,502]{2,1,0:T(8,128)} slice(f32[128,8,1014]{2,1,0:T(8,128)} %reshape.115), slice={[0:128], [0:8], [512:1014]} | slice | bytes 4112384 | tf_op jit(solution)/shard_map/cond/branch_1_fun/split | solution.py:72
  116.9 2.3 %dynamic-slice_bitcast_fusion = f32[2,2,2,2,2,2,8,502]{7,6,5,4,3,2,1,0:T(8,128)} fusion(f32[2,2,2,2,2,2,2,8,502]{8,7,6,5,4,3,2,1,0:T(8,128)} %bitcast.247, s32[]{:T(128)S(6)} %select_n.227), kind=kLoop, calls=%fused_computation.10 | loop fusion | bytes 2056196 | tf_op jit(solution)/shard_map/cond/branch_1_fun/jit(dynamic_index_in_dim)/squeeze | solution.py:65
  119.2 3.1 %split.20 = f32[128,8,512]{2,1,0:T(8,128)} slice(f32[128,8,1014]{2,1,0:T(8,128)} %reshape.115), slice={[0:128], [0:8], [0:512]} | slice | bytes 4194304 | tf_op jit(solution)/shard_map/cond/branch_1_fun/split | solution.py:72
  122.3 2.3 %dynamic-slice_bitcast_fusion.1 = f32[2,2,2,2,2,2,8,512]{7,6,5,4,3,2,1,0:T(8,128)} fusion(f32[2,2,2,2,2,2,2,8,512]{8,7,6,5,4,3,2,1,0:T(8,128)} %bitcast.249, s32[]{:T(128)S(6)} %select_n.225), kind=kLoop, calls=%fused_computation.11 | loop fusion | bytes 2097156 | tf_op jit(solution)/shard_map/cond/branch_1_fun/jit(dynamic_index_in_dim)/squeeze | solution.py:65
  125.4 9.0 %collective-permute-done.7 = f32[2,2,2,2,2,2,8,502]{7,6,5,4,3,2,1,0:T(8,128)} collective-permute-done((f32[2,2,2,2,2,2,8,502]{7,6,5,4,3,2,1,0:T(8,128)}, f32[2,2,2,2,2,2,8,502]{7,6,5,4,3,2,1,0:T(8,128)}, u32[]{:S(2)}, u32[]{:S(2)}) %collective-permute-start.7) | collective-permute-done | bytes 1028128 | tf_op jit(solution)/shard_map/cond/branch_1_fun/ppermute | solution.py:66
  142.9 2.0 collective-permute-start.1
  148.2 4.2 %collective-permute-done.1 = f32[2,2,2,2,2,8,512]{6,5,4,3,2,1,0:T(8,128)} collective-permute-done((f32[2,2,2,2,2,8,512]{6,5,4,3,2,1,0:T(8,128)}, f32[2,2,2,2,2,8,512]{6,5,4,3,2,1,0:T(8,128)}, u32[]{:S(2)}, u32[]{:S(2)}) %collective-permute-start.1) | collective-permute-done | bytes 524320 | tf_op jit(solution)/shard_map/cond/branch_1_fun/ppermute | solution.py:66
  154.6 2.4 %collective-permute-start.10 = (f32[2,2,2,8,502]{4,3,2,1,0:T(8,128)S(1)}, f32[2,2,2,8,502]{4,3,2,1,0:T(8,128)S(1)}, u32[]{:S(2)}, u32[]{:S(2)}) collective-permute-start(f32[2,2,2,8,502]{4,3,2,1,0:T(8,128)S(1)} %dynamic-slice_bitcast_fusion.6), channel_id=1, source_target_pairs={{0,16},{8,24},{16,0},{24,8},{32,48},{40,56},{48,32},{56,40},{64,80... | collective-permute-start | bytes 385544 | tf_op jit(solution)/shard_map/cond/branch_1_fun/ppermute | solution.py:66
  157.0 3.1 %collective-permute-done.2 = f32[2,2,2,2,8,512]{5,4,3,2,1,0:T(8,128)S(1)} collective-permute-done((f32[2,2,2,2,8,512]{5,4,3,2,1,0:T(8,128)S(1)}, f32[2,2,2,2,8,512]{5,4,3,2,1,0:T(8,128)S(1)}, u32[]{:S(2)}, u32[]{:S(2)}) %collective-permute-start.2) | collective-permute-done | bytes 262176 | tf_op jit(solution)/shard_map/cond/branch_1_fun/ppermute | solution.py:66
  160.1 4.6 %collective-permute-start.3 = (f32[2,2,2,8,512]{4,3,2,1,0:T(8,128)S(1)}, f32[2,2,2,8,512]{4,3,2,1,0:T(8,128)S(1)}, u32[]{:S(2)}, u32[]{:S(2)}) collective-permute-start(f32[2,2,2,8,512]{4,3,2,1,0:T(8,128)S(1)} %dynamic-slice_bitcast_fusion.7), channel_id=1, source_target_pairs={{0,2},{1,3},{2,0},{3,1},{4,6},{5,7},{6,4},{7,5},{8,10},{9,11},{10,... | collective-permute-start | bytes 393224 | tf_op jit(solution)/shard_map/cond/branch_1_fun/ppermute | solution.py:66
  164.8 2.8 %collective-permute-start.11 = (f32[2,2,8,502]{3,2,1,0:T(8,128)S(1)}, f32[2,2,8,502]{3,2,1,0:T(8,128)S(1)}, u32[]{:S(2)}, u32[]{:S(2)}) collective-permute-start(f32[2,2,8,502]{3,2,1,0:T(8,128)S(1)} %dynamic-slice_bitcast_fusion.8), channel_id=1, source_target_pairs={{0,32},{8,40},{16,48},{24,56},{32,0},{40,8},{48,16},{56,24},{64,96... | collective-permute-start | bytes 192776 | tf_op jit(solution)/shard_map/cond/branch_1_fun/ppermute | solution.py:66
  169.2 3.9 %collective-permute-done.11 = f32[2,2,8,502]{3,2,1,0:T(8,128)S(1)} collective-permute-done((f32[2,2,8,502]{3,2,1,0:T(8,128)S(1)}, f32[2,2,8,502]{3,2,1,0:T(8,128)S(1)}, u32[]{:S(2)}, u32[]{:S(2)}) %collective-permute-start.11) | collective-permute-done | bytes 64288 | tf_op jit(solution)/shard_map/cond/branch_1_fun/ppermute | solution.py:66
  174.0 3.4 %collective-permute-start.4 = (f32[2,2,8,512]{3,2,1,0:T(8,128)S(1)}, f32[2,2,8,512]{3,2,1,0:T(8,128)S(1)}, u32[]{:S(2)}, u32[]{:S(2)}) collective-permute-start(f32[2,2,8,512]{3,2,1,0:T(8,128)S(1)} %dynamic-slice_bitcast_fusion.9), channel_id=1, source_target_pairs={{0,16},{8,24},{16,0},{24,8},{32,48},{40,56},{48,32},{56,40},{64,80... | collective-permute-start | bytes 196616 | tf_op jit(solution)/shard_map/cond/branch_1_fun/ppermute | solution.py:66
  180.0 2.6 %collective-permute-start.5 = (f32[2,8,512]{2,1,0:T(8,128)S(1)}, f32[2,8,512]{2,1,0:T(8,128)S(1)}, u32[]{:S(2)}, u32[]{:S(2)}) collective-permute-start(f32[2,8,512]{2,1,0:T(8,128)S(1)} %dynamic-slice_bitcast_fusion.11), channel_id=1, source_target_pairs={{0,128},{8,136},{16,144},{24,152},{32,160},{40,168},{48,176},{56,1... | collective-permute-start | bytes 98312 | tf_op jit(solution)/shard_map/cond/branch_1_fun/ppermute | solution.py:66
  185.5 3.6 %collective-permute-start.6 = (f32[8,512]{1,0:T(8,128)S(1)}, f32[8,512]{1,0:T(8,128)S(1)}, u32[]{:S(2)}, u32[]{:S(2)}) collective-permute-start(f32[8,512]{1,0:T(8,128)S(1)} %dynamic-slice_bitcast_fusion.13), channel_id=1, source_target_pairs={{0,32},{8,40},{16,48},{24,56},{32,0},{40,8},{48,16},{56,24},{64,96... | collective-permute-start | bytes 49160 | tf_op jit(solution)/shard_map/cond/branch_1_fun/ppermute | solution.py:66
  189.1 4.4 %collective-permute-done.6 = f32[8,512]{1,0:T(8,128)S(1)} collective-permute-done((f32[8,512]{1,0:T(8,128)S(1)}, f32[8,512]{1,0:T(8,128)S(1)}, u32[]{:S(2)}, u32[]{:S(2)}) %collective-permute-start.6) | collective-permute-done | bytes 16416 | tf_op jit(solution)/shard_map/cond/branch_1_fun/ppermute | solution.py:66
  195.4 2.2 %collective-permute-start.47 = (f32[2496]{0:T(1024)S(1)}, f32[2496]{0:T(1024)S(1)}, u32[]{:S(2)}, u32[]{:S(2)}) collective-permute-start(f32[2496]{0:T(1024)S(1)} %add.434), channel_id=1, source_target_pairs={{0,2},{1,3},{2,0},{3,1},{4,6},{5,7},{6,4},{7,5},{8,10},{9,11},{10,... | collective-permute-start | bytes 29960 | tf_op jit(solution)/shard_map/ppermute | solution.py:79
  199.0 2.1 collective-permute-start.49
  201.2 2.1 copy.54
  205.8 2.5 %collective-permute-start.51 = (bf16[2,32,2496]{2,1,0:T(8,128)(2,1)S(1)}, bf16[2,32,2496]{2,1,0:T(8,128)(2,1)S(1)}, u32[]{:S(2)}, u32[]{:S(2)}) collective-permute-start(bf16[2,32,2496]{2,1,0:T(8,128)(2,1)S(1)} %get-tuple-element.195), channel_id=1, source_target_pairs={{1,0},{2,1},{3,2},{5,4},{6,5},{7,6},{9,8},{10,9},{11,10},{13,12},{... | collective-permute-start | bytes 958472 | tf_op jit(solution)/shard_map/ppermute | solution.py:15
  208.3 3.3 %collective-permute-start.50 = (bf16[2,32,2496]{2,1,0:T(8,128)(2,1)S(1)}, bf16[2,32,2496]{2,1,0:T(8,128)(2,1)S(1)}, u32[]{:S(2)}, u32[]{:S(2)}) collective-permute-start(bf16[2,32,2496]{2,1,0:T(8,128)(2,1)S(1)} %get-tuple-element.194), channel_id=1, source_target_pairs={{0,1},{1,2},{2,3},{4,5},{5,6},{6,7},{8,9},{9,10},{10,11},{12,13},{... | collective-permute-start | bytes 958472 | tf_op jit(solution)/shard_map/ppermute | solution.py:12
  211.7 3.1 %collective-permute-done.51 = bf16[2,32,2496]{2,1,0:T(8,128)(2,1)S(1)} collective-permute-done((bf16[2,32,2496]{2,1,0:T(8,128)(2,1)S(1)}, bf16[2,32,2496]{2,1,0:T(8,128)(2,1)S(1)}, u32[]{:S(2)}, u32[]{:S(2)}) %collective-permute-start.51) | collective-permute-done | bytes 319520 | tf_op jit(solution)/shard_map/ppermute | solution.py:15
  214.7 2.5 %collective-permute-done.50 = bf16[2,32,2496]{2,1,0:T(8,128)(2,1)S(1)} collective-permute-done((bf16[2,32,2496]{2,1,0:T(8,128)(2,1)S(1)}, bf16[2,32,2496]{2,1,0:T(8,128)(2,1)S(1)}, u32[]{:S(2)}, u32[]{:S(2)}) %collective-permute-start.50) | collective-permute-done | bytes 319520 | tf_op jit(solution)/shard_map/ppermute | solution.py:12
  (170 shorter events, 55.7 us)
Async XLA Ops:
  1.7 10.3 %collective-permute-start.35 = (bf16[16,253]{1,0:T(8,128)(2,1)S(1)}, bf16[16,253]{1,0:T(8,128)(2,1)S(1)}, u32[]{:S(2)}, u32[]{:S(2)}) collective-permute-start(bf16[16,253]{1,0:T(8,128)(2,1)S(1)} %split.25), channel_id=1, source_target_pairs={{0,128},{8,136},{16,144},{24,152},{32,160},{40,168},{48,176},{56,1... | collective-permute-start | bytes 24296 | tf_op jit(solution)/shard_map/ppermute | solution.py:41
  4.7 9.7 %collective-permute-start.28 = (bf16[16,254]{1,0:T(8,128)(2,1)S(1)}, bf16[16,254]{1,0:T(8,128)(2,1)S(1)}, u32[]{:S(2)}, u32[]{:S(2)}) collective-permute-start(bf16[16,254]{1,0:T(8,128)(2,1)S(1)} %split.24), channel_id=1, source_target_pairs={{0,32},{8,40},{16,48},{24,56},{32,0},{40,8},{48,16},{56,24},{64,96... | collective-permute-start | bytes 24392 | tf_op jit(solution)/shard_map/ppermute | solution.py:41
  12.1 5.3 %collective-permute-start.36 = (bf16[2,16,253]{2,1,0:T(8,128)(2,1)S(1)}, bf16[2,16,253]{2,1,0:T(8,128)(2,1)S(1)}, u32[]{:S(2)}, u32[]{:S(2)}) collective-permute-start(bf16[2,16,253]{2,1,0:T(8,128)(2,1)S(1)} %pad_maximum_fusion.16), channel_id=1, source_target_pairs={{0,2},{1,3},{2,0},{3,1},{4,6},{5,7},{6,4},{7,5},{8,10},{9,11},{10,... | collective-permute-start | bytes 48584 | tf_op jit(solution)/shard_map/ppermute | solution.py:41
  14.5 5.7 %collective-permute-start.29 = (bf16[2,16,254]{2,1,0:T(8,128)(2,1)S(1)}, bf16[2,16,254]{2,1,0:T(8,128)(2,1)S(1)}, u32[]{:S(2)}, u32[]{:S(2)}) collective-permute-start(bf16[2,16,254]{2,1,0:T(8,128)(2,1)S(1)} %pad_maximum_fusion.15), channel_id=1, source_target_pairs={{0,128},{8,136},{16,144},{24,152},{32,160},{40,168},{48,176},{56,1... | collective-permute-start | bytes 48776 | tf_op jit(solution)/shard_map/ppermute | solution.py:41
  17.4 8.1 %collective-permute-start.37 = (bf16[2,2,16,253]{3,2,1,0:T(8,128)(2,1)S(1)}, bf16[2,2,16,253]{3,2,1,0:T(8,128)(2,1)S(1)}, u32[]{:S(2)}, u32[]{:S(2)}) collective-permute-start(bf16[2,2,16,253]{3,2,1,0:T(8,128)(2,1)S(1)} %pad_maximum_fusion.14), channel_id=1, source_target_pairs={{0,32},{8,40},{16,48},{24,56},{32,0},{40,8},{48,16},{56,24},{64,96... | collective-permute-start | bytes 97160 | tf_op jit(solution)/shard_map/ppermute | solution.py:41
  20.2 6.8 %collective-permute-start.30 = (bf16[2,2,16,254]{3,2,1,0:T(8,128)(2,1)S(1)}, bf16[2,2,16,254]{3,2,1,0:T(8,128)(2,1)S(1)}, u32[]{:S(2)}, u32[]{:S(2)}) collective-permute-start(bf16[2,2,16,254]{3,2,1,0:T(8,128)(2,1)S(1)} %pad_maximum_fusion.13), channel_id=1, source_target_pairs={{0,16},{8,24},{16,0},{24,8},{32,48},{40,56},{48,32},{56,40},{64,80... | collective-permute-start | bytes 97544 | tf_op jit(solution)/shard_map/ppermute | solution.py:41
  25.6 6.0 %collective-permute-start.38 = (bf16[2,2,2,16,253]{4,3,2,1,0:T(8,128)(2,1)S(1)}, bf16[2,2,2,16,253]{4,3,2,1,0:T(8,128)(2,1)S(1)}, u32[]{:S(2)}, u32[]{:S(2)}) collective-permute-start(bf16[2,2,2,16,253]{4,3,2,1,0:T(8,128)(2,1)S(1)} %pad_maximum_fusion.12), channel_id=1, source_target_pairs={{0,16},{8,24},{16,0},{24,8},{32,48},{40,56},{48,32},{56,40},{64,80... | collective-permute-start | bytes 194312 | tf_op jit(solution)/shard_map/ppermute | solution.py:41
  27.1 6.3 %collective-permute-start.31 = (bf16[2,2,2,16,254]{4,3,2,1,0:T(8,128)(2,1)S(1)}, bf16[2,2,2,16,254]{4,3,2,1,0:T(8,128)(2,1)S(1)}, u32[]{:S(2)}, u32[]{:S(2)}) collective-permute-start(bf16[2,2,2,16,254]{4,3,2,1,0:T(8,128)(2,1)S(1)} %pad_maximum_fusion.11), channel_id=1, source_target_pairs={{0,2},{1,3},{2,0},{3,1},{4,6},{5,7},{6,4},{7,5},{8,10},{9,11},{10,... | collective-permute-start | bytes 195080 | tf_op jit(solution)/shard_map/ppermute | solution.py:41
  31.6 5.1 %collective-permute-start.39 = (bf16[2,2,2,2,16,253]{5,4,3,2,1,0:T(8,128)(2,1)S(1)}, bf16[2,2,2,2,16,253]{5,4,3,2,1,0:T(8,128)(2,1)S(1)}, u32[]{:S(2)}, u32[]{:S(2)}) collective-permute-start(bf16[2,2,2,2,16,253]{5,4,3,2,1,0:T(8,128)(2,1)S(1)} %pad_maximum_fusion.10), channel_id=1, source_target_pairs={{0,1},{1,0},{2,3},{3,2},{4,5},{5,4},{6,7},{7,6},{8,9},{9,8},{10,11... | collective-permute-start | bytes 388616 | tf_op jit(solution)/shard_map/ppermute | solution.py:41
  33.5 6.4 %collective-permute-start.32 = (bf16[2,2,2,2,16,254]{5,4,3,2,1,0:T(8,128)(2,1)S(1)}, bf16[2,2,2,2,16,254]{5,4,3,2,1,0:T(8,128)(2,1)S(1)}, u32[]{:S(2)}, u32[]{:S(2)}) collective-permute-start(bf16[2,2,2,2,16,254]{5,4,3,2,1,0:T(8,128)(2,1)S(1)} %pad_maximum_fusion.9), channel_id=1, source_target_pairs={{0,64},{8,72},{16,80},{24,88},{32,96},{40,104},{48,112},{56,120},{... | collective-permute-start | bytes 390152 | tf_op jit(solution)/shard_map/ppermute | solution.py:41
  36.8 6.6 %collective-permute-start.40 = (bf16[2,2,2,2,2,16,253]{6,5,4,3,2,1,0:T(8,128)(2,1)S(1)}, bf16[2,2,2,2,2,16,253]{6,5,4,3,2,1,0:T(8,128)(2,1)S(1)}, u32[]{:S(2)}, u32[]{:S(2)}) collective-permute-start(bf16[2,2,2,2,2,16,253]{6,5,4,3,2,1,0:T(8,128)(2,1)S(1)} %pad_maximum_fusion.8), channel_id=1, source_target_pairs={{0,64},{8,72},{16,80},{24,88},{32,96},{40,104},{48,112},{56,120},{... | collective-permute-start | bytes 777224 | tf_op jit(solution)/shard_map/ppermute | solution.py:41
  40.0 9.3 %collective-permute-start.33 = (bf16[2,2,2,2,2,16,254]{6,5,4,3,2,1,0:T(8,128)(2,1)S(1)}, bf16[2,2,2,2,2,16,254]{6,5,4,3,2,1,0:T(8,128)(2,1)S(1)}, u32[]{:S(2)}, u32[]{:S(2)}) collective-permute-start(bf16[2,2,2,2,2,16,254]{6,5,4,3,2,1,0:T(8,128)(2,1)S(1)} %pad_maximum_fusion.7), channel_id=1, source_target_pairs={{0,8},{8,0},{16,24},{24,16},{32,40},{40,32},{48,56},{56,48},{64,72... | collective-permute-start | bytes 780296 | tf_op jit(solution)/shard_map/ppermute | solution.py:41
  43.5 27.7 %collective-permute-start.41 = (bf16[2,2,2,2,2,2,16,253]{7,6,5,4,3,2,1,0:T(8,128)(2,1)S(1)}, bf16[2,2,2,2,2,2,16,253]{7,6,5,4,3,2,1,0:T(8,128)(2,1)}, u32[]{:S(2)}, u32[]{:S(2)}) collective-permute-start(bf16[2,2,2,2,2,2,16,253]{7,6,5,4,3,2,1,0:T(8,128)(2,1)S(1)} %pad_maximum_fusion.6), channel_id=1, source_target_pairs={{0,8},{8,0},{16,24},{24,16},{32,40},{40,32},{48,56},{56,48},{64,72... | collective-permute-start | bytes 1554440 | tf_op jit(solution)/shard_map/ppermute | solution.py:41
  49.3 23.0 %copy-start.13 = (bf16[1,2,2,2,2,2,16,254]{7,6,5,4,3,2,1,0:T(8,128)(2,1)}, bf16[1,2,2,2,2,2,16,254]{7,6,5,4,3,2,1,0:T(8,128)(2,1)S(1)}, u32[]{:S(2)}) copy-start(bf16[1,2,2,2,2,2,16,254]{7,6,5,4,3,2,1,0:T(8,128)(2,1)S(1)} %get-tuple-element.198) | copy-start | bytes 780292
  49.4 23.0 %copy-start.15 = (bf16[1,2,2,2,2,2,16,254]{7,6,5,4,3,2,1,0:T(8,128)(2,1)}, bf16[1,2,2,2,2,2,16,254]{7,6,5,4,3,2,1,0:T(8,128)(2,1)S(1)}, u32[]{:S(2)}) copy-start(bf16[1,2,2,2,2,2,16,254]{7,6,5,4,3,2,1,0:T(8,128)(2,1)S(1)} %get-tuple-element.199) | copy-start | bytes 780292
  50.4 22.4 %collective-permute-start.34 = (bf16[2,2,2,2,2,2,16,254]{7,6,5,4,3,2,1,0:T(8,128)(2,1)}, bf16[2,2,2,2,2,2,16,254]{7,6,5,4,3,2,1,0:T(8,128)(2,1)}, u32[]{:S(2)}, u32[]{:S(2)}) collective-permute-start(bf16[2,2,2,2,2,2,16,254]{7,6,5,4,3,2,1,0:T(8,128)(2,1)} %pad_maximum_fusion.5), channel_id=1, source_target_pairs={{0,1},{1,0},{2,3},{3,2},{4,5},{5,4},{6,7},{7,6},{8,9},{9,8},{10,11... | collective-permute-start | bytes 1560584 | tf_op jit(solution)/shard_map/ppermute | solution.py:41
  51.6 45.8 %collective-permute-start.45 = (bf16[2,32,2496]{2,1,0:T(8,128)(2,1)}, bf16[2,32,2496]{2,1,0:T(8,128)(2,1)}, u32[]{:S(2)}, u32[]{:S(2)}) collective-permute-start(bf16[2,32,2496]{2,1,0:T(8,128)(2,1)} %get-tuple-element.197), channel_id=1, source_target_pairs={{1,0},{2,1},{3,2},{5,4},{6,5},{7,6},{9,8},{10,9},{11,10},{13,12},{... | collective-permute-start | bytes 958472 | tf_op jit(solution)/shard_map/ppermute | solution.py:15
  55.2 42.2 %collective-permute-start.44 = (bf16[2,32,2496]{2,1,0:T(8,128)(2,1)}, bf16[2,32,2496]{2,1,0:T(8,128)(2,1)}, u32[]{:S(2)}, u32[]{:S(2)}) collective-permute-start(bf16[2,32,2496]{2,1,0:T(8,128)(2,1)} %get-tuple-element.196), channel_id=1, source_target_pairs={{0,1},{1,2},{2,3},{4,5},{5,6},{6,7},{8,9},{9,10},{10,11},{12,13},{... | collective-permute-start | bytes 958472 | tf_op jit(solution)/shard_map/ppermute | solution.py:12
  77.4 5.3 %copy-start.23 = (bf16[1,1,8,384]{3,2,1,0:T(8,128)(2,1)S(1)}, bf16[1,1,8,384]{3,2,1,0:T(8,128)(2,1)}, u32[]{:S(2)}) copy-start(bf16[1,1,8,384]{3,2,1,0:T(8,128)(2,1)} %param.26) | copy-start | bytes 18436
  92.3 9.8 %collective-permute-start.43 = (bf16[4,32,2496]{2,1,0:T(8,128)(2,1)}, bf16[4,32,2496]{2,1,0:T(8,128)(2,1)}, u32[]{:S(2)}, u32[]{:S(2)}) collective-permute-start(bf16[4,32,2496]{2,1,0:T(8,128)(2,1)} %get-tuple-element.109), channel_id=1, source_target_pairs={{0,4},{1,5},{2,6},{3,7},{8,12},{9,13},{10,14},{11,15},{16,20},{17,... | collective-permute-start | bytes 1916936 | tf_op jit(solution)/shard_map/ppermute | solution.py:23
  95.5 6.7 %collective-permute-start.42 = (bf16[4,32,416]{2,1,0:T(8,128)(2,1)}, bf16[4,32,416]{2,1,0:T(8,128)(2,1)}, u32[]{:S(2)}, u32[]{:S(2)}) collective-permute-start(bf16[4,32,416]{2,1,0:T(8,128)(2,1)} %get-tuple-element.238), channel_id=1, source_target_pairs={{0,4},{1,5},{2,6},{3,7},{8,12},{9,13},{10,14},{11,15},{16,20},{17,... | collective-permute-start | bytes 319496 | tf_op jit(solution)/shard_map/ppermute | solution.py:23
  100.1 95.3 %collective-permute-start.46 = (f32[2496]{0:T(1024)S(1)}, f32[2496]{0:T(1024)S(1)}, u32[]{:S(2)}, u32[]{:S(2)}) collective-permute-start(f32[2496]{0:T(1024)S(1)} %get-tuple-element.118), channel_id=1, source_target_pairs={{0,1},{1,0},{2,3},{3,2},{4,5},{5,4},{6,7},{7,6},{8,9},{9,8},{10,11... | collective-permute-start | bytes 29960 | tf_op jit(solution)/shard_map/ppermute | solution.py:79
  119.2 15.1 %collective-permute-start.7 = (f32[2,2,2,2,2,2,8,502]{7,6,5,4,3,2,1,0:T(8,128)}, f32[2,2,2,2,2,2,8,502]{7,6,5,4,3,2,1,0:T(8,128)}, u32[]{:S(2)}, u32[]{:S(2)}) collective-permute-start(f32[2,2,2,2,2,2,8,502]{7,6,5,4,3,2,1,0:T(8,128)} %dynamic-slice_bitcast_fusion), channel_id=1, source_target_pairs={{0,8},{8,0},{16,24},{24,16},{32,40},{40,32},{48,56},{56,48},{64,72... | collective-permute-start | bytes 3084296 | tf_op jit(solution)/shard_map/cond/branch_1_fun/ppermute | solution.py:66
  124.6 15.1 %collective-permute-start = (f32[2,2,2,2,2,2,8,512]{7,6,5,4,3,2,1,0:T(8,128)}, f32[2,2,2,2,2,2,8,512]{7,6,5,4,3,2,1,0:T(8,128)}, u32[]{:S(2)}, u32[]{:S(2)}) collective-permute-start(f32[2,2,2,2,2,2,8,512]{7,6,5,4,3,2,1,0:T(8,128)} %dynamic-slice_bitcast_fusion.1), channel_id=1, source_target_pairs={{0,1},{1,0},{2,3},{3,2},{4,5},{5,4},{6,7},{7,6},{8,9},{9,8},{10,11... | collective-permute-start | bytes 3145736 | tf_op jit(solution)/shard_map/cond/branch_1_fun/ppermute | solution.py:66
  134.3 5.4 %copy-start.3 = (f32[128,8,512]{2,1,0:T(8,128)S(1)}, f32[128,8,512]{2,1,0:T(8,128)}, u32[]{:S(2)}) copy-start(f32[128,8,512]{2,1,0:T(8,128)} %split.20) | copy-start | bytes 6291460 | tf_op jit(solution)/shard_map/cond
  137.2 9.5 %collective-permute-start.8 = (f32[2,2,2,2,2,8,502]{6,5,4,3,2,1,0:T(8,128)}, f32[2,2,2,2,2,8,502]{6,5,4,3,2,1,0:T(8,128)}, u32[]{:S(2)}, u32[]{:S(2)}) collective-permute-start(f32[2,2,2,2,2,8,502]{6,5,4,3,2,1,0:T(8,128)} %dynamic-slice_bitcast_fusion.2), channel_id=1, source_target_pairs={{0,64},{8,72},{16,80},{24,88},{32,96},{40,104},{48,112},{56,120},{... | collective-permute-start | bytes 1542152 | tf_op jit(solution)/shard_map/cond/branch_1_fun/ppermute | solution.py:66
  142.9 9.5 %collective-permute-start.1 = (f32[2,2,2,2,2,8,512]{6,5,4,3,2,1,0:T(8,128)}, f32[2,2,2,2,2,8,512]{6,5,4,3,2,1,0:T(8,128)}, u32[]{:S(2)}, u32[]{:S(2)}) collective-permute-start(f32[2,2,2,2,2,8,512]{6,5,4,3,2,1,0:T(8,128)} %dynamic-slice_bitcast_fusion.3), channel_id=1, source_target_pairs={{0,8},{8,0},{16,24},{24,16},{32,40},{40,32},{48,56},{56,48},{64,72... | collective-permute-start | bytes 1572872 | tf_op jit(solution)/shard_map/cond/branch_1_fun/ppermute | solution.py:66
  145.0 7.5 %copy-start.8 = (f32[2,2,2,2,2,2,8,512]{7,6,5,4,3,2,1,0:T(8,128)S(1)}, f32[2,2,2,2,2,2,8,512]{7,6,5,4,3,2,1,0:T(8,128)}, u32[]{:S(2)}) copy-start(f32[2,2,2,2,2,2,8,512]{7,6,5,4,3,2,1,0:T(8,128)} %copy-done.7) | copy-start | bytes 3145732 | tf_op jit(solution)/shard_map/cond
  148.0 6.5 %collective-permute-start.9 = (f32[2,2,2,2,8,502]{5,4,3,2,1,0:T(8,128)S(1)}, f32[2,2,2,2,8,502]{5,4,3,2,1,0:T(8,128)S(1)}, u32[]{:S(2)}, u32[]{:S(2)}) collective-permute-start(f32[2,2,2,2,8,502]{5,4,3,2,1,0:T(8,128)S(1)} %dynamic-slice_bitcast_fusion.4), channel_id=1, source_target_pairs={{0,1},{1,0},{2,3},{3,2},{4,5},{5,4},{6,7},{7,6},{8,9},{9,8},{10,11... | collective-permute-start | bytes 771080 | tf_op jit(solution)/shard_map/cond/branch_1_fun/ppermute | solution.py:66
  153.6 6.5 %collective-permute-start.2 = (f32[2,2,2,2,8,512]{5,4,3,2,1,0:T(8,128)S(1)}, f32[2,2,2,2,8,512]{5,4,3,2,1,0:T(8,128)S(1)}, u32[]{:S(2)}, u32[]{:S(2)}) collective-permute-start(f32[2,2,2,2,8,512]{5,4,3,2,1,0:T(8,128)S(1)} %dynamic-slice_bitcast_fusion.5), channel_id=1, source_target_pairs={{0,64},{8,72},{16,80},{24,88},{32,96},{40,104},{48,112},{56,120},{... | collective-permute-start | bytes 786440 | tf_op jit(solution)/shard_map/cond/branch_1_fun/ppermute | solution.py:66
  154.6 10.2 %collective-permute-start.10 = (f32[2,2,2,8,502]{4,3,2,1,0:T(8,128)S(1)}, f32[2,2,2,8,502]{4,3,2,1,0:T(8,128)S(1)}, u32[]{:S(2)}, u32[]{:S(2)}) collective-permute-start(f32[2,2,2,8,502]{4,3,2,1,0:T(8,128)S(1)} %dynamic-slice_bitcast_fusion.6), channel_id=1, source_target_pairs={{0,16},{8,24},{16,0},{24,8},{32,48},{40,56},{48,32},{56,40},{64,80... | collective-permute-start | bytes 385544 | tf_op jit(solution)/shard_map/cond/branch_1_fun/ppermute | solution.py:66
  160.1 9.0 %collective-permute-start.3 = (f32[2,2,2,8,512]{4,3,2,1,0:T(8,128)S(1)}, f32[2,2,2,8,512]{4,3,2,1,0:T(8,128)S(1)}, u32[]{:S(2)}, u32[]{:S(2)}) collective-permute-start(f32[2,2,2,8,512]{4,3,2,1,0:T(8,128)S(1)} %dynamic-slice_bitcast_fusion.7), channel_id=1, source_target_pairs={{0,2},{1,3},{2,0},{3,1},{4,6},{5,7},{6,4},{7,5},{8,10},{9,11},{10,... | collective-permute-start | bytes 393224 | tf_op jit(solution)/shard_map/cond/branch_1_fun/ppermute | solution.py:66
  164.8 8.3 %collective-permute-start.11 = (f32[2,2,8,502]{3,2,1,0:T(8,128)S(1)}, f32[2,2,8,502]{3,2,1,0:T(8,128)S(1)}, u32[]{:S(2)}, u32[]{:S(2)}) collective-permute-start(f32[2,2,8,502]{3,2,1,0:T(8,128)S(1)} %dynamic-slice_bitcast_fusion.8), channel_id=1, source_target_pairs={{0,32},{8,40},{16,48},{24,56},{32,0},{40,8},{48,16},{56,24},{64,96... | collective-permute-start | bytes 192776 | tf_op jit(solution)/shard_map/cond/branch_1_fun/ppermute | solution.py:66
  173.1 5.5 %collective-permute-start.12 = (f32[2,8,502]{2,1,0:T(8,128)S(1)}, f32[2,8,502]{2,1,0:T(8,128)S(1)}, u32[]{:S(2)}, u32[]{:S(2)}) collective-permute-start(f32[2,8,502]{2,1,0:T(8,128)S(1)} %dynamic-slice_bitcast_fusion.10), channel_id=1, source_target_pairs={{0,2},{1,3},{2,0},{3,1},{4,6},{5,7},{6,4},{7,5},{8,10},{9,11},{10,... | collective-permute-start | bytes 96392 | tf_op jit(solution)/shard_map/cond/branch_1_fun/ppermute | solution.py:66
  174.0 5.9 %collective-permute-start.4 = (f32[2,2,8,512]{3,2,1,0:T(8,128)S(1)}, f32[2,2,8,512]{3,2,1,0:T(8,128)S(1)}, u32[]{:S(2)}, u32[]{:S(2)}) collective-permute-start(f32[2,2,8,512]{3,2,1,0:T(8,128)S(1)} %dynamic-slice_bitcast_fusion.9), channel_id=1, source_target_pairs={{0,16},{8,24},{16,0},{24,8},{32,48},{40,56},{48,32},{56,40},{64,80... | collective-permute-start | bytes 196616 | tf_op jit(solution)/shard_map/cond/branch_1_fun/ppermute | solution.py:66
  180.0 5.5 %collective-permute-start.5 = (f32[2,8,512]{2,1,0:T(8,128)S(1)}, f32[2,8,512]{2,1,0:T(8,128)S(1)}, u32[]{:S(2)}, u32[]{:S(2)}) collective-permute-start(f32[2,8,512]{2,1,0:T(8,128)S(1)} %dynamic-slice_bitcast_fusion.11), channel_id=1, source_target_pairs={{0,128},{8,136},{16,144},{24,152},{32,160},{40,168},{48,176},{56,1... | collective-permute-start | bytes 98312 | tf_op jit(solution)/shard_map/cond/branch_1_fun/ppermute | solution.py:66
  182.5 6.6 %collective-permute-start.13 = (f32[8,502]{1,0:T(8,128)S(1)}, f32[8,502]{1,0:T(8,128)S(1)}, u32[]{:S(2)}, u32[]{:S(2)}) collective-permute-start(f32[8,502]{1,0:T(8,128)S(1)} %dynamic-slice_bitcast_fusion.12), channel_id=1, source_target_pairs={{0,128},{8,136},{16,144},{24,152},{32,160},{40,168},{48,176},{56,1... | collective-permute-start | bytes 48200 | tf_op jit(solution)/shard_map/cond/branch_1_fun/ppermute | solution.py:66
  185.5 8.0 %collective-permute-start.6 = (f32[8,512]{1,0:T(8,128)S(1)}, f32[8,512]{1,0:T(8,128)S(1)}, u32[]{:S(2)}, u32[]{:S(2)}) collective-permute-start(f32[8,512]{1,0:T(8,128)S(1)} %dynamic-slice_bitcast_fusion.13), channel_id=1, source_target_pairs={{0,32},{8,40},{16,48},{24,56},{32,0},{40,8},{48,16},{56,24},{64,96... | collective-permute-start | bytes 49160 | tf_op jit(solution)/shard_map/cond/branch_1_fun/ppermute | solution.py:66
  194.0 9.3 %copy-start.21 = (f32[8112]{0:T(1024)}, f32[8112]{0:T(1024)S(1)}, u32[]{:S(2)}) copy-start(f32[8112]{0:T(1024)S(1)} %get-tuple-element.240) | copy-start | bytes 97348
  195.2 3.8 %collective-permute-start.48 = (f32[2496]{0:T(1024)S(1)}, f32[2496]{0:T(1024)S(1)}, u32[]{:S(2)}, u32[]{:S(2)}) collective-permute-start(f32[2496]{0:T(1024)S(1)} %multiply_reduce_fusion), channel_id=1, source_target_pairs={{0,1},{1,0},{2,3},{3,2},{4,5},{5,4},{6,7},{7,6},{8,9},{9,8},{10,11... | collective-permute-start | bytes 29960 | tf_op jit(solution)/shard_map/ppermute | solution.py:79
  195.4 10.3 %collective-permute-start.47 = (f32[2496]{0:T(1024)S(1)}, f32[2496]{0:T(1024)S(1)}, u32[]{:S(2)}, u32[]{:S(2)}) collective-permute-start(f32[2496]{0:T(1024)S(1)} %add.434), channel_id=1, source_target_pairs={{0,2},{1,3},{2,0},{3,1},{4,6},{5,7},{6,4},{7,5},{8,10},{9,11},{10,... | collective-permute-start | bytes 29960 | tf_op jit(solution)/shard_map/ppermute | solution.py:79
  199.0 6.6 %collective-permute-start.49 = (f32[2496]{0:T(1024)S(1)}, f32[2496]{0:T(1024)S(1)}, u32[]{:S(2)}, u32[]{:S(2)}) collective-permute-start(f32[2496]{0:T(1024)S(1)} %add.435), channel_id=1, source_target_pairs={{0,2},{1,3},{2,0},{3,1},{4,6},{5,7},{6,4},{7,5},{8,10},{9,11},{10,... | collective-permute-start | bytes 29960 | tf_op jit(solution)/shard_map/ppermute | solution.py:79
  205.7 5.9 %copy-start.6 = (bf16[4,32,2496]{2,1,0:T(8,128)(2,1)}, bf16[4,32,2496]{2,1,0:T(8,128)(2,1)S(1)}, u32[]{:S(2)}) copy-start(bf16[4,32,2496]{2,1,0:T(8,128)(2,1)S(1)} %get-tuple-element.242) | copy-start | bytes 1916932
  205.8 9.0 %collective-permute-start.51 = (bf16[2,32,2496]{2,1,0:T(8,128)(2,1)S(1)}, bf16[2,32,2496]{2,1,0:T(8,128)(2,1)S(1)}, u32[]{:S(2)}, u32[]{:S(2)}) collective-permute-start(bf16[2,32,2496]{2,1,0:T(8,128)(2,1)S(1)} %get-tuple-element.195), channel_id=1, source_target_pairs={{1,0},{2,1},{3,2},{5,4},{6,5},{7,6},{9,8},{10,9},{11,10},{13,12},{... | collective-permute-start | bytes 958472 | tf_op jit(solution)/shard_map/ppermute | solution.py:15
  208.3 9.0 %collective-permute-start.50 = (bf16[2,32,2496]{2,1,0:T(8,128)(2,1)S(1)}, bf16[2,32,2496]{2,1,0:T(8,128)(2,1)S(1)}, u32[]{:S(2)}, u32[]{:S(2)}) collective-permute-start(bf16[2,32,2496]{2,1,0:T(8,128)(2,1)S(1)} %get-tuple-element.194), channel_id=1, source_target_pairs={{0,1},{1,2},{2,3},{4,5},{5,6},{6,7},{8,9},{9,10},{10,11},{12,13},{... | collective-permute-start | bytes 958472 | tf_op jit(solution)/shard_map/ppermute | solution.py:12
  211.6 6.9 %copy-start.5 = (bf16[1,1,4,32,2496]{4,3,2,1,0:T(8,128)(2,1)S(1)}, bf16[1,1,4,32,2496]{4,3,2,1,0:T(8,128)(2,1)}, u32[]{:S(2)}) copy-start(bf16[1,1,4,32,2496]{4,3,2,1,0:T(8,128)(2,1)} %param.23) | copy-start | bytes 1916932
  211.7 6.9 %copy-start.18 = (f32[25,2496]{1,0:T(8,128)S(1)}, f32[25,2496]{1,0:T(8,128)}, u32[]{:S(2)}) copy-start(f32[25,2496]{1,0:T(8,128)} %copy-done.17) | copy-start | bytes 748804
  211.7 6.9 %copy-start.20 = (bf16[1,4,32,416]{3,2,1,0:T(8,128)(2,1)S(1)}, bf16[1,4,32,416]{3,2,1,0:T(8,128)(2,1)}, u32[]{:S(2)}) copy-start(bf16[1,4,32,416]{3,2,1,0:T(8,128)(2,1)} %param.22) | copy-start | bytes 319492
  (9 other events, 24.7 us)
where the time goes:
time: 222 us; the launch traced here: 220 us
  starting transfers between devices  85.4 us (38%)
  waiting for transfers between devices  64.7 us (29%)
  local copies, waits for them, and re-layouts  37.6 us (17%)
  other arithmetic  24.9 us (11%)
  matrix products  4.03 us (2%)
    ppermute x14, waiting for transfers between devices, scatter_chunks(): buf = mine + lax.ppermute(other, axis, swap_pairs(axis, j))  34.6 us
    ppermute x14, starting transfers between devices, scatter_chunks(): buf = mine + lax.ppermute(other, axis, swap_pairs(axis, j))  25.4 us
    ppermute x14, starting transfers between devices, gather_chunks(): recv = lax.ppermute(buf, axis, swap_pairs(axis, j))  24 us
    ppermute x14, waiting for transfers between devices, gather_chunks(): recv = lax.ppermute(buf, axis, swap_pairs(axis, j))  23.1 us
    ppermute x2, starting transfers between devices, extended_2(): lax.ppermute(lax.slice_in_dim(block, block.shape[dim] - width, None, axis...  19.3 us
    reshape x1, local copies, waits for them, and re-layouts, spread(): flat_term = (term / images).reshape(shards, 8, -1)  7.15 us
    squeeze x14, local copies, waits for them, and re-layouts, scatter_chunks(): other = lax.dynamic_index_in_dim(buf, 1 - high, at, keepdims=False)  6.55 us
    ppermute x4, starting transfers between devices, rows_sum(): lax.ppermute(v, 'rows', swap_pairs('rows', j))  6.51 us
  transfers between devices with their start and end apart: 38, of which 23 were waited for; matrix products, arithmetic and copies ran while one was open for 28% of the time, Pallas kernels for 0%

commit v1 on v0

--- a/solution.py
+++ b/solution.py
@@ -75,9 +75,10 @@
 
 
 def rows_sum(values):
+    total = jnp.stack(values)
     for j in range(lax.axis_size("rows").bit_length() - 1):
-        values = tuple(v + lax.ppermute(v, "rows", swap_pairs("rows", j)) for v in values)
-    return values
+        total = total + lax.ppermute(total, "rows", swap_pairs("rows", j))
+    return tuple(total)
 
 
 GATHER_ORDERS = (
@@ -182,32 +183,26 @@
 
     dwo, act, pool_part = lax.cond(segment == 1, pool_branch, still_branch)
 
-    def head_branch():
+    def lead_branch():
         inner = grad_p6[0].astype(jnp.float32) + up_two(grad_p7[0].astype(jnp.float32)) / 4.0
         g = (grad_p5[0].astype(jnp.float32) + up_two(inner) / 4.0).astype(jnp.bfloat16)
-        grad_out = jnp.dot(
+        return jnp.dot(
             g.reshape(cells_here, -1), lateral.T, preferred_element_type=jnp.float32
         ).astype(jnp.bfloat16)
-        grad_proj = jnp.dot(grad_out, weight, preferred_element_type=jnp.float32).astype(
-            jnp.bfloat16
-        )
-        term = jnp.dot(
-            grad_out.T, held.reshape(cells_here, wide), preferred_element_type=jnp.float32
-        )
-        return (
-            grad_out.reshape(rows_here, cols, cin),
-            grad_proj.reshape(rows_here, cols, wide),
-            term,
-        )
+
+    def lead_still():
+        return jnp.zeros((cells_here, cin), jnp.bfloat16)
+
+    grad_out = lax.cond(segment == 0, lead_branch, lead_still)
+
+    def head_branch():
+        return jnp.dot(grad_out, weight, preferred_element_type=jnp.float32).astype(jnp.bfloat16)
 
     def head_still():
-        return (
-            jnp.zeros((rows_here, cols, cin), jnp.bfloat16),
-            jnp.zeros((rows_here, cols, wide), jnp.bfloat16),
-            jnp.zeros((cin, wide), jnp.float32),
-        )
-
-    grad_top, grad_proj, head_term = lax.cond(segment == 0, head_branch, head_still)
+        return jnp.zeros((cells_here, wide), jnp.bfloat16)
+
+    grad_proj = lax.cond(segment == 0, head_branch, head_still).reshape(rows_here, cols, wide)
+    grad_top = grad_out.reshape(rows_here, cols, cin)
     shards = lax.axis_size("dp") * row_count
     chunk = cin * wide // shards
 
@@ -219,7 +214,17 @@
         return jnp.zeros((chunk,), jnp.float32)
 
     sent_top, sent_mid = passed_along((grad_top, grad_proj), "segment", 1)
-    sent_top, sent_mid, head_term = lax.optimization_barrier((sent_top, sent_mid, head_term))
+    sent_top, sent_mid, grad_out = lax.optimization_barrier((sent_top, sent_mid, grad_out))
+
+    def term_branch():
+        return jnp.dot(
+            grad_out.T, held.reshape(cells_here, wide), preferred_element_type=jnp.float32
+        )
+
+    def term_still():
+        return jnp.zeros((cin, wide), jnp.float32)
+
+    head_term = lax.cond(segment == 0, term_branch, term_still)
     head_share = lax.cond(segment == 0, spread, spread_still, head_term)
     head_share, sent_top, sent_mid, act = lax.optimization_barrier(
         (head_share, sent_top, sent_mid, act)

time: 222 us -> 222 us (level)
  loops' own time: 1.48 us -> 14.5 us
  starting transfers between devices: 85.4 us -> 74.1 us
  local copies, waits for them, and re-layouts: 37.6 us -> 34.1 us
  matrix products: 4.03 us -> 6.54 us
  waiting for transfers between devices: 64.7 us -> 62.4 us
    ppermute x2, starting transfers between devices: 19.3 us -> 4.3 us  [extended_2(): lax.ppermute(lax.slice_in_dim(block, block.shape[dim] - width, None, axis...]
    another operation x0 -> x2, loops' own time: none -> 13 us  [the longest x1 13 us: body(): grad_out = lax.cond(segment == 0, lead_branch, lead_still)]
    ppermute x14, starting transfers between devices: 25.4 us -> 29.5 us  [scatter_chunks(): buf = mine + lax.ppermute(other, axis, swap_pairs(axis, j))]
    ppermute x14, waiting for transfers between devices: 34.6 us -> 30.5 us  [scatter_chunks(): buf = mine + lax.ppermute(other, axis, swap_pairs(axis, j))]
    dot_general x2, matrix products: 2.08 us -> 4.53 us  [the longest x1 3.6 us: term_branch(): jnp.dot(grad_out.T, held.reshape(cells_here, wide), preferred_element_typ...]
    ppermute x4 -> x2, starting transfers between devices: 6.51 us -> 4.95 us  [rows_sum(): total = total + lax.ppermute(total, 'rows', swap_pairs('rows', j))]
  transfers between devices with their start and end apart: 38 -> 36, of which waited for: 23 -> 22; matrix products, arithmetic and copies ran while one was open for 28% -> 18% of each run, Pallas kernels for 0% -> 0%
where the time goes in v1:
time: 222 us; the launch traced here: 219 us
  starting transfers between devices  74.1 us (33%)
  waiting for transfers between devices  62.4 us (28%)
  local copies, waits for them, and re-layouts  34.1 us (15%)
  other arithmetic  25.1 us (11%)
  loops' own time  14.5 us (7%)
  matrix products  6.54 us (3%)
  between operations  2.27 us (1%)
    ppermute x14, waiting for transfers between devices, scatter_chunks(): buf = mine + lax.ppermute(other, axis, swap_pairs(axis, j))  30.5 us
    ppermute x14, starting transfers between devices, scatter_chunks(): buf = mine + lax.ppermute(other, axis, swap_pairs(axis, j))  29.5 us
    ppermute x14, starting transfers between devices, gather_chunks(): recv = lax.ppermute(buf, axis, swap_pairs(axis, j))  24 us
    ppermute x14, waiting for transfers between devices, gather_chunks(): recv = lax.ppermute(buf, axis, swap_pairs(axis, j))  23.1 us
    another operation x1, loops' own time, body(): grad_out = lax.cond(segment == 0, lead_branch, lead_still)  13 us
    ppermute x2, starting transfers between devices, extended_2(): lax.ppermute(lax.slice_in_dim(block, 0, width, axis=dim), axis, backward)  8.13 us
    reshape x1, local copies, waits for them, and re-layouts, spread(): flat_term = (term / images).reshape(shards, 8, -1)  7.15 us
    squeeze x14, local copies, waits for them, and re-layouts, scatter_chunks(): other = lax.dynamic_index_in_dim(buf, 1 - high, at, keepdims=False)  6.55 us
  transfers between devices with their start and end apart: 36, of which 22 were waited for; matrix products, arithmetic and copies ran while one was open for 18% of the time, Pallas kernels for 0%

profile of v1, /device:TPU:8, one launch (start us, length us, event | category | flops | bytes accessed | tf_op | source)
XLA Modules:
  0.0 219.1 jit_solution(621846993313152160)
XLA Ops:
  1.7 3.0 %collective-permute-start.36 = (bf16[16,253]{1,0:T(8,128)(2,1)S(1)}, bf16[16,253]{1,0:T(8,128)(2,1)S(1)}, u32[]{:S(2)}, u32[]{:S(2)}) collective-permute-start(bf16[16,253]{1,0:T(8,128)(2,1)S(1)} %split.25), channel_id=1, source_target_pairs={{0,128},{8,136},{16,144},{24,152},{32,160},{40,168},{48,176},{56,1... | collective-permute-start | bytes 24296 | tf_op jit(solution)/shard_map/ppermute | solution.py:41
  4.7 7.2 %collective-permute-start.29 = (bf16[16,254]{1,0:T(8,128)(2,1)S(1)}, bf16[16,254]{1,0:T(8,128)(2,1)S(1)}, u32[]{:S(2)}, u32[]{:S(2)}) collective-permute-start(bf16[16,254]{1,0:T(8,128)(2,1)S(1)} %split.24), channel_id=1, source_target_pairs={{0,32},{8,40},{16,48},{24,56},{32,0},{40,8},{48,16},{56,24},{64,96... | collective-permute-start | bytes 24392 | tf_op jit(solution)/shard_map/ppermute | solution.py:41
  12.1 2.4 %collective-permute-start.37 = (bf16[2,16,253]{2,1,0:T(8,128)(2,1)S(1)}, bf16[2,16,253]{2,1,0:T(8,128)(2,1)S(1)}, u32[]{:S(2)}, u32[]{:S(2)}) collective-permute-start(bf16[2,16,253]{2,1,0:T(8,128)(2,1)S(1)} %pad_maximum_fusion.17), channel_id=1, source_target_pairs={{0,2},{1,3},{2,0},{3,1},{4,6},{5,7},{6,4},{7,5},{8,10},{9,11},{10,... | collective-permute-start | bytes 48584 | tf_op jit(solution)/shard_map/ppermute | solution.py:41
  15.1 2.3 %collective-permute-done.37 = bf16[2,16,253]{2,1,0:T(8,128)(2,1)S(1)} collective-permute-done((bf16[2,16,253]{2,1,0:T(8,128)(2,1)S(1)}, bf16[2,16,253]{2,1,0:T(8,128)(2,1)S(1)}, u32[]{:S(2)}, u32[]{:S(2)}) %collective-permute-start.37) | collective-permute-done | bytes 16224 | tf_op jit(solution)/shard_map/ppermute | solution.py:41
  17.4 2.8 %collective-permute-start.38 = (bf16[2,2,16,253]{3,2,1,0:T(8,128)(2,1)S(1)}, bf16[2,2,16,253]{3,2,1,0:T(8,128)(2,1)S(1)}, u32[]{:S(2)}, u32[]{:S(2)}) collective-permute-start(bf16[2,2,16,253]{3,2,1,0:T(8,128)(2,1)S(1)} %pad_maximum_fusion.14), channel_id=1, source_target_pairs={{0,32},{8,40},{16,48},{24,56},{32,0},{40,8},{48,16},{56,24},{64,96... | collective-permute-start | bytes 97160 | tf_op jit(solution)/shard_map/ppermute | solution.py:41
  21.8 3.8 %collective-permute-done.38 = bf16[2,2,16,253]{3,2,1,0:T(8,128)(2,1)S(1)} collective-permute-done((bf16[2,2,16,253]{3,2,1,0:T(8,128)(2,1)S(1)}, bf16[2,2,16,253]{3,2,1,0:T(8,128)(2,1)S(1)}, u32[]{:S(2)}, u32[]{:S(2)}) %collective-permute-start.38) | collective-permute-done | bytes 32416 | tf_op jit(solution)/shard_map/ppermute | solution.py:41
  27.1 2.4 %collective-permute-start.32 = (bf16[2,2,2,16,254]{4,3,2,1,0:T(8,128)(2,1)S(1)}, bf16[2,2,2,16,254]{4,3,2,1,0:T(8,128)(2,1)S(1)}, u32[]{:S(2)}, u32[]{:S(2)}) collective-permute-start(bf16[2,2,2,16,254]{4,3,2,1,0:T(8,128)(2,1)S(1)} %pad_maximum_fusion.11), channel_id=1, source_target_pairs={{0,2},{1,3},{2,0},{3,1},{4,6},{5,7},{6,4},{7,5},{8,10},{9,11},{10,... | collective-permute-start | bytes 195080 | tf_op jit(solution)/shard_map/ppermute | solution.py:41
  29.5 2.1 collective-permute-done.39
  34.1 2.5 %collective-permute-done.40 = bf16[2,2,2,2,16,253]{5,4,3,2,1,0:T(8,128)(2,1)S(1)} collective-permute-done((bf16[2,2,2,2,16,253]{5,4,3,2,1,0:T(8,128)(2,1)S(1)}, bf16[2,2,2,2,16,253]{5,4,3,2,1,0:T(8,128)(2,1)S(1)}, u32[]{:S(2)}, u32[]{:S(2)}) %collective-permute-start.40) | collective-permute-done | bytes 129568 | tf_op jit(solution)/shard_map/ppermute | solution.py:41
  37.4 2.5 %collective-permute-done.33 = bf16[2,2,2,2,16,254]{5,4,3,2,1,0:T(8,128)(2,1)S(1)} collective-permute-done((bf16[2,2,2,2,16,254]{5,4,3,2,1,0:T(8,128)(2,1)S(1)}, bf16[2,2,2,2,16,254]{5,4,3,2,1,0:T(8,128)(2,1)S(1)}, u32[]{:S(2)}, u32[]{:S(2)}) %collective-permute-start.33) | collective-permute-done | bytes 130080 | tf_op jit(solution)/shard_map/ppermute | solution.py:41
  40.1 3.2 %collective-permute-done.41 = bf16[2,2,2,2,2,16,253]{6,5,4,3,2,1,0:T(8,128)(2,1)S(1)} collective-permute-done((bf16[2,2,2,2,2,16,253]{6,5,4,3,2,1,0:T(8,128)(2,1)S(1)}, bf16[2,2,2,2,2,16,253]{6,5,4,3,2,1,0:T(8,128)(2,1)S(1)}, u32[]{:S(2)}, u32[]{:S(2)}) %collective-permute-start.41) | collective-permute-done | bytes 259104 | tf_op jit(solution)/shard_map/ppermute | solution.py:41
  43.8 5.5 %collective-permute-done.34 = bf16[2,2,2,2,2,16,254]{6,5,4,3,2,1,0:T(8,128)(2,1)S(1)} collective-permute-done((bf16[2,2,2,2,2,16,254]{6,5,4,3,2,1,0:T(8,128)(2,1)S(1)}, bf16[2,2,2,2,2,16,254]{6,5,4,3,2,1,0:T(8,128)(2,1)S(1)}, u32[]{:S(2)}, u32[]{:S(2)}) %collective-permute-start.34) | collective-permute-done | bytes 260128 | tf_op jit(solution)/shard_map/ppermute | solution.py:41
  51.5 3.6 %collective-permute-start.45 = (bf16[2,32,2496]{2,1,0:T(8,128)(2,1)}, bf16[2,32,2496]{2,1,0:T(8,128)(2,1)}, u32[]{:S(2)}, u32[]{:S(2)}) collective-permute-start(bf16[2,32,2496]{2,1,0:T(8,128)(2,1)} %get-tuple-element.224), channel_id=1, source_target_pairs={{1,0},{2,1},{3,2},{5,4},{6,5},{7,6},{9,8},{10,9},{11,10},{13,12},{... | collective-permute-start | bytes 958472 | tf_op jit(solution)/shard_map/ppermute | solution.py:15
  55.1 2.4 %collective-permute-start.44 = (bf16[2,32,2496]{2,1,0:T(8,128)(2,1)}, bf16[2,32,2496]{2,1,0:T(8,128)(2,1)}, u32[]{:S(2)}, u32[]{:S(2)}) collective-permute-start(bf16[2,32,2496]{2,1,0:T(8,128)(2,1)} %get-tuple-element.223), channel_id=1, source_target_pairs={{0,1},{1,2},{2,3},{4,5},{5,6},{6,7},{8,9},{9,10},{10,11},{12,13},{... | collective-permute-start | bytes 958472 | tf_op jit(solution)/shard_map/ppermute | solution.py:12
  57.6 15.2 %conditional.8 = (bf16[128,416]{0,1:T(8,128)(2,1)}, bf16[4,32,416]{2,1,0:T(8,128)(2,1)S(1)}) conditional(s32[]{:T(128)} %convert_element_type.235, () %tuple.71, (bf16[1,4,32,384]{3,2,1,0:T(8,128)(2,1)S(1)}, bf16[1,2,16,384]{3,2,1,0:T(8,128)(2,1)S(1)}, bf16[1,1,8,384]{3,2,1,0:T(8,128)(2,1)S(1)}, bf16[416,384]{1,0:T(8,128)(2,1)S(1)}) %tuple.193), branch_computations={%region_0.1_spmd, %region_1.2_spmd} | conditional | flops 41138176 | bytes 1972240 | solution.py:196
  75.9 2.2 %pad_maximum_fusion.2 = bf16[128,16,507]{2,1,0:T(8,128)(2,1)} fusion(bf16[128,16,253]{2,1,0:T(8,128)(2,1)S(1)} %bitcast.258, bf16[128,16,254]{2,1,0:T(8,128)(2,1)S(1)} %bitcast.259), kind=kLoop, calls=%fused_computation.199 | loop fusion | flops 4153344 | bytes 4153344 | tf_op jit(solution)/shard_map/concatenate | solution.py:53
  78.1 5.2 %reshape_reshape.3 = bf16[416,2496]{1,0:T(8,128)(2,1)S(1)} reshape(bf16[128,16,507]{2,1,0:T(8,128)(2,1)} %pad_maximum_fusion.2) | data formatting | bytes 4153344 | tf_op jit(solution)/shard_map/reshape;reshape | solution.py:155
  83.4 2.0 conditional.9
  83.4 2.0 convolution_convert_fusion.1
  87.8 1.9 collective-permute-start.28
  94.1 3.6 %conditional.10 = (f32[416,2496]{1,0:T(8,128)}) conditional(s32[]{:T(128)} %convert_element_type.235, () %tuple.74, (bf16[1,1,4,32,2496]{4,3,2,1,0:T(8,128)(2,1)S(1)}, bf16[128,416]{0,1:T(8,128)(2,1)}) %tuple.182), branch_computations={%region_4.5_spmd, %region_5.6_spmd} | conditional | flops 265814016 | bytes 4898824 | solution.py:227
  94.1 3.6 %fusion.34 = f32[416,2496]{1,0:T(8,128)} fusion(bf16[128,416]{0,1:T(8,128)(2,1)} %get-tuple-element.161, bf16[128,2496]{1,0:T(8,128)(2,1)S(1)} %bitcast.255), kind=kOutput, calls=%fused_computation.250 | convolution fusion | flops 265814016 | bytes 4898816 | tf_op jit(solution)/shard_map/cond/branch_1_fun/dot_general | solution.py:220
  97.7 92.0 %conditional.11 = (f32[8112]{0:T(1024)S(1)}) conditional(s32[]{:T(128)} %convert_element_type.235, () %tuple.73, f32[416,2496]{1,0:T(8,128)} %get-tuple-element.266), branch_computations={%region_6.7_spmd, %region_7.8_spmd} | conditional | flops 2076740 | bytes 83029064 | solution.py:228
  97.7 4.6 %broadcast_multiply_fusion = f32[416,2496]{1,0:T(8,128)} fusion(f32[416,2496]{1,0:T(8,128)} %param.7), kind=kLoop, calls=%fused_computation.7 | loop fusion | flops 1038336 | bytes 8306688 | tf_op jit(solution)/shard_map/cond/branch_1_fun/div | solution.py:210
  102.3 7.2 %reshape.120 = f32[128,8,1014]{2,1,0:T(8,128)} reshape(f32[416,2496]{1,0:T(8,128)} %broadcast_multiply_fusion) | data formatting | bytes 8306688 | tf_op jit(solution)/shard_map/cond/branch_1_fun/reshape | solution.py:210
  109.5 3.1 %split.21 = f32[128,8,502]{2,1,0:T(8,128)} slice(f32[128,8,1014]{2,1,0:T(8,128)} %reshape.120), slice={[0:128], [0:8], [512:1014]} | slice | bytes 4112384 | tf_op jit(solution)/shard_map/cond/branch_1_fun/split | solution.py:72
  112.5 2.3 %dynamic-slice_bitcast_fusion = f32[2,2,2,2,2,2,8,502]{7,6,5,4,3,2,1,0:T(8,128)} fusion(f32[2,2,2,2,2,2,2,8,502]{8,7,6,5,4,3,2,1,0:T(8,128)} %bitcast.249, s32[]{:T(128)S(6)} %select_n.227), kind=kLoop, calls=%fused_computation.10 | loop fusion | bytes 2056196 | tf_op jit(solution)/shard_map/cond/branch_1_fun/jit(dynamic_index_in_dim)/squeeze | solution.py:65
  115.5 3.1 %split.20 = f32[128,8,512]{2,1,0:T(8,128)} slice(f32[128,8,1014]{2,1,0:T(8,128)} %reshape.120), slice={[0:128], [0:8], [0:512]} | slice | bytes 4194304 | tf_op jit(solution)/shard_map/cond/branch_1_fun/split | solution.py:72
  118.6 2.3 %dynamic-slice_bitcast_fusion.1 = f32[2,2,2,2,2,2,8,512]{7,6,5,4,3,2,1,0:T(8,128)} fusion(f32[2,2,2,2,2,2,2,8,512]{8,7,6,5,4,3,2,1,0:T(8,128)} %bitcast.251, s32[]{:T(128)S(6)} %select_n.225), kind=kLoop, calls=%fused_computation.11 | loop fusion | bytes 2097156 | tf_op jit(solution)/shard_map/cond/branch_1_fun/jit(dynamic_index_in_dim)/squeeze | solution.py:65
  122.5 7.4 %collective-permute-done.7 = f32[2,2,2,2,2,2,8,502]{7,6,5,4,3,2,1,0:T(8,128)} collective-permute-done((f32[2,2,2,2,2,2,8,502]{7,6,5,4,3,2,1,0:T(8,128)}, f32[2,2,2,2,2,2,8,502]{7,6,5,4,3,2,1,0:T(8,128)}, u32[]{:S(2)}, u32[]{:S(2)}) %collective-permute-start.7) | collective-permute-done | bytes 1028128 | tf_op jit(solution)/shard_map/cond/branch_1_fun/ppermute | solution.py:66
  133.5 2.5 %collective-permute-done = f32[2,2,2,2,2,2,8,512]{7,6,5,4,3,2,1,0:T(8,128)} collective-permute-done((f32[2,2,2,2,2,2,8,512]{7,6,5,4,3,2,1,0:T(8,128)}, f32[2,2,2,2,2,2,8,512]{7,6,5,4,3,2,1,0:T(8,128)}, u32[]{:S(2)}, u32[]{:S(2)}) %collective-permute-start) | collective-permute-done | bytes 1048608 | tf_op jit(solution)/shard_map/cond/branch_1_fun/ppermute | solution.py:66
  143.6 2.4 %collective-permute-start.9 = (f32[2,2,2,2,8,502]{5,4,3,2,1,0:T(8,128)S(1)}, f32[2,2,2,2,8,502]{5,4,3,2,1,0:T(8,128)S(1)}, u32[]{:S(2)}, u32[]{:S(2)}) collective-permute-start(f32[2,2,2,2,8,502]{5,4,3,2,1,0:T(8,128)S(1)} %dynamic-slice_bitcast_fusion.4), channel_id=1, source_target_pairs={{0,1},{1,0},{2,3},{3,2},{4,5},{5,4},{6,7},{7,6},{8,9},{9,8},{10,11... | collective-permute-start | bytes 771080 | tf_op jit(solution)/shard_map/cond/branch_1_fun/ppermute | solution.py:66
  146.0 2.8 %collective-permute-done.1 = f32[2,2,2,2,2,8,512]{6,5,4,3,2,1,0:T(8,128)} collective-permute-done((f32[2,2,2,2,2,8,512]{6,5,4,3,2,1,0:T(8,128)}, f32[2,2,2,2,2,8,512]{6,5,4,3,2,1,0:T(8,128)}, u32[]{:S(2)}, u32[]{:S(2)}) %collective-permute-start.1) | collective-permute-done | bytes 524320 | tf_op jit(solution)/shard_map/cond/branch_1_fun/ppermute | solution.py:66
  150.7 2.6 %collective-permute-start.10 = (f32[2,2,2,8,502]{4,3,2,1,0:T(8,128)S(1)}, f32[2,2,2,8,502]{4,3,2,1,0:T(8,128)S(1)}, u32[]{:S(2)}, u32[]{:S(2)}) collective-permute-start(f32[2,2,2,8,502]{4,3,2,1,0:T(8,128)S(1)} %dynamic-slice_bitcast_fusion.6), channel_id=1, source_target_pairs={{0,16},{8,24},{16,0},{24,8},{32,48},{40,56},{48,32},{56,40},{64,80... | collective-permute-start | bytes 385544 | tf_op jit(solution)/shard_map/cond/branch_1_fun/ppermute | solution.py:66
  153.3 3.1 %collective-permute-done.2 = f32[2,2,2,2,8,512]{5,4,3,2,1,0:T(8,128)S(1)} collective-permute-done((f32[2,2,2,2,8,512]{5,4,3,2,1,0:T(8,128)S(1)}, f32[2,2,2,2,8,512]{5,4,3,2,1,0:T(8,128)S(1)}, u32[]{:S(2)}, u32[]{:S(2)}) %collective-permute-start.2) | collective-permute-done | bytes 262176 | tf_op jit(solution)/shard_map/cond/branch_1_fun/ppermute | solution.py:66
  156.5 3.8 %collective-permute-start.3 = (f32[2,2,2,8,512]{4,3,2,1,0:T(8,128)S(1)}, f32[2,2,2,8,512]{4,3,2,1,0:T(8,128)S(1)}, u32[]{:S(2)}, u32[]{:S(2)}) collective-permute-start(f32[2,2,2,8,512]{4,3,2,1,0:T(8,128)S(1)} %dynamic-slice_bitcast_fusion.7), channel_id=1, source_target_pairs={{0,2},{1,3},{2,0},{3,1},{4,6},{5,7},{6,4},{7,5},{8,10},{9,11},{10,... | collective-permute-start | bytes 393224 | tf_op jit(solution)/shard_map/cond/branch_1_fun/ppermute | solution.py:66
  160.3 3.5 %collective-permute-start.11 = (f32[2,2,8,502]{3,2,1,0:T(8,128)S(1)}, f32[2,2,8,502]{3,2,1,0:T(8,128)S(1)}, u32[]{:S(2)}, u32[]{:S(2)}) collective-permute-start(f32[2,2,8,502]{3,2,1,0:T(8,128)S(1)} %dynamic-slice_bitcast_fusion.8), channel_id=1, source_target_pairs={{0,32},{8,40},{16,48},{24,56},{32,0},{40,8},{48,16},{56,24},{64,96... | collective-permute-start | bytes 192776 | tf_op jit(solution)/shard_map/cond/branch_1_fun/ppermute | solution.py:66
  164.7 3.9 %collective-permute-done.11 = f32[2,2,8,502]{3,2,1,0:T(8,128)S(1)} collective-permute-done((f32[2,2,8,502]{3,2,1,0:T(8,128)S(1)}, f32[2,2,8,502]{3,2,1,0:T(8,128)S(1)}, u32[]{:S(2)}, u32[]{:S(2)}) %collective-permute-start.11) | collective-permute-done | bytes 64288 | tf_op jit(solution)/shard_map/cond/branch_1_fun/ppermute | solution.py:66
  170.0 3.4 %collective-permute-start.4 = (f32[2,2,8,512]{3,2,1,0:T(8,128)S(1)}, f32[2,2,8,512]{3,2,1,0:T(8,128)S(1)}, u32[]{:S(2)}, u32[]{:S(2)}) collective-permute-start(f32[2,2,8,512]{3,2,1,0:T(8,128)S(1)} %dynamic-slice_bitcast_fusion.9), channel_id=1, source_target_pairs={{0,16},{8,24},{16,0},{24,8},{32,48},{40,56},{48,32},{56,40},{64,80... | collective-permute-start | bytes 196616 | tf_op jit(solution)/shard_map/cond/branch_1_fun/ppermute | solution.py:66
  176.0 2.2 %collective-permute-start.5 = (f32[2,8,512]{2,1,0:T(8,128)S(1)}, f32[2,8,512]{2,1,0:T(8,128)S(1)}, u32[]{:S(2)}, u32[]{:S(2)}) collective-permute-start(f32[2,8,512]{2,1,0:T(8,128)S(1)} %dynamic-slice_bitcast_fusion.11), channel_id=1, source_target_pairs={{0,128},{8,136},{16,144},{24,152},{32,160},{40,168},{48,176},{56,1... | collective-permute-start | bytes 98312 | tf_op jit(solution)/shard_map/cond/branch_1_fun/ppermute | solution.py:66
  181.5 3.7 %collective-permute-start.6 = (f32[8,512]{1,0:T(8,128)S(1)}, f32[8,512]{1,0:T(8,128)S(1)}, u32[]{:S(2)}, u32[]{:S(2)}) collective-permute-start(f32[8,512]{1,0:T(8,128)S(1)} %dynamic-slice_bitcast_fusion.13), channel_id=1, source_target_pairs={{0,32},{8,40},{16,48},{24,56},{32,0},{40,8},{48,16},{56,24},{64,96... | collective-permute-start | bytes 49160 | tf_op jit(solution)/shard_map/cond/branch_1_fun/ppermute | solution.py:66
  185.2 4.0 %collective-permute-done.6 = f32[8,512]{1,0:T(8,128)S(1)} collective-permute-done((f32[8,512]{1,0:T(8,128)S(1)}, f32[8,512]{1,0:T(8,128)S(1)}, u32[]{:S(2)}, u32[]{:S(2)}) %collective-permute-start.6) | collective-permute-done | bytes 16416 | tf_op jit(solution)/shard_map/cond/branch_1_fun/ppermute | solution.py:66
  191.1 2.9 %collective-permute-start.46 = (f32[2,2496]{1,0:T(2,128)S(1)}, f32[2,2496]{1,0:T(2,128)S(1)}, u32[]{:S(2)}, u32[]{:S(2)}) collective-permute-start(f32[2,2496]{1,0:T(2,128)S(1)} %pad_maximum_fusion.15), channel_id=1, source_target_pairs={{0,1},{1,0},{2,3},{3,2},{4,5},{5,4},{6,7},{7,6},{8,9},{9,8},{10,11... | collective-permute-start | bytes 59912 | tf_op jit(solution)/shard_map/ppermute | solution.py:80
  195.8 2.0 collective-permute-start.47
  197.8 2.1 copy.62
  202.4 4.5 %collective-permute-start.49 = (bf16[2,32,2496]{2,1,0:T(8,128)(2,1)S(1)}, bf16[2,32,2496]{2,1,0:T(8,128)(2,1)S(1)}, u32[]{:S(2)}, u32[]{:S(2)}) collective-permute-start(bf16[2,32,2496]{2,1,0:T(8,128)(2,1)S(1)} %get-tuple-element.222), channel_id=1, source_target_pairs={{1,0},{2,1},{3,2},{5,4},{6,5},{7,6},{9,8},{10,9},{11,10},{13,12},{... | collective-permute-start | bytes 958472 | tf_op jit(solution)/shard_map/ppermute | solution.py:15
  208.9 2.6 %collective-permute-done.49 = bf16[2,32,2496]{2,1,0:T(8,128)(2,1)S(1)} collective-permute-done((bf16[2,32,2496]{2,1,0:T(8,128)(2,1)S(1)}, bf16[2,32,2496]{2,1,0:T(8,128)(2,1)S(1)}, u32[]{:S(2)}, u32[]{:S(2)}) %collective-permute-start.49) | collective-permute-done | bytes 319520 | tf_op jit(solution)/shard_map/ppermute | solution.py:15
  211.5 4.4 %collective-permute-done.48 = bf16[2,32,2496]{2,1,0:T(8,128)(2,1)S(1)} collective-permute-done((bf16[2,32,2496]{2,1,0:T(8,128)(2,1)S(1)}, bf16[2,32,2496]{2,1,0:T(8,128)(2,1)S(1)}, u32[]{:S(2)}, u32[]{:S(2)}) %collective-permute-start.48) | collective-permute-done | bytes 319520 | tf_op jit(solution)/shard_map/ppermute | solution.py:12
  (173 shorter events, 56.5 us)
Async XLA Ops:
  1.7 10.3 %collective-permute-start.36 = (bf16[16,253]{1,0:T(8,128)(2,1)S(1)}, bf16[16,253]{1,0:T(8,128)(2,1)S(1)}, u32[]{:S(2)}, u32[]{:S(2)}) collective-permute-start(bf16[16,253]{1,0:T(8,128)(2,1)S(1)} %split.25), channel_id=1, source_target_pairs={{0,128},{8,136},{16,144},{24,152},{32,160},{40,168},{48,176},{56,1... | collective-permute-start | bytes 24296 | tf_op jit(solution)/shard_map/ppermute | solution.py:41
  4.7 9.7 %collective-permute-start.29 = (bf16[16,254]{1,0:T(8,128)(2,1)S(1)}, bf16[16,254]{1,0:T(8,128)(2,1)S(1)}, u32[]{:S(2)}, u32[]{:S(2)}) collective-permute-start(bf16[16,254]{1,0:T(8,128)(2,1)S(1)} %split.24), channel_id=1, source_target_pairs={{0,32},{8,40},{16,48},{24,56},{32,0},{40,8},{48,16},{56,24},{64,96... | collective-permute-start | bytes 24392 | tf_op jit(solution)/shard_map/ppermute | solution.py:41
  12.1 5.3 %collective-permute-start.37 = (bf16[2,16,253]{2,1,0:T(8,128)(2,1)S(1)}, bf16[2,16,253]{2,1,0:T(8,128)(2,1)S(1)}, u32[]{:S(2)}, u32[]{:S(2)}) collective-permute-start(bf16[2,16,253]{2,1,0:T(8,128)(2,1)S(1)} %pad_maximum_fusion.17), channel_id=1, source_target_pairs={{0,2},{1,3},{2,0},{3,1},{4,6},{5,7},{6,4},{7,5},{8,10},{9,11},{10,... | collective-permute-start | bytes 48584 | tf_op jit(solution)/shard_map/ppermute | solution.py:41
  14.5 5.7 %collective-permute-start.30 = (bf16[2,16,254]{2,1,0:T(8,128)(2,1)S(1)}, bf16[2,16,254]{2,1,0:T(8,128)(2,1)S(1)}, u32[]{:S(2)}, u32[]{:S(2)}) collective-permute-start(bf16[2,16,254]{2,1,0:T(8,128)(2,1)S(1)} %pad_maximum_fusion.16), channel_id=1, source_target_pairs={{0,128},{8,136},{16,144},{24,152},{32,160},{40,168},{48,176},{56,1... | collective-permute-start | bytes 48776 | tf_op jit(solution)/shard_map/ppermute | solution.py:41
  17.4 8.1 %collective-permute-start.38 = (bf16[2,2,16,253]{3,2,1,0:T(8,128)(2,1)S(1)}, bf16[2,2,16,253]{3,2,1,0:T(8,128)(2,1)S(1)}, u32[]{:S(2)}, u32[]{:S(2)}) collective-permute-start(bf16[2,2,16,253]{3,2,1,0:T(8,128)(2,1)S(1)} %pad_maximum_fusion.14), channel_id=1, source_target_pairs={{0,32},{8,40},{16,48},{24,56},{32,0},{40,8},{48,16},{56,24},{64,96... | collective-permute-start | bytes 97160 | tf_op jit(solution)/shard_map/ppermute | solution.py:41
  20.2 6.8 %collective-permute-start.31 = (bf16[2,2,16,254]{3,2,1,0:T(8,128)(2,1)S(1)}, bf16[2,2,16,254]{3,2,1,0:T(8,128)(2,1)S(1)}, u32[]{:S(2)}, u32[]{:S(2)}) collective-permute-start(bf16[2,2,16,254]{3,2,1,0:T(8,128)(2,1)S(1)} %pad_maximum_fusion.13), channel_id=1, source_target_pairs={{0,16},{8,24},{16,0},{24,8},{32,48},{40,56},{48,32},{56,40},{64,80... | collective-permute-start | bytes 97544 | tf_op jit(solution)/shard_map/ppermute | solution.py:41
  25.6 6.0 %collective-permute-start.39 = (bf16[2,2,2,16,253]{4,3,2,1,0:T(8,128)(2,1)S(1)}, bf16[2,2,2,16,253]{4,3,2,1,0:T(8,128)(2,1)S(1)}, u32[]{:S(2)}, u32[]{:S(2)}) collective-permute-start(bf16[2,2,2,16,253]{4,3,2,1,0:T(8,128)(2,1)S(1)} %pad_maximum_fusion.12), channel_id=1, source_target_pairs={{0,16},{8,24},{16,0},{24,8},{32,48},{40,56},{48,32},{56,40},{64,80... | collective-permute-start | bytes 194312 | tf_op jit(solution)/shard_map/ppermute | solution.py:41
  27.1 6.3 %collective-permute-start.32 = (bf16[2,2,2,16,254]{4,3,2,1,0:T(8,128)(2,1)S(1)}, bf16[2,2,2,16,254]{4,3,2,1,0:T(8,128)(2,1)S(1)}, u32[]{:S(2)}, u32[]{:S(2)}) collective-permute-start(bf16[2,2,2,16,254]{4,3,2,1,0:T(8,128)(2,1)S(1)} %pad_maximum_fusion.11), channel_id=1, source_target_pairs={{0,2},{1,3},{2,0},{3,1},{4,6},{5,7},{6,4},{7,5},{8,10},{9,11},{10,... | collective-permute-start | bytes 195080 | tf_op jit(solution)/shard_map/ppermute | solution.py:41
  31.6 5.1 %collective-permute-start.40 = (bf16[2,2,2,2,16,253]{5,4,3,2,1,0:T(8,128)(2,1)S(1)}, bf16[2,2,2,2,16,253]{5,4,3,2,1,0:T(8,128)(2,1)S(1)}, u32[]{:S(2)}, u32[]{:S(2)}) collective-permute-start(bf16[2,2,2,2,16,253]{5,4,3,2,1,0:T(8,128)(2,1)S(1)} %pad_maximum_fusion.10), channel_id=1, source_target_pairs={{0,1},{1,0},{2,3},{3,2},{4,5},{5,4},{6,7},{7,6},{8,9},{9,8},{10,11... | collective-permute-start | bytes 388616 | tf_op jit(solution)/shard_map/ppermute | solution.py:41
  33.5 6.4 %collective-permute-start.33 = (bf16[2,2,2,2,16,254]{5,4,3,2,1,0:T(8,128)(2,1)S(1)}, bf16[2,2,2,2,16,254]{5,4,3,2,1,0:T(8,128)(2,1)S(1)}, u32[]{:S(2)}, u32[]{:S(2)}) collective-permute-start(bf16[2,2,2,2,16,254]{5,4,3,2,1,0:T(8,128)(2,1)S(1)} %pad_maximum_fusion.9), channel_id=1, source_target_pairs={{0,64},{8,72},{16,80},{24,88},{32,96},{40,104},{48,112},{56,120},{... | collective-permute-start | bytes 390152 | tf_op jit(solution)/shard_map/ppermute | solution.py:41
  36.8 6.6 %collective-permute-start.41 = (bf16[2,2,2,2,2,16,253]{6,5,4,3,2,1,0:T(8,128)(2,1)S(1)}, bf16[2,2,2,2,2,16,253]{6,5,4,3,2,1,0:T(8,128)(2,1)S(1)}, u32[]{:S(2)}, u32[]{:S(2)}) collective-permute-start(bf16[2,2,2,2,2,16,253]{6,5,4,3,2,1,0:T(8,128)(2,1)S(1)} %pad_maximum_fusion.8), channel_id=1, source_target_pairs={{0,64},{8,72},{16,80},{24,88},{32,96},{40,104},{48,112},{56,120},{... | collective-permute-start | bytes 777224 | tf_op jit(solution)/shard_map/ppermute | solution.py:41
  40.0 9.3 %collective-permute-start.34 = (bf16[2,2,2,2,2,16,254]{6,5,4,3,2,1,0:T(8,128)(2,1)S(1)}, bf16[2,2,2,2,2,16,254]{6,5,4,3,2,1,0:T(8,128)(2,1)S(1)}, u32[]{:S(2)}, u32[]{:S(2)}) collective-permute-start(bf16[2,2,2,2,2,16,254]{6,5,4,3,2,1,0:T(8,128)(2,1)S(1)} %pad_maximum_fusion.7), channel_id=1, source_target_pairs={{0,8},{8,0},{16,24},{24,16},{32,40},{40,32},{48,56},{56,48},{64,72... | collective-permute-start | bytes 780296 | tf_op jit(solution)/shard_map/ppermute | solution.py:41
  43.5 29.3 %collective-permute-start.42 = (bf16[2,2,2,2,2,2,16,253]{7,6,5,4,3,2,1,0:T(8,128)(2,1)S(1)}, bf16[2,2,2,2,2,2,16,253]{7,6,5,4,3,2,1,0:T(8,128)(2,1)}, u32[]{:S(2)}, u32[]{:S(2)}) collective-permute-start(bf16[2,2,2,2,2,2,16,253]{7,6,5,4,3,2,1,0:T(8,128)(2,1)S(1)} %pad_maximum_fusion.6), channel_id=1, source_target_pairs={{0,8},{8,0},{16,24},{24,16},{32,40},{40,32},{48,56},{56,48},{64,72... | collective-permute-start | bytes 1554440 | tf_op jit(solution)/shard_map/ppermute | solution.py:41
  49.3 8.2 %copy-start.21 = (bf16[416,384]{1,0:T(8,128)(2,1)S(1)}, bf16[416,384]{1,0:T(8,128)(2,1)}, u32[]{:S(2)}) copy-start(bf16[416,384]{1,0:T(8,128)(2,1)} %param.31) | copy-start | bytes 958468
  49.4 8.2 %copy-start.24 = (bf16[1,4,32,384]{3,2,1,0:T(8,128)(2,1)S(1)}, bf16[1,4,32,384]{3,2,1,0:T(8,128)(2,1)}, u32[]{:S(2)}) copy-start(bf16[1,4,32,384]{3,2,1,0:T(8,128)(2,1)} %param.28) | copy-start | bytes 294916
  49.4 8.2 %copy-start.26 = (bf16[1,2,16,384]{3,2,1,0:T(8,128)(2,1)S(1)}, bf16[1,2,16,384]{3,2,1,0:T(8,128)(2,1)}, u32[]{:S(2)}) copy-start(bf16[1,2,16,384]{3,2,1,0:T(8,128)(2,1)} %param.29) | copy-start | bytes 73732
  49.4 8.2 %copy-start.27 = (bf16[1,1,8,384]{3,2,1,0:T(8,128)(2,1)S(1)}, bf16[1,1,8,384]{3,2,1,0:T(8,128)(2,1)}, u32[]{:S(2)}) copy-start(bf16[1,1,8,384]{3,2,1,0:T(8,128)(2,1)} %param.30) | copy-start | bytes 18436
  50.3 24.1 %collective-permute-start.35 = (bf16[2,2,2,2,2,2,16,254]{7,6,5,4,3,2,1,0:T(8,128)(2,1)}, bf16[2,2,2,2,2,2,16,254]{7,6,5,4,3,2,1,0:T(8,128)(2,1)}, u32[]{:S(2)}, u32[]{:S(2)}) collective-permute-start(bf16[2,2,2,2,2,2,16,254]{7,6,5,4,3,2,1,0:T(8,128)(2,1)} %pad_maximum_fusion.5), channel_id=1, source_target_pairs={{0,1},{1,0},{2,3},{3,2},{4,5},{5,4},{6,7},{7,6},{8,9},{9,8},{10,11... | collective-permute-start | bytes 1560584 | tf_op jit(solution)/shard_map/ppermute | solution.py:41
  51.5 39.2 %collective-permute-start.45 = (bf16[2,32,2496]{2,1,0:T(8,128)(2,1)}, bf16[2,32,2496]{2,1,0:T(8,128)(2,1)}, u32[]{:S(2)}, u32[]{:S(2)}) collective-permute-start(bf16[2,32,2496]{2,1,0:T(8,128)(2,1)} %get-tuple-element.224), channel_id=1, source_target_pairs={{1,0},{2,1},{3,2},{5,4},{6,5},{7,6},{9,8},{10,9},{11,10},{13,12},{... | collective-permute-start | bytes 958472 | tf_op jit(solution)/shard_map/ppermute | solution.py:15
  55.1 35.6 %collective-permute-start.44 = (bf16[2,32,2496]{2,1,0:T(8,128)(2,1)}, bf16[2,32,2496]{2,1,0:T(8,128)(2,1)}, u32[]{:S(2)}, u32[]{:S(2)}) collective-permute-start(bf16[2,32,2496]{2,1,0:T(8,128)(2,1)} %get-tuple-element.223), channel_id=1, source_target_pairs={{0,1},{1,2},{2,3},{4,5},{5,6},{6,7},{8,9},{9,10},{10,11},{12,13},{... | collective-permute-start | bytes 958472 | tf_op jit(solution)/shard_map/ppermute | solution.py:12
  86.5 5.9 %collective-permute-start.43 = (bf16[4,32,2496]{2,1,0:T(8,128)(2,1)}, bf16[4,32,2496]{2,1,0:T(8,128)(2,1)S(1)}, u32[]{:S(2)}, u32[]{:S(2)}) collective-permute-start(bf16[4,32,2496]{2,1,0:T(8,128)(2,1)} %bitcast.260), channel_id=1, source_target_pairs={{0,4},{1,5},{2,6},{3,7},{8,12},{9,13},{10,14},{11,15},{16,20},{17,... | collective-permute-start | bytes 1916936 | tf_op jit(solution)/shard_map/ppermute | solution.py:23
  87.8 4.6 %collective-permute-start.28 = (bf16[4,32,416]{2,1,0:T(8,128)(2,1)}, bf16[4,32,416]{2,1,0:T(8,128)(2,1)}, u32[]{:S(2)}, u32[]{:S(2)}) collective-permute-start(bf16[4,32,416]{2,1,0:T(8,128)(2,1)} %copy-done.23), channel_id=1, source_target_pairs={{0,4},{1,5},{2,6},{3,7},{8,12},{9,13},{10,14},{11,15},{16,20},{17,... | collective-permute-start | bytes 319496 | tf_op jit(solution)/shard_map/ppermute | solution.py:23
  97.7 92.0 %copy-start.9 = (f32[4,32,2496]{2,1,0:T(8,128)S(1)}, f32[4,32,2496]{2,1,0:T(8,128)}, u32[]{:S(2)}) copy-start(f32[4,32,2496]{2,1,0:T(8,128)} %copy-done.8) | copy-start | bytes 3833860
  114.8 15.1 %collective-permute-start.7 = (f32[2,2,2,2,2,2,8,502]{7,6,5,4,3,2,1,0:T(8,128)}, f32[2,2,2,2,2,2,8,502]{7,6,5,4,3,2,1,0:T(8,128)}, u32[]{:S(2)}, u32[]{:S(2)}) collective-permute-start(f32[2,2,2,2,2,2,8,502]{7,6,5,4,3,2,1,0:T(8,128)} %dynamic-slice_bitcast_fusion), channel_id=1, source_target_pairs={{0,8},{8,0},{16,24},{24,16},{32,40},{40,32},{48,56},{56,48},{64,72... | collective-permute-start | bytes 3084296 | tf_op jit(solution)/shard_map/cond/branch_1_fun/ppermute | solution.py:66
  120.9 15.1 %collective-permute-start = (f32[2,2,2,2,2,2,8,512]{7,6,5,4,3,2,1,0:T(8,128)}, f32[2,2,2,2,2,2,8,512]{7,6,5,4,3,2,1,0:T(8,128)}, u32[]{:S(2)}, u32[]{:S(2)}) collective-permute-start(f32[2,2,2,2,2,2,8,512]{7,6,5,4,3,2,1,0:T(8,128)} %dynamic-slice_bitcast_fusion.1), channel_id=1, source_target_pairs={{0,1},{1,0},{2,3},{3,2},{4,5},{5,4},{6,7},{7,6},{8,9},{9,8},{10,11... | collective-permute-start | bytes 3145736 | tf_op jit(solution)/shard_map/cond/branch_1_fun/ppermute | solution.py:66
  129.9 6.1 %copy-start.2 = (f32[128,8,512]{2,1,0:T(8,128)S(1)}, f32[128,8,512]{2,1,0:T(8,128)}, u32[]{:S(2)}) copy-start(f32[128,8,512]{2,1,0:T(8,128)} %split.20) | copy-start | bytes 6291460 | tf_op jit(solution)/shard_map/cond
  132.8 9.5 %collective-permute-start.8 = (f32[2,2,2,2,2,8,502]{6,5,4,3,2,1,0:T(8,128)}, f32[2,2,2,2,2,8,502]{6,5,4,3,2,1,0:T(8,128)}, u32[]{:S(2)}, u32[]{:S(2)}) collective-permute-start(f32[2,2,2,2,2,8,502]{6,5,4,3,2,1,0:T(8,128)} %dynamic-slice_bitcast_fusion.2), channel_id=1, source_target_pairs={{0,64},{8,72},{16,80},{24,88},{32,96},{40,104},{48,112},{56,120},{... | collective-permute-start | bytes 1542152 | tf_op jit(solution)/shard_map/cond/branch_1_fun/ppermute | solution.py:66
  139.3 9.5 %collective-permute-start.1 = (f32[2,2,2,2,2,8,512]{6,5,4,3,2,1,0:T(8,128)}, f32[2,2,2,2,2,8,512]{6,5,4,3,2,1,0:T(8,128)}, u32[]{:S(2)}, u32[]{:S(2)}) collective-permute-start(f32[2,2,2,2,2,8,512]{6,5,4,3,2,1,0:T(8,128)} %dynamic-slice_bitcast_fusion.3), channel_id=1, source_target_pairs={{0,8},{8,0},{16,24},{24,16},{32,40},{40,32},{48,56},{56,48},{64,72... | collective-permute-start | bytes 1572872 | tf_op jit(solution)/shard_map/cond/branch_1_fun/ppermute | solution.py:66
  140.9 7.9 %copy-start.11 = (f32[2,2,2,2,2,2,8,512]{7,6,5,4,3,2,1,0:T(8,128)S(1)}, f32[2,2,2,2,2,2,8,512]{7,6,5,4,3,2,1,0:T(8,128)}, u32[]{:S(2)}) copy-start(f32[2,2,2,2,2,2,8,512]{7,6,5,4,3,2,1,0:T(8,128)} %copy-done.10) | copy-start | bytes 3145732 | tf_op jit(solution)/shard_map/cond
  143.6 7.0 %collective-permute-start.9 = (f32[2,2,2,2,8,502]{5,4,3,2,1,0:T(8,128)S(1)}, f32[2,2,2,2,8,502]{5,4,3,2,1,0:T(8,128)S(1)}, u32[]{:S(2)}, u32[]{:S(2)}) collective-permute-start(f32[2,2,2,2,8,502]{5,4,3,2,1,0:T(8,128)S(1)} %dynamic-slice_bitcast_fusion.4), channel_id=1, source_target_pairs={{0,1},{1,0},{2,3},{3,2},{4,5},{5,4},{6,7},{7,6},{8,9},{9,8},{10,11... | collective-permute-start | bytes 771080 | tf_op jit(solution)/shard_map/cond/branch_1_fun/ppermute | solution.py:66
  150.0 6.5 %collective-permute-start.2 = (f32[2,2,2,2,8,512]{5,4,3,2,1,0:T(8,128)S(1)}, f32[2,2,2,2,8,512]{5,4,3,2,1,0:T(8,128)S(1)}, u32[]{:S(2)}, u32[]{:S(2)}) collective-permute-start(f32[2,2,2,2,8,512]{5,4,3,2,1,0:T(8,128)S(1)} %dynamic-slice_bitcast_fusion.5), channel_id=1, source_target_pairs={{0,64},{8,72},{16,80},{24,88},{32,96},{40,104},{48,112},{56,120},{... | collective-permute-start | bytes 786440 | tf_op jit(solution)/shard_map/cond/branch_1_fun/ppermute | solution.py:66
  150.7 9.6 %collective-permute-start.10 = (f32[2,2,2,8,502]{4,3,2,1,0:T(8,128)S(1)}, f32[2,2,2,8,502]{4,3,2,1,0:T(8,128)S(1)}, u32[]{:S(2)}, u32[]{:S(2)}) collective-permute-start(f32[2,2,2,8,502]{4,3,2,1,0:T(8,128)S(1)} %dynamic-slice_bitcast_fusion.6), channel_id=1, source_target_pairs={{0,16},{8,24},{16,0},{24,8},{32,48},{40,56},{48,32},{56,40},{64,80... | collective-permute-start | bytes 385544 | tf_op jit(solution)/shard_map/cond/branch_1_fun/ppermute | solution.py:66
  156.5 8.2 %collective-permute-start.3 = (f32[2,2,2,8,512]{4,3,2,1,0:T(8,128)S(1)}, f32[2,2,2,8,512]{4,3,2,1,0:T(8,128)S(1)}, u32[]{:S(2)}, u32[]{:S(2)}) collective-permute-start(f32[2,2,2,8,512]{4,3,2,1,0:T(8,128)S(1)} %dynamic-slice_bitcast_fusion.7), channel_id=1, source_target_pairs={{0,2},{1,3},{2,0},{3,1},{4,6},{5,7},{6,4},{7,5},{8,10},{9,11},{10,... | collective-permute-start | bytes 393224 | tf_op jit(solution)/shard_map/cond/branch_1_fun/ppermute | solution.py:66
  160.3 8.3 %collective-permute-start.11 = (f32[2,2,8,502]{3,2,1,0:T(8,128)S(1)}, f32[2,2,8,502]{3,2,1,0:T(8,128)S(1)}, u32[]{:S(2)}, u32[]{:S(2)}) collective-permute-start(f32[2,2,8,502]{3,2,1,0:T(8,128)S(1)} %dynamic-slice_bitcast_fusion.8), channel_id=1, source_target_pairs={{0,32},{8,40},{16,48},{24,56},{32,0},{40,8},{48,16},{56,24},{64,96... | collective-permute-start | bytes 192776 | tf_op jit(solution)/shard_map/cond/branch_1_fun/ppermute | solution.py:66
  168.6 5.5 %collective-permute-start.12 = (f32[2,8,502]{2,1,0:T(8,128)S(1)}, f32[2,8,502]{2,1,0:T(8,128)S(1)}, u32[]{:S(2)}, u32[]{:S(2)}) collective-permute-start(f32[2,8,502]{2,1,0:T(8,128)S(1)} %dynamic-slice_bitcast_fusion.10), channel_id=1, source_target_pairs={{0,2},{1,3},{2,0},{3,1},{4,6},{5,7},{6,4},{7,5},{8,10},{9,11},{10,... | collective-permute-start | bytes 96392 | tf_op jit(solution)/shard_map/cond/branch_1_fun/ppermute | solution.py:66
  170.0 5.9 %collective-permute-start.4 = (f32[2,2,8,512]{3,2,1,0:T(8,128)S(1)}, f32[2,2,8,512]{3,2,1,0:T(8,128)S(1)}, u32[]{:S(2)}, u32[]{:S(2)}) collective-permute-start(f32[2,2,8,512]{3,2,1,0:T(8,128)S(1)} %dynamic-slice_bitcast_fusion.9), channel_id=1, source_target_pairs={{0,16},{8,24},{16,0},{24,8},{32,48},{40,56},{48,32},{56,40},{64,80... | collective-permute-start | bytes 196616 | tf_op jit(solution)/shard_map/cond/branch_1_fun/ppermute | solution.py:66
  176.0 5.5 %collective-permute-start.5 = (f32[2,8,512]{2,1,0:T(8,128)S(1)}, f32[2,8,512]{2,1,0:T(8,128)S(1)}, u32[]{:S(2)}, u32[]{:S(2)}) collective-permute-start(f32[2,8,512]{2,1,0:T(8,128)S(1)} %dynamic-slice_bitcast_fusion.11), channel_id=1, source_target_pairs={{0,128},{8,136},{16,144},{24,152},{32,160},{40,168},{48,176},{56,1... | collective-permute-start | bytes 98312 | tf_op jit(solution)/shard_map/cond/branch_1_fun/ppermute | solution.py:66
  178.2 7.0 %collective-permute-start.13 = (f32[8,502]{1,0:T(8,128)S(1)}, f32[8,502]{1,0:T(8,128)S(1)}, u32[]{:S(2)}, u32[]{:S(2)}) collective-permute-start(f32[8,502]{1,0:T(8,128)S(1)} %dynamic-slice_bitcast_fusion.12), channel_id=1, source_target_pairs={{0,128},{8,136},{16,144},{24,152},{32,160},{40,168},{48,176},{56,1... | collective-permute-start | bytes 48200 | tf_op jit(solution)/shard_map/cond/branch_1_fun/ppermute | solution.py:66
  181.5 7.7 %collective-permute-start.6 = (f32[8,512]{1,0:T(8,128)S(1)}, f32[8,512]{1,0:T(8,128)S(1)}, u32[]{:S(2)}, u32[]{:S(2)}) collective-permute-start(f32[8,512]{1,0:T(8,128)S(1)} %dynamic-slice_bitcast_fusion.13), channel_id=1, source_target_pairs={{0,32},{8,40},{16,48},{24,56},{32,0},{40,8},{48,16},{56,24},{64,96... | collective-permute-start | bytes 49160 | tf_op jit(solution)/shard_map/cond/branch_1_fun/ppermute | solution.py:66
  189.7 10.2 %copy-start.25 = (f32[8112]{0:T(1024)}, f32[8112]{0:T(1024)S(1)}, u32[]{:S(2)}) copy-start(f32[8112]{0:T(1024)S(1)} %get-tuple-element.267) | copy-start | bytes 97348
  191.1 4.7 %collective-permute-start.46 = (f32[2,2496]{1,0:T(2,128)S(1)}, f32[2,2496]{1,0:T(2,128)S(1)}, u32[]{:S(2)}, u32[]{:S(2)}) collective-permute-start(f32[2,2496]{1,0:T(2,128)S(1)} %pad_maximum_fusion.15), channel_id=1, source_target_pairs={{0,1},{1,0},{2,3},{3,2},{4,5},{5,4},{6,7},{7,6},{8,9},{9,8},{10,11... | collective-permute-start | bytes 59912 | tf_op jit(solution)/shard_map/ppermute | solution.py:80
  195.8 6.5 %collective-permute-start.47 = (f32[2,2496]{1,0:T(2,128)S(1)}, f32[2,2496]{1,0:T(2,128)S(1)}, u32[]{:S(2)}, u32[]{:S(2)}) collective-permute-start(f32[2,2496]{1,0:T(2,128)S(1)} %fusion.30), channel_id=1, source_target_pairs={{0,2},{1,3},{2,0},{3,1},{4,6},{5,7},{6,4},{7,5},{8,10},{9,11},{10,... | collective-permute-start | bytes 59912 | tf_op jit(solution)/shard_map/ppermute | solution.py:80
  202.3 6.5 %copy-start.5 = (bf16[4,32,2496]{2,1,0:T(8,128)(2,1)}, bf16[4,32,2496]{2,1,0:T(8,128)(2,1)S(1)}, u32[]{:S(2)}) copy-start(bf16[4,32,2496]{2,1,0:T(8,128)(2,1)S(1)} %get-tuple-element.269) | copy-start | bytes 1916932
  202.4 9.1 %collective-permute-start.49 = (bf16[2,32,2496]{2,1,0:T(8,128)(2,1)S(1)}, bf16[2,32,2496]{2,1,0:T(8,128)(2,1)S(1)}, u32[]{:S(2)}, u32[]{:S(2)}) collective-permute-start(bf16[2,32,2496]{2,1,0:T(8,128)(2,1)S(1)} %get-tuple-element.222), channel_id=1, source_target_pairs={{1,0},{2,1},{3,2},{5,4},{6,5},{7,6},{9,8},{10,9},{11,10},{13,12},{... | collective-permute-start | bytes 958472 | tf_op jit(solution)/shard_map/ppermute | solution.py:15
  206.9 9.0 %collective-permute-start.48 = (bf16[2,32,2496]{2,1,0:T(8,128)(2,1)S(1)}, bf16[2,32,2496]{2,1,0:T(8,128)(2,1)S(1)}, u32[]{:S(2)}, u32[]{:S(2)}) collective-permute-start(bf16[2,32,2496]{2,1,0:T(8,128)(2,1)S(1)} %get-tuple-element.221), channel_id=1, source_target_pairs={{0,1},{1,2},{2,3},{4,5},{5,6},{6,7},{8,9},{9,10},{10,11},{12,13},{... | collective-permute-start | bytes 958472 | tf_op jit(solution)/shard_map/ppermute | solution.py:12
  208.9 8.3 %copy-start.4 = (bf16[1,1,4,32,2496]{4,3,2,1,0:T(8,128)(2,1)S(1)}, bf16[1,1,4,32,2496]{4,3,2,1,0:T(8,128)(2,1)}, u32[]{:S(2)}) copy-start(bf16[1,1,4,32,2496]{4,3,2,1,0:T(8,128)(2,1)} %param.27) | copy-start | bytes 1916932
  208.9 8.3 %copy-start.19 = (f32[25,2496]{1,0:T(8,128)S(1)}, f32[25,2496]{1,0:T(8,128)}, u32[]{:S(2)}) copy-start(f32[25,2496]{1,0:T(8,128)} %copy-done.18) | copy-start | bytes 748804
  208.9 8.3 %copy-start.22 = (bf16[1,4,32,416]{3,2,1,0:T(8,128)(2,1)S(1)}, bf16[1,4,32,416]{3,2,1,0:T(8,128)(2,1)}, u32[]{:S(2)}) copy-start(bf16[1,4,32,416]{3,2,1,0:T(8,128)(2,1)} %param.26) | copy-start | bytes 319492
  (9 other events, 11.1 us)

commit v2 on v1

--- a/solution.py
+++ b/solution.py
@@ -33,31 +33,33 @@
     return [(i, i ^ (1 << j)) for i in range(lax.axis_size(axis))]
 
 
-def gather_chunks(piece, order):
+def gather_steps(buf, lead, order):
     bits = flat_bits()
-    buf = piece
-    lead = []
     for axis, j in order:
         recv = lax.ppermute(buf, axis, swap_pairs(axis, j))
         high = (lax.axis_index(axis) >> j) & 1
         buf = jnp.stack([jnp.where(high == 0, buf, recv), jnp.where(high == 0, recv, buf)])
-        lead.insert(0, bits.index((axis, j)))
-    count = len(bits)
-    perm = [lead.index(k) for k in reversed(range(count))] + [count, count + 1]
-    return jnp.transpose(buf, perm).reshape((2**count,) + piece.shape)
-
-
-def gather_streams(piece, orders, cuts):
-    parts = jnp.split(piece, cuts, axis=-1)
-    done = [gather_chunks(part, order) for part, order in zip(parts, orders)]
+        lead = [bits.index((axis, j))] + lead
+    return buf, lead
+
+
+def gather_natural(buf, lead):
+    count = len(lead)
+    perm = [lead.index(k) for k in reversed(range(count))]
+    perm += list(range(count, buf.ndim))
+    return jnp.transpose(buf, perm).reshape((2**count,) + buf.shape[count:])
+
+
+def gather_all(piece, common, orders, cuts):
+    buf, lead = gather_steps(piece, [], common)
+    parts = jnp.split(buf, cuts, axis=-1)
+    done = [gather_natural(*gather_steps(part, lead, order)) for part, order in zip(parts, orders)]
     return jnp.concatenate(done, axis=-1).reshape(-1)
 
 
-def scatter_chunks(full, order):
+def scatter_steps(buf, live, order):
     bits = flat_bits()
-    count = len(bits)
-    buf = full.reshape((2,) * count + full.shape[1:])
-    live = list(reversed(range(count)))
+    live = list(live)
     for axis, j in order:
         at = live.index(bits.index((axis, j)))
         high = (lax.axis_index(axis) >> j) & 1
@@ -65,13 +67,18 @@
         other = lax.dynamic_index_in_dim(buf, 1 - high, at, keepdims=False)
         buf = mine + lax.ppermute(other, axis, swap_pairs(axis, j))
         live.pop(at)
-    return buf
-
-
-def scatter_streams(full, orders, cuts):
-    parts = jnp.split(full, cuts, axis=-1)
-    done = [scatter_chunks(part, order) for part, order in zip(parts, orders)]
-    return jnp.concatenate(done, axis=-1).reshape(-1)
+    return buf, live
+
+
+def scatter_all(full, orders, cuts, common):
+    count = len(flat_bits())
+    buf = full.reshape((2,) * count + full.shape[1:])
+    live = list(reversed(range(count)))
+    parts = jnp.split(buf, cuts, axis=-1)
+    done = [scatter_steps(part, live, order) for part, order in zip(parts, orders)]
+    buf = jnp.concatenate([part for part, _ in done], axis=-1)
+    buf, _ = scatter_steps(buf, done[0][1], common)
+    return buf.reshape(-1)
 
 
 def rows_sum(values):
@@ -81,11 +88,10 @@
     return tuple(total)
 
 
-GATHER_ORDERS = (
-    [("dp", 2), ("dp", 4), ("dp", 1), ("rows", 1), ("dp", 3), ("dp", 0), ("rows", 0)],
-    [("dp", 4), ("rows", 1), ("dp", 2), ("dp", 1), ("rows", 0), ("dp", 3), ("dp", 0)],
-)
+GATHER_COMMON = [("dp", 2), ("dp", 4), ("dp", 1), ("rows", 1), ("dp", 3)]
+GATHER_ORDERS = ([("dp", 0), ("rows", 0)], [("rows", 0), ("dp", 0)])
 SCATTER_ORDERS = tuple(order[::-1] for order in GATHER_ORDERS)
+SCATTER_COMMON = GATHER_COMMON[::-1]
 
 
 def up_two(v):
@@ -151,7 +157,7 @@
     row_count = lax.axis_size("rows")
     cells = cells_here * row_count
     images = block_input.shape[0] * lax.axis_size("dp")
-    flat = gather_streams(stacked[0].reshape(16, -1), GATHER_ORDERS, [254])
+    flat = gather_all(stacked[0].reshape(16, -1), GATHER_COMMON, GATHER_ORDERS, [254])
     weight = flat.reshape(cin, wide)
     segment = lax.axis_index("segment")
     held = saved_maps[0, 0]
@@ -208,7 +214,7 @@
 
     def spread(term):
         flat_term = (term / images).reshape(shards, 8, -1)
-        return scatter_streams(flat_term, SCATTER_ORDERS, [512])
+        return scatter_all(flat_term, SCATTER_ORDERS, [512], SCATTER_COMMON)
 
     def spread_still(term):
         return jnp.zeros((chunk,), jnp.float32)

time: 222 us -> 235 us (1.059)
  waiting for transfers between devices: 62.4 us -> 83.2 us
  loops' own time: 14.5 us -> 0.29 us
  starting transfers between devices: 74.1 us -> 66.6 us
  local copies, waits for them, and re-layouts: 34.1 us -> 40.8 us
  other arithmetic: 25.1 us -> 31.5 us
    ppermute x28 -> x18, waiting for transfers between devices: 53.7 us -> 74.5 us  [the longest x9 49.4 us: scatter_steps(): buf = mine + lax.ppermute(other, axis, swap_pairs(axis, j))]
    ppermute x28 -> x18, starting transfers between devices: 53.5 us -> 35.9 us  [the longest x9 18.7 us: gather_steps(): recv = lax.ppermute(buf, axis, swap_pairs(axis, j))]
    another operation x1, loops' own time: 13 us -> 0.07 us  [body(): grad_out = lax.cond(segment == 0, lead_branch, lead_still)]
    ppermute x2, starting transfers between devices: 4.95 us -> 14 us  [rows_sum(): total = total + lax.ppermute(total, 'rows', swap_pairs('rows', j))]
    add x14 -> x9, other arithmetic: 5.89 us -> 10.7 us  [scatter_steps(): buf = mine + lax.ppermute(other, axis, swap_pairs(axis, j))]
    unnamed x35 -> x41, local copies, waits for them, and re-layouts: 3.9 us -> 5.78 us
    squeeze x14 -> x8, local copies, waits for them, and re-layouts: 6.55 us -> 7.86 us  [scatter_steps(): other = lax.dynamic_index_in_dim(buf, 1 - high, at, keepdims=False)]
    another operation x26 -> x17, other arithmetic: 4.01 us -> 4.8 us  [gather_steps(): jnp.stack([jnp.where(high == 0, buf, recv), jnp.where(high == 0, recv, bu...]
  transfers between devices with their start and end apart: 36 -> 26, of which waited for: 22 -> 19; matrix products, arithmetic and copies ran while one was open for 18% -> 17% of each run, Pallas kernels for 0% -> 0%
where the time goes in v2:
time: 235 us; the launch traced here: 231 us
  waiting for transfers between devices  83.2 us (35%)
  starting transfers between devices  66.6 us (28%)
  local copies, waits for them, and re-layouts  40.8 us (17%)
  other arithmetic  31.5 us (13%)
  matrix products  7.38 us (3%)
    ppermute x9, waiting for transfers between devices, scatter_steps(): buf = mine + lax.ppermute(other, axis, swap_pairs(axis, j))  49.4 us
    ppermute x9, waiting for transfers between devices, gather_steps(): recv = lax.ppermute(buf, axis, swap_pairs(axis, j))  25 us
    ppermute x9, starting transfers between devices, gather_steps(): recv = lax.ppermute(buf, axis, swap_pairs(axis, j))  18.7 us
    ppermute x9, starting transfers between devices, scatter_steps(): buf = mine + lax.ppermute(other, axis, swap_pairs(axis, j))  17.1 us
    ppermute x2, starting transfers between devices, rows_sum(): total = total + lax.ppermute(total, 'rows', swap_pairs('rows', j))  14 us
    add x9, other arithmetic, scatter_steps(): buf = mine + lax.ppermute(other, axis, swap_pairs(axis, j))  10.7 us
    squeeze x8, local copies, waits for them, and re-layouts, scatter_steps(): other = lax.dynamic_index_in_dim(buf, 1 - high, at, keepdims=False)  7.86 us
    reshape x1, local copies, waits for them, and re-layouts, scatter_all(): buf = full.reshape((2,) * count + full.shape[1:])  7.15 us
  transfers between devices with their start and end apart: 26, of which 19 were waited for; matrix products, arithmetic and copies ran while one was open for 17% of the time, Pallas kernels for 0%

profile of v2, /device:TPU:8, one launch (start us, length us, event | category | flops | bytes accessed | tf_op | source)
XLA Modules:
  0.0 231.1 jit_solution(8552998023404407340)
XLA Ops:
  1.6 7.3 %collective-permute-start.19 = (bf16[16,507]{1,0:T(8,128)(2,1)S(1)}, bf16[16,507]{1,0:T(8,128)(2,1)S(1)}, u32[]{:S(2)}, u32[]{:S(2)}) collective-permute-start(bf16[16,507]{1,0:T(8,128)(2,1)S(1)} %reshape_squeeze.9), channel_id=1, source_target_pairs={{0,32},{8,40},{16,48},{24,56},{32,0},{40,8},{48,16},{56,24},{64,96... | collective-permute-start | bytes 48680 | tf_op jit(solution)/shard_map/ppermute | solution.py:39
  10.6 3.1 %collective-permute-start.20 = (bf16[2,16,507]{2,1,0:T(8,128)(2,1)S(1)}, bf16[2,16,507]{2,1,0:T(8,128)(2,1)S(1)}, u32[]{:S(2)}, u32[]{:S(2)}) collective-permute-start(bf16[2,16,507]{2,1,0:T(8,128)(2,1)S(1)} %pad_maximum_fusion.9), channel_id=1, source_target_pairs={{0,128},{8,136},{16,144},{24,152},{32,160},{40,168},{48,176},{56,1... | collective-permute-start | bytes 97352 | tf_op jit(solution)/shard_map/ppermute | solution.py:39
  13.7 2.4 %collective-permute-done.20 = bf16[2,16,507]{2,1,0:T(8,128)(2,1)S(1)} collective-permute-done((bf16[2,16,507]{2,1,0:T(8,128)(2,1)S(1)}, bf16[2,16,507]{2,1,0:T(8,128)(2,1)S(1)}, u32[]{:S(2)}, u32[]{:S(2)}) %collective-permute-start.20) | collective-permute-done | bytes 32480 | tf_op jit(solution)/shard_map/ppermute | solution.py:39
  16.1 2.1 collective-permute-start.21
  18.2 3.9 %collective-permute-done.21 = bf16[2,2,16,507]{3,2,1,0:T(8,128)(2,1)S(1)} collective-permute-done((bf16[2,2,16,507]{3,2,1,0:T(8,128)(2,1)S(1)}, bf16[2,2,16,507]{3,2,1,0:T(8,128)(2,1)S(1)}, u32[]{:S(2)}, u32[]{:S(2)}) %collective-permute-start.21) | collective-permute-done | bytes 64928 | tf_op jit(solution)/shard_map/ppermute | solution.py:39
  22.1 2.4 %collective-permute-start.22 = (bf16[2,2,2,16,507]{4,3,2,1,0:T(8,128)(2,1)S(1)}, bf16[2,2,2,16,507]{4,3,2,1,0:T(8,128)(2,1)S(1)}, u32[]{:S(2)}, u32[]{:S(2)}) collective-permute-start(bf16[2,2,2,16,507]{4,3,2,1,0:T(8,128)(2,1)S(1)} %pad_maximum_fusion.7), channel_id=1, source_target_pairs={{0,2},{1,3},{2,0},{3,1},{4,6},{5,7},{6,4},{7,5},{8,10},{9,11},{10,... | collective-permute-start | bytes 389384 | tf_op jit(solution)/shard_map/ppermute | solution.py:39
  24.5 4.2 %collective-permute-done.22 = bf16[2,2,2,16,507]{4,3,2,1,0:T(8,128)(2,1)S(1)} collective-permute-done((bf16[2,2,2,16,507]{4,3,2,1,0:T(8,128)(2,1)S(1)}, bf16[2,2,2,16,507]{4,3,2,1,0:T(8,128)(2,1)S(1)}, u32[]{:S(2)}, u32[]{:S(2)}) %collective-permute-start.22) | collective-permute-done | bytes 129824 | tf_op jit(solution)/shard_map/ppermute | solution.py:39
  30.4 4.9 %collective-permute-done.23 = bf16[2,2,2,2,16,507]{5,4,3,2,1,0:T(8,128)(2,1)S(1)} collective-permute-done((bf16[2,2,2,2,16,507]{5,4,3,2,1,0:T(8,128)(2,1)S(1)}, bf16[2,2,2,2,16,507]{5,4,3,2,1,0:T(8,128)(2,1)S(1)}, u32[]{:S(2)}, u32[]{:S(2)}) %collective-permute-start.23) | collective-permute-done | bytes 259616 | tf_op jit(solution)/shard_map/ppermute | solution.py:39
  36.6 6.6 %collective-permute-done.26 = bf16[2,2,2,2,2,16,253]{6,5,4,3,2,1,0:T(8,128)(2,1)S(1)} collective-permute-done((bf16[2,2,2,2,2,16,253]{6,5,4,3,2,1,0:T(8,128)(2,1)S(1)}, bf16[2,2,2,2,2,16,253]{6,5,4,3,2,1,0:T(8,128)(2,1)S(1)}, u32[]{:S(2)}, u32[]{:S(2)}) %collective-permute-start.26) | collective-permute-done | bytes 259104 | tf_op jit(solution)/shard_map/ppermute | solution.py:39
  48.9 3.4 %collective-permute-start.29 = (bf16[2,32,2496]{2,1,0:T(8,128)(2,1)}, bf16[2,32,2496]{2,1,0:T(8,128)(2,1)}, u32[]{:S(2)}, u32[]{:S(2)}) collective-permute-start(bf16[2,32,2496]{2,1,0:T(8,128)(2,1)} %get-tuple-element.219), channel_id=1, source_target_pairs={{0,1},{1,2},{2,3},{4,5},{5,6},{6,7},{8,9},{9,10},{10,11},{12,13},{... | collective-permute-start | bytes 958472 | tf_op jit(solution)/shard_map/ppermute | solution.py:12
  52.3 3.2 %collective-permute-start.30 = (bf16[2,32,2496]{2,1,0:T(8,128)(2,1)}, bf16[2,32,2496]{2,1,0:T(8,128)(2,1)}, u32[]{:S(2)}, u32[]{:S(2)}) collective-permute-start(bf16[2,32,2496]{2,1,0:T(8,128)(2,1)} %get-tuple-element.220), channel_id=1, source_target_pairs={{1,0},{2,1},{3,2},{5,4},{6,5},{7,6},{9,8},{10,9},{11,10},{13,12},{... | collective-permute-start | bytes 958472 | tf_op jit(solution)/shard_map/ppermute | solution.py:15
  55.5 2.3 conditional.8
  62.4 2.2 pad_maximum_fusion
  64.6 5.2 %reshape_reshape.3 = bf16[416,2496]{1,0:T(8,128)(2,1)S(1)} reshape(bf16[128,16,507]{2,1,0:T(8,128)(2,1)} %pad_maximum_fusion) | data formatting | bytes 4153344 | tf_op jit(solution)/shard_map/reshape;reshape | solution.py:161
  69.9 2.9 %conditional.9 = (bf16[128,2496]{0,1:T(8,128)(2,1)}) conditional(s32[]{:T(128)} %convert_element_type.235, () %tuple.75, (bf16[128,416]{0,1:T(8,128)(2,1)}, bf16[416,2496]{1,0:T(8,128)(2,1)S(1)}) %tuple.76), branch_computations={%region_2.3_spmd, %region_3.4_spmd} | conditional | flops 266133504 | bytes 2822152 | solution.py:210
  69.9 2.8 %convolution_convert_fusion.1 = bf16[128,2496]{0,1:T(8,128)(2,1)} fusion(bf16[128,416]{0,1:T(8,128)(2,1)} %get-tuple-element.150, bf16[416,2496]{1,0:T(8,128)(2,1)S(1)} %get-tuple-element.87), kind=kOutput, calls=%fused_computation.6 | convolution fusion | flops 266133504 | bytes 2822144 | tf_op jit(solution)/shard_map/cond/branch_1_fun/dot_general | solution.py:205
  72.8 2.2 copy.38
  74.9 2.1 collective-permute-start.28
  77.1 2.2 collective-permute-start.18
  83.4 3.6 %conditional.10 = (f32[416,2496]{1,0:T(8,128)}) conditional(s32[]{:T(128)} %convert_element_type.235, () %tuple.74, (bf16[1,1,4,32,2496]{4,3,2,1,0:T(8,128)(2,1)S(1)}, bf16[128,416]{0,1:T(8,128)(2,1)}) %tuple.175), branch_computations={%region_4.5_spmd, %region_5.6_spmd} | conditional | flops 265814016 | bytes 4898824 | solution.py:233
  83.4 3.6 %fusion.45 = f32[416,2496]{1,0:T(8,128)} fusion(bf16[128,416]{0,1:T(8,128)(2,1)} %get-tuple-element.153, bf16[128,2496]{1,0:T(8,128)(2,1)S(1)} %bitcast.181), kind=kOutput, calls=%fused_computation.234 | convolution fusion | flops 265814016 | bytes 4898816 | tf_op jit(solution)/shard_map/cond/branch_1_fun/dot_general | solution.py:226
  87.0 107.5 %conditional.11 = (f32[8112]{0:T(1024)S(1)}) conditional(s32[]{:T(128)} %convert_element_type.235, () %tuple.73, f32[416,2496]{1,0:T(8,128)} %get-tuple-element.252), branch_computations={%region_6.7_spmd, %region_7.8_spmd} | conditional | flops 2328212 | bytes 91789992 | solution.py:234
  87.0 4.6 %broadcast_multiply_fusion = f32[416,2496]{1,0:T(8,128)} fusion(f32[416,2496]{1,0:T(8,128)} %param.7), kind=kLoop, calls=%fused_computation.7 | loop fusion | flops 1038336 | bytes 8306688 | tf_op jit(solution)/shard_map/cond/branch_1_fun/div | solution.py:216
  91.5 7.2 %reshape.112 = f32[2,2,2,2,2,2,2,8,1014]{8,7,6,5,4,3,2,1,0:T(8,128)} reshape(f32[416,2496]{1,0:T(8,128)} %broadcast_multiply_fusion) | data formatting | bytes 8306688 | tf_op jit(solution)/shard_map/cond/branch_1_fun/reshape;cond/branch_1_fun/reshape | solution.py:75
  98.7 3.2 %split.21 = f32[2,2,2,2,2,2,2,8,502]{8,7,6,5,4,3,2,1,0:T(8,128)} slice(f32[2,2,2,2,2,2,2,8,1014]{8,7,6,5,4,3,2,1,0:T(8,128)} %reshape.112), slice={[0:2], [0:2], [0:2], [0:2], [0:2], [0:2], [0:2], [0:8], [512:1014]} | slice | bytes 4112384 | tf_op jit(solution)/shard_map/cond/branch_1_fun/split | solution.py:77
  101.9 2.3 dynamic-slice_bitcast_fusion
  104.8 3.3 %split.20 = f32[2,2,2,2,2,2,2,8,512]{8,7,6,5,4,3,2,1,0:T(8,128)} slice(f32[2,2,2,2,2,2,2,8,1014]{8,7,6,5,4,3,2,1,0:T(8,128)} %reshape.112), slice={[0:2], [0:2], [0:2], [0:2], [0:2], [0:2], [0:2], [0:8], [0:512]} | slice | bytes 4194304 | tf_op jit(solution)/shard_map/cond/branch_1_fun/split | solution.py:77
  108.0 2.3 dynamic-slice_bitcast_fusion.1
  110.3 9.0 %collective-permute-done.2 = f32[2,2,2,2,2,2,8,502]{7,6,5,4,3,2,1,0:T(8,128)} collective-permute-done((f32[2,2,2,2,2,2,8,502]{7,6,5,4,3,2,1,0:T(8,128)}, f32[2,2,2,2,2,2,8,502]{7,6,5,4,3,2,1,0:T(8,128)}, u32[]{:S(2)}, u32[]{:S(2)}) %collective-permute-start.2) | collective-permute-done | bytes 1028128 | tf_op jit(solution)/shard_map/cond/branch_1_fun/ppermute | solution.py:68
  122.2 6.8 %collective-permute-done = f32[2,2,2,2,2,2,8,512]{7,6,5,4,3,2,1,0:T(8,128)} collective-permute-done((f32[2,2,2,2,2,2,8,512]{7,6,5,4,3,2,1,0:T(8,128)}, f32[2,2,2,2,2,2,8,512]{7,6,5,4,3,2,1,0:T(8,128)}, u32[]{:S(2)}, u32[]{:S(2)}) %collective-permute-start) | collective-permute-done | bytes 1048608 | tf_op jit(solution)/shard_map/cond/branch_1_fun/ppermute | solution.py:68
  135.8 5.2 %collective-permute-done.1 = f32[2,2,2,2,2,8,512]{6,5,4,3,2,1,0:T(8,128)} collective-permute-done((f32[2,2,2,2,2,8,512]{6,5,4,3,2,1,0:T(8,128)}, f32[2,2,2,2,2,8,512]{6,5,4,3,2,1,0:T(8,128)}, u32[]{:S(2)}, u32[]{:S(2)}) %collective-permute-start.1) | collective-permute-done | bytes 524320 | tf_op jit(solution)/shard_map/cond/branch_1_fun/ppermute | solution.py:68
  145.1 8.2 %collective-permute-done.4 = f32[2,2,2,2,8,1014]{5,4,3,2,1,0:T(8,128)} collective-permute-done((f32[2,2,2,2,8,1014]{5,4,3,2,1,0:T(8,128)}, f32[2,2,2,2,8,1014]{5,4,3,2,1,0:T(8,128)}, u32[]{:S(2)}, u32[]{:S(2)}) %collective-permute-start.4) | collective-permute-done | bytes 519200 | tf_op jit(solution)/shard_map/cond/branch_1_fun/ppermute | solution.py:68
  156.1 2.1 collective-permute-start.5
  158.1 9.0 %collective-permute-done.5 = f32[2,2,2,8,1014]{4,3,2,1,0:T(8,128)} collective-permute-done((f32[2,2,2,8,1014]{4,3,2,1,0:T(8,128)}, f32[2,2,2,8,1014]{4,3,2,1,0:T(8,128)}, u32[]{:S(2)}, u32[]{:S(2)}) %collective-permute-start.5) | collective-permute-done | bytes 259616 | tf_op jit(solution)/shard_map/cond/branch_1_fun/ppermute | solution.py:68
  169.6 2.9 %collective-permute-start.6 = (f32[2,2,8,1014]{3,2,1,0:T(8,128)}, f32[2,2,8,1014]{3,2,1,0:T(8,128)}, u32[]{:S(2)}, u32[]{:S(2)}) collective-permute-start(f32[2,2,8,1014]{3,2,1,0:T(8,128)} %dynamic-slice_bitcast_fusion.5), channel_id=1, source_target_pairs={{0,16},{8,24},{16,0},{24,8},{32,48},{40,56},{48,32},{56,40},{64,80... | collective-permute-start | bytes 389384 | tf_op jit(solution)/shard_map/cond/branch_1_fun/ppermute | solution.py:68
  172.4 4.7 %collective-permute-done.6 = f32[2,2,8,1014]{3,2,1,0:T(8,128)} collective-permute-done((f32[2,2,8,1014]{3,2,1,0:T(8,128)}, f32[2,2,8,1014]{3,2,1,0:T(8,128)}, u32[]{:S(2)}, u32[]{:S(2)}) %collective-permute-start.6) | collective-permute-done | bytes 129824 | tf_op jit(solution)/shard_map/cond/branch_1_fun/ppermute | solution.py:68
  178.8 3.0 %collective-permute-start.7 = (f32[2,8,1014]{2,1,0:T(8,128)S(1)}, f32[2,8,1014]{2,1,0:T(8,128)}, u32[]{:S(2)}, u32[]{:S(2)}) collective-permute-start(f32[2,8,1014]{2,1,0:T(8,128)S(1)} %dynamic-slice_bitcast_fusion.6), channel_id=1, source_target_pairs={{0,128},{8,136},{16,144},{24,152},{32,160},{40,168},{48,176},{56,1... | collective-permute-start | bytes 194696 | tf_op jit(solution)/shard_map/cond/branch_1_fun/ppermute | solution.py:68
  181.8 2.9 %collective-permute-done.7 = f32[2,8,1014]{2,1,0:T(8,128)} collective-permute-done((f32[2,8,1014]{2,1,0:T(8,128)S(1)}, f32[2,8,1014]{2,1,0:T(8,128)}, u32[]{:S(2)}, u32[]{:S(2)}) %collective-permute-start.7) | collective-permute-done | bytes 64928 | tf_op jit(solution)/shard_map/cond/branch_1_fun/ppermute | solution.py:68
  185.6 5.8 %collective-permute-start.8 = (f32[8,1014]{1,0:T(8,128)S(1)}, f32[8,1014]{1,0:T(8,128)}, u32[]{:S(2)}, u32[]{:S(2)}) collective-permute-start(f32[8,1014]{1,0:T(8,128)S(1)} %dynamic-slice_bitcast_fusion.7), channel_id=1, source_target_pairs={{0,32},{8,40},{16,48},{24,56},{32,0},{40,8},{48,16},{56,24},{64,96... | collective-permute-start | bytes 97352 | tf_op jit(solution)/shard_map/cond/branch_1_fun/ppermute | solution.py:68
  191.4 2.2 collective-permute-done.8
  196.3 11.7 %collective-permute-start.31 = (f32[2,2496]{1,0:T(2,128)S(1)}, f32[2,2496]{1,0:T(2,128)S(1)}, u32[]{:S(2)}, u32[]{:S(2)}) collective-permute-start(f32[2,2496]{1,0:T(2,128)S(1)} %pad_maximum_fusion.10), channel_id=1, source_target_pairs={{0,1},{1,0},{2,3},{3,2},{4,5},{5,4},{6,7},{7,6},{8,9},{9,8},{10,11... | collective-permute-start | bytes 59912 | tf_op jit(solution)/shard_map/ppermute | solution.py:87
  208.0 3.8 %collective-permute-done.31 = f32[2,2496]{1,0:T(2,128)S(1)} collective-permute-done((f32[2,2496]{1,0:T(2,128)S(1)}, f32[2,2496]{1,0:T(2,128)S(1)}, u32[]{:S(2)}, u32[]{:S(2)}) %collective-permute-start.31) | collective-permute-done | bytes 20000 | tf_op jit(solution)/shard_map/ppermute | solution.py:87
  211.8 2.3 %collective-permute-start.32 = (f32[2,2496]{1,0:T(2,128)S(1)}, f32[2,2496]{1,0:T(2,128)S(1)}, u32[]{:S(2)}, u32[]{:S(2)}) collective-permute-start(f32[2,2496]{1,0:T(2,128)S(1)} %fusion.41), channel_id=1, source_target_pairs={{0,2},{1,3},{2,0},{3,1},{4,6},{5,7},{6,4},{7,5},{8,10},{9,11},{10,... | collective-permute-start | bytes 59912 | tf_op jit(solution)/shard_map/ppermute | solution.py:87
  214.1 2.1 copy.40
  218.7 1.9 collective-permute-start.33
  220.7 3.9 %collective-permute-start.34 = (bf16[2,32,2496]{2,1,0:T(8,128)(2,1)S(1)}, bf16[2,32,2496]{2,1,0:T(8,128)(2,1)S(1)}, u32[]{:S(2)}, u32[]{:S(2)}) collective-permute-start(bf16[2,32,2496]{2,1,0:T(8,128)(2,1)S(1)} %get-tuple-element.218), channel_id=1, source_target_pairs={{1,0},{2,1},{3,2},{5,4},{6,5},{7,6},{9,8},{10,9},{11,10},{13,12},{... | collective-permute-start | bytes 958472 | tf_op jit(solution)/shard_map/ppermute | solution.py:15
  224.7 3.0 %collective-permute-done.33 = bf16[2,32,2496]{2,1,0:T(8,128)(2,1)S(1)} collective-permute-done((bf16[2,32,2496]{2,1,0:T(8,128)(2,1)S(1)}, bf16[2,32,2496]{2,1,0:T(8,128)(2,1)S(1)}, u32[]{:S(2)}, u32[]{:S(2)}) %collective-permute-start.33) | collective-permute-done | bytes 319520 | tf_op jit(solution)/shard_map/ppermute | solution.py:12
  227.7 1.9 collective-permute-done.34
  (147 shorter events, 51.0 us)
Async XLA Ops:
  1.6 9.0 %collective-permute-start.19 = (bf16[16,507]{1,0:T(8,128)(2,1)S(1)}, bf16[16,507]{1,0:T(8,128)(2,1)S(1)}, u32[]{:S(2)}, u32[]{:S(2)}) collective-permute-start(bf16[16,507]{1,0:T(8,128)(2,1)S(1)} %reshape_squeeze.9), channel_id=1, source_target_pairs={{0,32},{8,40},{16,48},{24,56},{32,0},{40,8},{48,16},{56,24},{64,96... | collective-permute-start | bytes 48680 | tf_op jit(solution)/shard_map/ppermute | solution.py:39
  10.6 5.5 %collective-permute-start.20 = (bf16[2,16,507]{2,1,0:T(8,128)(2,1)S(1)}, bf16[2,16,507]{2,1,0:T(8,128)(2,1)S(1)}, u32[]{:S(2)}, u32[]{:S(2)}) collective-permute-start(bf16[2,16,507]{2,1,0:T(8,128)(2,1)S(1)} %pad_maximum_fusion.9), channel_id=1, source_target_pairs={{0,128},{8,136},{16,144},{24,152},{32,160},{40,168},{48,176},{56,1... | collective-permute-start | bytes 97352 | tf_op jit(solution)/shard_map/ppermute | solution.py:39
  16.1 6.0 %collective-permute-start.21 = (bf16[2,2,16,507]{3,2,1,0:T(8,128)(2,1)S(1)}, bf16[2,2,16,507]{3,2,1,0:T(8,128)(2,1)S(1)}, u32[]{:S(2)}, u32[]{:S(2)}) collective-permute-start(bf16[2,2,16,507]{3,2,1,0:T(8,128)(2,1)S(1)} %pad_maximum_fusion.8), channel_id=1, source_target_pairs={{0,16},{8,24},{16,0},{24,8},{32,48},{40,56},{48,32},{56,40},{64,80... | collective-permute-start | bytes 194696 | tf_op jit(solution)/shard_map/ppermute | solution.py:39
  22.1 6.6 %collective-permute-start.22 = (bf16[2,2,2,16,507]{4,3,2,1,0:T(8,128)(2,1)S(1)}, bf16[2,2,2,16,507]{4,3,2,1,0:T(8,128)(2,1)S(1)}, u32[]{:S(2)}, u32[]{:S(2)}) collective-permute-start(bf16[2,2,2,16,507]{4,3,2,1,0:T(8,128)(2,1)S(1)} %pad_maximum_fusion.7), channel_id=1, source_target_pairs={{0,2},{1,3},{2,0},{3,1},{4,6},{5,7},{6,4},{7,5},{8,10},{9,11},{10,... | collective-permute-start | bytes 389384 | tf_op jit(solution)/shard_map/ppermute | solution.py:39
  28.7 7.7 %copy-start.3 = (bf16[1,1,4,32,2496]{4,3,2,1,0:T(8,128)(2,1)S(1)}, bf16[1,1,4,32,2496]{4,3,2,1,0:T(8,128)(2,1)}, u32[]{:S(2)}) copy-start(bf16[1,1,4,32,2496]{4,3,2,1,0:T(8,128)(2,1)} %param.27) | copy-start | bytes 1916932
  28.8 6.5 %collective-permute-start.23 = (bf16[2,2,2,2,16,507]{5,4,3,2,1,0:T(8,128)(2,1)S(1)}, bf16[2,2,2,2,16,507]{5,4,3,2,1,0:T(8,128)(2,1)S(1)}, u32[]{:S(2)}, u32[]{:S(2)}) collective-permute-start(bf16[2,2,2,2,16,507]{5,4,3,2,1,0:T(8,128)(2,1)S(1)} %pad_maximum_fusion.6), channel_id=1, source_target_pairs={{0,64},{8,72},{16,80},{24,88},{32,96},{40,104},{48,112},{56,120},{... | collective-permute-start | bytes 778760 | tf_op jit(solution)/shard_map/ppermute | solution.py:39
  35.4 7.8 %collective-permute-start.26 = (bf16[2,2,2,2,2,16,253]{6,5,4,3,2,1,0:T(8,128)(2,1)S(1)}, bf16[2,2,2,2,2,16,253]{6,5,4,3,2,1,0:T(8,128)(2,1)S(1)}, u32[]{:S(2)}, u32[]{:S(2)}) collective-permute-start(bf16[2,2,2,2,2,16,253]{6,5,4,3,2,1,0:T(8,128)(2,1)S(1)} %pad_maximum_fusion.5), channel_id=1, source_target_pairs={{0,1},{1,0},{2,3},{3,2},{4,5},{5,4},{6,7},{7,6},{8,9},{9,8},{10,11... | collective-permute-start | bytes 777224 | tf_op jit(solution)/shard_map/ppermute | solution.py:39
  36.5 9.2 %collective-permute-start.24 = (bf16[2,2,2,2,2,16,254]{6,5,4,3,2,1,0:T(8,128)(2,1)S(1)}, bf16[2,2,2,2,2,16,254]{6,5,4,3,2,1,0:T(8,128)(2,1)S(1)}, u32[]{:S(2)}, u32[]{:S(2)}) collective-permute-start(bf16[2,2,2,2,2,16,254]{6,5,4,3,2,1,0:T(8,128)(2,1)S(1)} %fusion.40), channel_id=1, source_target_pairs={{0,8},{8,0},{16,24},{24,16},{32,40},{40,32},{48,56},{56,48},{64,72... | collective-permute-start | bytes 780296 | tf_op jit(solution)/shard_map/ppermute | solution.py:39
  44.4 14.0 %collective-permute-start.27 = (bf16[2,2,2,2,2,2,16,253]{7,6,5,4,3,2,1,0:T(8,128)(2,1)}, bf16[2,2,2,2,2,2,16,253]{7,6,5,4,3,2,1,0:T(8,128)(2,1)}, u32[]{:S(2)}, u32[]{:S(2)}) collective-permute-start(bf16[2,2,2,2,2,2,16,253]{7,6,5,4,3,2,1,0:T(8,128)(2,1)} %pad_maximum_fusion.4), channel_id=1, source_target_pairs={{0,8},{8,0},{16,24},{24,16},{32,40},{40,32},{48,56},{56,48},{64,72... | collective-permute-start | bytes 1554440 | tf_op jit(solution)/shard_map/ppermute | solution.py:39
  45.8 9.7 %copy-start.16 = (bf16[1,2,2,2,2,2,16,254]{7,6,5,4,3,2,1,0:T(8,128)(2,1)}, bf16[1,2,2,2,2,2,16,254]{7,6,5,4,3,2,1,0:T(8,128)(2,1)S(1)}, u32[]{:S(2)}) copy-start(bf16[1,2,2,2,2,2,16,254]{7,6,5,4,3,2,1,0:T(8,128)(2,1)S(1)} %get-tuple-element.221) | copy-start | bytes 780292
  45.8 9.7 %copy-start.18 = (bf16[1,2,2,2,2,2,16,254]{7,6,5,4,3,2,1,0:T(8,128)(2,1)}, bf16[1,2,2,2,2,2,16,254]{7,6,5,4,3,2,1,0:T(8,128)(2,1)S(1)}, u32[]{:S(2)}) copy-start(bf16[1,2,2,2,2,2,16,254]{7,6,5,4,3,2,1,0:T(8,128)(2,1)S(1)} %get-tuple-element.222) | copy-start | bytes 780292
  45.9 9.6 %copy-start.28 = (bf16[416,384]{1,0:T(8,128)(2,1)S(1)}, bf16[416,384]{1,0:T(8,128)(2,1)}, u32[]{:S(2)}) copy-start(bf16[416,384]{1,0:T(8,128)(2,1)} %param.31) | copy-start | bytes 958468
  45.9 9.6 %copy-start.31 = (bf16[1,4,32,384]{3,2,1,0:T(8,128)(2,1)S(1)}, bf16[1,4,32,384]{3,2,1,0:T(8,128)(2,1)}, u32[]{:S(2)}) copy-start(bf16[1,4,32,384]{3,2,1,0:T(8,128)(2,1)} %param.28) | copy-start | bytes 294916
  45.9 9.6 %copy-start.33 = (bf16[1,2,16,384]{3,2,1,0:T(8,128)(2,1)S(1)}, bf16[1,2,16,384]{3,2,1,0:T(8,128)(2,1)}, u32[]{:S(2)}) copy-start(bf16[1,2,16,384]{3,2,1,0:T(8,128)(2,1)} %param.29) | copy-start | bytes 73732
  45.9 9.6 %copy-start.34 = (bf16[1,1,8,384]{3,2,1,0:T(8,128)(2,1)S(1)}, bf16[1,1,8,384]{3,2,1,0:T(8,128)(2,1)}, u32[]{:S(2)}) copy-start(bf16[1,1,8,384]{3,2,1,0:T(8,128)(2,1)} %param.30) | copy-start | bytes 18436
  46.8 13.2 %collective-permute-start.25 = (bf16[2,2,2,2,2,2,16,254]{7,6,5,4,3,2,1,0:T(8,128)(2,1)}, bf16[2,2,2,2,2,2,16,254]{7,6,5,4,3,2,1,0:T(8,128)(2,1)}, u32[]{:S(2)}, u32[]{:S(2)}) collective-permute-start(bf16[2,2,2,2,2,2,16,254]{7,6,5,4,3,2,1,0:T(8,128)(2,1)} %pad_maximum_fusion.3), channel_id=1, source_target_pairs={{0,1},{1,0},{2,3},{3,2},{4,5},{5,4},{6,7},{7,6},{8,9},{9,8},{10,11... | collective-permute-start | bytes 1560584 | tf_op jit(solution)/shard_map/ppermute | solution.py:39
  48.9 31.3 %collective-permute-start.29 = (bf16[2,32,2496]{2,1,0:T(8,128)(2,1)}, bf16[2,32,2496]{2,1,0:T(8,128)(2,1)}, u32[]{:S(2)}, u32[]{:S(2)}) collective-permute-start(bf16[2,32,2496]{2,1,0:T(8,128)(2,1)} %get-tuple-element.219), channel_id=1, source_target_pairs={{0,1},{1,2},{2,3},{4,5},{5,6},{6,7},{8,9},{9,10},{10,11},{12,13},{... | collective-permute-start | bytes 958472 | tf_op jit(solution)/shard_map/ppermute | solution.py:12
  52.3 27.9 %collective-permute-start.30 = (bf16[2,32,2496]{2,1,0:T(8,128)(2,1)}, bf16[2,32,2496]{2,1,0:T(8,128)(2,1)}, u32[]{:S(2)}, u32[]{:S(2)}) collective-permute-start(bf16[2,32,2496]{2,1,0:T(8,128)(2,1)} %get-tuple-element.220), channel_id=1, source_target_pairs={{1,0},{2,1},{3,2},{5,4},{6,5},{7,6},{9,8},{10,9},{11,10},{13,12},{... | collective-permute-start | bytes 958472 | tf_op jit(solution)/shard_map/ppermute | solution.py:15
  59.9 1.0 copy-start.19
  74.9 7.0 %collective-permute-start.28 = (bf16[4,32,2496]{2,1,0:T(8,128)(2,1)}, bf16[4,32,2496]{2,1,0:T(8,128)(2,1)}, u32[]{:S(2)}, u32[]{:S(2)}) collective-permute-start(bf16[4,32,2496]{2,1,0:T(8,128)(2,1)} %bitcast.186), channel_id=1, source_target_pairs={{0,4},{1,5},{2,6},{3,7},{8,12},{9,13},{10,14},{11,15},{16,20},{17,... | collective-permute-start | bytes 1916936 | tf_op jit(solution)/shard_map/ppermute | solution.py:23
  77.1 4.8 %collective-permute-start.18 = (bf16[4,32,416]{2,1,0:T(8,128)(2,1)}, bf16[4,32,416]{2,1,0:T(8,128)(2,1)}, u32[]{:S(2)}, u32[]{:S(2)}) collective-permute-start(bf16[4,32,416]{2,1,0:T(8,128)(2,1)} %copy-done.30), channel_id=1, source_target_pairs={{0,4},{1,5},{2,6},{3,7},{8,12},{9,13},{10,14},{11,15},{16,20},{17,... | collective-permute-start | bytes 319496 | tf_op jit(solution)/shard_map/ppermute | solution.py:23
  80.2 1.4 copy-start.20
  81.9 1.1 copy-start.6
  81.9 1.5 copy-start.8
  87.0 108.1 %copy-start.9 = (f32[4,32,2496]{2,1,0:T(8,128)S(1)}, f32[4,32,2496]{2,1,0:T(8,128)}, u32[]{:S(2)}) copy-start(f32[4,32,2496]{2,1,0:T(8,128)} %copy-done.8) | copy-start | bytes 3833860
  104.2 15.1 %collective-permute-start.2 = (f32[2,2,2,2,2,2,8,502]{7,6,5,4,3,2,1,0:T(8,128)}, f32[2,2,2,2,2,2,8,502]{7,6,5,4,3,2,1,0:T(8,128)}, u32[]{:S(2)}, u32[]{:S(2)}) collective-permute-start(f32[2,2,2,2,2,2,8,502]{7,6,5,4,3,2,1,0:T(8,128)} %dynamic-slice_bitcast_fusion), channel_id=1, source_target_pairs={{0,8},{8,0},{16,24},{24,16},{32,40},{40,32},{48,56},{56,48},{64,72... | collective-permute-start | bytes 3084296 | tf_op jit(solution)/shard_map/cond/branch_1_fun/ppermute | solution.py:68
  110.3 18.6 %collective-permute-start = (f32[2,2,2,2,2,2,8,512]{7,6,5,4,3,2,1,0:T(8,128)}, f32[2,2,2,2,2,2,8,512]{7,6,5,4,3,2,1,0:T(8,128)}, u32[]{:S(2)}, u32[]{:S(2)}) collective-permute-start(f32[2,2,2,2,2,2,8,512]{7,6,5,4,3,2,1,0:T(8,128)} %dynamic-slice_bitcast_fusion.1), channel_id=1, source_target_pairs={{0,1},{1,0},{2,3},{3,2},{4,5},{5,4},{6,7},{7,6},{8,9},{9,8},{10,11... | collective-permute-start | bytes 3145736 | tf_op jit(solution)/shard_map/cond/branch_1_fun/ppermute | solution.py:68
  119.3 9.6 %copy-start.2 = (f32[2,2,2,2,2,2,2,8,512]{8,7,6,5,4,3,2,1,0:T(8,128)S(1)}, f32[2,2,2,2,2,2,2,8,512]{8,7,6,5,4,3,2,1,0:T(8,128)}, u32[]{:S(2)}) copy-start(f32[2,2,2,2,2,2,2,8,512]{8,7,6,5,4,3,2,1,0:T(8,128)} %split.20) | copy-start | bytes 6291460 | tf_op jit(solution)/shard_map/cond
  121.2 9.2 %copy-start.13 = (f32[2,2,2,2,2,2,8,502]{7,6,5,4,3,2,1,0:T(8,128)}, f32[2,2,2,2,2,2,8,502]{7,6,5,4,3,2,1,0:T(8,128)S(1)}, u32[]{:S(2)}) copy-start(f32[2,2,2,2,2,2,8,502]{7,6,5,4,3,2,1,0:T(8,128)S(1)} %bitcast_add_fusion) | copy-start | bytes 3084292 | tf_op jit(solution)/shard_map/cond
  122.2 12.4 %collective-permute-start.3 = (f32[2,2,2,2,2,8,502]{6,5,4,3,2,1,0:T(8,128)}, f32[2,2,2,2,2,8,502]{6,5,4,3,2,1,0:T(8,128)}, u32[]{:S(2)}, u32[]{:S(2)}) collective-permute-start(f32[2,2,2,2,2,8,502]{6,5,4,3,2,1,0:T(8,128)} %dynamic-slice_bitcast_fusion.2), channel_id=1, source_target_pairs={{0,1},{1,0},{2,3},{3,2},{4,5},{5,4},{6,7},{7,6},{8,9},{9,8},{10,11... | collective-permute-start | bytes 1542152 | tf_op jit(solution)/shard_map/cond/branch_1_fun/ppermute | solution.py:68
  130.4 1.2 copy-start.14
  131.5 9.5 %collective-permute-start.1 = (f32[2,2,2,2,2,8,512]{6,5,4,3,2,1,0:T(8,128)}, f32[2,2,2,2,2,8,512]{6,5,4,3,2,1,0:T(8,128)}, u32[]{:S(2)}, u32[]{:S(2)}) collective-permute-start(f32[2,2,2,2,2,8,512]{6,5,4,3,2,1,0:T(8,128)} %dynamic-slice_bitcast_fusion.3), channel_id=1, source_target_pairs={{0,8},{8,0},{16,24},{24,16},{32,40},{40,32},{48,56},{56,48},{64,72... | collective-permute-start | bytes 1572872 | tf_op jit(solution)/shard_map/cond/branch_1_fun/ppermute | solution.py:68
  133.0 8.1 %copy-start.15 = (f32[2,2,2,2,2,2,8,512]{7,6,5,4,3,2,1,0:T(8,128)S(1)}, f32[2,2,2,2,2,2,8,512]{7,6,5,4,3,2,1,0:T(8,128)}, u32[]{:S(2)}) copy-start(f32[2,2,2,2,2,2,8,512]{7,6,5,4,3,2,1,0:T(8,128)} %copy-done.14) | copy-start | bytes 3145732 | tf_op jit(solution)/shard_map/cond
  135.8 8.0 %copy-start.11 = (f32[2,2,2,2,2,8,502]{6,5,4,3,2,1,0:T(8,128)}, f32[2,2,2,2,2,8,502]{6,5,4,3,2,1,0:T(8,128)S(1)}, u32[]{:S(2)}) copy-start(f32[2,2,2,2,2,8,502]{6,5,4,3,2,1,0:T(8,128)S(1)} %bitcast_add_fusion.2) | copy-start | bytes 1542148 | tf_op jit(solution)/shard_map/cond
  143.8 9.5 %collective-permute-start.4 = (f32[2,2,2,2,8,1014]{5,4,3,2,1,0:T(8,128)}, f32[2,2,2,2,8,1014]{5,4,3,2,1,0:T(8,128)}, u32[]{:S(2)}, u32[]{:S(2)}) collective-permute-start(f32[2,2,2,2,8,1014]{5,4,3,2,1,0:T(8,128)} %fusion.4), channel_id=1, source_target_pairs={{0,64},{8,72},{16,80},{24,88},{32,96},{40,104},{48,112},{56,120},{... | collective-permute-start | bytes 1557512 | tf_op jit(solution)/shard_map/cond/branch_1_fun/ppermute | solution.py:68
  156.1 11.1 %collective-permute-start.5 = (f32[2,2,2,8,1014]{4,3,2,1,0:T(8,128)}, f32[2,2,2,8,1014]{4,3,2,1,0:T(8,128)}, u32[]{:S(2)}, u32[]{:S(2)}) collective-permute-start(f32[2,2,2,8,1014]{4,3,2,1,0:T(8,128)} %dynamic-slice_bitcast_fusion.4), channel_id=1, source_target_pairs={{0,2},{1,3},{2,0},{3,1},{4,6},{5,7},{6,4},{7,5},{8,10},{9,11},{10,... | collective-permute-start | bytes 778760 | tf_op jit(solution)/shard_map/cond/branch_1_fun/ppermute | solution.py:68
  169.6 7.6 %collective-permute-start.6 = (f32[2,2,8,1014]{3,2,1,0:T(8,128)}, f32[2,2,8,1014]{3,2,1,0:T(8,128)}, u32[]{:S(2)}, u32[]{:S(2)}) collective-permute-start(f32[2,2,8,1014]{3,2,1,0:T(8,128)} %dynamic-slice_bitcast_fusion.5), channel_id=1, source_target_pairs={{0,16},{8,24},{16,0},{24,8},{32,48},{40,56},{48,32},{56,40},{64,80... | collective-permute-start | bytes 389384 | tf_op jit(solution)/shard_map/cond/branch_1_fun/ppermute | solution.py:68
  178.8 5.9 %collective-permute-start.7 = (f32[2,8,1014]{2,1,0:T(8,128)S(1)}, f32[2,8,1014]{2,1,0:T(8,128)}, u32[]{:S(2)}, u32[]{:S(2)}) collective-permute-start(f32[2,8,1014]{2,1,0:T(8,128)S(1)} %dynamic-slice_bitcast_fusion.6), channel_id=1, source_target_pairs={{0,128},{8,136},{16,144},{24,152},{32,160},{40,168},{48,176},{56,1... | collective-permute-start | bytes 194696 | tf_op jit(solution)/shard_map/cond/branch_1_fun/ppermute | solution.py:68
  185.6 8.0 %collective-permute-start.8 = (f32[8,1014]{1,0:T(8,128)S(1)}, f32[8,1014]{1,0:T(8,128)}, u32[]{:S(2)}, u32[]{:S(2)}) collective-permute-start(f32[8,1014]{1,0:T(8,128)S(1)} %dynamic-slice_bitcast_fusion.7), channel_id=1, source_target_pairs={{0,32},{8,40},{16,48},{24,56},{32,0},{40,8},{48,16},{56,24},{64,96... | collective-permute-start | bytes 97352 | tf_op jit(solution)/shard_map/cond/branch_1_fun/ppermute | solution.py:68
  196.3 15.4 %collective-permute-start.31 = (f32[2,2496]{1,0:T(2,128)S(1)}, f32[2,2496]{1,0:T(2,128)S(1)}, u32[]{:S(2)}, u32[]{:S(2)}) collective-permute-start(f32[2,2496]{1,0:T(2,128)S(1)} %pad_maximum_fusion.10), channel_id=1, source_target_pairs={{0,1},{1,0},{2,3},{3,2},{4,5},{5,4},{6,7},{7,6},{8,9},{9,8},{10,11... | collective-permute-start | bytes 59912 | tf_op jit(solution)/shard_map/ppermute | solution.py:87
  211.8 6.8 %collective-permute-start.32 = (f32[2,2496]{1,0:T(2,128)S(1)}, f32[2,2496]{1,0:T(2,128)S(1)}, u32[]{:S(2)}, u32[]{:S(2)}) collective-permute-start(f32[2,2496]{1,0:T(2,128)S(1)} %fusion.41), channel_id=1, source_target_pairs={{0,2},{1,3},{2,0},{3,1},{4,6},{5,7},{6,4},{7,5},{8,10},{9,11},{10,... | collective-permute-start | bytes 59912 | tf_op jit(solution)/shard_map/ppermute | solution.py:87
  216.3 1.2 copy-start.25
  218.7 5.9 %copy-start.5 = (bf16[4,32,2496]{2,1,0:T(8,128)(2,1)}, bf16[4,32,2496]{2,1,0:T(8,128)(2,1)S(1)}, u32[]{:S(2)}) copy-start(bf16[4,32,2496]{2,1,0:T(8,128)(2,1)S(1)} %get-tuple-element.255) | copy-start | bytes 1916932
  218.7 9.0 %collective-permute-start.33 = (bf16[2,32,2496]{2,1,0:T(8,128)(2,1)S(1)}, bf16[2,32,2496]{2,1,0:T(8,128)(2,1)S(1)}, u32[]{:S(2)}, u32[]{:S(2)}) collective-permute-start(bf16[2,32,2496]{2,1,0:T(8,128)(2,1)S(1)} %get-tuple-element.217), channel_id=1, source_target_pairs={{0,1},{1,2},{2,3},{4,5},{5,6},{6,7},{8,9},{9,10},{10,11},{12,13},{... | collective-permute-start | bytes 958472 | tf_op jit(solution)/shard_map/ppermute | solution.py:12
  220.7 9.0 %collective-permute-start.34 = (bf16[2,32,2496]{2,1,0:T(8,128)(2,1)S(1)}, bf16[2,32,2496]{2,1,0:T(8,128)(2,1)S(1)}, u32[]{:S(2)}, u32[]{:S(2)}) collective-permute-start(bf16[2,32,2496]{2,1,0:T(8,128)(2,1)S(1)} %get-tuple-element.218), channel_id=1, source_target_pairs={{1,0},{2,1},{3,2},{5,4},{6,5},{7,6},{9,8},{10,9},{11,10},{13,12},{... | collective-permute-start | bytes 958472 | tf_op jit(solution)/shard_map/ppermute | solution.py:15
  224.6 6.3 %copy-start.4 = (bf16[1,1,4,32,2496]{4,3,2,1,0:T(8,128)(2,1)S(1)}, bf16[1,1,4,32,2496]{4,3,2,1,0:T(8,128)(2,1)}, u32[]{:S(2)}) copy-start(bf16[1,1,4,32,2496]{4,3,2,1,0:T(8,128)(2,1)} %param.27) | copy-start | bytes 1916932
  224.6 6.3 %copy-start.21 = (f32[25,2496]{1,0:T(8,128)S(1)}, f32[25,2496]{1,0:T(8,128)}, u32[]{:S(2)}) copy-start(f32[25,2496]{1,0:T(8,128)} %copy-done.20) | copy-start | bytes 748804
  224.6 6.3 %copy-start.29 = (bf16[1,4,32,416]{3,2,1,0:T(8,128)(2,1)S(1)}, bf16[1,4,32,416]{3,2,1,0:T(8,128)(2,1)}, u32[]{:S(2)}) copy-start(bf16[1,4,32,416]{3,2,1,0:T(8,128)(2,1)} %param.26) | copy-start | bytes 319492
  (7 other events, 5.2 us)

commit v3 on v1

--- a/solution.py
+++ b/solution.py
@@ -53,17 +53,21 @@
     return jnp.concatenate(done, axis=-1).reshape(-1)
 
 
-def scatter_chunks(full, order):
+def scatter_chunks(full, order, narrow=2):
     bits = flat_bits()
     count = len(bits)
     buf = full.reshape((2,) * count + full.shape[1:])
     live = list(reversed(range(count)))
-    for axis, j in order:
+    for step, (axis, j) in enumerate(order):
         at = live.index(bits.index((axis, j)))
         high = (lax.axis_index(axis) >> j) & 1
         mine = lax.dynamic_index_in_dim(buf, high, at, keepdims=False)
         other = lax.dynamic_index_in_dim(buf, 1 - high, at, keepdims=False)
-        buf = mine + lax.ppermute(other, axis, swap_pairs(axis, j))
+        shape = other.shape
+        if step < narrow:
+            other = other.reshape(shape[:-3] + (-1, shape[-1])).astype(jnp.bfloat16)
+        moved = lax.ppermute(other, axis, swap_pairs(axis, j))
+        buf = mine + moved.astype(jnp.float32).reshape(shape)
         live.pop(at)
     return buf
 

time: 222 us -> 201 us (0.905)
  waiting for transfers between devices: 62.4 us -> 55.6 us
  starting transfers between devices: 74.1 us -> 67.4 us
  local copies, waits for them, and re-layouts: 34.1 us -> 31.1 us
  other arithmetic: 25.1 us -> 22.3 us
    ppermute x14, waiting for transfers between devices: 30.5 us -> 23.8 us  [scatter_chunks(): moved = lax.ppermute(other, axis, swap_pairs(axis, j))]
    squeeze x14 -> x10, local copies, waits for them, and re-layouts: 6.55 us -> 0.16 us  [scatter_chunks(): other = lax.dynamic_index_in_dim(buf, 1 - high, at, keepdims=False)]
    ppermute x14, starting transfers between devices: 29.5 us -> 24.1 us  [scatter_chunks(): moved = lax.ppermute(other, axis, swap_pairs(axis, j))]
    convert_element_type x0 -> x4, local copies, waits for them, and re-layouts: none -> 4.35 us  [scatter_chunks(): other = other.reshape(shape[:-3] + (-1, shape[-1])).astype(jnp.bfloat16)]
    add x14, other arithmetic: 5.89 us -> 3.08 us  [scatter_chunks(): buf = mine + moved.astype(jnp.float32).reshape(shape)]
  transfers between devices with their start and end apart: 36 -> 36, of which waited for: 22 -> 21; matrix products, arithmetic and copies ran while one was open for 18% -> 17% of each run, Pallas kernels for 0% -> 0%
where the time goes in v3:
time: 201 us; the launch traced here: 200 us
  starting transfers between devices  67.4 us (34%)
  waiting for transfers between devices  55.6 us (28%)
  local copies, waits for them, and re-layouts  31.1 us (15%)
  other arithmetic  22.3 us (11%)
  loops' own time  14.3 us (7%)
  matrix products  6.54 us (3%)
  between operations  2.27 us (1%)
    ppermute x14, starting transfers between devices, scatter_chunks(): moved = lax.ppermute(other, axis, swap_pairs(axis, j))  24.1 us
    ppermute x14, starting transfers between devices, gather_chunks(): recv = lax.ppermute(buf, axis, swap_pairs(axis, j))  24 us
    ppermute x14, waiting for transfers between devices, scatter_chunks(): moved = lax.ppermute(other, axis, swap_pairs(axis, j))  23.8 us
    ppermute x14, waiting for transfers between devices, gather_chunks(): recv = lax.ppermute(buf, axis, swap_pairs(axis, j))  23.1 us
    another operation x1, loops' own time, body(): grad_out = lax.cond(segment == 0, lead_branch, lead_still)  12.9 us
    ppermute x2, starting transfers between devices, extended_2(): lax.ppermute(lax.slice_in_dim(block, 0, width, axis=dim), axis, backward)  7.74 us
    reshape x1, local copies, waits for them, and re-layouts, spread(): flat_term = (term / images).reshape(shards, 8, -1)  7.15 us
    split x2, local copies, waits for them, and re-layouts, scatter_streams(): parts = jnp.split(full, cuts, axis=-1)  6.17 us
  transfers between devices with their start and end apart: 36, of which 21 were waited for; matrix products, arithmetic and copies ran while one was open for 17% of the time, Pallas kernels for 0%

profile of v3, /device:TPU:8, one launch (start us, length us, event | category | flops | bytes accessed | tf_op | source)
XLA Modules:
  0.0 199.6 jit_solution(1536120994059738848)
XLA Ops:
  1.7 3.0 %collective-permute-start.36 = (bf16[16,253]{1,0:T(8,128)(2,1)S(1)}, bf16[16,253]{1,0:T(8,128)(2,1)S(1)}, u32[]{:S(2)}, u32[]{:S(2)}) collective-permute-start(bf16[16,253]{1,0:T(8,128)(2,1)S(1)} %split.25), channel_id=1, source_target_pairs={{0,128},{8,136},{16,144},{24,152},{32,160},{40,168},{48,176},{56,1... | collective-permute-start | bytes 24296 | tf_op jit(solution)/shard_map/ppermute | solution.py:41
  4.7 7.2 %collective-permute-start.29 = (bf16[16,254]{1,0:T(8,128)(2,1)S(1)}, bf16[16,254]{1,0:T(8,128)(2,1)S(1)}, u32[]{:S(2)}, u32[]{:S(2)}) collective-permute-start(bf16[16,254]{1,0:T(8,128)(2,1)S(1)} %split.24), channel_id=1, source_target_pairs={{0,32},{8,40},{16,48},{24,56},{32,0},{40,8},{48,16},{56,24},{64,96... | collective-permute-start | bytes 24392 | tf_op jit(solution)/shard_map/ppermute | solution.py:41
  12.1 2.4 %collective-permute-start.37 = (bf16[2,16,253]{2,1,0:T(8,128)(2,1)S(1)}, bf16[2,16,253]{2,1,0:T(8,128)(2,1)S(1)}, u32[]{:S(2)}, u32[]{:S(2)}) collective-permute-start(bf16[2,16,253]{2,1,0:T(8,128)(2,1)S(1)} %pad_maximum_fusion.17), channel_id=1, source_target_pairs={{0,2},{1,3},{2,0},{3,1},{4,6},{5,7},{6,4},{7,5},{8,10},{9,11},{10,... | collective-permute-start | bytes 48584 | tf_op jit(solution)/shard_map/ppermute | solution.py:41
  15.1 2.3 %collective-permute-done.37 = bf16[2,16,253]{2,1,0:T(8,128)(2,1)S(1)} collective-permute-done((bf16[2,16,253]{2,1,0:T(8,128)(2,1)S(1)}, bf16[2,16,253]{2,1,0:T(8,128)(2,1)S(1)}, u32[]{:S(2)}, u32[]{:S(2)}) %collective-permute-start.37) | collective-permute-done | bytes 16224 | tf_op jit(solution)/shard_map/ppermute | solution.py:41
  17.4 2.8 %collective-permute-start.38 = (bf16[2,2,16,253]{3,2,1,0:T(8,128)(2,1)S(1)}, bf16[2,2,16,253]{3,2,1,0:T(8,128)(2,1)S(1)}, u32[]{:S(2)}, u32[]{:S(2)}) collective-permute-start(bf16[2,2,16,253]{3,2,1,0:T(8,128)(2,1)S(1)} %pad_maximum_fusion.14), channel_id=1, source_target_pairs={{0,32},{8,40},{16,48},{24,56},{32,0},{40,8},{48,16},{56,24},{64,96... | collective-permute-start | bytes 97160 | tf_op jit(solution)/shard_map/ppermute | solution.py:41
  21.8 3.8 %collective-permute-done.38 = bf16[2,2,16,253]{3,2,1,0:T(8,128)(2,1)S(1)} collective-permute-done((bf16[2,2,16,253]{3,2,1,0:T(8,128)(2,1)S(1)}, bf16[2,2,16,253]{3,2,1,0:T(8,128)(2,1)S(1)}, u32[]{:S(2)}, u32[]{:S(2)}) %collective-permute-start.38) | collective-permute-done | bytes 32416 | tf_op jit(solution)/shard_map/ppermute | solution.py:41
  27.1 2.4 %collective-permute-start.32 = (bf16[2,2,2,16,254]{4,3,2,1,0:T(8,128)(2,1)S(1)}, bf16[2,2,2,16,254]{4,3,2,1,0:T(8,128)(2,1)S(1)}, u32[]{:S(2)}, u32[]{:S(2)}) collective-permute-start(bf16[2,2,2,16,254]{4,3,2,1,0:T(8,128)(2,1)S(1)} %pad_maximum_fusion.11), channel_id=1, source_target_pairs={{0,2},{1,3},{2,0},{3,1},{4,6},{5,7},{6,4},{7,5},{8,10},{9,11},{10,... | collective-permute-start | bytes 195080 | tf_op jit(solution)/shard_map/ppermute | solution.py:41
  29.5 2.1 %collective-permute-done.39 = bf16[2,2,2,16,253]{4,3,2,1,0:T(8,128)(2,1)S(1)} collective-permute-done((bf16[2,2,2,16,253]{4,3,2,1,0:T(8,128)(2,1)S(1)}, bf16[2,2,2,16,253]{4,3,2,1,0:T(8,128)(2,1)S(1)}, u32[]{:S(2)}, u32[]{:S(2)}) %collective-permute-start.39) | collective-permute-done | bytes 64800 | tf_op jit(solution)/shard_map/ppermute | solution.py:41
  34.1 2.5 %collective-permute-done.40 = bf16[2,2,2,2,16,253]{5,4,3,2,1,0:T(8,128)(2,1)S(1)} collective-permute-done((bf16[2,2,2,2,16,253]{5,4,3,2,1,0:T(8,128)(2,1)S(1)}, bf16[2,2,2,2,16,253]{5,4,3,2,1,0:T(8,128)(2,1)S(1)}, u32[]{:S(2)}, u32[]{:S(2)}) %collective-permute-start.40) | collective-permute-done | bytes 129568 | tf_op jit(solution)/shard_map/ppermute | solution.py:41
  37.4 2.5 %collective-permute-done.33 = bf16[2,2,2,2,16,254]{5,4,3,2,1,0:T(8,128)(2,1)S(1)} collective-permute-done((bf16[2,2,2,2,16,254]{5,4,3,2,1,0:T(8,128)(2,1)S(1)}, bf16[2,2,2,2,16,254]{5,4,3,2,1,0:T(8,128)(2,1)S(1)}, u32[]{:S(2)}, u32[]{:S(2)}) %collective-permute-start.33) | collective-permute-done | bytes 130080 | tf_op jit(solution)/shard_map/ppermute | solution.py:41
  40.1 3.2 %collective-permute-done.41 = bf16[2,2,2,2,2,16,253]{6,5,4,3,2,1,0:T(8,128)(2,1)S(1)} collective-permute-done((bf16[2,2,2,2,2,16,253]{6,5,4,3,2,1,0:T(8,128)(2,1)S(1)}, bf16[2,2,2,2,2,16,253]{6,5,4,3,2,1,0:T(8,128)(2,1)S(1)}, u32[]{:S(2)}, u32[]{:S(2)}) %collective-permute-start.41) | collective-permute-done | bytes 259104 | tf_op jit(solution)/shard_map/ppermute | solution.py:41
  43.8 5.5 %collective-permute-done.34 = bf16[2,2,2,2,2,16,254]{6,5,4,3,2,1,0:T(8,128)(2,1)S(1)} collective-permute-done((bf16[2,2,2,2,2,16,254]{6,5,4,3,2,1,0:T(8,128)(2,1)S(1)}, bf16[2,2,2,2,2,16,254]{6,5,4,3,2,1,0:T(8,128)(2,1)S(1)}, u32[]{:S(2)}, u32[]{:S(2)}) %collective-permute-start.34) | collective-permute-done | bytes 260128 | tf_op jit(solution)/shard_map/ppermute | solution.py:41
  51.5 3.6 %collective-permute-start.45 = (bf16[2,32,2496]{2,1,0:T(8,128)(2,1)}, bf16[2,32,2496]{2,1,0:T(8,128)(2,1)}, u32[]{:S(2)}, u32[]{:S(2)}) collective-permute-start(bf16[2,32,2496]{2,1,0:T(8,128)(2,1)} %get-tuple-element.224), channel_id=1, source_target_pairs={{1,0},{2,1},{3,2},{5,4},{6,5},{7,6},{9,8},{10,9},{11,10},{13,12},{... | collective-permute-start | bytes 958472 | tf_op jit(solution)/shard_map/ppermute | solution.py:15
  55.1 2.4 %collective-permute-start.44 = (bf16[2,32,2496]{2,1,0:T(8,128)(2,1)}, bf16[2,32,2496]{2,1,0:T(8,128)(2,1)}, u32[]{:S(2)}, u32[]{:S(2)}) collective-permute-start(bf16[2,32,2496]{2,1,0:T(8,128)(2,1)} %get-tuple-element.223), channel_id=1, source_target_pairs={{0,1},{1,2},{2,3},{4,5},{5,6},{6,7},{8,9},{9,10},{10,11},{12,13},{... | collective-permute-start | bytes 958472 | tf_op jit(solution)/shard_map/ppermute | solution.py:12
  57.6 15.1 %conditional.8 = (bf16[128,416]{0,1:T(8,128)(2,1)}, bf16[4,32,416]{2,1,0:T(8,128)(2,1)S(1)}) conditional(s32[]{:T(128)} %convert_element_type.291, () %tuple.71, (bf16[1,4,32,384]{3,2,1,0:T(8,128)(2,1)S(1)}, bf16[1,2,16,384]{3,2,1,0:T(8,128)(2,1)S(1)}, bf16[1,1,8,384]{3,2,1,0:T(8,128)(2,1)S(1)}, bf16[416,384]{1,0:T(8,128)(2,1)S(1)}) %tuple.193), branch_computations={%region_0.1_spmd, %region_1.2_spmd} | conditional | flops 41138176 | bytes 1972240 | solution.py:200
  75.8 2.2 %pad_maximum_fusion.2 = bf16[128,16,507]{2,1,0:T(8,128)(2,1)} fusion(bf16[128,16,253]{2,1,0:T(8,128)(2,1)S(1)} %bitcast.278, bf16[128,16,254]{2,1,0:T(8,128)(2,1)S(1)} %bitcast.279), kind=kLoop, calls=%fused_computation.207 | loop fusion | flops 4153344 | bytes 4153344 | tf_op jit(solution)/shard_map/concatenate | solution.py:53
  78.0 5.2 %reshape_reshape.3 = bf16[416,2496]{1,0:T(8,128)(2,1)S(1)} reshape(bf16[128,16,507]{2,1,0:T(8,128)(2,1)} %pad_maximum_fusion.2) | data formatting | bytes 4153344 | tf_op jit(solution)/shard_map/reshape;reshape | solution.py:159
  83.3 2.0 %conditional.9 = (bf16[128,2496]{0,1:T(8,128)(2,1)S(1)}) conditional(s32[]{:T(128)} %convert_element_type.291, () %tuple.75, (bf16[128,416]{0,1:T(8,128)(2,1)}, bf16[416,2496]{1,0:T(8,128)(2,1)S(1)}) %tuple.76), branch_computations={%region_2.3_spmd, %region_3.4_spmd} | conditional | flops 266133504 | bytes 2822152 | solution.py:208
  83.3 2.0 %convolution_convert_fusion.1 = bf16[128,2496]{0,1:T(8,128)(2,1)S(1)} fusion(bf16[128,416]{0,1:T(8,128)(2,1)} %get-tuple-element.158, bf16[416,2496]{1,0:T(8,128)(2,1)S(1)} %get-tuple-element.87), kind=kOutput, calls=%fused_computation.6 | convolution fusion | flops 266133504 | bytes 2822144 | tf_op jit(solution)/shard_map/cond/branch_1_fun/dot_general | solution.py:203
  87.7 1.9 collective-permute-start.28
  94.0 3.6 %conditional.10 = (f32[416,2496]{1,0:T(8,128)}) conditional(s32[]{:T(128)} %convert_element_type.291, () %tuple.74, (bf16[1,1,4,32,2496]{4,3,2,1,0:T(8,128)(2,1)S(1)}, bf16[128,416]{0,1:T(8,128)(2,1)}) %tuple.182), branch_computations={%region_4.5_spmd, %region_5.6_spmd} | conditional | flops 265814016 | bytes 4898824 | solution.py:231
  94.0 3.6 %fusion.42 = f32[416,2496]{1,0:T(8,128)} fusion(bf16[128,416]{0,1:T(8,128)(2,1)} %get-tuple-element.161, bf16[128,2496]{1,0:T(8,128)(2,1)S(1)} %bitcast.275), kind=kOutput, calls=%fused_computation.258 | convolution fusion | flops 265814016 | bytes 4898816 | tf_op jit(solution)/shard_map/cond/branch_1_fun/dot_general | solution.py:224
  97.6 74.0 %conditional.11 = (f32[8112]{0:T(1024)S(1)}) conditional(s32[]{:T(128)} %convert_element_type.291, () %tuple.73, f32[416,2496]{1,0:T(8,128)} %get-tuple-element.266), branch_computations={%region_6.7_spmd, %region_7.8_spmd} | conditional | flops 2855492 | bytes 59625460 | solution.py:232
  97.6 4.6 %broadcast_multiply_fusion = f32[416,2496]{1,0:T(8,128)} fusion(f32[416,2496]{1,0:T(8,128)} %param.7), kind=kLoop, calls=%fused_computation.7 | loop fusion | flops 1038336 | bytes 8306688 | tf_op jit(solution)/shard_map/cond/branch_1_fun/div | solution.py:214
  102.1 7.2 %reshape.176 = f32[128,8,1014]{2,1,0:T(8,128)} reshape(f32[416,2496]{1,0:T(8,128)} %broadcast_multiply_fusion) | data formatting | bytes 8306688 | tf_op jit(solution)/shard_map/cond/branch_1_fun/reshape | solution.py:214
  109.3 3.1 %split.21 = f32[128,8,502]{2,1,0:T(8,128)} slice(f32[128,8,1014]{2,1,0:T(8,128)} %reshape.176), slice={[0:128], [0:8], [512:1014]} | slice | bytes 4112384 | tf_op jit(solution)/shard_map/cond/branch_1_fun/split | solution.py:76
  112.4 2.1 %fusion.4 = bf16[2,2,2,2,2,16,502]{6,5,4,3,2,1,0:T(8,128)(2,1)} fusion(f32[2,2,2,2,2,2,2,8,502]{8,7,6,5,4,3,2,1,0:T(8,128)} %bitcast.267, s32[]{:T(128)S(6)} %select_n.227), kind=kLoop, calls=%fused_computation.13 | loop fusion | bytes 1028100 | tf_op jit(solution)/shard_map/cond/branch_1_fun/convert_element_type | solution.py:68
  115.2 3.1 %split.20 = f32[128,8,512]{2,1,0:T(8,128)} slice(f32[128,8,1014]{2,1,0:T(8,128)} %reshape.176), slice={[0:128], [0:8], [0:512]} | slice | bytes 4194304 | tf_op jit(solution)/shard_map/cond/branch_1_fun/split | solution.py:76
  118.3 2.1 %fusion.3 = bf16[2,2,2,2,2,16,512]{6,5,4,3,2,1,0:T(8,128)(2,1)} fusion(f32[2,2,2,2,2,2,2,8,512]{8,7,6,5,4,3,2,1,0:T(8,128)} %bitcast.271, s32[]{:T(128)S(6)} %select_n.225), kind=kLoop, calls=%fused_computation.12 | loop fusion | bytes 1048580 | tf_op jit(solution)/shard_map/cond/branch_1_fun/convert_element_type | solution.py:68
  122.0 2.0 %collective-permute-done.7 = bf16[2,2,2,2,2,16,502]{6,5,4,3,2,1,0:T(8,128)(2,1)} collective-permute-done((bf16[2,2,2,2,2,16,502]{6,5,4,3,2,1,0:T(8,128)(2,1)}, bf16[2,2,2,2,2,16,502]{6,5,4,3,2,1,0:T(8,128)(2,1)}, u32[]{:S(2)}, u32[]{:S(2)}) %collective-permute-start.7) | collective-permute-done | bytes 514080 | tf_op jit(solution)/shard_map/cond/branch_1_fun/ppermute | solution.py:69
  126.4 3.5 %collective-permute-done = bf16[2,2,2,2,2,16,512]{6,5,4,3,2,1,0:T(8,128)(2,1)} collective-permute-done((bf16[2,2,2,2,2,16,512]{6,5,4,3,2,1,0:T(8,128)(2,1)}, bf16[2,2,2,2,2,16,512]{6,5,4,3,2,1,0:T(8,128)(2,1)}, u32[]{:S(2)}, u32[]{:S(2)}) %collective-permute-start) | collective-permute-done | bytes 524320 | tf_op jit(solution)/shard_map/cond/branch_1_fun/ppermute | solution.py:69
  133.0 2.1 %collective-permute-start.9 = (f32[2,2,2,2,8,502]{5,4,3,2,1,0:T(8,128)S(1)}, f32[2,2,2,2,8,502]{5,4,3,2,1,0:T(8,128)S(1)}, u32[]{:S(2)}, u32[]{:S(2)}) collective-permute-start(f32[2,2,2,2,8,502]{5,4,3,2,1,0:T(8,128)S(1)} %dynamic-slice_bitcast_fusion), channel_id=1, source_target_pairs={{0,1},{1,0},{2,3},{3,2},{4,5},{5,4},{6,7},{7,6},{8,9},{9,8},{10,11... | collective-permute-start | bytes 771080 | tf_op jit(solution)/shard_map/cond/branch_1_fun/ppermute | solution.py:69
  135.1 2.5 %collective-permute-done.1 = bf16[2,2,2,2,16,512]{5,4,3,2,1,0:T(8,128)(2,1)S(1)} collective-permute-done((bf16[2,2,2,2,16,512]{5,4,3,2,1,0:T(8,128)(2,1)S(1)}, bf16[2,2,2,2,16,512]{5,4,3,2,1,0:T(8,128)(2,1)S(1)}, u32[]{:S(2)}, u32[]{:S(2)}) %collective-permute-start.1) | collective-permute-done | bytes 262176 | tf_op jit(solution)/shard_map/cond/branch_1_fun/ppermute | solution.py:69
  140.6 3.7 %collective-permute-done.2 = f32[2,2,2,2,8,512]{5,4,3,2,1,0:T(8,128)S(1)} collective-permute-done((f32[2,2,2,2,8,512]{5,4,3,2,1,0:T(8,128)S(1)}, f32[2,2,2,2,8,512]{5,4,3,2,1,0:T(8,128)S(1)}, u32[]{:S(2)}, u32[]{:S(2)}) %collective-permute-start.2) | collective-permute-done | bytes 262176 | tf_op jit(solution)/shard_map/cond/branch_1_fun/ppermute | solution.py:69
  144.3 2.3 %collective-permute-start.3 = (f32[2,2,2,8,512]{4,3,2,1,0:T(8,128)S(1)}, f32[2,2,2,8,512]{4,3,2,1,0:T(8,128)S(1)}, u32[]{:S(2)}, u32[]{:S(2)}) collective-permute-start(f32[2,2,2,8,512]{4,3,2,1,0:T(8,128)S(1)} %dynamic-slice_bitcast_fusion.3), channel_id=1, source_target_pairs={{0,2},{1,3},{2,0},{3,1},{4,6},{5,7},{6,4},{7,5},{8,10},{9,11},{10,... | collective-permute-start | bytes 393224 | tf_op jit(solution)/shard_map/cond/branch_1_fun/ppermute | solution.py:69
  146.9 2.7 %collective-permute-start.11 = (f32[2,2,8,502]{3,2,1,0:T(8,128)S(1)}, f32[2,2,8,502]{3,2,1,0:T(8,128)S(1)}, u32[]{:S(2)}, u32[]{:S(2)}) collective-permute-start(f32[2,2,8,502]{3,2,1,0:T(8,128)S(1)} %dynamic-slice_bitcast_fusion.4), channel_id=1, source_target_pairs={{0,32},{8,40},{16,48},{24,56},{32,0},{40,8},{48,16},{56,24},{64,96... | collective-permute-start | bytes 192776 | tf_op jit(solution)/shard_map/cond/branch_1_fun/ppermute | solution.py:69
  150.9 2.1 %collective-permute-start.4 = (f32[2,2,8,512]{3,2,1,0:T(8,128)S(1)}, f32[2,2,8,512]{3,2,1,0:T(8,128)S(1)}, u32[]{:S(2)}, u32[]{:S(2)}) collective-permute-start(f32[2,2,8,512]{3,2,1,0:T(8,128)S(1)} %dynamic-slice_bitcast_fusion.5), channel_id=1, source_target_pairs={{0,16},{8,24},{16,0},{24,8},{32,48},{40,56},{48,32},{56,40},{64,80... | collective-permute-start | bytes 196616 | tf_op jit(solution)/shard_map/cond/branch_1_fun/ppermute | solution.py:69
  153.0 3.0 %collective-permute-done.11 = f32[2,2,8,502]{3,2,1,0:T(8,128)S(1)} collective-permute-done((f32[2,2,8,502]{3,2,1,0:T(8,128)S(1)}, f32[2,2,8,502]{3,2,1,0:T(8,128)S(1)}, u32[]{:S(2)}, u32[]{:S(2)}) %collective-permute-start.11) | collective-permute-done | bytes 64288 | tf_op jit(solution)/shard_map/cond/branch_1_fun/ppermute | solution.py:69
  159.1 2.4 %collective-permute-done.12 = f32[2,8,502]{2,1,0:T(8,128)S(1)} collective-permute-done((f32[2,8,502]{2,1,0:T(8,128)S(1)}, f32[2,8,502]{2,1,0:T(8,128)S(1)}, u32[]{:S(2)}, u32[]{:S(2)}) %collective-permute-start.12) | collective-permute-done | bytes 32160 | tf_op jit(solution)/shard_map/cond/branch_1_fun/ppermute | solution.py:69
  161.5 1.8 collective-permute-start.13
  163.3 3.6 %collective-permute-start.6 = (f32[8,512]{1,0:T(8,128)S(1)}, f32[8,512]{1,0:T(8,128)S(1)}, u32[]{:S(2)}, u32[]{:S(2)}) collective-permute-start(f32[8,512]{1,0:T(8,128)S(1)} %dynamic-slice_bitcast_fusion.9), channel_id=1, source_target_pairs={{0,32},{8,40},{16,48},{24,56},{32,0},{40,8},{48,16},{56,24},{64,96... | collective-permute-start | bytes 49160 | tf_op jit(solution)/shard_map/cond/branch_1_fun/ppermute | solution.py:69
  167.0 4.1 %collective-permute-done.6 = f32[8,512]{1,0:T(8,128)S(1)} collective-permute-done((f32[8,512]{1,0:T(8,128)S(1)}, f32[8,512]{1,0:T(8,128)S(1)}, u32[]{:S(2)}, u32[]{:S(2)}) %collective-permute-start.6) | collective-permute-done | bytes 16416 | tf_op jit(solution)/shard_map/cond/branch_1_fun/ppermute | solution.py:69
  172.9 2.7 %collective-permute-start.46 = (f32[2,2496]{1,0:T(2,128)S(1)}, f32[2,2496]{1,0:T(2,128)S(1)}, u32[]{:S(2)}, u32[]{:S(2)}) collective-permute-start(f32[2,2496]{1,0:T(2,128)S(1)} %pad_maximum_fusion.15), channel_id=1, source_target_pairs={{0,1},{1,0},{2,3},{3,2},{4,5},{5,4},{6,7},{7,6},{8,9},{9,8},{10,11... | collective-permute-start | bytes 59912 | tf_op jit(solution)/shard_map/ppermute | solution.py:84
  178.7 2.1 %copy.60 = bf16[2496,104]{1,0:T(8,128)(2,1)} copy(bf16[2496,104]{0,1:T(8,128)(2,1)} %param.34) | data formatting | bytes 1038336 | tf_op args[8]
  183.3 4.1 %collective-permute-start.49 = (bf16[2,32,2496]{2,1,0:T(8,128)(2,1)S(1)}, bf16[2,32,2496]{2,1,0:T(8,128)(2,1)S(1)}, u32[]{:S(2)}, u32[]{:S(2)}) collective-permute-start(bf16[2,32,2496]{2,1,0:T(8,128)(2,1)S(1)} %get-tuple-element.222), channel_id=1, source_target_pairs={{1,0},{2,1},{3,2},{5,4},{6,5},{7,6},{9,8},{10,9},{11,10},{13,12},{... | collective-permute-start | bytes 958472 | tf_op jit(solution)/shard_map/ppermute | solution.py:15
  187.4 2.0 collective-permute-start.48
  189.5 3.1 %collective-permute-done.49 = bf16[2,32,2496]{2,1,0:T(8,128)(2,1)S(1)} collective-permute-done((bf16[2,32,2496]{2,1,0:T(8,128)(2,1)S(1)}, bf16[2,32,2496]{2,1,0:T(8,128)(2,1)S(1)}, u32[]{:S(2)}, u32[]{:S(2)}) %collective-permute-start.49) | collective-permute-done | bytes 319520 | tf_op jit(solution)/shard_map/ppermute | solution.py:15
  192.5 3.9 %collective-permute-done.48 = bf16[2,32,2496]{2,1,0:T(8,128)(2,1)S(1)} collective-permute-done((bf16[2,32,2496]{2,1,0:T(8,128)(2,1)S(1)}, bf16[2,32,2496]{2,1,0:T(8,128)(2,1)S(1)}, u32[]{:S(2)}, u32[]{:S(2)}) %collective-permute-start.48) | collective-permute-done | bytes 319520 | tf_op jit(solution)/shard_map/ppermute | solution.py:12
  (167 shorter events, 47.8 us)
Async XLA Ops:
  1.7 10.3 %collective-permute-start.36 = (bf16[16,253]{1,0:T(8,128)(2,1)S(1)}, bf16[16,253]{1,0:T(8,128)(2,1)S(1)}, u32[]{:S(2)}, u32[]{:S(2)}) collective-permute-start(bf16[16,253]{1,0:T(8,128)(2,1)S(1)} %split.25), channel_id=1, source_target_pairs={{0,128},{8,136},{16,144},{24,152},{32,160},{40,168},{48,176},{56,1... | collective-permute-start | bytes 24296 | tf_op jit(solution)/shard_map/ppermute | solution.py:41
  4.7 9.7 %collective-permute-start.29 = (bf16[16,254]{1,0:T(8,128)(2,1)S(1)}, bf16[16,254]{1,0:T(8,128)(2,1)S(1)}, u32[]{:S(2)}, u32[]{:S(2)}) collective-permute-start(bf16[16,254]{1,0:T(8,128)(2,1)S(1)} %split.24), channel_id=1, source_target_pairs={{0,32},{8,40},{16,48},{24,56},{32,0},{40,8},{48,16},{56,24},{64,96... | collective-permute-start | bytes 24392 | tf_op jit(solution)/shard_map/ppermute | solution.py:41
  12.1 5.3 %collective-permute-start.37 = (bf16[2,16,253]{2,1,0:T(8,128)(2,1)S(1)}, bf16[2,16,253]{2,1,0:T(8,128)(2,1)S(1)}, u32[]{:S(2)}, u32[]{:S(2)}) collective-permute-start(bf16[2,16,253]{2,1,0:T(8,128)(2,1)S(1)} %pad_maximum_fusion.17), channel_id=1, source_target_pairs={{0,2},{1,3},{2,0},{3,1},{4,6},{5,7},{6,4},{7,5},{8,10},{9,11},{10,... | collective-permute-start | bytes 48584 | tf_op jit(solution)/shard_map/ppermute | solution.py:41
  14.5 5.7 %collective-permute-start.30 = (bf16[2,16,254]{2,1,0:T(8,128)(2,1)S(1)}, bf16[2,16,254]{2,1,0:T(8,128)(2,1)S(1)}, u32[]{:S(2)}, u32[]{:S(2)}) collective-permute-start(bf16[2,16,254]{2,1,0:T(8,128)(2,1)S(1)} %pad_maximum_fusion.16), channel_id=1, source_target_pairs={{0,128},{8,136},{16,144},{24,152},{32,160},{40,168},{48,176},{56,1... | collective-permute-start | bytes 48776 | tf_op jit(solution)/shard_map/ppermute | solution.py:41
  17.4 8.1 %collective-permute-start.38 = (bf16[2,2,16,253]{3,2,1,0:T(8,128)(2,1)S(1)}, bf16[2,2,16,253]{3,2,1,0:T(8,128)(2,1)S(1)}, u32[]{:S(2)}, u32[]{:S(2)}) collective-permute-start(bf16[2,2,16,253]{3,2,1,0:T(8,128)(2,1)S(1)} %pad_maximum_fusion.14), channel_id=1, source_target_pairs={{0,32},{8,40},{16,48},{24,56},{32,0},{40,8},{48,16},{56,24},{64,96... | collective-permute-start | bytes 97160 | tf_op jit(solution)/shard_map/ppermute | solution.py:41
  20.2 6.8 %collective-permute-start.31 = (bf16[2,2,16,254]{3,2,1,0:T(8,128)(2,1)S(1)}, bf16[2,2,16,254]{3,2,1,0:T(8,128)(2,1)S(1)}, u32[]{:S(2)}, u32[]{:S(2)}) collective-permute-start(bf16[2,2,16,254]{3,2,1,0:T(8,128)(2,1)S(1)} %pad_maximum_fusion.13), channel_id=1, source_target_pairs={{0,16},{8,24},{16,0},{24,8},{32,48},{40,56},{48,32},{56,40},{64,80... | collective-permute-start | bytes 97544 | tf_op jit(solution)/shard_map/ppermute | solution.py:41
  25.6 6.0 %collective-permute-start.39 = (bf16[2,2,2,16,253]{4,3,2,1,0:T(8,128)(2,1)S(1)}, bf16[2,2,2,16,253]{4,3,2,1,0:T(8,128)(2,1)S(1)}, u32[]{:S(2)}, u32[]{:S(2)}) collective-permute-start(bf16[2,2,2,16,253]{4,3,2,1,0:T(8,128)(2,1)S(1)} %pad_maximum_fusion.12), channel_id=1, source_target_pairs={{0,16},{8,24},{16,0},{24,8},{32,48},{40,56},{48,32},{56,40},{64,80... | collective-permute-start | bytes 194312 | tf_op jit(solution)/shard_map/ppermute | solution.py:41
  27.1 6.3 %collective-permute-start.32 = (bf16[2,2,2,16,254]{4,3,2,1,0:T(8,128)(2,1)S(1)}, bf16[2,2,2,16,254]{4,3,2,1,0:T(8,128)(2,1)S(1)}, u32[]{:S(2)}, u32[]{:S(2)}) collective-permute-start(bf16[2,2,2,16,254]{4,3,2,1,0:T(8,128)(2,1)S(1)} %pad_maximum_fusion.11), channel_id=1, source_target_pairs={{0,2},{1,3},{2,0},{3,1},{4,6},{5,7},{6,4},{7,5},{8,10},{9,11},{10,... | collective-permute-start | bytes 195080 | tf_op jit(solution)/shard_map/ppermute | solution.py:41
  31.6 5.1 %collective-permute-start.40 = (bf16[2,2,2,2,16,253]{5,4,3,2,1,0:T(8,128)(2,1)S(1)}, bf16[2,2,2,2,16,253]{5,4,3,2,1,0:T(8,128)(2,1)S(1)}, u32[]{:S(2)}, u32[]{:S(2)}) collective-permute-start(bf16[2,2,2,2,16,253]{5,4,3,2,1,0:T(8,128)(2,1)S(1)} %pad_maximum_fusion.10), channel_id=1, source_target_pairs={{0,1},{1,0},{2,3},{3,2},{4,5},{5,4},{6,7},{7,6},{8,9},{9,8},{10,11... | collective-permute-start | bytes 388616 | tf_op jit(solution)/shard_map/ppermute | solution.py:41
  33.5 6.4 %collective-permute-start.33 = (bf16[2,2,2,2,16,254]{5,4,3,2,1,0:T(8,128)(2,1)S(1)}, bf16[2,2,2,2,16,254]{5,4,3,2,1,0:T(8,128)(2,1)S(1)}, u32[]{:S(2)}, u32[]{:S(2)}) collective-permute-start(bf16[2,2,2,2,16,254]{5,4,3,2,1,0:T(8,128)(2,1)S(1)} %pad_maximum_fusion.9), channel_id=1, source_target_pairs={{0,64},{8,72},{16,80},{24,88},{32,96},{40,104},{48,112},{56,120},{... | collective-permute-start | bytes 390152 | tf_op jit(solution)/shard_map/ppermute | solution.py:41
  36.8 6.6 %collective-permute-start.41 = (bf16[2,2,2,2,2,16,253]{6,5,4,3,2,1,0:T(8,128)(2,1)S(1)}, bf16[2,2,2,2,2,16,253]{6,5,4,3,2,1,0:T(8,128)(2,1)S(1)}, u32[]{:S(2)}, u32[]{:S(2)}) collective-permute-start(bf16[2,2,2,2,2,16,253]{6,5,4,3,2,1,0:T(8,128)(2,1)S(1)} %pad_maximum_fusion.8), channel_id=1, source_target_pairs={{0,64},{8,72},{16,80},{24,88},{32,96},{40,104},{48,112},{56,120},{... | collective-permute-start | bytes 777224 | tf_op jit(solution)/shard_map/ppermute | solution.py:41
  40.0 9.3 %collective-permute-start.34 = (bf16[2,2,2,2,2,16,254]{6,5,4,3,2,1,0:T(8,128)(2,1)S(1)}, bf16[2,2,2,2,2,16,254]{6,5,4,3,2,1,0:T(8,128)(2,1)S(1)}, u32[]{:S(2)}, u32[]{:S(2)}) collective-permute-start(bf16[2,2,2,2,2,16,254]{6,5,4,3,2,1,0:T(8,128)(2,1)S(1)} %pad_maximum_fusion.7), channel_id=1, source_target_pairs={{0,8},{8,0},{16,24},{24,16},{32,40},{40,32},{48,56},{56,48},{64,72... | collective-permute-start | bytes 780296 | tf_op jit(solution)/shard_map/ppermute | solution.py:41
  43.5 29.1 %collective-permute-start.42 = (bf16[2,2,2,2,2,2,16,253]{7,6,5,4,3,2,1,0:T(8,128)(2,1)S(1)}, bf16[2,2,2,2,2,2,16,253]{7,6,5,4,3,2,1,0:T(8,128)(2,1)}, u32[]{:S(2)}, u32[]{:S(2)}) collective-permute-start(bf16[2,2,2,2,2,2,16,253]{7,6,5,4,3,2,1,0:T(8,128)(2,1)S(1)} %pad_maximum_fusion.6), channel_id=1, source_target_pairs={{0,8},{8,0},{16,24},{24,16},{32,40},{40,32},{48,56},{56,48},{64,72... | collective-permute-start | bytes 1554440 | tf_op jit(solution)/shard_map/ppermute | solution.py:41
  49.3 8.2 %copy-start.15 = (bf16[416,384]{1,0:T(8,128)(2,1)S(1)}, bf16[416,384]{1,0:T(8,128)(2,1)}, u32[]{:S(2)}) copy-start(bf16[416,384]{1,0:T(8,128)(2,1)} %param.31) | copy-start | bytes 958468
  49.4 8.2 %copy-start.18 = (bf16[1,4,32,384]{3,2,1,0:T(8,128)(2,1)S(1)}, bf16[1,4,32,384]{3,2,1,0:T(8,128)(2,1)}, u32[]{:S(2)}) copy-start(bf16[1,4,32,384]{3,2,1,0:T(8,128)(2,1)} %param.28) | copy-start | bytes 294916
  49.4 8.2 %copy-start.20 = (bf16[1,2,16,384]{3,2,1,0:T(8,128)(2,1)S(1)}, bf16[1,2,16,384]{3,2,1,0:T(8,128)(2,1)}, u32[]{:S(2)}) copy-start(bf16[1,2,16,384]{3,2,1,0:T(8,128)(2,1)} %param.29) | copy-start | bytes 73732
  49.4 8.2 %copy-start.21 = (bf16[1,1,8,384]{3,2,1,0:T(8,128)(2,1)S(1)}, bf16[1,1,8,384]{3,2,1,0:T(8,128)(2,1)}, u32[]{:S(2)}) copy-start(bf16[1,1,8,384]{3,2,1,0:T(8,128)(2,1)} %param.30) | copy-start | bytes 18436
  50.3 24.0 %collective-permute-start.35 = (bf16[2,2,2,2,2,2,16,254]{7,6,5,4,3,2,1,0:T(8,128)(2,1)}, bf16[2,2,2,2,2,2,16,254]{7,6,5,4,3,2,1,0:T(8,128)(2,1)}, u32[]{:S(2)}, u32[]{:S(2)}) collective-permute-start(bf16[2,2,2,2,2,2,16,254]{7,6,5,4,3,2,1,0:T(8,128)(2,1)} %pad_maximum_fusion.5), channel_id=1, source_target_pairs={{0,1},{1,0},{2,3},{3,2},{4,5},{5,4},{6,7},{7,6},{8,9},{9,8},{10,11... | collective-permute-start | bytes 1560584 | tf_op jit(solution)/shard_map/ppermute | solution.py:41
  51.5 39.1 %collective-permute-start.45 = (bf16[2,32,2496]{2,1,0:T(8,128)(2,1)}, bf16[2,32,2496]{2,1,0:T(8,128)(2,1)}, u32[]{:S(2)}, u32[]{:S(2)}) collective-permute-start(bf16[2,32,2496]{2,1,0:T(8,128)(2,1)} %get-tuple-element.224), channel_id=1, source_target_pairs={{1,0},{2,1},{3,2},{5,4},{6,5},{7,6},{9,8},{10,9},{11,10},{13,12},{... | collective-permute-start | bytes 958472 | tf_op jit(solution)/shard_map/ppermute | solution.py:15
  55.1 35.5 %collective-permute-start.44 = (bf16[2,32,2496]{2,1,0:T(8,128)(2,1)}, bf16[2,32,2496]{2,1,0:T(8,128)(2,1)}, u32[]{:S(2)}, u32[]{:S(2)}) collective-permute-start(bf16[2,32,2496]{2,1,0:T(8,128)(2,1)} %get-tuple-element.223), channel_id=1, source_target_pairs={{0,1},{1,2},{2,3},{4,5},{5,6},{6,7},{8,9},{9,10},{10,11},{12,13},{... | collective-permute-start | bytes 958472 | tf_op jit(solution)/shard_map/ppermute | solution.py:12
  86.4 5.9 %collective-permute-start.43 = (bf16[4,32,2496]{2,1,0:T(8,128)(2,1)}, bf16[4,32,2496]{2,1,0:T(8,128)(2,1)S(1)}, u32[]{:S(2)}, u32[]{:S(2)}) collective-permute-start(bf16[4,32,2496]{2,1,0:T(8,128)(2,1)} %bitcast.280), channel_id=1, source_target_pairs={{0,4},{1,5},{2,6},{3,7},{8,12},{9,13},{10,14},{11,15},{16,20},{17,... | collective-permute-start | bytes 1916936 | tf_op jit(solution)/shard_map/ppermute | solution.py:23
  87.7 4.6 %collective-permute-start.28 = (bf16[4,32,416]{2,1,0:T(8,128)(2,1)}, bf16[4,32,416]{2,1,0:T(8,128)(2,1)}, u32[]{:S(2)}, u32[]{:S(2)}) collective-permute-start(bf16[4,32,416]{2,1,0:T(8,128)(2,1)} %copy-done.17), channel_id=1, source_target_pairs={{0,4},{1,5},{2,6},{3,7},{8,12},{9,13},{10,14},{11,15},{16,20},{17,... | collective-permute-start | bytes 319496 | tf_op jit(solution)/shard_map/ppermute | solution.py:23
  92.3 1.5 copy-start.8
  97.6 74.0 %copy-start.9 = (f32[4,32,2496]{2,1,0:T(8,128)S(1)}, f32[4,32,2496]{2,1,0:T(8,128)}, u32[]{:S(2)}) copy-start(f32[4,32,2496]{2,1,0:T(8,128)} %copy-done.8) | copy-start | bytes 3833860
  114.5 9.5 %collective-permute-start.7 = (bf16[2,2,2,2,2,16,502]{6,5,4,3,2,1,0:T(8,128)(2,1)}, bf16[2,2,2,2,2,16,502]{6,5,4,3,2,1,0:T(8,128)(2,1)}, u32[]{:S(2)}, u32[]{:S(2)}) collective-permute-start(bf16[2,2,2,2,2,16,502]{6,5,4,3,2,1,0:T(8,128)(2,1)} %fusion.4), channel_id=1, source_target_pairs={{0,8},{8,0},{16,24},{24,16},{32,40},{40,32},{48,56},{56,48},{64,72... | collective-permute-start | bytes 1542152 | tf_op jit(solution)/shard_map/cond/branch_1_fun/ppermute | solution.py:69
  120.4 9.5 %collective-permute-start = (bf16[2,2,2,2,2,16,512]{6,5,4,3,2,1,0:T(8,128)(2,1)}, bf16[2,2,2,2,2,16,512]{6,5,4,3,2,1,0:T(8,128)(2,1)}, u32[]{:S(2)}, u32[]{:S(2)}) collective-permute-start(bf16[2,2,2,2,2,16,512]{6,5,4,3,2,1,0:T(8,128)(2,1)} %fusion.3), channel_id=1, source_target_pairs={{0,1},{1,0},{2,3},{3,2},{4,5},{5,4},{6,7},{7,6},{8,9},{9,8},{10,11... | collective-permute-start | bytes 1572872 | tf_op jit(solution)/shard_map/cond/branch_1_fun/ppermute | solution.py:69
  122.0 7.9 %copy-start.2 = (f32[128,8,512]{2,1,0:T(8,128)S(1)}, f32[128,8,512]{2,1,0:T(8,128)}, u32[]{:S(2)}) copy-start(f32[128,8,512]{2,1,0:T(8,128)} %split.20) | copy-start | bytes 6291460 | tf_op jit(solution)/shard_map/cond
  125.6 7.3 %collective-permute-start.8 = (bf16[2,2,2,2,16,502]{5,4,3,2,1,0:T(8,128)(2,1)S(1)}, bf16[2,2,2,2,16,502]{5,4,3,2,1,0:T(8,128)(2,1)S(1)}, u32[]{:S(2)}, u32[]{:S(2)}) collective-permute-start(bf16[2,2,2,2,16,502]{5,4,3,2,1,0:T(8,128)(2,1)S(1)} %fusion.6), channel_id=1, source_target_pairs={{0,64},{8,72},{16,80},{24,88},{32,96},{40,104},{48,112},{56,120},{... | collective-permute-start | bytes 771080 | tf_op jit(solution)/shard_map/cond/branch_1_fun/ppermute | solution.py:69
  131.2 6.5 %collective-permute-start.1 = (bf16[2,2,2,2,16,512]{5,4,3,2,1,0:T(8,128)(2,1)S(1)}, bf16[2,2,2,2,16,512]{5,4,3,2,1,0:T(8,128)(2,1)S(1)}, u32[]{:S(2)}, u32[]{:S(2)}) collective-permute-start(bf16[2,2,2,2,16,512]{5,4,3,2,1,0:T(8,128)(2,1)S(1)} %fusion.5), channel_id=1, source_target_pairs={{0,8},{8,0},{16,24},{24,16},{32,40},{40,32},{48,56},{56,48},{64,72... | collective-permute-start | bytes 786440 | tf_op jit(solution)/shard_map/cond/branch_1_fun/ppermute | solution.py:69
  133.0 6.5 %collective-permute-start.9 = (f32[2,2,2,2,8,502]{5,4,3,2,1,0:T(8,128)S(1)}, f32[2,2,2,2,8,502]{5,4,3,2,1,0:T(8,128)S(1)}, u32[]{:S(2)}, u32[]{:S(2)}) collective-permute-start(f32[2,2,2,2,8,502]{5,4,3,2,1,0:T(8,128)S(1)} %dynamic-slice_bitcast_fusion), channel_id=1, source_target_pairs={{0,1},{1,0},{2,3},{3,2},{4,5},{5,4},{6,7},{7,6},{8,9},{9,8},{10,11... | collective-permute-start | bytes 771080 | tf_op jit(solution)/shard_map/cond/branch_1_fun/ppermute | solution.py:69
  137.8 6.5 %collective-permute-start.2 = (f32[2,2,2,2,8,512]{5,4,3,2,1,0:T(8,128)S(1)}, f32[2,2,2,2,8,512]{5,4,3,2,1,0:T(8,128)S(1)}, u32[]{:S(2)}, u32[]{:S(2)}) collective-permute-start(f32[2,2,2,2,8,512]{5,4,3,2,1,0:T(8,128)S(1)} %dynamic-slice_bitcast_fusion.1), channel_id=1, source_target_pairs={{0,64},{8,72},{16,80},{24,88},{32,96},{40,104},{48,112},{56,120},{... | collective-permute-start | bytes 786440 | tf_op jit(solution)/shard_map/cond/branch_1_fun/ppermute | solution.py:69
  139.5 7.3 %collective-permute-start.10 = (f32[2,2,2,8,502]{4,3,2,1,0:T(8,128)S(1)}, f32[2,2,2,8,502]{4,3,2,1,0:T(8,128)S(1)}, u32[]{:S(2)}, u32[]{:S(2)}) collective-permute-start(f32[2,2,2,8,502]{4,3,2,1,0:T(8,128)S(1)} %dynamic-slice_bitcast_fusion.2), channel_id=1, source_target_pairs={{0,16},{8,24},{16,0},{24,8},{32,48},{40,56},{48,32},{56,40},{64,80... | collective-permute-start | bytes 385544 | tf_op jit(solution)/shard_map/cond/branch_1_fun/ppermute | solution.py:69
  144.3 6.6 %collective-permute-start.3 = (f32[2,2,2,8,512]{4,3,2,1,0:T(8,128)S(1)}, f32[2,2,2,8,512]{4,3,2,1,0:T(8,128)S(1)}, u32[]{:S(2)}, u32[]{:S(2)}) collective-permute-start(f32[2,2,2,8,512]{4,3,2,1,0:T(8,128)S(1)} %dynamic-slice_bitcast_fusion.3), channel_id=1, source_target_pairs={{0,2},{1,3},{2,0},{3,1},{4,6},{5,7},{6,4},{7,5},{8,10},{9,11},{10,... | collective-permute-start | bytes 393224 | tf_op jit(solution)/shard_map/cond/branch_1_fun/ppermute | solution.py:69
  146.9 9.0 %collective-permute-start.11 = (f32[2,2,8,502]{3,2,1,0:T(8,128)S(1)}, f32[2,2,8,502]{3,2,1,0:T(8,128)S(1)}, u32[]{:S(2)}, u32[]{:S(2)}) collective-permute-start(f32[2,2,8,502]{3,2,1,0:T(8,128)S(1)} %dynamic-slice_bitcast_fusion.4), channel_id=1, source_target_pairs={{0,32},{8,40},{16,48},{24,56},{32,0},{40,8},{48,16},{56,24},{64,96... | collective-permute-start | bytes 192776 | tf_op jit(solution)/shard_map/cond/branch_1_fun/ppermute | solution.py:69
  150.9 6.4 %collective-permute-start.4 = (f32[2,2,8,512]{3,2,1,0:T(8,128)S(1)}, f32[2,2,8,512]{3,2,1,0:T(8,128)S(1)}, u32[]{:S(2)}, u32[]{:S(2)}) collective-permute-start(f32[2,2,8,512]{3,2,1,0:T(8,128)S(1)} %dynamic-slice_bitcast_fusion.5), channel_id=1, source_target_pairs={{0,16},{8,24},{16,0},{24,8},{32,48},{40,56},{48,32},{56,40},{64,80... | collective-permute-start | bytes 196616 | tf_op jit(solution)/shard_map/cond/branch_1_fun/ppermute | solution.py:69
  156.0 5.5 %collective-permute-start.12 = (f32[2,8,502]{2,1,0:T(8,128)S(1)}, f32[2,8,502]{2,1,0:T(8,128)S(1)}, u32[]{:S(2)}, u32[]{:S(2)}) collective-permute-start(f32[2,8,502]{2,1,0:T(8,128)S(1)} %dynamic-slice_bitcast_fusion.6), channel_id=1, source_target_pairs={{0,2},{1,3},{2,0},{3,1},{4,6},{5,7},{6,4},{7,5},{8,10},{9,11},{10,... | collective-permute-start | bytes 96392 | tf_op jit(solution)/shard_map/cond/branch_1_fun/ppermute | solution.py:69
  157.4 5.9 %collective-permute-start.5 = (f32[2,8,512]{2,1,0:T(8,128)S(1)}, f32[2,8,512]{2,1,0:T(8,128)S(1)}, u32[]{:S(2)}, u32[]{:S(2)}) collective-permute-start(f32[2,8,512]{2,1,0:T(8,128)S(1)} %dynamic-slice_bitcast_fusion.7), channel_id=1, source_target_pairs={{0,128},{8,136},{16,144},{24,152},{32,160},{40,168},{48,176},{56,1... | collective-permute-start | bytes 98312 | tf_op jit(solution)/shard_map/cond/branch_1_fun/ppermute | solution.py:69
  161.5 5.5 %collective-permute-start.13 = (f32[8,502]{1,0:T(8,128)S(1)}, f32[8,502]{1,0:T(8,128)S(1)}, u32[]{:S(2)}, u32[]{:S(2)}) collective-permute-start(f32[8,502]{1,0:T(8,128)S(1)} %dynamic-slice_bitcast_fusion.8), channel_id=1, source_target_pairs={{0,128},{8,136},{16,144},{24,152},{32,160},{40,168},{48,176},{56,1... | collective-permute-start | bytes 48200 | tf_op jit(solution)/shard_map/cond/branch_1_fun/ppermute | solution.py:69
  163.3 7.7 %collective-permute-start.6 = (f32[8,512]{1,0:T(8,128)S(1)}, f32[8,512]{1,0:T(8,128)S(1)}, u32[]{:S(2)}, u32[]{:S(2)}) collective-permute-start(f32[8,512]{1,0:T(8,128)S(1)} %dynamic-slice_bitcast_fusion.9), channel_id=1, source_target_pairs={{0,32},{8,40},{16,48},{24,56},{32,0},{40,8},{48,16},{56,24},{64,96... | collective-permute-start | bytes 49160 | tf_op jit(solution)/shard_map/cond/branch_1_fun/ppermute | solution.py:69
  171.6 9.3 %copy-start.19 = (f32[8112]{0:T(1024)}, f32[8112]{0:T(1024)S(1)}, u32[]{:S(2)}) copy-start(f32[8112]{0:T(1024)S(1)} %get-tuple-element.267) | copy-start | bytes 97348
  172.9 4.5 %collective-permute-start.46 = (f32[2,2496]{1,0:T(2,128)S(1)}, f32[2,2496]{1,0:T(2,128)S(1)}, u32[]{:S(2)}, u32[]{:S(2)}) collective-permute-start(f32[2,2496]{1,0:T(2,128)S(1)} %pad_maximum_fusion.15), channel_id=1, source_target_pairs={{0,1},{1,0},{2,3},{3,2},{4,5},{5,4},{6,7},{7,6},{8,9},{9,8},{10,11... | collective-permute-start | bytes 59912 | tf_op jit(solution)/shard_map/ppermute | solution.py:84
  177.4 5.7 %collective-permute-start.47 = (f32[2,2496]{1,0:T(2,128)S(1)}, f32[2,2496]{1,0:T(2,128)S(1)}, u32[]{:S(2)}, u32[]{:S(2)}) collective-permute-start(f32[2,2496]{1,0:T(2,128)S(1)} %fusion.38), channel_id=1, source_target_pairs={{0,2},{1,3},{2,0},{3,1},{4,6},{5,7},{6,4},{7,5},{8,10},{9,11},{10,... | collective-permute-start | bytes 59912 | tf_op jit(solution)/shard_map/ppermute | solution.py:84
  183.2 6.2 %copy-start.5 = (bf16[4,32,2496]{2,1,0:T(8,128)(2,1)}, bf16[4,32,2496]{2,1,0:T(8,128)(2,1)S(1)}, u32[]{:S(2)}) copy-start(bf16[4,32,2496]{2,1,0:T(8,128)(2,1)S(1)} %get-tuple-element.269) | copy-start | bytes 1916932
  183.3 9.3 %collective-permute-start.49 = (bf16[2,32,2496]{2,1,0:T(8,128)(2,1)S(1)}, bf16[2,32,2496]{2,1,0:T(8,128)(2,1)S(1)}, u32[]{:S(2)}, u32[]{:S(2)}) collective-permute-start(bf16[2,32,2496]{2,1,0:T(8,128)(2,1)S(1)} %get-tuple-element.222), channel_id=1, source_target_pairs={{1,0},{2,1},{3,2},{5,4},{6,5},{7,6},{9,8},{10,9},{11,10},{13,12},{... | collective-permute-start | bytes 958472 | tf_op jit(solution)/shard_map/ppermute | solution.py:15
  187.4 9.0 %collective-permute-start.48 = (bf16[2,32,2496]{2,1,0:T(8,128)(2,1)S(1)}, bf16[2,32,2496]{2,1,0:T(8,128)(2,1)S(1)}, u32[]{:S(2)}, u32[]{:S(2)}) collective-permute-start(bf16[2,32,2496]{2,1,0:T(8,128)(2,1)S(1)} %get-tuple-element.221), channel_id=1, source_target_pairs={{0,1},{1,2},{2,3},{4,5},{5,6},{6,7},{8,9},{9,10},{10,11},{12,13},{... | collective-permute-start | bytes 958472 | tf_op jit(solution)/shard_map/ppermute | solution.py:12
  189.4 8.2 %copy-start.4 = (bf16[1,1,4,32,2496]{4,3,2,1,0:T(8,128)(2,1)S(1)}, bf16[1,1,4,32,2496]{4,3,2,1,0:T(8,128)(2,1)}, u32[]{:S(2)}) copy-start(bf16[1,1,4,32,2496]{4,3,2,1,0:T(8,128)(2,1)} %param.27) | copy-start | bytes 1916932
  189.4 8.2 %copy-start.13 = (f32[25,2496]{1,0:T(8,128)S(1)}, f32[25,2496]{1,0:T(8,128)}, u32[]{:S(2)}) copy-start(f32[25,2496]{1,0:T(8,128)} %copy-done.12) | copy-start | bytes 748804
  189.5 8.2 %copy-start.16 = (bf16[1,4,32,416]{3,2,1,0:T(8,128)(2,1)S(1)}, bf16[1,4,32,416]{3,2,1,0:T(8,128)(2,1)}, u32[]{:S(2)}) copy-start(bf16[1,4,32,416]{3,2,1,0:T(8,128)(2,1)} %param.26) | copy-start | bytes 319492
  (6 other events, 7.0 us)

commit v4 on v3

--- a/solution.py
+++ b/solution.py
@@ -72,10 +72,9 @@
     return buf
 
 
-def scatter_streams(full, orders, cuts):
-    parts = jnp.split(full, cuts, axis=-1)
-    done = [scatter_chunks(part, order) for part, order in zip(parts, orders)]
-    return jnp.concatenate(done, axis=-1).reshape(-1)
+def scatter_streams(full, orders):
+    done = [scatter_chunks(full[:, k], order) for k, order in enumerate(orders)]
+    return jnp.stack(done).reshape(-1)
 
 
 def rows_sum(values):
@@ -211,8 +210,8 @@
     chunk = cin * wide // shards
 
     def spread(term):
-        flat_term = (term / images).reshape(shards, 8, -1)
-        return scatter_streams(flat_term, SCATTER_ORDERS, [512])
+        flat_term = (term / images).reshape(shards, len(SCATTER_ORDERS), 8, -1)
+        return scatter_streams(flat_term, SCATTER_ORDERS)
 
     def spread_still(term):
         return jnp.zeros((chunk,), jnp.float32)

time: 201 us -> 203 us (level)
  waiting for transfers between devices: 55.6 us -> 60.6 us
    split x2 -> x0, local copies, waits for them, and re-layouts: 6.17 us -> none  [scatter_streams(): parts = jnp.split(full, cuts, axis=-1)]
    ppermute x14, waiting for transfers between devices: 23.8 us -> 28.7 us  [scatter_chunks(): moved = lax.ppermute(other, axis, swap_pairs(axis, j))]
    slice x0 -> x1, local copies, waits for them, and re-layouts: none -> 4.59 us  [scatter_streams(): done = [scatter_chunks(full[:, k], order) for k, order in enumerate(orders)]]
  transfers between devices with their start and end apart: 36 -> 36, of which waited for: 21 -> 22; matrix products, arithmetic and copies ran while one was open for 17% -> 15% of each run, Pallas kernels for 0% -> 0%
where the time goes in v4:
time: 203 us; the launch traced here: 201 us
  starting transfers between devices  65.9 us (32%)
  waiting for transfers between devices  60.6 us (30%)
  local copies, waits for them, and re-layouts  29.4 us (14%)
  other arithmetic  22.3 us (11%)
  loops' own time  14.4 us (7%)
  matrix products  6.54 us (3%)
  between operations  2.27 us (1%)
    ppermute x14, waiting for transfers between devices, scatter_chunks(): moved = lax.ppermute(other, axis, swap_pairs(axis, j))  28.7 us
    ppermute x14, starting transfers between devices, gather_chunks(): recv = lax.ppermute(buf, axis, swap_pairs(axis, j))  24 us
    ppermute x14, waiting for transfers between devices, gather_chunks(): recv = lax.ppermute(buf, axis, swap_pairs(axis, j))  23.1 us
    ppermute x14, starting transfers between devices, scatter_chunks(): moved = lax.ppermute(other, axis, swap_pairs(axis, j))  22.4 us
    another operation x1, loops' own time, body(): grad_out = lax.cond(segment == 0, lead_branch, lead_still)  13 us
    ppermute x2, starting transfers between devices, extended_2(): lax.ppermute(lax.slice_in_dim(block, 0, width, axis=dim), axis, backward)  7.9 us
    reshape x1, local copies, waits for them, and re-layouts, spread(): flat_term = (term / images).reshape(shards, len(SCATTER_ORDERS), 8, -1)  7.13 us
    another operation x1, local copies, waits for them, and re-layouts, body(): weight = flat.reshape(cin, wide)  5.24 us
  transfers between devices with their start and end apart: 36, of which 22 were waited for; matrix products, arithmetic and copies ran while one was open for 15% of the time, Pallas kernels for 0%

profile of v4, /device:TPU:8, one launch (start us, length us, event | category | flops | bytes accessed | tf_op | source)
XLA Modules:
  0.0 201.4 jit_solution(17163070187822177084)
XLA Ops:
  1.7 3.0 %collective-permute-start.36 = (bf16[16,253]{1,0:T(8,128)(2,1)S(1)}, bf16[16,253]{1,0:T(8,128)(2,1)S(1)}, u32[]{:S(2)}, u32[]{:S(2)}) collective-permute-start(bf16[16,253]{1,0:T(8,128)(2,1)S(1)} %split.9), channel_id=1, source_target_pairs={{0,128},{8,136},{16,144},{24,152},{32,160},{40,168},{48,176},{56,1... | collective-permute-start | bytes 24296 | tf_op jit(solution)/shard_map/ppermute | solution.py:41
  4.7 7.2 %collective-permute-start.29 = (bf16[16,254]{1,0:T(8,128)(2,1)S(1)}, bf16[16,254]{1,0:T(8,128)(2,1)S(1)}, u32[]{:S(2)}, u32[]{:S(2)}) collective-permute-start(bf16[16,254]{1,0:T(8,128)(2,1)S(1)} %split.8), channel_id=1, source_target_pairs={{0,32},{8,40},{16,48},{24,56},{32,0},{40,8},{48,16},{56,24},{64,96... | collective-permute-start | bytes 24392 | tf_op jit(solution)/shard_map/ppermute | solution.py:41
  12.1 2.4 %collective-permute-start.37 = (bf16[2,16,253]{2,1,0:T(8,128)(2,1)S(1)}, bf16[2,16,253]{2,1,0:T(8,128)(2,1)S(1)}, u32[]{:S(2)}, u32[]{:S(2)}) collective-permute-start(bf16[2,16,253]{2,1,0:T(8,128)(2,1)S(1)} %pad_maximum_fusion.17), channel_id=1, source_target_pairs={{0,2},{1,3},{2,0},{3,1},{4,6},{5,7},{6,4},{7,5},{8,10},{9,11},{10,... | collective-permute-start | bytes 48584 | tf_op jit(solution)/shard_map/ppermute | solution.py:41
  15.1 2.3 %collective-permute-done.37 = bf16[2,16,253]{2,1,0:T(8,128)(2,1)S(1)} collective-permute-done((bf16[2,16,253]{2,1,0:T(8,128)(2,1)S(1)}, bf16[2,16,253]{2,1,0:T(8,128)(2,1)S(1)}, u32[]{:S(2)}, u32[]{:S(2)}) %collective-permute-start.37) | collective-permute-done | bytes 16224 | tf_op jit(solution)/shard_map/ppermute | solution.py:41
  17.4 2.8 %collective-permute-start.38 = (bf16[2,2,16,253]{3,2,1,0:T(8,128)(2,1)S(1)}, bf16[2,2,16,253]{3,2,1,0:T(8,128)(2,1)S(1)}, u32[]{:S(2)}, u32[]{:S(2)}) collective-permute-start(bf16[2,2,16,253]{3,2,1,0:T(8,128)(2,1)S(1)} %pad_maximum_fusion.14), channel_id=1, source_target_pairs={{0,32},{8,40},{16,48},{24,56},{32,0},{40,8},{48,16},{56,24},{64,96... | collective-permute-start | bytes 97160 | tf_op jit(solution)/shard_map/ppermute | solution.py:41
  21.8 3.8 %collective-permute-done.38 = bf16[2,2,16,253]{3,2,1,0:T(8,128)(2,1)S(1)} collective-permute-done((bf16[2,2,16,253]{3,2,1,0:T(8,128)(2,1)S(1)}, bf16[2,2,16,253]{3,2,1,0:T(8,128)(2,1)S(1)}, u32[]{:S(2)}, u32[]{:S(2)}) %collective-permute-start.38) | collective-permute-done | bytes 32416 | tf_op jit(solution)/shard_map/ppermute | solution.py:41
  27.1 2.4 %collective-permute-start.32 = (bf16[2,2,2,16,254]{4,3,2,1,0:T(8,128)(2,1)S(1)}, bf16[2,2,2,16,254]{4,3,2,1,0:T(8,128)(2,1)S(1)}, u32[]{:S(2)}, u32[]{:S(2)}) collective-permute-start(bf16[2,2,2,16,254]{4,3,2,1,0:T(8,128)(2,1)S(1)} %pad_maximum_fusion.11), channel_id=1, source_target_pairs={{0,2},{1,3},{2,0},{3,1},{4,6},{5,7},{6,4},{7,5},{8,10},{9,11},{10,... | collective-permute-start | bytes 195080 | tf_op jit(solution)/shard_map/ppermute | solution.py:41
  29.5 2.1 %collective-permute-done.39 = bf16[2,2,2,16,253]{4,3,2,1,0:T(8,128)(2,1)S(1)} collective-permute-done((bf16[2,2,2,16,253]{4,3,2,1,0:T(8,128)(2,1)S(1)}, bf16[2,2,2,16,253]{4,3,2,1,0:T(8,128)(2,1)S(1)}, u32[]{:S(2)}, u32[]{:S(2)}) %collective-permute-start.39) | collective-permute-done | bytes 64800 | tf_op jit(solution)/shard_map/ppermute | solution.py:41
  34.1 2.5 %collective-permute-done.40 = bf16[2,2,2,2,16,253]{5,4,3,2,1,0:T(8,128)(2,1)S(1)} collective-permute-done((bf16[2,2,2,2,16,253]{5,4,3,2,1,0:T(8,128)(2,1)S(1)}, bf16[2,2,2,2,16,253]{5,4,3,2,1,0:T(8,128)(2,1)S(1)}, u32[]{:S(2)}, u32[]{:S(2)}) %collective-permute-start.40) | collective-permute-done | bytes 129568 | tf_op jit(solution)/shard_map/ppermute | solution.py:41
  37.4 2.5 %collective-permute-done.33 = bf16[2,2,2,2,16,254]{5,4,3,2,1,0:T(8,128)(2,1)S(1)} collective-permute-done((bf16[2,2,2,2,16,254]{5,4,3,2,1,0:T(8,128)(2,1)S(1)}, bf16[2,2,2,2,16,254]{5,4,3,2,1,0:T(8,128)(2,1)S(1)}, u32[]{:S(2)}, u32[]{:S(2)}) %collective-permute-start.33) | collective-permute-done | bytes 130080 | tf_op jit(solution)/shard_map/ppermute | solution.py:41
  40.1 3.2 %collective-permute-done.41 = bf16[2,2,2,2,2,16,253]{6,5,4,3,2,1,0:T(8,128)(2,1)S(1)} collective-permute-done((bf16[2,2,2,2,2,16,253]{6,5,4,3,2,1,0:T(8,128)(2,1)S(1)}, bf16[2,2,2,2,2,16,253]{6,5,4,3,2,1,0:T(8,128)(2,1)S(1)}, u32[]{:S(2)}, u32[]{:S(2)}) %collective-permute-start.41) | collective-permute-done | bytes 259104 | tf_op jit(solution)/shard_map/ppermute | solution.py:41
  43.8 5.5 %collective-permute-done.34 = bf16[2,2,2,2,2,16,254]{6,5,4,3,2,1,0:T(8,128)(2,1)S(1)} collective-permute-done((bf16[2,2,2,2,2,16,254]{6,5,4,3,2,1,0:T(8,128)(2,1)S(1)}, bf16[2,2,2,2,2,16,254]{6,5,4,3,2,1,0:T(8,128)(2,1)S(1)}, u32[]{:S(2)}, u32[]{:S(2)}) %collective-permute-start.34) | collective-permute-done | bytes 260128 | tf_op jit(solution)/shard_map/ppermute | solution.py:41
  51.5 3.6 %collective-permute-start.45 = (bf16[2,32,2496]{2,1,0:T(8,128)(2,1)}, bf16[2,32,2496]{2,1,0:T(8,128)(2,1)}, u32[]{:S(2)}, u32[]{:S(2)}) collective-permute-start(bf16[2,32,2496]{2,1,0:T(8,128)(2,1)} %get-tuple-element.228), channel_id=1, source_target_pairs={{1,0},{2,1},{3,2},{5,4},{6,5},{7,6},{9,8},{10,9},{11,10},{13,12},{... | collective-permute-start | bytes 958472 | tf_op jit(solution)/shard_map/ppermute | solution.py:15
  55.1 2.4 %collective-permute-start.44 = (bf16[2,32,2496]{2,1,0:T(8,128)(2,1)}, bf16[2,32,2496]{2,1,0:T(8,128)(2,1)}, u32[]{:S(2)}, u32[]{:S(2)}) collective-permute-start(bf16[2,32,2496]{2,1,0:T(8,128)(2,1)} %get-tuple-element.227), channel_id=1, source_target_pairs={{0,1},{1,2},{2,3},{4,5},{5,6},{6,7},{8,9},{9,10},{10,11},{12,13},{... | collective-permute-start | bytes 958472 | tf_op jit(solution)/shard_map/ppermute | solution.py:12
  57.6 15.2 %conditional.8 = (bf16[128,416]{0,1:T(8,128)(2,1)}, bf16[4,32,416]{2,1,0:T(8,128)(2,1)S(1)}) conditional(s32[]{:T(128)} %convert_element_type.291, () %tuple.71, (bf16[1,4,32,384]{3,2,1,0:T(8,128)(2,1)S(1)}, bf16[1,2,16,384]{3,2,1,0:T(8,128)(2,1)S(1)}, bf16[1,1,8,384]{3,2,1,0:T(8,128)(2,1)S(1)}, bf16[416,384]{1,0:T(8,128)(2,1)S(1)}) %tuple.195), branch_computations={%region_0.1_spmd, %region_1.2_spmd} | conditional | flops 41138176 | bytes 1972240 | solution.py:199
  75.9 2.2 %pad_maximum_fusion.2 = bf16[128,16,507]{2,1,0:T(8,128)(2,1)} fusion(bf16[128,16,253]{2,1,0:T(8,128)(2,1)S(1)} %bitcast.294, bf16[128,16,254]{2,1,0:T(8,128)(2,1)S(1)} %bitcast.295), kind=kLoop, calls=%fused_computation.211 | loop fusion | flops 4153344 | bytes 4153344 | tf_op jit(solution)/shard_map/concatenate | solution.py:53
  78.1 5.2 %reshape_reshape.3 = bf16[416,2496]{1,0:T(8,128)(2,1)S(1)} reshape(bf16[128,16,507]{2,1,0:T(8,128)(2,1)} %pad_maximum_fusion.2) | data formatting | bytes 4153344 | tf_op jit(solution)/shard_map/reshape;reshape | solution.py:158
  83.4 2.0 %conditional.9 = (bf16[128,2496]{0,1:T(8,128)(2,1)S(1)}) conditional(s32[]{:T(128)} %convert_element_type.291, () %tuple.75, (bf16[128,416]{0,1:T(8,128)(2,1)}, bf16[416,2496]{1,0:T(8,128)(2,1)S(1)}) %tuple.76), branch_computations={%region_2.3_spmd, %region_3.4_spmd} | conditional | flops 266133504 | bytes 2822152 | solution.py:207
  83.4 2.0 %convolution_convert_fusion.1 = bf16[128,2496]{0,1:T(8,128)(2,1)S(1)} fusion(bf16[128,416]{0,1:T(8,128)(2,1)} %get-tuple-element.158, bf16[416,2496]{1,0:T(8,128)(2,1)S(1)} %get-tuple-element.87), kind=kOutput, calls=%fused_computation.6 | convolution fusion | flops 266133504 | bytes 2822144 | tf_op jit(solution)/shard_map/cond/branch_1_fun/dot_general | solution.py:202
  87.8 2.0 collective-permute-start.28
  94.1 3.6 %conditional.10 = (f32[416,2496]{1,0:T(8,128)}) conditional(s32[]{:T(128)} %convert_element_type.291, () %tuple.74, (bf16[1,1,4,32,2496]{4,3,2,1,0:T(8,128)(2,1)S(1)}, bf16[128,416]{0,1:T(8,128)(2,1)}) %tuple.184), branch_computations={%region_4.5_spmd, %region_5.6_spmd} | conditional | flops 265814016 | bytes 4898824 | solution.py:230
  94.1 3.6 %fusion.48 = f32[416,2496]{1,0:T(8,128)} fusion(bf16[128,416]{0,1:T(8,128)(2,1)} %get-tuple-element.161, bf16[128,2496]{1,0:T(8,128)(2,1)S(1)} %bitcast.291), kind=kOutput, calls=%fused_computation.264 | convolution fusion | flops 265814016 | bytes 4898816 | tf_op jit(solution)/shard_map/cond/branch_1_fun/dot_general | solution.py:223
  97.7 75.5 %conditional.11 = (f32[8112]{0:T(1024)S(1)}) conditional(s32[]{:T(128)} %convert_element_type.291, () %tuple.73, f32[416,2496]{1,0:T(8,128)} %get-tuple-element.270), branch_computations={%region_6.7_spmd, %region_7.8_spmd} | conditional | flops 2855492 | bytes 59543540 | solution.py:231
  97.7 4.6 %broadcast_multiply_fusion = f32[416,2496]{1,0:T(8,128)} fusion(f32[416,2496]{1,0:T(8,128)} %param.7), kind=kLoop, calls=%fused_computation.7 | loop fusion | flops 1038336 | bytes 8306688 | tf_op jit(solution)/shard_map/cond/branch_1_fun/div | solution.py:213
  102.2 7.1 %reshape.168 = f32[128,2,8,507]{3,2,1,0:T(8,128)} reshape(f32[416,2496]{1,0:T(8,128)} %broadcast_multiply_fusion) | data formatting | bytes 8306688 | tf_op jit(solution)/shard_map/cond/branch_1_fun/reshape | solution.py:213
  109.4 4.6 %fusion.44 = (f32[128,1,8,507]{3,2,1,0:T(8,128)}, f32[128,1,8,507]{3,2,1,0:T(8,128)}) fusion(f32[128,2,8,507]{3,2,1,0:T(8,128)} %reshape.168), kind=kLoop, calls=%fused_computation.260 | loop fusion | bytes 8306688 | tf_op jit(solution)/shard_map/cond/branch_1_fun/slice | solution.py:76
  114.0 2.1 %fusion.4 = bf16[2,2,2,2,2,16,507]{6,5,4,3,2,1,0:T(8,128)(2,1)} fusion(f32[2,2,2,2,2,2,2,8,507]{8,7,6,5,4,3,2,1,0:T(8,128)} %bitcast.287, s32[]{:T(128)S(6)} %select_n.226), kind=kLoop, calls=%fused_computation.13 | loop fusion | bytes 1038340 | tf_op jit(solution)/shard_map/cond/branch_1_fun/convert_element_type | solution.py:68
  116.7 2.1 %fusion.3 = bf16[2,2,2,2,2,16,507]{6,5,4,3,2,1,0:T(8,128)(2,1)} fusion(f32[2,2,2,2,2,2,2,8,507]{8,7,6,5,4,3,2,1,0:T(8,128)} %bitcast.283, s32[]{:T(128)S(6)} %select_n.224), kind=kLoop, calls=%fused_computation.12 | loop fusion | bytes 1038340 | tf_op jit(solution)/shard_map/cond/branch_1_fun/convert_element_type | solution.py:68
  120.4 5.1 %collective-permute-done.7 = bf16[2,2,2,2,2,16,507]{6,5,4,3,2,1,0:T(8,128)(2,1)} collective-permute-done((bf16[2,2,2,2,2,16,507]{6,5,4,3,2,1,0:T(8,128)(2,1)}, bf16[2,2,2,2,2,16,507]{6,5,4,3,2,1,0:T(8,128)(2,1)}, u32[]{:S(2)}, u32[]{:S(2)}) %collective-permute-start.7) | collective-permute-done | bytes 519200 | tf_op jit(solution)/shard_map/cond/branch_1_fun/ppermute | solution.py:69
  131.3 2.3 %collective-permute-done.8 = bf16[2,2,2,2,16,507]{5,4,3,2,1,0:T(8,128)(2,1)S(1)} collective-permute-done((bf16[2,2,2,2,16,507]{5,4,3,2,1,0:T(8,128)(2,1)S(1)}, bf16[2,2,2,2,16,507]{5,4,3,2,1,0:T(8,128)(2,1)S(1)}, u32[]{:S(2)}, u32[]{:S(2)}) %collective-permute-start.8) | collective-permute-done | bytes 259616 | tf_op jit(solution)/shard_map/cond/branch_1_fun/ppermute | solution.py:69
  133.7 2.4 %collective-permute-start.9 = (f32[2,2,2,2,8,507]{5,4,3,2,1,0:T(8,128)S(1)}, f32[2,2,2,2,8,507]{5,4,3,2,1,0:T(8,128)S(1)}, u32[]{:S(2)}, u32[]{:S(2)}) collective-permute-start(f32[2,2,2,2,8,507]{5,4,3,2,1,0:T(8,128)S(1)} %dynamic-slice_bitcast_fusion), channel_id=1, source_target_pairs={{0,1},{1,0},{2,3},{3,2},{4,5},{5,4},{6,7},{7,6},{8,9},{9,8},{10,11... | collective-permute-start | bytes 778760 | tf_op jit(solution)/shard_map/cond/branch_1_fun/ppermute | solution.py:69
  137.4 3.0 %collective-permute-done.9 = f32[2,2,2,2,8,507]{5,4,3,2,1,0:T(8,128)S(1)} collective-permute-done((f32[2,2,2,2,8,507]{5,4,3,2,1,0:T(8,128)S(1)}, f32[2,2,2,2,8,507]{5,4,3,2,1,0:T(8,128)S(1)}, u32[]{:S(2)}, u32[]{:S(2)}) %collective-permute-start.9) | collective-permute-done | bytes 259616 | tf_op jit(solution)/shard_map/cond/branch_1_fun/ppermute | solution.py:69
  143.2 1.8 collective-permute-start.3
  145.0 2.7 %collective-permute-done.10 = f32[2,2,2,8,507]{4,3,2,1,0:T(8,128)S(1)} collective-permute-done((f32[2,2,2,8,507]{4,3,2,1,0:T(8,128)S(1)}, f32[2,2,2,8,507]{4,3,2,1,0:T(8,128)S(1)}, u32[]{:S(2)}, u32[]{:S(2)}) %collective-permute-start.10) | collective-permute-done | bytes 129824 | tf_op jit(solution)/shard_map/cond/branch_1_fun/ppermute | solution.py:69
  147.8 2.4 %collective-permute-start.11 = (f32[2,2,8,507]{3,2,1,0:T(8,128)S(1)}, f32[2,2,8,507]{3,2,1,0:T(8,128)S(1)}, u32[]{:S(2)}, u32[]{:S(2)}) collective-permute-start(f32[2,2,8,507]{3,2,1,0:T(8,128)S(1)} %dynamic-slice_bitcast_fusion.4), channel_id=1, source_target_pairs={{0,32},{8,40},{16,48},{24,56},{32,0},{40,8},{48,16},{56,24},{64,96... | collective-permute-start | bytes 194696 | tf_op jit(solution)/shard_map/cond/branch_1_fun/ppermute | solution.py:69
  151.4 6.0 %collective-permute-done.11 = f32[2,2,8,507]{3,2,1,0:T(8,128)S(1)} collective-permute-done((f32[2,2,8,507]{3,2,1,0:T(8,128)S(1)}, f32[2,2,8,507]{3,2,1,0:T(8,128)S(1)}, u32[]{:S(2)}, u32[]{:S(2)}) %collective-permute-start.11) | collective-permute-done | bytes 64928 | tf_op jit(solution)/shard_map/cond/branch_1_fun/ppermute | solution.py:69
  158.8 2.1 %collective-permute-start.5 = (f32[2,8,507]{2,1,0:T(8,128)S(1)}, f32[2,8,507]{2,1,0:T(8,128)S(1)}, u32[]{:S(2)}, u32[]{:S(2)}) collective-permute-start(f32[2,8,507]{2,1,0:T(8,128)S(1)} %dynamic-slice_bitcast_fusion.7), channel_id=1, source_target_pairs={{0,128},{8,136},{16,144},{24,152},{32,160},{40,168},{48,176},{56,1... | collective-permute-start | bytes 97352 | tf_op jit(solution)/shard_map/cond/branch_1_fun/ppermute | solution.py:69
  160.9 2.0 collective-permute-done.12
  162.9 2.0 collective-permute-start.13
  165.0 3.1 %collective-permute-start.6 = (f32[8,507]{1,0:T(8,128)S(1)}, f32[8,507]{1,0:T(8,128)S(1)}, u32[]{:S(2)}, u32[]{:S(2)}) collective-permute-start(f32[8,507]{1,0:T(8,128)S(1)} %dynamic-slice_bitcast_fusion.9), channel_id=1, source_target_pairs={{0,32},{8,40},{16,48},{24,56},{32,0},{40,8},{48,16},{56,24},{64,96... | collective-permute-start | bytes 48680 | tf_op jit(solution)/shard_map/cond/branch_1_fun/ppermute | solution.py:69
  168.3 4.4 %collective-permute-done.6 = f32[8,507]{1,0:T(8,128)S(1)} collective-permute-done((f32[8,507]{1,0:T(8,128)S(1)}, f32[8,507]{1,0:T(8,128)S(1)}, u32[]{:S(2)}, u32[]{:S(2)}) %collective-permute-start.6) | collective-permute-done | bytes 16256 | tf_op jit(solution)/shard_map/cond/branch_1_fun/ppermute | solution.py:69
  174.5 2.3 %collective-permute-start.46 = (f32[2,2496]{1,0:T(2,128)S(1)}, f32[2,2496]{1,0:T(2,128)S(1)}, u32[]{:S(2)}, u32[]{:S(2)}) collective-permute-start(f32[2,2496]{1,0:T(2,128)S(1)} %pad_maximum_fusion.15), channel_id=1, source_target_pairs={{0,1},{1,0},{2,3},{3,2},{4,5},{5,4},{6,7},{7,6},{8,9},{9,8},{10,11... | collective-permute-start | bytes 59912 | tf_op jit(solution)/shard_map/ppermute | solution.py:83
  176.8 1.8 collective-permute-done.46
  180.3 2.1 %copy.60 = bf16[2496,104]{1,0:T(8,128)(2,1)} copy(bf16[2496,104]{0,1:T(8,128)(2,1)} %param.34) | data formatting | bytes 1038336 | tf_op args[8]
  184.9 4.3 %collective-permute-start.49 = (bf16[2,32,2496]{2,1,0:T(8,128)(2,1)S(1)}, bf16[2,32,2496]{2,1,0:T(8,128)(2,1)S(1)}, u32[]{:S(2)}, u32[]{:S(2)}) collective-permute-start(bf16[2,32,2496]{2,1,0:T(8,128)(2,1)S(1)} %get-tuple-element.226), channel_id=1, source_target_pairs={{1,0},{2,1},{3,2},{5,4},{6,5},{7,6},{9,8},{10,9},{11,10},{13,12},{... | collective-permute-start | bytes 958472 | tf_op jit(solution)/shard_map/ppermute | solution.py:15
  189.2 1.9 collective-permute-start.48
  191.2 2.7 %collective-permute-done.49 = bf16[2,32,2496]{2,1,0:T(8,128)(2,1)S(1)} collective-permute-done((bf16[2,32,2496]{2,1,0:T(8,128)(2,1)S(1)}, bf16[2,32,2496]{2,1,0:T(8,128)(2,1)S(1)}, u32[]{:S(2)}, u32[]{:S(2)}) %collective-permute-start.49) | collective-permute-done | bytes 319520 | tf_op jit(solution)/shard_map/ppermute | solution.py:15
  193.9 4.3 %collective-permute-done.48 = bf16[2,32,2496]{2,1,0:T(8,128)(2,1)S(1)} collective-permute-done((bf16[2,32,2496]{2,1,0:T(8,128)(2,1)S(1)}, bf16[2,32,2496]{2,1,0:T(8,128)(2,1)S(1)}, u32[]{:S(2)}, u32[]{:S(2)}) %collective-permute-start.48) | collective-permute-done | bytes 319520 | tf_op jit(solution)/shard_map/ppermute | solution.py:12
  (166 shorter events, 46.0 us)
Async XLA Ops:
  1.7 10.3 %collective-permute-start.36 = (bf16[16,253]{1,0:T(8,128)(2,1)S(1)}, bf16[16,253]{1,0:T(8,128)(2,1)S(1)}, u32[]{:S(2)}, u32[]{:S(2)}) collective-permute-start(bf16[16,253]{1,0:T(8,128)(2,1)S(1)} %split.9), channel_id=1, source_target_pairs={{0,128},{8,136},{16,144},{24,152},{32,160},{40,168},{48,176},{56,1... | collective-permute-start | bytes 24296 | tf_op jit(solution)/shard_map/ppermute | solution.py:41
  4.7 9.7 %collective-permute-start.29 = (bf16[16,254]{1,0:T(8,128)(2,1)S(1)}, bf16[16,254]{1,0:T(8,128)(2,1)S(1)}, u32[]{:S(2)}, u32[]{:S(2)}) collective-permute-start(bf16[16,254]{1,0:T(8,128)(2,1)S(1)} %split.8), channel_id=1, source_target_pairs={{0,32},{8,40},{16,48},{24,56},{32,0},{40,8},{48,16},{56,24},{64,96... | collective-permute-start | bytes 24392 | tf_op jit(solution)/shard_map/ppermute | solution.py:41
  12.1 5.3 %collective-permute-start.37 = (bf16[2,16,253]{2,1,0:T(8,128)(2,1)S(1)}, bf16[2,16,253]{2,1,0:T(8,128)(2,1)S(1)}, u32[]{:S(2)}, u32[]{:S(2)}) collective-permute-start(bf16[2,16,253]{2,1,0:T(8,128)(2,1)S(1)} %pad_maximum_fusion.17), channel_id=1, source_target_pairs={{0,2},{1,3},{2,0},{3,1},{4,6},{5,7},{6,4},{7,5},{8,10},{9,11},{10,... | collective-permute-start | bytes 48584 | tf_op jit(solution)/shard_map/ppermute | solution.py:41
  14.5 5.7 %collective-permute-start.30 = (bf16[2,16,254]{2,1,0:T(8,128)(2,1)S(1)}, bf16[2,16,254]{2,1,0:T(8,128)(2,1)S(1)}, u32[]{:S(2)}, u32[]{:S(2)}) collective-permute-start(bf16[2,16,254]{2,1,0:T(8,128)(2,1)S(1)} %pad_maximum_fusion.16), channel_id=1, source_target_pairs={{0,128},{8,136},{16,144},{24,152},{32,160},{40,168},{48,176},{56,1... | collective-permute-start | bytes 48776 | tf_op jit(solution)/shard_map/ppermute | solution.py:41
  17.4 8.1 %collective-permute-start.38 = (bf16[2,2,16,253]{3,2,1,0:T(8,128)(2,1)S(1)}, bf16[2,2,16,253]{3,2,1,0:T(8,128)(2,1)S(1)}, u32[]{:S(2)}, u32[]{:S(2)}) collective-permute-start(bf16[2,2,16,253]{3,2,1,0:T(8,128)(2,1)S(1)} %pad_maximum_fusion.14), channel_id=1, source_target_pairs={{0,32},{8,40},{16,48},{24,56},{32,0},{40,8},{48,16},{56,24},{64,96... | collective-permute-start | bytes 97160 | tf_op jit(solution)/shard_map/ppermute | solution.py:41
  20.2 6.8 %collective-permute-start.31 = (bf16[2,2,16,254]{3,2,1,0:T(8,128)(2,1)S(1)}, bf16[2,2,16,254]{3,2,1,0:T(8,128)(2,1)S(1)}, u32[]{:S(2)}, u32[]{:S(2)}) collective-permute-start(bf16[2,2,16,254]{3,2,1,0:T(8,128)(2,1)S(1)} %pad_maximum_fusion.13), channel_id=1, source_target_pairs={{0,16},{8,24},{16,0},{24,8},{32,48},{40,56},{48,32},{56,40},{64,80... | collective-permute-start | bytes 97544 | tf_op jit(solution)/shard_map/ppermute | solution.py:41
  25.6 6.0 %collective-permute-start.39 = (bf16[2,2,2,16,253]{4,3,2,1,0:T(8,128)(2,1)S(1)}, bf16[2,2,2,16,253]{4,3,2,1,0:T(8,128)(2,1)S(1)}, u32[]{:S(2)}, u32[]{:S(2)}) collective-permute-start(bf16[2,2,2,16,253]{4,3,2,1,0:T(8,128)(2,1)S(1)} %pad_maximum_fusion.12), channel_id=1, source_target_pairs={{0,16},{8,24},{16,0},{24,8},{32,48},{40,56},{48,32},{56,40},{64,80... | collective-permute-start | bytes 194312 | tf_op jit(solution)/shard_map/ppermute | solution.py:41
  27.1 6.3 %collective-permute-start.32 = (bf16[2,2,2,16,254]{4,3,2,1,0:T(8,128)(2,1)S(1)}, bf16[2,2,2,16,254]{4,3,2,1,0:T(8,128)(2,1)S(1)}, u32[]{:S(2)}, u32[]{:S(2)}) collective-permute-start(bf16[2,2,2,16,254]{4,3,2,1,0:T(8,128)(2,1)S(1)} %pad_maximum_fusion.11), channel_id=1, source_target_pairs={{0,2},{1,3},{2,0},{3,1},{4,6},{5,7},{6,4},{7,5},{8,10},{9,11},{10,... | collective-permute-start | bytes 195080 | tf_op jit(solution)/shard_map/ppermute | solution.py:41
  31.6 5.1 %collective-permute-start.40 = (bf16[2,2,2,2,16,253]{5,4,3,2,1,0:T(8,128)(2,1)S(1)}, bf16[2,2,2,2,16,253]{5,4,3,2,1,0:T(8,128)(2,1)S(1)}, u32[]{:S(2)}, u32[]{:S(2)}) collective-permute-start(bf16[2,2,2,2,16,253]{5,4,3,2,1,0:T(8,128)(2,1)S(1)} %pad_maximum_fusion.10), channel_id=1, source_target_pairs={{0,1},{1,0},{2,3},{3,2},{4,5},{5,4},{6,7},{7,6},{8,9},{9,8},{10,11... | collective-permute-start | bytes 388616 | tf_op jit(solution)/shard_map/ppermute | solution.py:41
  33.5 6.4 %collective-permute-start.33 = (bf16[2,2,2,2,16,254]{5,4,3,2,1,0:T(8,128)(2,1)S(1)}, bf16[2,2,2,2,16,254]{5,4,3,2,1,0:T(8,128)(2,1)S(1)}, u32[]{:S(2)}, u32[]{:S(2)}) collective-permute-start(bf16[2,2,2,2,16,254]{5,4,3,2,1,0:T(8,128)(2,1)S(1)} %pad_maximum_fusion.9), channel_id=1, source_target_pairs={{0,64},{8,72},{16,80},{24,88},{32,96},{40,104},{48,112},{56,120},{... | collective-permute-start | bytes 390152 | tf_op jit(solution)/shard_map/ppermute | solution.py:41
  36.8 6.6 %collective-permute-start.41 = (bf16[2,2,2,2,2,16,253]{6,5,4,3,2,1,0:T(8,128)(2,1)S(1)}, bf16[2,2,2,2,2,16,253]{6,5,4,3,2,1,0:T(8,128)(2,1)S(1)}, u32[]{:S(2)}, u32[]{:S(2)}) collective-permute-start(bf16[2,2,2,2,2,16,253]{6,5,4,3,2,1,0:T(8,128)(2,1)S(1)} %pad_maximum_fusion.8), channel_id=1, source_target_pairs={{0,64},{8,72},{16,80},{24,88},{32,96},{40,104},{48,112},{56,120},{... | collective-permute-start | bytes 777224 | tf_op jit(solution)/shard_map/ppermute | solution.py:41
  40.0 9.3 %collective-permute-start.34 = (bf16[2,2,2,2,2,16,254]{6,5,4,3,2,1,0:T(8,128)(2,1)S(1)}, bf16[2,2,2,2,2,16,254]{6,5,4,3,2,1,0:T(8,128)(2,1)S(1)}, u32[]{:S(2)}, u32[]{:S(2)}) collective-permute-start(bf16[2,2,2,2,2,16,254]{6,5,4,3,2,1,0:T(8,128)(2,1)S(1)} %pad_maximum_fusion.7), channel_id=1, source_target_pairs={{0,8},{8,0},{16,24},{24,16},{32,40},{40,32},{48,56},{56,48},{64,72... | collective-permute-start | bytes 780296 | tf_op jit(solution)/shard_map/ppermute | solution.py:41
  43.5 29.2 %collective-permute-start.42 = (bf16[2,2,2,2,2,2,16,253]{7,6,5,4,3,2,1,0:T(8,128)(2,1)S(1)}, bf16[2,2,2,2,2,2,16,253]{7,6,5,4,3,2,1,0:T(8,128)(2,1)}, u32[]{:S(2)}, u32[]{:S(2)}) collective-permute-start(bf16[2,2,2,2,2,2,16,253]{7,6,5,4,3,2,1,0:T(8,128)(2,1)S(1)} %pad_maximum_fusion.6), channel_id=1, source_target_pairs={{0,8},{8,0},{16,24},{24,16},{32,40},{40,32},{48,56},{56,48},{64,72... | collective-permute-start | bytes 1554440 | tf_op jit(solution)/shard_map/ppermute | solution.py:41
  49.3 8.2 %copy-start.15 = (bf16[416,384]{1,0:T(8,128)(2,1)S(1)}, bf16[416,384]{1,0:T(8,128)(2,1)}, u32[]{:S(2)}) copy-start(bf16[416,384]{1,0:T(8,128)(2,1)} %param.31) | copy-start | bytes 958468
  49.4 8.2 %copy-start.18 = (bf16[1,4,32,384]{3,2,1,0:T(8,128)(2,1)S(1)}, bf16[1,4,32,384]{3,2,1,0:T(8,128)(2,1)}, u32[]{:S(2)}) copy-start(bf16[1,4,32,384]{3,2,1,0:T(8,128)(2,1)} %param.28) | copy-start | bytes 294916
  49.4 8.2 %copy-start.20 = (bf16[1,2,16,384]{3,2,1,0:T(8,128)(2,1)S(1)}, bf16[1,2,16,384]{3,2,1,0:T(8,128)(2,1)}, u32[]{:S(2)}) copy-start(bf16[1,2,16,384]{3,2,1,0:T(8,128)(2,1)} %param.29) | copy-start | bytes 73732
  49.4 8.2 %copy-start.21 = (bf16[1,1,8,384]{3,2,1,0:T(8,128)(2,1)S(1)}, bf16[1,1,8,384]{3,2,1,0:T(8,128)(2,1)}, u32[]{:S(2)}) copy-start(bf16[1,1,8,384]{3,2,1,0:T(8,128)(2,1)} %param.30) | copy-start | bytes 18436
  50.3 24.0 %collective-permute-start.35 = (bf16[2,2,2,2,2,2,16,254]{7,6,5,4,3,2,1,0:T(8,128)(2,1)}, bf16[2,2,2,2,2,2,16,254]{7,6,5,4,3,2,1,0:T(8,128)(2,1)}, u32[]{:S(2)}, u32[]{:S(2)}) collective-permute-start(bf16[2,2,2,2,2,2,16,254]{7,6,5,4,3,2,1,0:T(8,128)(2,1)} %pad_maximum_fusion.5), channel_id=1, source_target_pairs={{0,1},{1,0},{2,3},{3,2},{4,5},{5,4},{6,7},{7,6},{8,9},{9,8},{10,11... | collective-permute-start | bytes 1560584 | tf_op jit(solution)/shard_map/ppermute | solution.py:41
  51.5 39.2 %collective-permute-start.45 = (bf16[2,32,2496]{2,1,0:T(8,128)(2,1)}, bf16[2,32,2496]{2,1,0:T(8,128)(2,1)}, u32[]{:S(2)}, u32[]{:S(2)}) collective-permute-start(bf16[2,32,2496]{2,1,0:T(8,128)(2,1)} %get-tuple-element.228), channel_id=1, source_target_pairs={{1,0},{2,1},{3,2},{5,4},{6,5},{7,6},{9,8},{10,9},{11,10},{13,12},{... | collective-permute-start | bytes 958472 | tf_op jit(solution)/shard_map/ppermute | solution.py:15
  55.1 35.6 %collective-permute-start.44 = (bf16[2,32,2496]{2,1,0:T(8,128)(2,1)}, bf16[2,32,2496]{2,1,0:T(8,128)(2,1)}, u32[]{:S(2)}, u32[]{:S(2)}) collective-permute-start(bf16[2,32,2496]{2,1,0:T(8,128)(2,1)} %get-tuple-element.227), channel_id=1, source_target_pairs={{0,1},{1,2},{2,3},{4,5},{5,6},{6,7},{8,9},{9,10},{10,11},{12,13},{... | collective-permute-start | bytes 958472 | tf_op jit(solution)/shard_map/ppermute | solution.py:12
  86.5 5.9 %collective-permute-start.43 = (bf16[4,32,2496]{2,1,0:T(8,128)(2,1)}, bf16[4,32,2496]{2,1,0:T(8,128)(2,1)S(1)}, u32[]{:S(2)}, u32[]{:S(2)}) collective-permute-start(bf16[4,32,2496]{2,1,0:T(8,128)(2,1)} %bitcast.296), channel_id=1, source_target_pairs={{0,4},{1,5},{2,6},{3,7},{8,12},{9,13},{10,14},{11,15},{16,20},{17,... | collective-permute-start | bytes 1916936 | tf_op jit(solution)/shard_map/ppermute | solution.py:23
  87.8 4.6 %collective-permute-start.28 = (bf16[4,32,416]{2,1,0:T(8,128)(2,1)}, bf16[4,32,416]{2,1,0:T(8,128)(2,1)}, u32[]{:S(2)}, u32[]{:S(2)}) collective-permute-start(bf16[4,32,416]{2,1,0:T(8,128)(2,1)} %copy-done.17), channel_id=1, source_target_pairs={{0,4},{1,5},{2,6},{3,7},{8,12},{9,13},{10,14},{11,15},{16,20},{17,... | collective-permute-start | bytes 319496 | tf_op jit(solution)/shard_map/ppermute | solution.py:23
  92.4 1.5 copy-start.8
  97.7 75.6 %copy-start.9 = (f32[4,32,2496]{2,1,0:T(8,128)S(1)}, f32[4,32,2496]{2,1,0:T(8,128)}, u32[]{:S(2)}) copy-start(f32[4,32,2496]{2,1,0:T(8,128)} %copy-done.8) | copy-start | bytes 3833860
  116.0 9.5 %collective-permute-start.7 = (bf16[2,2,2,2,2,16,507]{6,5,4,3,2,1,0:T(8,128)(2,1)}, bf16[2,2,2,2,2,16,507]{6,5,4,3,2,1,0:T(8,128)(2,1)}, u32[]{:S(2)}, u32[]{:S(2)}) collective-permute-start(bf16[2,2,2,2,2,16,507]{6,5,4,3,2,1,0:T(8,128)(2,1)} %fusion.4), channel_id=1, source_target_pairs={{0,8},{8,0},{16,24},{24,16},{32,40},{40,32},{48,56},{56,48},{64,72... | collective-permute-start | bytes 1557512 | tf_op jit(solution)/shard_map/cond/branch_1_fun/ppermute | solution.py:69
  118.8 9.9 %collective-permute-start = (bf16[2,2,2,2,2,16,507]{6,5,4,3,2,1,0:T(8,128)(2,1)}, bf16[2,2,2,2,2,16,507]{6,5,4,3,2,1,0:T(8,128)(2,1)}, u32[]{:S(2)}, u32[]{:S(2)}) collective-permute-start(bf16[2,2,2,2,2,16,507]{6,5,4,3,2,1,0:T(8,128)(2,1)} %fusion.3), channel_id=1, source_target_pairs={{0,1},{1,0},{2,3},{3,2},{4,5},{5,4},{6,7},{7,6},{8,9},{9,8},{10,11... | collective-permute-start | bytes 1557512 | tf_op jit(solution)/shard_map/cond/branch_1_fun/ppermute | solution.py:69
  120.4 8.3 %copy-start.2 = (f32[128,1,8,507]{3,2,1,0:T(8,128)S(1)}, f32[128,1,8,507]{3,2,1,0:T(8,128)}, u32[]{:S(2)}) copy-start(f32[128,1,8,507]{3,2,1,0:T(8,128)} %get-tuple-element.215) | copy-start | bytes 6230020 | tf_op jit(solution)/shard_map/cond
  127.1 6.5 %collective-permute-start.8 = (bf16[2,2,2,2,16,507]{5,4,3,2,1,0:T(8,128)(2,1)S(1)}, bf16[2,2,2,2,16,507]{5,4,3,2,1,0:T(8,128)(2,1)S(1)}, u32[]{:S(2)}, u32[]{:S(2)}) collective-permute-start(bf16[2,2,2,2,16,507]{5,4,3,2,1,0:T(8,128)(2,1)S(1)} %fusion.6), channel_id=1, source_target_pairs={{0,64},{8,72},{16,80},{24,88},{32,96},{40,104},{48,112},{56,120},{... | collective-permute-start | bytes 778760 | tf_op jit(solution)/shard_map/cond/branch_1_fun/ppermute | solution.py:69
  130.1 6.5 %collective-permute-start.1 = (bf16[2,2,2,2,16,507]{5,4,3,2,1,0:T(8,128)(2,1)S(1)}, bf16[2,2,2,2,16,507]{5,4,3,2,1,0:T(8,128)(2,1)S(1)}, u32[]{:S(2)}, u32[]{:S(2)}) collective-permute-start(bf16[2,2,2,2,16,507]{5,4,3,2,1,0:T(8,128)(2,1)S(1)} %fusion.5), channel_id=1, source_target_pairs={{0,8},{8,0},{16,24},{24,16},{32,40},{40,32},{48,56},{56,48},{64,72... | collective-permute-start | bytes 778760 | tf_op jit(solution)/shard_map/cond/branch_1_fun/ppermute | solution.py:69
  133.7 6.7 %collective-permute-start.9 = (f32[2,2,2,2,8,507]{5,4,3,2,1,0:T(8,128)S(1)}, f32[2,2,2,2,8,507]{5,4,3,2,1,0:T(8,128)S(1)}, u32[]{:S(2)}, u32[]{:S(2)}) collective-permute-start(f32[2,2,2,2,8,507]{5,4,3,2,1,0:T(8,128)S(1)} %dynamic-slice_bitcast_fusion), channel_id=1, source_target_pairs={{0,1},{1,0},{2,3},{3,2},{4,5},{5,4},{6,7},{7,6},{8,9},{9,8},{10,11... | collective-permute-start | bytes 778760 | tf_op jit(solution)/shard_map/cond/branch_1_fun/ppermute | solution.py:69
  136.6 6.5 %collective-permute-start.2 = (f32[2,2,2,2,8,507]{5,4,3,2,1,0:T(8,128)S(1)}, f32[2,2,2,2,8,507]{5,4,3,2,1,0:T(8,128)S(1)}, u32[]{:S(2)}, u32[]{:S(2)}) collective-permute-start(f32[2,2,2,2,8,507]{5,4,3,2,1,0:T(8,128)S(1)} %dynamic-slice_bitcast_fusion.1), channel_id=1, source_target_pairs={{0,64},{8,72},{16,80},{24,88},{32,96},{40,104},{48,112},{56,120},{... | collective-permute-start | bytes 778760 | tf_op jit(solution)/shard_map/cond/branch_1_fun/ppermute | solution.py:69
  140.5 7.2 %collective-permute-start.10 = (f32[2,2,2,8,507]{4,3,2,1,0:T(8,128)S(1)}, f32[2,2,2,8,507]{4,3,2,1,0:T(8,128)S(1)}, u32[]{:S(2)}, u32[]{:S(2)}) collective-permute-start(f32[2,2,2,8,507]{4,3,2,1,0:T(8,128)S(1)} %dynamic-slice_bitcast_fusion.2), channel_id=1, source_target_pairs={{0,16},{8,24},{16,0},{24,8},{32,48},{40,56},{48,32},{56,40},{64,80... | collective-permute-start | bytes 389384 | tf_op jit(solution)/shard_map/cond/branch_1_fun/ppermute | solution.py:69
  143.2 7.0 %collective-permute-start.3 = (f32[2,2,2,8,507]{4,3,2,1,0:T(8,128)S(1)}, f32[2,2,2,8,507]{4,3,2,1,0:T(8,128)S(1)}, u32[]{:S(2)}, u32[]{:S(2)}) collective-permute-start(f32[2,2,2,8,507]{4,3,2,1,0:T(8,128)S(1)} %dynamic-slice_bitcast_fusion.3), channel_id=1, source_target_pairs={{0,2},{1,3},{2,0},{3,1},{4,6},{5,7},{6,4},{7,5},{8,10},{9,11},{10,... | collective-permute-start | bytes 389384 | tf_op jit(solution)/shard_map/cond/branch_1_fun/ppermute | solution.py:69
  147.8 9.6 %collective-permute-start.11 = (f32[2,2,8,507]{3,2,1,0:T(8,128)S(1)}, f32[2,2,8,507]{3,2,1,0:T(8,128)S(1)}, u32[]{:S(2)}, u32[]{:S(2)}) collective-permute-start(f32[2,2,8,507]{3,2,1,0:T(8,128)S(1)} %dynamic-slice_bitcast_fusion.4), channel_id=1, source_target_pairs={{0,32},{8,40},{16,48},{24,56},{32,0},{40,8},{48,16},{56,24},{64,96... | collective-permute-start | bytes 194696 | tf_op jit(solution)/shard_map/cond/branch_1_fun/ppermute | solution.py:69
  150.2 8.6 %collective-permute-start.4 = (f32[2,2,8,507]{3,2,1,0:T(8,128)S(1)}, f32[2,2,8,507]{3,2,1,0:T(8,128)S(1)}, u32[]{:S(2)}, u32[]{:S(2)}) collective-permute-start(f32[2,2,8,507]{3,2,1,0:T(8,128)S(1)} %dynamic-slice_bitcast_fusion.5), channel_id=1, source_target_pairs={{0,16},{8,24},{16,0},{24,8},{32,48},{40,56},{48,32},{56,40},{64,80... | collective-permute-start | bytes 194696 | tf_op jit(solution)/shard_map/cond/branch_1_fun/ppermute | solution.py:69
  157.4 5.5 %collective-permute-start.12 = (f32[2,8,507]{2,1,0:T(8,128)S(1)}, f32[2,8,507]{2,1,0:T(8,128)S(1)}, u32[]{:S(2)}, u32[]{:S(2)}) collective-permute-start(f32[2,8,507]{2,1,0:T(8,128)S(1)} %dynamic-slice_bitcast_fusion.6), channel_id=1, source_target_pairs={{0,2},{1,3},{2,0},{3,1},{4,6},{5,7},{6,4},{7,5},{8,10},{9,11},{10,... | collective-permute-start | bytes 97352 | tf_op jit(solution)/shard_map/cond/branch_1_fun/ppermute | solution.py:69
  158.8 6.1 %collective-permute-start.5 = (f32[2,8,507]{2,1,0:T(8,128)S(1)}, f32[2,8,507]{2,1,0:T(8,128)S(1)}, u32[]{:S(2)}, u32[]{:S(2)}) collective-permute-start(f32[2,8,507]{2,1,0:T(8,128)S(1)} %dynamic-slice_bitcast_fusion.7), channel_id=1, source_target_pairs={{0,128},{8,136},{16,144},{24,152},{32,160},{40,168},{48,176},{56,1... | collective-permute-start | bytes 97352 | tf_op jit(solution)/shard_map/cond/branch_1_fun/ppermute | solution.py:69
  162.9 5.3 %collective-permute-start.13 = (f32[8,507]{1,0:T(8,128)S(1)}, f32[8,507]{1,0:T(8,128)S(1)}, u32[]{:S(2)}, u32[]{:S(2)}) collective-permute-start(f32[8,507]{1,0:T(8,128)S(1)} %dynamic-slice_bitcast_fusion.8), channel_id=1, source_target_pairs={{0,128},{8,136},{16,144},{24,152},{32,160},{40,168},{48,176},{56,1... | collective-permute-start | bytes 48680 | tf_op jit(solution)/shard_map/cond/branch_1_fun/ppermute | solution.py:69
  165.0 7.7 %collective-permute-start.6 = (f32[8,507]{1,0:T(8,128)S(1)}, f32[8,507]{1,0:T(8,128)S(1)}, u32[]{:S(2)}, u32[]{:S(2)}) collective-permute-start(f32[8,507]{1,0:T(8,128)S(1)} %dynamic-slice_bitcast_fusion.9), channel_id=1, source_target_pairs={{0,32},{8,40},{16,48},{24,56},{32,0},{40,8},{48,16},{56,24},{64,96... | collective-permute-start | bytes 48680 | tf_op jit(solution)/shard_map/cond/branch_1_fun/ppermute | solution.py:69
  173.2 9.2 %copy-start.19 = (f32[8112]{0:T(1024)}, f32[8112]{0:T(1024)S(1)}, u32[]{:S(2)}) copy-start(f32[8112]{0:T(1024)S(1)} %get-tuple-element.271) | copy-start | bytes 97348
  174.5 4.0 %collective-permute-start.46 = (f32[2,2496]{1,0:T(2,128)S(1)}, f32[2,2496]{1,0:T(2,128)S(1)}, u32[]{:S(2)}, u32[]{:S(2)}) collective-permute-start(f32[2,2496]{1,0:T(2,128)S(1)} %pad_maximum_fusion.15), channel_id=1, source_target_pairs={{0,1},{1,0},{2,3},{3,2},{4,5},{5,4},{6,7},{7,6},{8,9},{9,8},{10,11... | collective-permute-start | bytes 59912 | tf_op jit(solution)/shard_map/ppermute | solution.py:83
  178.6 6.2 %collective-permute-start.47 = (f32[2,2496]{1,0:T(2,128)S(1)}, f32[2,2496]{1,0:T(2,128)S(1)}, u32[]{:S(2)}, u32[]{:S(2)}) collective-permute-start(f32[2,2496]{1,0:T(2,128)S(1)} %fusion.42), channel_id=1, source_target_pairs={{0,2},{1,3},{2,0},{3,1},{4,6},{5,7},{6,4},{7,5},{8,10},{9,11},{10,... | collective-permute-start | bytes 59912 | tf_op jit(solution)/shard_map/ppermute | solution.py:83
  184.8 6.3 %copy-start.5 = (bf16[4,32,2496]{2,1,0:T(8,128)(2,1)}, bf16[4,32,2496]{2,1,0:T(8,128)(2,1)S(1)}, u32[]{:S(2)}) copy-start(bf16[4,32,2496]{2,1,0:T(8,128)(2,1)S(1)} %get-tuple-element.273) | copy-start | bytes 1916932
  184.9 9.0 %collective-permute-start.49 = (bf16[2,32,2496]{2,1,0:T(8,128)(2,1)S(1)}, bf16[2,32,2496]{2,1,0:T(8,128)(2,1)S(1)}, u32[]{:S(2)}, u32[]{:S(2)}) collective-permute-start(bf16[2,32,2496]{2,1,0:T(8,128)(2,1)S(1)} %get-tuple-element.226), channel_id=1, source_target_pairs={{1,0},{2,1},{3,2},{5,4},{6,5},{7,6},{9,8},{10,9},{11,10},{13,12},{... | collective-permute-start | bytes 958472 | tf_op jit(solution)/shard_map/ppermute | solution.py:15
  189.2 9.0 %collective-permute-start.48 = (bf16[2,32,2496]{2,1,0:T(8,128)(2,1)S(1)}, bf16[2,32,2496]{2,1,0:T(8,128)(2,1)S(1)}, u32[]{:S(2)}, u32[]{:S(2)}) collective-permute-start(bf16[2,32,2496]{2,1,0:T(8,128)(2,1)S(1)} %get-tuple-element.225), channel_id=1, source_target_pairs={{0,1},{1,2},{2,3},{4,5},{5,6},{6,7},{8,9},{9,10},{10,11},{12,13},{... | collective-permute-start | bytes 958472 | tf_op jit(solution)/shard_map/ppermute | solution.py:12
  191.2 8.3 %copy-start.4 = (bf16[1,1,4,32,2496]{4,3,2,1,0:T(8,128)(2,1)S(1)}, bf16[1,1,4,32,2496]{4,3,2,1,0:T(8,128)(2,1)}, u32[]{:S(2)}) copy-start(bf16[1,1,4,32,2496]{4,3,2,1,0:T(8,128)(2,1)} %param.27) | copy-start | bytes 1916932
  191.2 8.3 %copy-start.13 = (f32[25,2496]{1,0:T(8,128)S(1)}, f32[25,2496]{1,0:T(8,128)}, u32[]{:S(2)}) copy-start(f32[25,2496]{1,0:T(8,128)} %copy-done.12) | copy-start | bytes 748804
  191.2 8.3 %copy-start.16 = (bf16[1,4,32,416]{3,2,1,0:T(8,128)(2,1)S(1)}, bf16[1,4,32,416]{3,2,1,0:T(8,128)(2,1)}, u32[]{:S(2)}) copy-start(bf16[1,4,32,416]{3,2,1,0:T(8,128)(2,1)} %param.26) | copy-start | bytes 319492
  (6 other events, 7.0 us)

commit v5 on v3

--- a/solution.py
+++ b/solution.py
@@ -217,7 +217,8 @@
     def spread_still(term):
         return jnp.zeros((chunk,), jnp.float32)
 
-    sent_top, sent_mid = passed_along((grad_top, grad_proj), "segment", 1)
+    sent_top = passed_along(grad_top, "segment", 1)
+    sent_mid = passed_along(grad_proj, "segment", 1)
     sent_top, sent_mid, grad_out = lax.optimization_barrier((sent_top, sent_mid, grad_out))
 
     def term_branch():

time: 201 us -> 201 us (level)
  no operation moved by 1% of the time
where the time goes in v5:
time: 201 us; the launch traced here: 200 us
  starting transfers between devices  67.4 us (34%)
  waiting for transfers between devices  55.6 us (28%)
  local copies, waits for them, and re-layouts  31.1 us (15%)
  other arithmetic  22.3 us (11%)
  loops' own time  14.3 us (7%)
  matrix products  6.54 us (3%)
  between operations  2.27 us (1%)
    ppermute x14, starting transfers between devices, scatter_chunks(): moved = lax.ppermute(other, axis, swap_pairs(axis, j))  24.1 us
    ppermute x14, starting transfers between devices, gather_chunks(): recv = lax.ppermute(buf, axis, swap_pairs(axis, j))  24 us
    ppermute x14, waiting for transfers between devices, scatter_chunks(): moved = lax.ppermute(other, axis, swap_pairs(axis, j))  23.8 us
    ppermute x14, waiting for transfers between devices, gather_chunks(): recv = lax.ppermute(buf, axis, swap_pairs(axis, j))  23.1 us
    another operation x1, loops' own time, body(): grad_out = lax.cond(segment == 0, lead_branch, lead_still)  12.9 us
    ppermute x2, starting transfers between devices, extended_2(): lax.ppermute(lax.slice_in_dim(block, 0, width, axis=dim), axis, backward)  7.74 us
    reshape x1, local copies, waits for them, and re-layouts, spread(): flat_term = (term / images).reshape(shards, 8, -1)  7.15 us
    split x2, local copies, waits for them, and re-layouts, scatter_streams(): parts = jnp.split(full, cuts, axis=-1)  6.17 us
  transfers between devices with their start and end apart: 36, of which 21 were waited for; matrix products, arithmetic and copies ran while one was open for 17% of the time, Pallas kernels for 0%

profile of v5, /device:TPU:8, one launch (start us, length us, event | category | flops | bytes accessed | tf_op | source)
XLA Modules:
  0.0 199.6 jit_solution(1536120994059738848)
XLA Ops:
  1.7 3.0 %collective-permute-start.36 = (bf16[16,253]{1,0:T(8,128)(2,1)S(1)}, bf16[16,253]{1,0:T(8,128)(2,1)S(1)}, u32[]{:S(2)}, u32[]{:S(2)}) collective-permute-start(bf16[16,253]{1,0:T(8,128)(2,1)S(1)} %split.25), channel_id=1, source_target_pairs={{0,128},{8,136},{16,144},{24,152},{32,160},{40,168},{48,176},{56,1... | collective-permute-start | bytes 24296 | tf_op jit(solution)/shard_map/ppermute | solution.py:41
  4.7 7.2 %collective-permute-start.29 = (bf16[16,254]{1,0:T(8,128)(2,1)S(1)}, bf16[16,254]{1,0:T(8,128)(2,1)S(1)}, u32[]{:S(2)}, u32[]{:S(2)}) collective-permute-start(bf16[16,254]{1,0:T(8,128)(2,1)S(1)} %split.24), channel_id=1, source_target_pairs={{0,32},{8,40},{16,48},{24,56},{32,0},{40,8},{48,16},{56,24},{64,96... | collective-permute-start | bytes 24392 | tf_op jit(solution)/shard_map/ppermute | solution.py:41
  12.1 2.4 %collective-permute-start.37 = (bf16[2,16,253]{2,1,0:T(8,128)(2,1)S(1)}, bf16[2,16,253]{2,1,0:T(8,128)(2,1)S(1)}, u32[]{:S(2)}, u32[]{:S(2)}) collective-permute-start(bf16[2,16,253]{2,1,0:T(8,128)(2,1)S(1)} %pad_maximum_fusion.17), channel_id=1, source_target_pairs={{0,2},{1,3},{2,0},{3,1},{4,6},{5,7},{6,4},{7,5},{8,10},{9,11},{10,... | collective-permute-start | bytes 48584 | tf_op jit(solution)/shard_map/ppermute | solution.py:41
  15.1 2.3 %collective-permute-done.37 = bf16[2,16,253]{2,1,0:T(8,128)(2,1)S(1)} collective-permute-done((bf16[2,16,253]{2,1,0:T(8,128)(2,1)S(1)}, bf16[2,16,253]{2,1,0:T(8,128)(2,1)S(1)}, u32[]{:S(2)}, u32[]{:S(2)}) %collective-permute-start.37) | collective-permute-done | bytes 16224 | tf_op jit(solution)/shard_map/ppermute | solution.py:41
  17.4 2.8 %collective-permute-start.38 = (bf16[2,2,16,253]{3,2,1,0:T(8,128)(2,1)S(1)}, bf16[2,2,16,253]{3,2,1,0:T(8,128)(2,1)S(1)}, u32[]{:S(2)}, u32[]{:S(2)}) collective-permute-start(bf16[2,2,16,253]{3,2,1,0:T(8,128)(2,1)S(1)} %pad_maximum_fusion.14), channel_id=1, source_target_pairs={{0,32},{8,40},{16,48},{24,56},{32,0},{40,8},{48,16},{56,24},{64,96... | collective-permute-start | bytes 97160 | tf_op jit(solution)/shard_map/ppermute | solution.py:41
  21.8 3.8 %collective-permute-done.38 = bf16[2,2,16,253]{3,2,1,0:T(8,128)(2,1)S(1)} collective-permute-done((bf16[2,2,16,253]{3,2,1,0:T(8,128)(2,1)S(1)}, bf16[2,2,16,253]{3,2,1,0:T(8,128)(2,1)S(1)}, u32[]{:S(2)}, u32[]{:S(2)}) %collective-permute-start.38) | collective-permute-done | bytes 32416 | tf_op jit(solution)/shard_map/ppermute | solution.py:41
  27.1 2.4 %collective-permute-start.32 = (bf16[2,2,2,16,254]{4,3,2,1,0:T(8,128)(2,1)S(1)}, bf16[2,2,2,16,254]{4,3,2,1,0:T(8,128)(2,1)S(1)}, u32[]{:S(2)}, u32[]{:S(2)}) collective-permute-start(bf16[2,2,2,16,254]{4,3,2,1,0:T(8,128)(2,1)S(1)} %pad_maximum_fusion.11), channel_id=1, source_target_pairs={{0,2},{1,3},{2,0},{3,1},{4,6},{5,7},{6,4},{7,5},{8,10},{9,11},{10,... | collective-permute-start | bytes 195080 | tf_op jit(solution)/shard_map/ppermute | solution.py:41
  29.5 2.1 %collective-permute-done.39 = bf16[2,2,2,16,253]{4,3,2,1,0:T(8,128)(2,1)S(1)} collective-permute-done((bf16[2,2,2,16,253]{4,3,2,1,0:T(8,128)(2,1)S(1)}, bf16[2,2,2,16,253]{4,3,2,1,0:T(8,128)(2,1)S(1)}, u32[]{:S(2)}, u32[]{:S(2)}) %collective-permute-start.39) | collective-permute-done | bytes 64800 | tf_op jit(solution)/shard_map/ppermute | solution.py:41
  34.1 2.5 %collective-permute-done.40 = bf16[2,2,2,2,16,253]{5,4,3,2,1,0:T(8,128)(2,1)S(1)} collective-permute-done((bf16[2,2,2,2,16,253]{5,4,3,2,1,0:T(8,128)(2,1)S(1)}, bf16[2,2,2,2,16,253]{5,4,3,2,1,0:T(8,128)(2,1)S(1)}, u32[]{:S(2)}, u32[]{:S(2)}) %collective-permute-start.40) | collective-permute-done | bytes 129568 | tf_op jit(solution)/shard_map/ppermute | solution.py:41
  37.4 2.5 %collective-permute-done.33 = bf16[2,2,2,2,16,254]{5,4,3,2,1,0:T(8,128)(2,1)S(1)} collective-permute-done((bf16[2,2,2,2,16,254]{5,4,3,2,1,0:T(8,128)(2,1)S(1)}, bf16[2,2,2,2,16,254]{5,4,3,2,1,0:T(8,128)(2,1)S(1)}, u32[]{:S(2)}, u32[]{:S(2)}) %collective-permute-start.33) | collective-permute-done | bytes 130080 | tf_op jit(solution)/shard_map/ppermute | solution.py:41
  40.1 3.2 %collective-permute-done.41 = bf16[2,2,2,2,2,16,253]{6,5,4,3,2,1,0:T(8,128)(2,1)S(1)} collective-permute-done((bf16[2,2,2,2,2,16,253]{6,5,4,3,2,1,0:T(8,128)(2,1)S(1)}, bf16[2,2,2,2,2,16,253]{6,5,4,3,2,1,0:T(8,128)(2,1)S(1)}, u32[]{:S(2)}, u32[]{:S(2)}) %collective-permute-start.41) | collective-permute-done | bytes 259104 | tf_op jit(solution)/shard_map/ppermute | solution.py:41
  43.8 5.5 %collective-permute-done.34 = bf16[2,2,2,2,2,16,254]{6,5,4,3,2,1,0:T(8,128)(2,1)S(1)} collective-permute-done((bf16[2,2,2,2,2,16,254]{6,5,4,3,2,1,0:T(8,128)(2,1)S(1)}, bf16[2,2,2,2,2,16,254]{6,5,4,3,2,1,0:T(8,128)(2,1)S(1)}, u32[]{:S(2)}, u32[]{:S(2)}) %collective-permute-start.34) | collective-permute-done | bytes 260128 | tf_op jit(solution)/shard_map/ppermute | solution.py:41
  51.5 3.6 %collective-permute-start.45 = (bf16[2,32,2496]{2,1,0:T(8,128)(2,1)}, bf16[2,32,2496]{2,1,0:T(8,128)(2,1)}, u32[]{:S(2)}, u32[]{:S(2)}) collective-permute-start(bf16[2,32,2496]{2,1,0:T(8,128)(2,1)} %get-tuple-element.224), channel_id=1, source_target_pairs={{1,0},{2,1},{3,2},{5,4},{6,5},{7,6},{9,8},{10,9},{11,10},{13,12},{... | collective-permute-start | bytes 958472 | tf_op jit(solution)/shard_map/ppermute | solution.py:15
  55.1 2.4 %collective-permute-start.44 = (bf16[2,32,2496]{2,1,0:T(8,128)(2,1)}, bf16[2,32,2496]{2,1,0:T(8,128)(2,1)}, u32[]{:S(2)}, u32[]{:S(2)}) collective-permute-start(bf16[2,32,2496]{2,1,0:T(8,128)(2,1)} %get-tuple-element.223), channel_id=1, source_target_pairs={{0,1},{1,2},{2,3},{4,5},{5,6},{6,7},{8,9},{9,10},{10,11},{12,13},{... | collective-permute-start | bytes 958472 | tf_op jit(solution)/shard_map/ppermute | solution.py:12
  57.6 15.1 %conditional.8 = (bf16[128,416]{0,1:T(8,128)(2,1)}, bf16[4,32,416]{2,1,0:T(8,128)(2,1)S(1)}) conditional(s32[]{:T(128)} %convert_element_type.291, () %tuple.71, (bf16[1,4,32,384]{3,2,1,0:T(8,128)(2,1)S(1)}, bf16[1,2,16,384]{3,2,1,0:T(8,128)(2,1)S(1)}, bf16[1,1,8,384]{3,2,1,0:T(8,128)(2,1)S(1)}, bf16[416,384]{1,0:T(8,128)(2,1)S(1)}) %tuple.193), branch_computations={%region_0.1_spmd, %region_1.2_spmd} | conditional | flops 41138176 | bytes 1972240 | solution.py:200
  75.8 2.2 %pad_maximum_fusion.2 = bf16[128,16,507]{2,1,0:T(8,128)(2,1)} fusion(bf16[128,16,253]{2,1,0:T(8,128)(2,1)S(1)} %bitcast.278, bf16[128,16,254]{2,1,0:T(8,128)(2,1)S(1)} %bitcast.279), kind=kLoop, calls=%fused_computation.207 | loop fusion | flops 4153344 | bytes 4153344 | tf_op jit(solution)/shard_map/concatenate | solution.py:53
  78.0 5.2 %reshape_reshape.3 = bf16[416,2496]{1,0:T(8,128)(2,1)S(1)} reshape(bf16[128,16,507]{2,1,0:T(8,128)(2,1)} %pad_maximum_fusion.2) | data formatting | bytes 4153344 | tf_op jit(solution)/shard_map/reshape;reshape | solution.py:159
  83.3 2.0 %conditional.9 = (bf16[128,2496]{0,1:T(8,128)(2,1)S(1)}) conditional(s32[]{:T(128)} %convert_element_type.291, () %tuple.75, (bf16[128,416]{0,1:T(8,128)(2,1)}, bf16[416,2496]{1,0:T(8,128)(2,1)S(1)}) %tuple.76), branch_computations={%region_2.3_spmd, %region_3.4_spmd} | conditional | flops 266133504 | bytes 2822152 | solution.py:208
  83.3 2.0 %convolution_convert_fusion.1 = bf16[128,2496]{0,1:T(8,128)(2,1)S(1)} fusion(bf16[128,416]{0,1:T(8,128)(2,1)} %get-tuple-element.158, bf16[416,2496]{1,0:T(8,128)(2,1)S(1)} %get-tuple-element.87), kind=kOutput, calls=%fused_computation.6 | convolution fusion | flops 266133504 | bytes 2822144 | tf_op jit(solution)/shard_map/cond/branch_1_fun/dot_general | solution.py:203
  87.7 1.9 collective-permute-start.28
  94.0 3.6 %conditional.10 = (f32[416,2496]{1,0:T(8,128)}) conditional(s32[]{:T(128)} %convert_element_type.291, () %tuple.74, (bf16[1,1,4,32,2496]{4,3,2,1,0:T(8,128)(2,1)S(1)}, bf16[128,416]{0,1:T(8,128)(2,1)}) %tuple.182), branch_computations={%region_4.5_spmd, %region_5.6_spmd} | conditional | flops 265814016 | bytes 4898824 | solution.py:232
  94.0 3.6 %fusion.42 = f32[416,2496]{1,0:T(8,128)} fusion(bf16[128,416]{0,1:T(8,128)(2,1)} %get-tuple-element.161, bf16[128,2496]{1,0:T(8,128)(2,1)S(1)} %bitcast.275), kind=kOutput, calls=%fused_computation.258 | convolution fusion | flops 265814016 | bytes 4898816 | tf_op jit(solution)/shard_map/cond/branch_1_fun/dot_general | solution.py:225
  97.6 74.0 %conditional.11 = (f32[8112]{0:T(1024)S(1)}) conditional(s32[]{:T(128)} %convert_element_type.291, () %tuple.73, f32[416,2496]{1,0:T(8,128)} %get-tuple-element.266), branch_computations={%region_6.7_spmd, %region_7.8_spmd} | conditional | flops 2855492 | bytes 59625460 | solution.py:233
  97.6 4.6 %broadcast_multiply_fusion = f32[416,2496]{1,0:T(8,128)} fusion(f32[416,2496]{1,0:T(8,128)} %param.7), kind=kLoop, calls=%fused_computation.7 | loop fusion | flops 1038336 | bytes 8306688 | tf_op jit(solution)/shard_map/cond/branch_1_fun/div | solution.py:214
  102.1 7.2 %reshape.176 = f32[128,8,1014]{2,1,0:T(8,128)} reshape(f32[416,2496]{1,0:T(8,128)} %broadcast_multiply_fusion) | data formatting | bytes 8306688 | tf_op jit(solution)/shard_map/cond/branch_1_fun/reshape | solution.py:214
  109.3 3.1 %split.21 = f32[128,8,502]{2,1,0:T(8,128)} slice(f32[128,8,1014]{2,1,0:T(8,128)} %reshape.176), slice={[0:128], [0:8], [512:1014]} | slice | bytes 4112384 | tf_op jit(solution)/shard_map/cond/branch_1_fun/split | solution.py:76
  112.4 2.1 %fusion.4 = bf16[2,2,2,2,2,16,502]{6,5,4,3,2,1,0:T(8,128)(2,1)} fusion(f32[2,2,2,2,2,2,2,8,502]{8,7,6,5,4,3,2,1,0:T(8,128)} %bitcast.267, s32[]{:T(128)S(6)} %select_n.227), kind=kLoop, calls=%fused_computation.13 | loop fusion | bytes 1028100 | tf_op jit(solution)/shard_map/cond/branch_1_fun/convert_element_type | solution.py:68
  115.2 3.1 %split.20 = f32[128,8,512]{2,1,0:T(8,128)} slice(f32[128,8,1014]{2,1,0:T(8,128)} %reshape.176), slice={[0:128], [0:8], [0:512]} | slice | bytes 4194304 | tf_op jit(solution)/shard_map/cond/branch_1_fun/split | solution.py:76
  118.3 2.1 %fusion.3 = bf16[2,2,2,2,2,16,512]{6,5,4,3,2,1,0:T(8,128)(2,1)} fusion(f32[2,2,2,2,2,2,2,8,512]{8,7,6,5,4,3,2,1,0:T(8,128)} %bitcast.271, s32[]{:T(128)S(6)} %select_n.225), kind=kLoop, calls=%fused_computation.12 | loop fusion | bytes 1048580 | tf_op jit(solution)/shard_map/cond/branch_1_fun/convert_element_type | solution.py:68
  122.0 2.0 %collective-permute-done.7 = bf16[2,2,2,2,2,16,502]{6,5,4,3,2,1,0:T(8,128)(2,1)} collective-permute-done((bf16[2,2,2,2,2,16,502]{6,5,4,3,2,1,0:T(8,128)(2,1)}, bf16[2,2,2,2,2,16,502]{6,5,4,3,2,1,0:T(8,128)(2,1)}, u32[]{:S(2)}, u32[]{:S(2)}) %collective-permute-start.7) | collective-permute-done | bytes 514080 | tf_op jit(solution)/shard_map/cond/branch_1_fun/ppermute | solution.py:69
  126.4 3.5 %collective-permute-done = bf16[2,2,2,2,2,16,512]{6,5,4,3,2,1,0:T(8,128)(2,1)} collective-permute-done((bf16[2,2,2,2,2,16,512]{6,5,4,3,2,1,0:T(8,128)(2,1)}, bf16[2,2,2,2,2,16,512]{6,5,4,3,2,1,0:T(8,128)(2,1)}, u32[]{:S(2)}, u32[]{:S(2)}) %collective-permute-start) | collective-permute-done | bytes 524320 | tf_op jit(solution)/shard_map/cond/branch_1_fun/ppermute | solution.py:69
  133.0 2.1 %collective-permute-start.9 = (f32[2,2,2,2,8,502]{5,4,3,2,1,0:T(8,128)S(1)}, f32[2,2,2,2,8,502]{5,4,3,2,1,0:T(8,128)S(1)}, u32[]{:S(2)}, u32[]{:S(2)}) collective-permute-start(f32[2,2,2,2,8,502]{5,4,3,2,1,0:T(8,128)S(1)} %dynamic-slice_bitcast_fusion), channel_id=1, source_target_pairs={{0,1},{1,0},{2,3},{3,2},{4,5},{5,4},{6,7},{7,6},{8,9},{9,8},{10,11... | collective-permute-start | bytes 771080 | tf_op jit(solution)/shard_map/cond/branch_1_fun/ppermute | solution.py:69
  135.1 2.5 %collective-permute-done.1 = bf16[2,2,2,2,16,512]{5,4,3,2,1,0:T(8,128)(2,1)S(1)} collective-permute-done((bf16[2,2,2,2,16,512]{5,4,3,2,1,0:T(8,128)(2,1)S(1)}, bf16[2,2,2,2,16,512]{5,4,3,2,1,0:T(8,128)(2,1)S(1)}, u32[]{:S(2)}, u32[]{:S(2)}) %collective-permute-start.1) | collective-permute-done | bytes 262176 | tf_op jit(solution)/shard_map/cond/branch_1_fun/ppermute | solution.py:69
  140.6 3.7 %collective-permute-done.2 = f32[2,2,2,2,8,512]{5,4,3,2,1,0:T(8,128)S(1)} collective-permute-done((f32[2,2,2,2,8,512]{5,4,3,2,1,0:T(8,128)S(1)}, f32[2,2,2,2,8,512]{5,4,3,2,1,0:T(8,128)S(1)}, u32[]{:S(2)}, u32[]{:S(2)}) %collective-permute-start.2) | collective-permute-done | bytes 262176 | tf_op jit(solution)/shard_map/cond/branch_1_fun/ppermute | solution.py:69
  144.3 2.3 %collective-permute-start.3 = (f32[2,2,2,8,512]{4,3,2,1,0:T(8,128)S(1)}, f32[2,2,2,8,512]{4,3,2,1,0:T(8,128)S(1)}, u32[]{:S(2)}, u32[]{:S(2)}) collective-permute-start(f32[2,2,2,8,512]{4,3,2,1,0:T(8,128)S(1)} %dynamic-slice_bitcast_fusion.3), channel_id=1, source_target_pairs={{0,2},{1,3},{2,0},{3,1},{4,6},{5,7},{6,4},{7,5},{8,10},{9,11},{10,... | collective-permute-start | bytes 393224 | tf_op jit(solution)/shard_map/cond/branch_1_fun/ppermute | solution.py:69
  146.9 2.7 %collective-permute-start.11 = (f32[2,2,8,502]{3,2,1,0:T(8,128)S(1)}, f32[2,2,8,502]{3,2,1,0:T(8,128)S(1)}, u32[]{:S(2)}, u32[]{:S(2)}) collective-permute-start(f32[2,2,8,502]{3,2,1,0:T(8,128)S(1)} %dynamic-slice_bitcast_fusion.4), channel_id=1, source_target_pairs={{0,32},{8,40},{16,48},{24,56},{32,0},{40,8},{48,16},{56,24},{64,96... | collective-permute-start | bytes 192776 | tf_op jit(solution)/shard_map/cond/branch_1_fun/ppermute | solution.py:69
  150.9 2.1 %collective-permute-start.4 = (f32[2,2,8,512]{3,2,1,0:T(8,128)S(1)}, f32[2,2,8,512]{3,2,1,0:T(8,128)S(1)}, u32[]{:S(2)}, u32[]{:S(2)}) collective-permute-start(f32[2,2,8,512]{3,2,1,0:T(8,128)S(1)} %dynamic-slice_bitcast_fusion.5), channel_id=1, source_target_pairs={{0,16},{8,24},{16,0},{24,8},{32,48},{40,56},{48,32},{56,40},{64,80... | collective-permute-start | bytes 196616 | tf_op jit(solution)/shard_map/cond/branch_1_fun/ppermute | solution.py:69
  153.0 3.0 %collective-permute-done.11 = f32[2,2,8,502]{3,2,1,0:T(8,128)S(1)} collective-permute-done((f32[2,2,8,502]{3,2,1,0:T(8,128)S(1)}, f32[2,2,8,502]{3,2,1,0:T(8,128)S(1)}, u32[]{:S(2)}, u32[]{:S(2)}) %collective-permute-start.11) | collective-permute-done | bytes 64288 | tf_op jit(solution)/shard_map/cond/branch_1_fun/ppermute | solution.py:69
  159.1 2.4 %collective-permute-done.12 = f32[2,8,502]{2,1,0:T(8,128)S(1)} collective-permute-done((f32[2,8,502]{2,1,0:T(8,128)S(1)}, f32[2,8,502]{2,1,0:T(8,128)S(1)}, u32[]{:S(2)}, u32[]{:S(2)}) %collective-permute-start.12) | collective-permute-done | bytes 32160 | tf_op jit(solution)/shard_map/cond/branch_1_fun/ppermute | solution.py:69
  161.5 1.8 collective-permute-start.13
  163.3 3.6 %collective-permute-start.6 = (f32[8,512]{1,0:T(8,128)S(1)}, f32[8,512]{1,0:T(8,128)S(1)}, u32[]{:S(2)}, u32[]{:S(2)}) collective-permute-start(f32[8,512]{1,0:T(8,128)S(1)} %dynamic-slice_bitcast_fusion.9), channel_id=1, source_target_pairs={{0,32},{8,40},{16,48},{24,56},{32,0},{40,8},{48,16},{56,24},{64,96... | collective-permute-start | bytes 49160 | tf_op jit(solution)/shard_map/cond/branch_1_fun/ppermute | solution.py:69
  167.0 4.1 %collective-permute-done.6 = f32[8,512]{1,0:T(8,128)S(1)} collective-permute-done((f32[8,512]{1,0:T(8,128)S(1)}, f32[8,512]{1,0:T(8,128)S(1)}, u32[]{:S(2)}, u32[]{:S(2)}) %collective-permute-start.6) | collective-permute-done | bytes 16416 | tf_op jit(solution)/shard_map/cond/branch_1_fun/ppermute | solution.py:69
  172.9 2.7 %collective-permute-start.46 = (f32[2,2496]{1,0:T(2,128)S(1)}, f32[2,2496]{1,0:T(2,128)S(1)}, u32[]{:S(2)}, u32[]{:S(2)}) collective-permute-start(f32[2,2496]{1,0:T(2,128)S(1)} %pad_maximum_fusion.15), channel_id=1, source_target_pairs={{0,1},{1,0},{2,3},{3,2},{4,5},{5,4},{6,7},{7,6},{8,9},{9,8},{10,11... | collective-permute-start | bytes 59912 | tf_op jit(solution)/shard_map/ppermute | solution.py:84
  178.7 2.1 %copy.60 = bf16[2496,104]{1,0:T(8,128)(2,1)} copy(bf16[2496,104]{0,1:T(8,128)(2,1)} %param.34) | data formatting | bytes 1038336 | tf_op args[8]
  183.3 4.1 %collective-permute-start.49 = (bf16[2,32,2496]{2,1,0:T(8,128)(2,1)S(1)}, bf16[2,32,2496]{2,1,0:T(8,128)(2,1)S(1)}, u32[]{:S(2)}, u32[]{:S(2)}) collective-permute-start(bf16[2,32,2496]{2,1,0:T(8,128)(2,1)S(1)} %get-tuple-element.222), channel_id=1, source_target_pairs={{1,0},{2,1},{3,2},{5,4},{6,5},{7,6},{9,8},{10,9},{11,10},{13,12},{... | collective-permute-start | bytes 958472 | tf_op jit(solution)/shard_map/ppermute | solution.py:15
  187.4 2.0 collective-permute-start.48
  189.5 3.1 %collective-permute-done.49 = bf16[2,32,2496]{2,1,0:T(8,128)(2,1)S(1)} collective-permute-done((bf16[2,32,2496]{2,1,0:T(8,128)(2,1)S(1)}, bf16[2,32,2496]{2,1,0:T(8,128)(2,1)S(1)}, u32[]{:S(2)}, u32[]{:S(2)}) %collective-permute-start.49) | collective-permute-done | bytes 319520 | tf_op jit(solution)/shard_map/ppermute | solution.py:15
  192.5 3.9 %collective-permute-done.48 = bf16[2,32,2496]{2,1,0:T(8,128)(2,1)S(1)} collective-permute-done((bf16[2,32,2496]{2,1,0:T(8,128)(2,1)S(1)}, bf16[2,32,2496]{2,1,0:T(8,128)(2,1)S(1)}, u32[]{:S(2)}, u32[]{:S(2)}) %collective-permute-start.48) | collective-permute-done | bytes 319520 | tf_op jit(solution)/shard_map/ppermute | solution.py:12
  (167 shorter events, 47.8 us)
Async XLA Ops:
  1.7 10.3 %collective-permute-start.36 = (bf16[16,253]{1,0:T(8,128)(2,1)S(1)}, bf16[16,253]{1,0:T(8,128)(2,1)S(1)}, u32[]{:S(2)}, u32[]{:S(2)}) collective-permute-start(bf16[16,253]{1,0:T(8,128)(2,1)S(1)} %split.25), channel_id=1, source_target_pairs={{0,128},{8,136},{16,144},{24,152},{32,160},{40,168},{48,176},{56,1... | collective-permute-start | bytes 24296 | tf_op jit(solution)/shard_map/ppermute | solution.py:41
  4.7 9.7 %collective-permute-start.29 = (bf16[16,254]{1,0:T(8,128)(2,1)S(1)}, bf16[16,254]{1,0:T(8,128)(2,1)S(1)}, u32[]{:S(2)}, u32[]{:S(2)}) collective-permute-start(bf16[16,254]{1,0:T(8,128)(2,1)S(1)} %split.24), channel_id=1, source_target_pairs={{0,32},{8,40},{16,48},{24,56},{32,0},{40,8},{48,16},{56,24},{64,96... | collective-permute-start | bytes 24392 | tf_op jit(solution)/shard_map/ppermute | solution.py:41
  12.1 5.3 %collective-permute-start.37 = (bf16[2,16,253]{2,1,0:T(8,128)(2,1)S(1)}, bf16[2,16,253]{2,1,0:T(8,128)(2,1)S(1)}, u32[]{:S(2)}, u32[]{:S(2)}) collective-permute-start(bf16[2,16,253]{2,1,0:T(8,128)(2,1)S(1)} %pad_maximum_fusion.17), channel_id=1, source_target_pairs={{0,2},{1,3},{2,0},{3,1},{4,6},{5,7},{6,4},{7,5},{8,10},{9,11},{10,... | collective-permute-start | bytes 48584 | tf_op jit(solution)/shard_map/ppermute | solution.py:41
  14.5 5.7 %collective-permute-start.30 = (bf16[2,16,254]{2,1,0:T(8,128)(2,1)S(1)}, bf16[2,16,254]{2,1,0:T(8,128)(2,1)S(1)}, u32[]{:S(2)}, u32[]{:S(2)}) collective-permute-start(bf16[2,16,254]{2,1,0:T(8,128)(2,1)S(1)} %pad_maximum_fusion.16), channel_id=1, source_target_pairs={{0,128},{8,136},{16,144},{24,152},{32,160},{40,168},{48,176},{56,1... | collective-permute-start | bytes 48776 | tf_op jit(solution)/shard_map/ppermute | solution.py:41
  17.4 8.1 %collective-permute-start.38 = (bf16[2,2,16,253]{3,2,1,0:T(8,128)(2,1)S(1)}, bf16[2,2,16,253]{3,2,1,0:T(8,128)(2,1)S(1)}, u32[]{:S(2)}, u32[]{:S(2)}) collective-permute-start(bf16[2,2,16,253]{3,2,1,0:T(8,128)(2,1)S(1)} %pad_maximum_fusion.14), channel_id=1, source_target_pairs={{0,32},{8,40},{16,48},{24,56},{32,0},{40,8},{48,16},{56,24},{64,96... | collective-permute-start | bytes 97160 | tf_op jit(solution)/shard_map/ppermute | solution.py:41
  20.2 6.8 %collective-permute-start.31 = (bf16[2,2,16,254]{3,2,1,0:T(8,128)(2,1)S(1)}, bf16[2,2,16,254]{3,2,1,0:T(8,128)(2,1)S(1)}, u32[]{:S(2)}, u32[]{:S(2)}) collective-permute-start(bf16[2,2,16,254]{3,2,1,0:T(8,128)(2,1)S(1)} %pad_maximum_fusion.13), channel_id=1, source_target_pairs={{0,16},{8,24},{16,0},{24,8},{32,48},{40,56},{48,32},{56,40},{64,80... | collective-permute-start | bytes 97544 | tf_op jit(solution)/shard_map/ppermute | solution.py:41
  25.6 6.0 %collective-permute-start.39 = (bf16[2,2,2,16,253]{4,3,2,1,0:T(8,128)(2,1)S(1)}, bf16[2,2,2,16,253]{4,3,2,1,0:T(8,128)(2,1)S(1)}, u32[]{:S(2)}, u32[]{:S(2)}) collective-permute-start(bf16[2,2,2,16,253]{4,3,2,1,0:T(8,128)(2,1)S(1)} %pad_maximum_fusion.12), channel_id=1, source_target_pairs={{0,16},{8,24},{16,0},{24,8},{32,48},{40,56},{48,32},{56,40},{64,80... | collective-permute-start | bytes 194312 | tf_op jit(solution)/shard_map/ppermute | solution.py:41
  27.1 6.3 %collective-permute-start.32 = (bf16[2,2,2,16,254]{4,3,2,1,0:T(8,128)(2,1)S(1)}, bf16[2,2,2,16,254]{4,3,2,1,0:T(8,128)(2,1)S(1)}, u32[]{:S(2)}, u32[]{:S(2)}) collective-permute-start(bf16[2,2,2,16,254]{4,3,2,1,0:T(8,128)(2,1)S(1)} %pad_maximum_fusion.11), channel_id=1, source_target_pairs={{0,2},{1,3},{2,0},{3,1},{4,6},{5,7},{6,4},{7,5},{8,10},{9,11},{10,... | collective-permute-start | bytes 195080 | tf_op jit(solution)/shard_map/ppermute | solution.py:41
  31.6 5.1 %collective-permute-start.40 = (bf16[2,2,2,2,16,253]{5,4,3,2,1,0:T(8,128)(2,1)S(1)}, bf16[2,2,2,2,16,253]{5,4,3,2,1,0:T(8,128)(2,1)S(1)}, u32[]{:S(2)}, u32[]{:S(2)}) collective-permute-start(bf16[2,2,2,2,16,253]{5,4,3,2,1,0:T(8,128)(2,1)S(1)} %pad_maximum_fusion.10), channel_id=1, source_target_pairs={{0,1},{1,0},{2,3},{3,2},{4,5},{5,4},{6,7},{7,6},{8,9},{9,8},{10,11... | collective-permute-start | bytes 388616 | tf_op jit(solution)/shard_map/ppermute | solution.py:41
  33.5 6.4 %collective-permute-start.33 = (bf16[2,2,2,2,16,254]{5,4,3,2,1,0:T(8,128)(2,1)S(1)}, bf16[2,2,2,2,16,254]{5,4,3,2,1,0:T(8,128)(2,1)S(1)}, u32[]{:S(2)}, u32[]{:S(2)}) collective-permute-start(bf16[2,2,2,2,16,254]{5,4,3,2,1,0:T(8,128)(2,1)S(1)} %pad_maximum_fusion.9), channel_id=1, source_target_pairs={{0,64},{8,72},{16,80},{24,88},{32,96},{40,104},{48,112},{56,120},{... | collective-permute-start | bytes 390152 | tf_op jit(solution)/shard_map/ppermute | solution.py:41
  36.8 6.6 %collective-permute-start.41 = (bf16[2,2,2,2,2,16,253]{6,5,4,3,2,1,0:T(8,128)(2,1)S(1)}, bf16[2,2,2,2,2,16,253]{6,5,4,3,2,1,0:T(8,128)(2,1)S(1)}, u32[]{:S(2)}, u32[]{:S(2)}) collective-permute-start(bf16[2,2,2,2,2,16,253]{6,5,4,3,2,1,0:T(8,128)(2,1)S(1)} %pad_maximum_fusion.8), channel_id=1, source_target_pairs={{0,64},{8,72},{16,80},{24,88},{32,96},{40,104},{48,112},{56,120},{... | collective-permute-start | bytes 777224 | tf_op jit(solution)/shard_map/ppermute | solution.py:41
  40.0 9.3 %collective-permute-start.34 = (bf16[2,2,2,2,2,16,254]{6,5,4,3,2,1,0:T(8,128)(2,1)S(1)}, bf16[2,2,2,2,2,16,254]{6,5,4,3,2,1,0:T(8,128)(2,1)S(1)}, u32[]{:S(2)}, u32[]{:S(2)}) collective-permute-start(bf16[2,2,2,2,2,16,254]{6,5,4,3,2,1,0:T(8,128)(2,1)S(1)} %pad_maximum_fusion.7), channel_id=1, source_target_pairs={{0,8},{8,0},{16,24},{24,16},{32,40},{40,32},{48,56},{56,48},{64,72... | collective-permute-start | bytes 780296 | tf_op jit(solution)/shard_map/ppermute | solution.py:41
  43.5 29.1 %collective-permute-start.42 = (bf16[2,2,2,2,2,2,16,253]{7,6,5,4,3,2,1,0:T(8,128)(2,1)S(1)}, bf16[2,2,2,2,2,2,16,253]{7,6,5,4,3,2,1,0:T(8,128)(2,1)}, u32[]{:S(2)}, u32[]{:S(2)}) collective-permute-start(bf16[2,2,2,2,2,2,16,253]{7,6,5,4,3,2,1,0:T(8,128)(2,1)S(1)} %pad_maximum_fusion.6), channel_id=1, source_target_pairs={{0,8},{8,0},{16,24},{24,16},{32,40},{40,32},{48,56},{56,48},{64,72... | collective-permute-start | bytes 1554440 | tf_op jit(solution)/shard_map/ppermute | solution.py:41
  49.3 8.2 %copy-start.15 = (bf16[416,384]{1,0:T(8,128)(2,1)S(1)}, bf16[416,384]{1,0:T(8,128)(2,1)}, u32[]{:S(2)}) copy-start(bf16[416,384]{1,0:T(8,128)(2,1)} %param.31) | copy-start | bytes 958468
  49.4 8.2 %copy-start.18 = (bf16[1,4,32,384]{3,2,1,0:T(8,128)(2,1)S(1)}, bf16[1,4,32,384]{3,2,1,0:T(8,128)(2,1)}, u32[]{:S(2)}) copy-start(bf16[1,4,32,384]{3,2,1,0:T(8,128)(2,1)} %param.28) | copy-start | bytes 294916
  49.4 8.2 %copy-start.20 = (bf16[1,2,16,384]{3,2,1,0:T(8,128)(2,1)S(1)}, bf16[1,2,16,384]{3,2,1,0:T(8,128)(2,1)}, u32[]{:S(2)}) copy-start(bf16[1,2,16,384]{3,2,1,0:T(8,128)(2,1)} %param.29) | copy-start | bytes 73732
  49.4 8.2 %copy-start.21 = (bf16[1,1,8,384]{3,2,1,0:T(8,128)(2,1)S(1)}, bf16[1,1,8,384]{3,2,1,0:T(8,128)(2,1)}, u32[]{:S(2)}) copy-start(bf16[1,1,8,384]{3,2,1,0:T(8,128)(2,1)} %param.30) | copy-start | bytes 18436
  50.3 24.0 %collective-permute-start.35 = (bf16[2,2,2,2,2,2,16,254]{7,6,5,4,3,2,1,0:T(8,128)(2,1)}, bf16[2,2,2,2,2,2,16,254]{7,6,5,4,3,2,1,0:T(8,128)(2,1)}, u32[]{:S(2)}, u32[]{:S(2)}) collective-permute-start(bf16[2,2,2,2,2,2,16,254]{7,6,5,4,3,2,1,0:T(8,128)(2,1)} %pad_maximum_fusion.5), channel_id=1, source_target_pairs={{0,1},{1,0},{2,3},{3,2},{4,5},{5,4},{6,7},{7,6},{8,9},{9,8},{10,11... | collective-permute-start | bytes 1560584 | tf_op jit(solution)/shard_map/ppermute | solution.py:41
  51.5 39.1 %collective-permute-start.45 = (bf16[2,32,2496]{2,1,0:T(8,128)(2,1)}, bf16[2,32,2496]{2,1,0:T(8,128)(2,1)}, u32[]{:S(2)}, u32[]{:S(2)}) collective-permute-start(bf16[2,32,2496]{2,1,0:T(8,128)(2,1)} %get-tuple-element.224), channel_id=1, source_target_pairs={{1,0},{2,1},{3,2},{5,4},{6,5},{7,6},{9,8},{10,9},{11,10},{13,12},{... | collective-permute-start | bytes 958472 | tf_op jit(solution)/shard_map/ppermute | solution.py:15
  55.1 35.5 %collective-permute-start.44 = (bf16[2,32,2496]{2,1,0:T(8,128)(2,1)}, bf16[2,32,2496]{2,1,0:T(8,128)(2,1)}, u32[]{:S(2)}, u32[]{:S(2)}) collective-permute-start(bf16[2,32,2496]{2,1,0:T(8,128)(2,1)} %get-tuple-element.223), channel_id=1, source_target_pairs={{0,1},{1,2},{2,3},{4,5},{5,6},{6,7},{8,9},{9,10},{10,11},{12,13},{... | collective-permute-start | bytes 958472 | tf_op jit(solution)/shard_map/ppermute | solution.py:12
  86.4 5.9 %collective-permute-start.43 = (bf16[4,32,2496]{2,1,0:T(8,128)(2,1)}, bf16[4,32,2496]{2,1,0:T(8,128)(2,1)S(1)}, u32[]{:S(2)}, u32[]{:S(2)}) collective-permute-start(bf16[4,32,2496]{2,1,0:T(8,128)(2,1)} %bitcast.280), channel_id=1, source_target_pairs={{0,4},{1,5},{2,6},{3,7},{8,12},{9,13},{10,14},{11,15},{16,20},{17,... | collective-permute-start | bytes 1916936 | tf_op jit(solution)/shard_map/ppermute | solution.py:23
  87.7 4.6 %collective-permute-start.28 = (bf16[4,32,416]{2,1,0:T(8,128)(2,1)}, bf16[4,32,416]{2,1,0:T(8,128)(2,1)}, u32[]{:S(2)}, u32[]{:S(2)}) collective-permute-start(bf16[4,32,416]{2,1,0:T(8,128)(2,1)} %copy-done.17), channel_id=1, source_target_pairs={{0,4},{1,5},{2,6},{3,7},{8,12},{9,13},{10,14},{11,15},{16,20},{17,... | collective-permute-start | bytes 319496 | tf_op jit(solution)/shard_map/ppermute | solution.py:23
  92.3 1.5 copy-start.8
  97.6 74.0 %copy-start.9 = (f32[4,32,2496]{2,1,0:T(8,128)S(1)}, f32[4,32,2496]{2,1,0:T(8,128)}, u32[]{:S(2)}) copy-start(f32[4,32,2496]{2,1,0:T(8,128)} %copy-done.8) | copy-start | bytes 3833860
  114.5 9.5 %collective-permute-start.7 = (bf16[2,2,2,2,2,16,502]{6,5,4,3,2,1,0:T(8,128)(2,1)}, bf16[2,2,2,2,2,16,502]{6,5,4,3,2,1,0:T(8,128)(2,1)}, u32[]{:S(2)}, u32[]{:S(2)}) collective-permute-start(bf16[2,2,2,2,2,16,502]{6,5,4,3,2,1,0:T(8,128)(2,1)} %fusion.4), channel_id=1, source_target_pairs={{0,8},{8,0},{16,24},{24,16},{32,40},{40,32},{48,56},{56,48},{64,72... | collective-permute-start | bytes 1542152 | tf_op jit(solution)/shard_map/cond/branch_1_fun/ppermute | solution.py:69
  120.4 9.5 %collective-permute-start = (bf16[2,2,2,2,2,16,512]{6,5,4,3,2,1,0:T(8,128)(2,1)}, bf16[2,2,2,2,2,16,512]{6,5,4,3,2,1,0:T(8,128)(2,1)}, u32[]{:S(2)}, u32[]{:S(2)}) collective-permute-start(bf16[2,2,2,2,2,16,512]{6,5,4,3,2,1,0:T(8,128)(2,1)} %fusion.3), channel_id=1, source_target_pairs={{0,1},{1,0},{2,3},{3,2},{4,5},{5,4},{6,7},{7,6},{8,9},{9,8},{10,11... | collective-permute-start | bytes 1572872 | tf_op jit(solution)/shard_map/cond/branch_1_fun/ppermute | solution.py:69
  122.0 7.9 %copy-start.2 = (f32[128,8,512]{2,1,0:T(8,128)S(1)}, f32[128,8,512]{2,1,0:T(8,128)}, u32[]{:S(2)}) copy-start(f32[128,8,512]{2,1,0:T(8,128)} %split.20) | copy-start | bytes 6291460 | tf_op jit(solution)/shard_map/cond
  125.6 7.3 %collective-permute-start.8 = (bf16[2,2,2,2,16,502]{5,4,3,2,1,0:T(8,128)(2,1)S(1)}, bf16[2,2,2,2,16,502]{5,4,3,2,1,0:T(8,128)(2,1)S(1)}, u32[]{:S(2)}, u32[]{:S(2)}) collective-permute-start(bf16[2,2,2,2,16,502]{5,4,3,2,1,0:T(8,128)(2,1)S(1)} %fusion.6), channel_id=1, source_target_pairs={{0,64},{8,72},{16,80},{24,88},{32,96},{40,104},{48,112},{56,120},{... | collective-permute-start | bytes 771080 | tf_op jit(solution)/shard_map/cond/branch_1_fun/ppermute | solution.py:69
  131.2 6.5 %collective-permute-start.1 = (bf16[2,2,2,2,16,512]{5,4,3,2,1,0:T(8,128)(2,1)S(1)}, bf16[2,2,2,2,16,512]{5,4,3,2,1,0:T(8,128)(2,1)S(1)}, u32[]{:S(2)}, u32[]{:S(2)}) collective-permute-start(bf16[2,2,2,2,16,512]{5,4,3,2,1,0:T(8,128)(2,1)S(1)} %fusion.5), channel_id=1, source_target_pairs={{0,8},{8,0},{16,24},{24,16},{32,40},{40,32},{48,56},{56,48},{64,72... | collective-permute-start | bytes 786440 | tf_op jit(solution)/shard_map/cond/branch_1_fun/ppermute | solution.py:69
  133.0 6.5 %collective-permute-start.9 = (f32[2,2,2,2,8,502]{5,4,3,2,1,0:T(8,128)S(1)}, f32[2,2,2,2,8,502]{5,4,3,2,1,0:T(8,128)S(1)}, u32[]{:S(2)}, u32[]{:S(2)}) collective-permute-start(f32[2,2,2,2,8,502]{5,4,3,2,1,0:T(8,128)S(1)} %dynamic-slice_bitcast_fusion), channel_id=1, source_target_pairs={{0,1},{1,0},{2,3},{3,2},{4,5},{5,4},{6,7},{7,6},{8,9},{9,8},{10,11... | collective-permute-start | bytes 771080 | tf_op jit(solution)/shard_map/cond/branch_1_fun/ppermute | solution.py:69
  137.8 6.5 %collective-permute-start.2 = (f32[2,2,2,2,8,512]{5,4,3,2,1,0:T(8,128)S(1)}, f32[2,2,2,2,8,512]{5,4,3,2,1,0:T(8,128)S(1)}, u32[]{:S(2)}, u32[]{:S(2)}) collective-permute-start(f32[2,2,2,2,8,512]{5,4,3,2,1,0:T(8,128)S(1)} %dynamic-slice_bitcast_fusion.1), channel_id=1, source_target_pairs={{0,64},{8,72},{16,80},{24,88},{32,96},{40,104},{48,112},{56,120},{... | collective-permute-start | bytes 786440 | tf_op jit(solution)/shard_map/cond/branch_1_fun/ppermute | solution.py:69
  139.5 7.3 %collective-permute-start.10 = (f32[2,2,2,8,502]{4,3,2,1,0:T(8,128)S(1)}, f32[2,2,2,8,502]{4,3,2,1,0:T(8,128)S(1)}, u32[]{:S(2)}, u32[]{:S(2)}) collective-permute-start(f32[2,2,2,8,502]{4,3,2,1,0:T(8,128)S(1)} %dynamic-slice_bitcast_fusion.2), channel_id=1, source_target_pairs={{0,16},{8,24},{16,0},{24,8},{32,48},{40,56},{48,32},{56,40},{64,80... | collective-permute-start | bytes 385544 | tf_op jit(solution)/shard_map/cond/branch_1_fun/ppermute | solution.py:69
  144.3 6.6 %collective-permute-start.3 = (f32[2,2,2,8,512]{4,3,2,1,0:T(8,128)S(1)}, f32[2,2,2,8,512]{4,3,2,1,0:T(8,128)S(1)}, u32[]{:S(2)}, u32[]{:S(2)}) collective-permute-start(f32[2,2,2,8,512]{4,3,2,1,0:T(8,128)S(1)} %dynamic-slice_bitcast_fusion.3), channel_id=1, source_target_pairs={{0,2},{1,3},{2,0},{3,1},{4,6},{5,7},{6,4},{7,5},{8,10},{9,11},{10,... | collective-permute-start | bytes 393224 | tf_op jit(solution)/shard_map/cond/branch_1_fun/ppermute | solution.py:69
  146.9 9.0 %collective-permute-start.11 = (f32[2,2,8,502]{3,2,1,0:T(8,128)S(1)}, f32[2,2,8,502]{3,2,1,0:T(8,128)S(1)}, u32[]{:S(2)}, u32[]{:S(2)}) collective-permute-start(f32[2,2,8,502]{3,2,1,0:T(8,128)S(1)} %dynamic-slice_bitcast_fusion.4), channel_id=1, source_target_pairs={{0,32},{8,40},{16,48},{24,56},{32,0},{40,8},{48,16},{56,24},{64,96... | collective-permute-start | bytes 192776 | tf_op jit(solution)/shard_map/cond/branch_1_fun/ppermute | solution.py:69
  150.9 6.4 %collective-permute-start.4 = (f32[2,2,8,512]{3,2,1,0:T(8,128)S(1)}, f32[2,2,8,512]{3,2,1,0:T(8,128)S(1)}, u32[]{:S(2)}, u32[]{:S(2)}) collective-permute-start(f32[2,2,8,512]{3,2,1,0:T(8,128)S(1)} %dynamic-slice_bitcast_fusion.5), channel_id=1, source_target_pairs={{0,16},{8,24},{16,0},{24,8},{32,48},{40,56},{48,32},{56,40},{64,80... | collective-permute-start | bytes 196616 | tf_op jit(solution)/shard_map/cond/branch_1_fun/ppermute | solution.py:69
  156.0 5.5 %collective-permute-start.12 = (f32[2,8,502]{2,1,0:T(8,128)S(1)}, f32[2,8,502]{2,1,0:T(8,128)S(1)}, u32[]{:S(2)}, u32[]{:S(2)}) collective-permute-start(f32[2,8,502]{2,1,0:T(8,128)S(1)} %dynamic-slice_bitcast_fusion.6), channel_id=1, source_target_pairs={{0,2},{1,3},{2,0},{3,1},{4,6},{5,7},{6,4},{7,5},{8,10},{9,11},{10,... | collective-permute-start | bytes 96392 | tf_op jit(solution)/shard_map/cond/branch_1_fun/ppermute | solution.py:69
  157.4 5.9 %collective-permute-start.5 = (f32[2,8,512]{2,1,0:T(8,128)S(1)}, f32[2,8,512]{2,1,0:T(8,128)S(1)}, u32[]{:S(2)}, u32[]{:S(2)}) collective-permute-start(f32[2,8,512]{2,1,0:T(8,128)S(1)} %dynamic-slice_bitcast_fusion.7), channel_id=1, source_target_pairs={{0,128},{8,136},{16,144},{24,152},{32,160},{40,168},{48,176},{56,1... | collective-permute-start | bytes 98312 | tf_op jit(solution)/shard_map/cond/branch_1_fun/ppermute | solution.py:69
  161.5 5.5 %collective-permute-start.13 = (f32[8,502]{1,0:T(8,128)S(1)}, f32[8,502]{1,0:T(8,128)S(1)}, u32[]{:S(2)}, u32[]{:S(2)}) collective-permute-start(f32[8,502]{1,0:T(8,128)S(1)} %dynamic-slice_bitcast_fusion.8), channel_id=1, source_target_pairs={{0,128},{8,136},{16,144},{24,152},{32,160},{40,168},{48,176},{56,1... | collective-permute-start | bytes 48200 | tf_op jit(solution)/shard_map/cond/branch_1_fun/ppermute | solution.py:69
  163.3 7.7 %collective-permute-start.6 = (f32[8,512]{1,0:T(8,128)S(1)}, f32[8,512]{1,0:T(8,128)S(1)}, u32[]{:S(2)}, u32[]{:S(2)}) collective-permute-start(f32[8,512]{1,0:T(8,128)S(1)} %dynamic-slice_bitcast_fusion.9), channel_id=1, source_target_pairs={{0,32},{8,40},{16,48},{24,56},{32,0},{40,8},{48,16},{56,24},{64,96... | collective-permute-start | bytes 49160 | tf_op jit(solution)/shard_map/cond/branch_1_fun/ppermute | solution.py:69
  171.6 9.3 %copy-start.19 = (f32[8112]{0:T(1024)}, f32[8112]{0:T(1024)S(1)}, u32[]{:S(2)}) copy-start(f32[8112]{0:T(1024)S(1)} %get-tuple-element.267) | copy-start | bytes 97348
  172.9 4.5 %collective-permute-start.46 = (f32[2,2496]{1,0:T(2,128)S(1)}, f32[2,2496]{1,0:T(2,128)S(1)}, u32[]{:S(2)}, u32[]{:S(2)}) collective-permute-start(f32[2,2496]{1,0:T(2,128)S(1)} %pad_maximum_fusion.15), channel_id=1, source_target_pairs={{0,1},{1,0},{2,3},{3,2},{4,5},{5,4},{6,7},{7,6},{8,9},{9,8},{10,11... | collective-permute-start | bytes 59912 | tf_op jit(solution)/shard_map/ppermute | solution.py:84
  177.4 5.7 %collective-permute-start.47 = (f32[2,2496]{1,0:T(2,128)S(1)}, f32[2,2496]{1,0:T(2,128)S(1)}, u32[]{:S(2)}, u32[]{:S(2)}) collective-permute-start(f32[2,2496]{1,0:T(2,128)S(1)} %fusion.38), channel_id=1, source_target_pairs={{0,2},{1,3},{2,0},{3,1},{4,6},{5,7},{6,4},{7,5},{8,10},{9,11},{10,... | collective-permute-start | bytes 59912 | tf_op jit(solution)/shard_map/ppermute | solution.py:84
  183.2 6.2 %copy-start.5 = (bf16[4,32,2496]{2,1,0:T(8,128)(2,1)}, bf16[4,32,2496]{2,1,0:T(8,128)(2,1)S(1)}, u32[]{:S(2)}) copy-start(bf16[4,32,2496]{2,1,0:T(8,128)(2,1)S(1)} %get-tuple-element.269) | copy-start | bytes 1916932
  183.3 9.3 %collective-permute-start.49 = (bf16[2,32,2496]{2,1,0:T(8,128)(2,1)S(1)}, bf16[2,32,2496]{2,1,0:T(8,128)(2,1)S(1)}, u32[]{:S(2)}, u32[]{:S(2)}) collective-permute-start(bf16[2,32,2496]{2,1,0:T(8,128)(2,1)S(1)} %get-tuple-element.222), channel_id=1, source_target_pairs={{1,0},{2,1},{3,2},{5,4},{6,5},{7,6},{9,8},{10,9},{11,10},{13,12},{... | collective-permute-start | bytes 958472 | tf_op jit(solution)/shard_map/ppermute | solution.py:15
  187.4 9.0 %collective-permute-start.48 = (bf16[2,32,2496]{2,1,0:T(8,128)(2,1)S(1)}, bf16[2,32,2496]{2,1,0:T(8,128)(2,1)S(1)}, u32[]{:S(2)}, u32[]{:S(2)}) collective-permute-start(bf16[2,32,2496]{2,1,0:T(8,128)(2,1)S(1)} %get-tuple-element.221), channel_id=1, source_target_pairs={{0,1},{1,2},{2,3},{4,5},{5,6},{6,7},{8,9},{9,10},{10,11},{12,13},{... | collective-permute-start | bytes 958472 | tf_op jit(solution)/shard_map/ppermute | solution.py:12
  189.4 8.2 %copy-start.4 = (bf16[1,1,4,32,2496]{4,3,2,1,0:T(8,128)(2,1)S(1)}, bf16[1,1,4,32,2496]{4,3,2,1,0:T(8,128)(2,1)}, u32[]{:S(2)}) copy-start(bf16[1,1,4,32,2496]{4,3,2,1,0:T(8,128)(2,1)} %param.27) | copy-start | bytes 1916932
  189.4 8.2 %copy-start.13 = (f32[25,2496]{1,0:T(8,128)S(1)}, f32[25,2496]{1,0:T(8,128)}, u32[]{:S(2)}) copy-start(f32[25,2496]{1,0:T(8,128)} %copy-done.12) | copy-start | bytes 748804
  189.5 8.2 %copy-start.16 = (bf16[1,4,32,416]{3,2,1,0:T(8,128)(2,1)S(1)}, bf16[1,4,32,416]{3,2,1,0:T(8,128)(2,1)}, u32[]{:S(2)}) copy-start(bf16[1,4,32,416]{3,2,1,0:T(8,128)(2,1)} %param.26) | copy-start | bytes 319492
  (6 other events, 7.0 us)

commit v6 on v3

--- a/solution.py
+++ b/solution.py
@@ -233,8 +233,9 @@
     head_share, sent_top, sent_mid, act = lax.optimization_barrier(
         (head_share, sent_top, sent_mid, act)
     )
+    (pool_total,) = rows_sum((pool_part,))
     grad_part = jnp.sum(sent_mid.astype(jnp.float32) * act, axis=(0, 1))
-    pool_total, grad_total = rows_sum((pool_part, grad_part))
+    (grad_total,) = rows_sum((grad_part,))
 
     def gate_branch():
         gate, dpool = squeeze_gate(pool_total, grad_total, cells, reduce_w, expand_w)

time: 201 us -> 201 us (level)
    ppermute x14, starting transfers between devices: 24.1 us -> 21.7 us  [scatter_chunks(): moved = lax.ppermute(other, axis, swap_pairs(axis, j))]
    ppermute x2 -> x4, starting transfers between devices: 4.01 us -> 6.02 us  [rows_sum(): total = total + lax.ppermute(total, 'rows', swap_pairs('rows', j))]
  transfers between devices with their start and end apart: 36 -> 38, of which waited for: 21 -> 22; matrix products, arithmetic and copies ran while one was open for 17% -> 28% of each run, Pallas kernels for 0% -> 0%
where the time goes in v6:
time: 201 us; the launch traced here: 200 us
  starting transfers between devices  66.8 us (33%)
  waiting for transfers between devices  56.8 us (28%)
  local copies, waits for them, and re-layouts  30.3 us (15%)
  other arithmetic  22.2 us (11%)
  loops' own time  14.7 us (7%)
  matrix products  6.54 us (3%)
  between operations  2.28 us (1%)
    ppermute x14, waiting for transfers between devices, scatter_chunks(): moved = lax.ppermute(other, axis, swap_pairs(axis, j))  25.8 us
    ppermute x14, starting transfers between devices, gather_chunks(): recv = lax.ppermute(buf, axis, swap_pairs(axis, j))  24 us
    ppermute x14, waiting for transfers between devices, gather_chunks(): recv = lax.ppermute(buf, axis, swap_pairs(axis, j))  23.1 us
    ppermute x14, starting transfers between devices, scatter_chunks(): moved = lax.ppermute(other, axis, swap_pairs(axis, j))  21.7 us
    another operation x1, loops' own time, body(): grad_out = lax.cond(segment == 0, lead_branch, lead_still)  13.2 us
    reshape x1, local copies, waits for them, and re-layouts, spread(): flat_term = (term / images).reshape(shards, 8, -1)  7.15 us
    ppermute x2, starting transfers between devices, extended_2(): lax.ppermute(lax.slice_in_dim(block, 0, width, axis=dim), axis, backward)  6.77 us
    split x2, local copies, waits for them, and re-layouts, scatter_streams(): parts = jnp.split(full, cuts, axis=-1)  6.17 us
  transfers between devices with their start and end apart: 38, of which 22 were waited for; matrix products, arithmetic and copies ran while one was open for 28% of the time, Pallas kernels for 0%

profile of v6, /device:TPU:8, one launch (start us, length us, event | category | flops | bytes accessed | tf_op | source)
XLA Modules:
  0.0 199.6 jit_solution(9449351184900791074)
XLA Ops:
  1.7 3.0 %collective-permute-start.36 = (bf16[16,253]{1,0:T(8,128)(2,1)S(1)}, bf16[16,253]{1,0:T(8,128)(2,1)S(1)}, u32[]{:S(2)}, u32[]{:S(2)}) collective-permute-start(bf16[16,253]{1,0:T(8,128)(2,1)S(1)} %split.25), channel_id=1, source_target_pairs={{0,128},{8,136},{16,144},{24,152},{32,160},{40,168},{48,176},{56,1... | collective-permute-start | bytes 24296 | tf_op jit(solution)/shard_map/ppermute | solution.py:41
  4.7 7.2 %collective-permute-start.29 = (bf16[16,254]{1,0:T(8,128)(2,1)S(1)}, bf16[16,254]{1,0:T(8,128)(2,1)S(1)}, u32[]{:S(2)}, u32[]{:S(2)}) collective-permute-start(bf16[16,254]{1,0:T(8,128)(2,1)S(1)} %split.24), channel_id=1, source_target_pairs={{0,32},{8,40},{16,48},{24,56},{32,0},{40,8},{48,16},{56,24},{64,96... | collective-permute-start | bytes 24392 | tf_op jit(solution)/shard_map/ppermute | solution.py:41
  12.1 2.4 %collective-permute-start.37 = (bf16[2,16,253]{2,1,0:T(8,128)(2,1)S(1)}, bf16[2,16,253]{2,1,0:T(8,128)(2,1)S(1)}, u32[]{:S(2)}, u32[]{:S(2)}) collective-permute-start(bf16[2,16,253]{2,1,0:T(8,128)(2,1)S(1)} %pad_maximum_fusion.16), channel_id=1, source_target_pairs={{0,2},{1,3},{2,0},{3,1},{4,6},{5,7},{6,4},{7,5},{8,10},{9,11},{10,... | collective-permute-start | bytes 48584 | tf_op jit(solution)/shard_map/ppermute | solution.py:41
  15.1 2.3 %collective-permute-done.37 = bf16[2,16,253]{2,1,0:T(8,128)(2,1)S(1)} collective-permute-done((bf16[2,16,253]{2,1,0:T(8,128)(2,1)S(1)}, bf16[2,16,253]{2,1,0:T(8,128)(2,1)S(1)}, u32[]{:S(2)}, u32[]{:S(2)}) %collective-permute-start.37) | collective-permute-done | bytes 16224 | tf_op jit(solution)/shard_map/ppermute | solution.py:41
  17.4 2.8 %collective-permute-start.38 = (bf16[2,2,16,253]{3,2,1,0:T(8,128)(2,1)S(1)}, bf16[2,2,16,253]{3,2,1,0:T(8,128)(2,1)S(1)}, u32[]{:S(2)}, u32[]{:S(2)}) collective-permute-start(bf16[2,2,16,253]{3,2,1,0:T(8,128)(2,1)S(1)} %pad_maximum_fusion.14), channel_id=1, source_target_pairs={{0,32},{8,40},{16,48},{24,56},{32,0},{40,8},{48,16},{56,24},{64,96... | collective-permute-start | bytes 97160 | tf_op jit(solution)/shard_map/ppermute | solution.py:41
  21.8 3.8 %collective-permute-done.38 = bf16[2,2,16,253]{3,2,1,0:T(8,128)(2,1)S(1)} collective-permute-done((bf16[2,2,16,253]{3,2,1,0:T(8,128)(2,1)S(1)}, bf16[2,2,16,253]{3,2,1,0:T(8,128)(2,1)S(1)}, u32[]{:S(2)}, u32[]{:S(2)}) %collective-permute-start.38) | collective-permute-done | bytes 32416 | tf_op jit(solution)/shard_map/ppermute | solution.py:41
  27.1 2.4 %collective-permute-start.32 = (bf16[2,2,2,16,254]{4,3,2,1,0:T(8,128)(2,1)S(1)}, bf16[2,2,2,16,254]{4,3,2,1,0:T(8,128)(2,1)S(1)}, u32[]{:S(2)}, u32[]{:S(2)}) collective-permute-start(bf16[2,2,2,16,254]{4,3,2,1,0:T(8,128)(2,1)S(1)} %pad_maximum_fusion.11), channel_id=1, source_target_pairs={{0,2},{1,3},{2,0},{3,1},{4,6},{5,7},{6,4},{7,5},{8,10},{9,11},{10,... | collective-permute-start | bytes 195080 | tf_op jit(solution)/shard_map/ppermute | solution.py:41
  29.5 2.1 %collective-permute-done.39 = bf16[2,2,2,16,253]{4,3,2,1,0:T(8,128)(2,1)S(1)} collective-permute-done((bf16[2,2,2,16,253]{4,3,2,1,0:T(8,128)(2,1)S(1)}, bf16[2,2,2,16,253]{4,3,2,1,0:T(8,128)(2,1)S(1)}, u32[]{:S(2)}, u32[]{:S(2)}) %collective-permute-start.39) | collective-permute-done | bytes 64800 | tf_op jit(solution)/shard_map/ppermute | solution.py:41
  34.1 2.5 %collective-permute-done.40 = bf16[2,2,2,2,16,253]{5,4,3,2,1,0:T(8,128)(2,1)S(1)} collective-permute-done((bf16[2,2,2,2,16,253]{5,4,3,2,1,0:T(8,128)(2,1)S(1)}, bf16[2,2,2,2,16,253]{5,4,3,2,1,0:T(8,128)(2,1)S(1)}, u32[]{:S(2)}, u32[]{:S(2)}) %collective-permute-start.40) | collective-permute-done | bytes 129568 | tf_op jit(solution)/shard_map/ppermute | solution.py:41
  37.4 2.5 %collective-permute-done.33 = bf16[2,2,2,2,16,254]{5,4,3,2,1,0:T(8,128)(2,1)S(1)} collective-permute-done((bf16[2,2,2,2,16,254]{5,4,3,2,1,0:T(8,128)(2,1)S(1)}, bf16[2,2,2,2,16,254]{5,4,3,2,1,0:T(8,128)(2,1)S(1)}, u32[]{:S(2)}, u32[]{:S(2)}) %collective-permute-start.33) | collective-permute-done | bytes 130080 | tf_op jit(solution)/shard_map/ppermute | solution.py:41
  40.1 3.2 %collective-permute-done.41 = bf16[2,2,2,2,2,16,253]{6,5,4,3,2,1,0:T(8,128)(2,1)S(1)} collective-permute-done((bf16[2,2,2,2,2,16,253]{6,5,4,3,2,1,0:T(8,128)(2,1)S(1)}, bf16[2,2,2,2,2,16,253]{6,5,4,3,2,1,0:T(8,128)(2,1)S(1)}, u32[]{:S(2)}, u32[]{:S(2)}) %collective-permute-start.41) | collective-permute-done | bytes 259104 | tf_op jit(solution)/shard_map/ppermute | solution.py:41
  43.8 5.5 %collective-permute-done.34 = bf16[2,2,2,2,2,16,254]{6,5,4,3,2,1,0:T(8,128)(2,1)S(1)} collective-permute-done((bf16[2,2,2,2,2,16,254]{6,5,4,3,2,1,0:T(8,128)(2,1)S(1)}, bf16[2,2,2,2,2,16,254]{6,5,4,3,2,1,0:T(8,128)(2,1)S(1)}, u32[]{:S(2)}, u32[]{:S(2)}) %collective-permute-start.34) | collective-permute-done | bytes 260128 | tf_op jit(solution)/shard_map/ppermute | solution.py:41
  51.5 3.6 %collective-permute-start.45 = (bf16[2,32,2496]{2,1,0:T(8,128)(2,1)}, bf16[2,32,2496]{2,1,0:T(8,128)(2,1)}, u32[]{:S(2)}, u32[]{:S(2)}) collective-permute-start(bf16[2,32,2496]{2,1,0:T(8,128)(2,1)} %get-tuple-element.228), channel_id=1, source_target_pairs={{1,0},{2,1},{3,2},{5,4},{6,5},{7,6},{9,8},{10,9},{11,10},{13,12},{... | collective-permute-start | bytes 958472 | tf_op jit(solution)/shard_map/ppermute | solution.py:15
  55.1 2.4 %collective-permute-start.44 = (bf16[2,32,2496]{2,1,0:T(8,128)(2,1)}, bf16[2,32,2496]{2,1,0:T(8,128)(2,1)}, u32[]{:S(2)}, u32[]{:S(2)}) collective-permute-start(bf16[2,32,2496]{2,1,0:T(8,128)(2,1)} %get-tuple-element.227), channel_id=1, source_target_pairs={{0,1},{1,2},{2,3},{4,5},{5,6},{6,7},{8,9},{9,10},{10,11},{12,13},{... | collective-permute-start | bytes 958472 | tf_op jit(solution)/shard_map/ppermute | solution.py:12
  57.6 15.4 %conditional.8 = (bf16[128,416]{0,1:T(8,128)(2,1)}, bf16[4,32,416]{2,1,0:T(8,128)(2,1)S(1)}) conditional(s32[]{:T(128)} %convert_element_type.291, () %tuple.71, (bf16[1,4,32,384]{3,2,1,0:T(8,128)(2,1)S(1)}, bf16[1,2,16,384]{3,2,1,0:T(8,128)(2,1)S(1)}, bf16[1,1,8,384]{3,2,1,0:T(8,128)(2,1)S(1)}, bf16[416,384]{1,0:T(8,128)(2,1)S(1)}) %tuple.193), branch_computations={%region_0.1_spmd, %region_1.2_spmd} | conditional | flops 41138176 | bytes 1972240 | solution.py:200
  76.1 2.2 %pad_maximum_fusion.2 = bf16[128,16,507]{2,1,0:T(8,128)(2,1)} fusion(bf16[128,16,253]{2,1,0:T(8,128)(2,1)S(1)} %bitcast.278, bf16[128,16,254]{2,1,0:T(8,128)(2,1)S(1)} %bitcast.279), kind=kLoop, calls=%fused_computation.208 | loop fusion | flops 4153344 | bytes 4153344 | tf_op jit(solution)/shard_map/concatenate | solution.py:53
  78.4 5.2 %reshape_reshape.3 = bf16[416,2496]{1,0:T(8,128)(2,1)S(1)} reshape(bf16[128,16,507]{2,1,0:T(8,128)(2,1)} %pad_maximum_fusion.2) | data formatting | bytes 4153344 | tf_op jit(solution)/shard_map/reshape;reshape | solution.py:159
  83.6 2.0 %conditional.9 = (bf16[128,2496]{0,1:T(8,128)(2,1)S(1)}) conditional(s32[]{:T(128)} %convert_element_type.291, () %tuple.75, (bf16[128,416]{0,1:T(8,128)(2,1)}, bf16[416,2496]{1,0:T(8,128)(2,1)S(1)}) %tuple.76), branch_computations={%region_2.3_spmd, %region_3.4_spmd} | conditional | flops 266133504 | bytes 2822152 | solution.py:208
  83.6 2.0 %convolution_convert_fusion.1 = bf16[128,2496]{0,1:T(8,128)(2,1)S(1)} fusion(bf16[128,416]{0,1:T(8,128)(2,1)} %get-tuple-element.162, bf16[416,2496]{1,0:T(8,128)(2,1)S(1)} %get-tuple-element.89), kind=kOutput, calls=%fused_computation.6 | convolution fusion | flops 266133504 | bytes 2822144 | tf_op jit(solution)/shard_map/cond/branch_1_fun/dot_general | solution.py:203
  92.6 2.4 %collective-permute-start.46 = (f32[1,2496]{1,0:T(1,128)S(1)}, f32[1,2496]{1,0:T(1,128)S(1)}, u32[]{:S(2)}, u32[]{:S(2)}) collective-permute-start(f32[1,2496]{1,0:T(1,128)S(1)} %get-tuple-element.133), channel_id=1, source_target_pairs={{0,1},{1,0},{2,3},{3,2},{4,5},{5,4},{6,7},{7,6},{8,9},{9,8},{10,11... | collective-permute-start | bytes 29960 | tf_op jit(solution)/shard_map/ppermute | solution.py:84
  95.9 3.6 %conditional.10 = (f32[416,2496]{1,0:T(8,128)}) conditional(s32[]{:T(128)} %convert_element_type.291, () %tuple.74, (bf16[1,1,4,32,2496]{4,3,2,1,0:T(8,128)(2,1)S(1)}, bf16[128,416]{0,1:T(8,128)(2,1)}) %tuple.182), branch_computations={%region_4.5_spmd, %region_5.6_spmd} | conditional | flops 265814016 | bytes 4898824 | solution.py:231
  95.9 3.6 %fusion.42 = f32[416,2496]{1,0:T(8,128)} fusion(bf16[128,416]{0,1:T(8,128)(2,1)} %get-tuple-element.165, bf16[128,2496]{1,0:T(8,128)(2,1)S(1)} %bitcast.275), kind=kOutput, calls=%fused_computation.257 | convolution fusion | flops 265814016 | bytes 4898816 | tf_op jit(solution)/shard_map/cond/branch_1_fun/dot_general | solution.py:224
  99.5 73.7 %conditional.11 = (f32[8112]{0:T(1024)S(1)}) conditional(s32[]{:T(128)} %convert_element_type.291, () %tuple.73, f32[416,2496]{1,0:T(8,128)} %get-tuple-element.270), branch_computations={%region_6.7_spmd, %region_7.8_spmd} | conditional | flops 2855492 | bytes 59625460 | solution.py:232
  99.5 4.6 %broadcast_multiply_fusion = f32[416,2496]{1,0:T(8,128)} fusion(f32[416,2496]{1,0:T(8,128)} %param.7), kind=kLoop, calls=%fused_computation.7 | loop fusion | flops 1038336 | bytes 8306688 | tf_op jit(solution)/shard_map/cond/branch_1_fun/div | solution.py:214
  104.0 7.2 %reshape.176 = f32[128,8,1014]{2,1,0:T(8,128)} reshape(f32[416,2496]{1,0:T(8,128)} %broadcast_multiply_fusion) | data formatting | bytes 8306688 | tf_op jit(solution)/shard_map/cond/branch_1_fun/reshape | solution.py:214
  111.2 3.1 %split.21 = f32[128,8,502]{2,1,0:T(8,128)} slice(f32[128,8,1014]{2,1,0:T(8,128)} %reshape.176), slice={[0:128], [0:8], [512:1014]} | slice | bytes 4112384 | tf_op jit(solution)/shard_map/cond/branch_1_fun/split | solution.py:76
  114.3 2.1 %fusion.4 = bf16[2,2,2,2,2,16,502]{6,5,4,3,2,1,0:T(8,128)(2,1)} fusion(f32[2,2,2,2,2,2,2,8,502]{8,7,6,5,4,3,2,1,0:T(8,128)} %bitcast.267, s32[]{:T(128)S(6)} %select_n.227), kind=kLoop, calls=%fused_computation.13 | loop fusion | bytes 1028100 | tf_op jit(solution)/shard_map/cond/branch_1_fun/convert_element_type | solution.py:68
  116.4 3.1 %split.20 = f32[128,8,512]{2,1,0:T(8,128)} slice(f32[128,8,1014]{2,1,0:T(8,128)} %reshape.176), slice={[0:128], [0:8], [0:512]} | slice | bytes 4194304 | tf_op jit(solution)/shard_map/cond/branch_1_fun/split | solution.py:76
  119.5 2.1 %fusion.3 = bf16[2,2,2,2,2,16,512]{6,5,4,3,2,1,0:T(8,128)(2,1)} fusion(f32[2,2,2,2,2,2,2,8,512]{8,7,6,5,4,3,2,1,0:T(8,128)} %bitcast.271, s32[]{:T(128)S(6)} %select_n.225), kind=kLoop, calls=%fused_computation.12 | loop fusion | bytes 1048580 | tf_op jit(solution)/shard_map/cond/branch_1_fun/convert_element_type | solution.py:68
  122.3 3.6 %collective-permute-done.7 = bf16[2,2,2,2,2,16,502]{6,5,4,3,2,1,0:T(8,128)(2,1)} collective-permute-done((bf16[2,2,2,2,2,16,502]{6,5,4,3,2,1,0:T(8,128)(2,1)}, bf16[2,2,2,2,2,16,502]{6,5,4,3,2,1,0:T(8,128)(2,1)}, u32[]{:S(2)}, u32[]{:S(2)}) %collective-permute-start.7) | collective-permute-done | bytes 514080 | tf_op jit(solution)/shard_map/cond/branch_1_fun/ppermute | solution.py:69
  128.1 3.0 %collective-permute-done = bf16[2,2,2,2,2,16,512]{6,5,4,3,2,1,0:T(8,128)(2,1)} collective-permute-done((bf16[2,2,2,2,2,16,512]{6,5,4,3,2,1,0:T(8,128)(2,1)}, bf16[2,2,2,2,2,16,512]{6,5,4,3,2,1,0:T(8,128)(2,1)}, u32[]{:S(2)}, u32[]{:S(2)}) %collective-permute-start) | collective-permute-done | bytes 524320 | tf_op jit(solution)/shard_map/cond/branch_1_fun/ppermute | solution.py:69
  132.4 2.1 %collective-permute-start.1 = (bf16[2,2,2,2,16,512]{5,4,3,2,1,0:T(8,128)(2,1)S(1)}, bf16[2,2,2,2,16,512]{5,4,3,2,1,0:T(8,128)(2,1)S(1)}, u32[]{:S(2)}, u32[]{:S(2)}) collective-permute-start(bf16[2,2,2,2,16,512]{5,4,3,2,1,0:T(8,128)(2,1)S(1)} %fusion.5), channel_id=1, source_target_pairs={{0,8},{8,0},{16,24},{24,16},{32,40},{40,32},{48,56},{56,48},{64,72... | collective-permute-start | bytes 786440 | tf_op jit(solution)/shard_map/cond/branch_1_fun/ppermute | solution.py:69
  135.5 3.4 %collective-permute-done.1 = bf16[2,2,2,2,16,512]{5,4,3,2,1,0:T(8,128)(2,1)S(1)} collective-permute-done((bf16[2,2,2,2,16,512]{5,4,3,2,1,0:T(8,128)(2,1)S(1)}, bf16[2,2,2,2,16,512]{5,4,3,2,1,0:T(8,128)(2,1)S(1)}, u32[]{:S(2)}, u32[]{:S(2)}) %collective-permute-start.1) | collective-permute-done | bytes 262176 | tf_op jit(solution)/shard_map/cond/branch_1_fun/ppermute | solution.py:69
  142.2 3.2 %collective-permute-done.2 = f32[2,2,2,2,8,512]{5,4,3,2,1,0:T(8,128)S(1)} collective-permute-done((f32[2,2,2,2,8,512]{5,4,3,2,1,0:T(8,128)S(1)}, f32[2,2,2,2,8,512]{5,4,3,2,1,0:T(8,128)S(1)}, u32[]{:S(2)}, u32[]{:S(2)}) %collective-permute-start.2) | collective-permute-done | bytes 262176 | tf_op jit(solution)/shard_map/cond/branch_1_fun/ppermute | solution.py:69
  145.5 2.7 %collective-permute-start.3 = (f32[2,2,2,8,512]{4,3,2,1,0:T(8,128)S(1)}, f32[2,2,2,8,512]{4,3,2,1,0:T(8,128)S(1)}, u32[]{:S(2)}, u32[]{:S(2)}) collective-permute-start(f32[2,2,2,8,512]{4,3,2,1,0:T(8,128)S(1)} %dynamic-slice_bitcast_fusion.3), channel_id=1, source_target_pairs={{0,2},{1,3},{2,0},{3,1},{4,6},{5,7},{6,4},{7,5},{8,10},{9,11},{10,... | collective-permute-start | bytes 393224 | tf_op jit(solution)/shard_map/cond/branch_1_fun/ppermute | solution.py:69
  148.6 2.1 %collective-permute-start.11 = (f32[2,2,8,502]{3,2,1,0:T(8,128)S(1)}, f32[2,2,8,502]{3,2,1,0:T(8,128)S(1)}, u32[]{:S(2)}, u32[]{:S(2)}) collective-permute-start(f32[2,2,8,502]{3,2,1,0:T(8,128)S(1)} %dynamic-slice_bitcast_fusion.4), channel_id=1, source_target_pairs={{0,32},{8,40},{16,48},{24,56},{32,0},{40,8},{48,16},{56,24},{64,96... | collective-permute-start | bytes 192776 | tf_op jit(solution)/shard_map/cond/branch_1_fun/ppermute | solution.py:69
  152.1 2.5 %collective-permute-start.4 = (f32[2,2,8,512]{3,2,1,0:T(8,128)S(1)}, f32[2,2,8,512]{3,2,1,0:T(8,128)S(1)}, u32[]{:S(2)}, u32[]{:S(2)}) collective-permute-start(f32[2,2,8,512]{3,2,1,0:T(8,128)S(1)} %dynamic-slice_bitcast_fusion.5), channel_id=1, source_target_pairs={{0,16},{8,24},{16,0},{24,8},{32,48},{40,56},{48,32},{56,40},{64,80... | collective-permute-start | bytes 196616 | tf_op jit(solution)/shard_map/cond/branch_1_fun/ppermute | solution.py:69
  154.6 2.3 %collective-permute-done.11 = f32[2,2,8,502]{3,2,1,0:T(8,128)S(1)} collective-permute-done((f32[2,2,8,502]{3,2,1,0:T(8,128)S(1)}, f32[2,2,8,502]{3,2,1,0:T(8,128)S(1)}, u32[]{:S(2)}, u32[]{:S(2)}) %collective-permute-start.11) | collective-permute-done | bytes 64288 | tf_op jit(solution)/shard_map/cond/branch_1_fun/ppermute | solution.py:69
  157.0 2.4 %collective-permute-start.12 = (f32[2,8,502]{2,1,0:T(8,128)S(1)}, f32[2,8,502]{2,1,0:T(8,128)S(1)}, u32[]{:S(2)}, u32[]{:S(2)}) collective-permute-start(f32[2,8,502]{2,1,0:T(8,128)S(1)} %dynamic-slice_bitcast_fusion.6), channel_id=1, source_target_pairs={{0,2},{1,3},{2,0},{3,1},{4,6},{5,7},{6,4},{7,5},{8,10},{9,11},{10,... | collective-permute-start | bytes 96392 | tf_op jit(solution)/shard_map/cond/branch_1_fun/ppermute | solution.py:69
  160.5 1.9 collective-permute-done.12
  162.5 2.0 %collective-permute-start.13 = (f32[8,502]{1,0:T(8,128)S(1)}, f32[8,502]{1,0:T(8,128)S(1)}, u32[]{:S(2)}, u32[]{:S(2)}) collective-permute-start(f32[8,502]{1,0:T(8,128)S(1)} %dynamic-slice_bitcast_fusion.8), channel_id=1, source_target_pairs={{0,128},{8,136},{16,144},{24,152},{32,160},{40,168},{48,176},{56,1... | collective-permute-start | bytes 48200 | tf_op jit(solution)/shard_map/cond/branch_1_fun/ppermute | solution.py:69
  164.9 3.0 %collective-permute-start.6 = (f32[8,512]{1,0:T(8,128)S(1)}, f32[8,512]{1,0:T(8,128)S(1)}, u32[]{:S(2)}, u32[]{:S(2)}) collective-permute-start(f32[8,512]{1,0:T(8,128)S(1)} %dynamic-slice_bitcast_fusion.9), channel_id=1, source_target_pairs={{0,32},{8,40},{16,48},{24,56},{32,0},{40,8},{48,16},{56,24},{64,96... | collective-permute-start | bytes 49160 | tf_op jit(solution)/shard_map/cond/branch_1_fun/ppermute | solution.py:69
  167.9 4.8 %collective-permute-done.6 = f32[8,512]{1,0:T(8,128)S(1)} collective-permute-done((f32[8,512]{1,0:T(8,128)S(1)}, f32[8,512]{1,0:T(8,128)S(1)}, u32[]{:S(2)}, u32[]{:S(2)}) %collective-permute-start.6) | collective-permute-done | bytes 16416 | tf_op jit(solution)/shard_map/cond/branch_1_fun/ppermute | solution.py:69
  179.7 2.1 %copy.60 = bf16[2496,104]{1,0:T(8,128)(2,1)} copy(bf16[2496,104]{0,1:T(8,128)(2,1)} %param.34) | data formatting | bytes 1038336 | tf_op args[8]
  184.3 3.2 %collective-permute-start.51 = (bf16[2,32,2496]{2,1,0:T(8,128)(2,1)S(1)}, bf16[2,32,2496]{2,1,0:T(8,128)(2,1)S(1)}, u32[]{:S(2)}, u32[]{:S(2)}) collective-permute-start(bf16[2,32,2496]{2,1,0:T(8,128)(2,1)S(1)} %get-tuple-element.226), channel_id=1, source_target_pairs={{1,0},{2,1},{3,2},{5,4},{6,5},{7,6},{9,8},{10,9},{11,10},{13,12},{... | collective-permute-start | bytes 958472 | tf_op jit(solution)/shard_map/ppermute | solution.py:15
  187.5 2.7 %collective-permute-start.50 = (bf16[2,32,2496]{2,1,0:T(8,128)(2,1)S(1)}, bf16[2,32,2496]{2,1,0:T(8,128)(2,1)S(1)}, u32[]{:S(2)}, u32[]{:S(2)}) collective-permute-start(bf16[2,32,2496]{2,1,0:T(8,128)(2,1)S(1)} %get-tuple-element.225), channel_id=1, source_target_pairs={{0,1},{1,2},{2,3},{4,5},{5,6},{6,7},{8,9},{9,10},{10,11},{12,13},{... | collective-permute-start | bytes 958472 | tf_op jit(solution)/shard_map/ppermute | solution.py:12
  190.2 3.1 %collective-permute-done.51 = bf16[2,32,2496]{2,1,0:T(8,128)(2,1)S(1)} collective-permute-done((bf16[2,32,2496]{2,1,0:T(8,128)(2,1)S(1)}, bf16[2,32,2496]{2,1,0:T(8,128)(2,1)S(1)}, u32[]{:S(2)}, u32[]{:S(2)}) %collective-permute-start.51) | collective-permute-done | bytes 319520 | tf_op jit(solution)/shard_map/ppermute | solution.py:15
  193.3 3.2 %collective-permute-done.50 = bf16[2,32,2496]{2,1,0:T(8,128)(2,1)S(1)} collective-permute-done((bf16[2,32,2496]{2,1,0:T(8,128)(2,1)S(1)}, bf16[2,32,2496]{2,1,0:T(8,128)(2,1)S(1)}, u32[]{:S(2)}, u32[]{:S(2)}) %collective-permute-start.50) | collective-permute-done | bytes 319520 | tf_op jit(solution)/shard_map/ppermute | solution.py:12
  (171 shorter events, 47.5 us)
Async XLA Ops:
  1.7 10.3 %collective-permute-start.36 = (bf16[16,253]{1,0:T(8,128)(2,1)S(1)}, bf16[16,253]{1,0:T(8,128)(2,1)S(1)}, u32[]{:S(2)}, u32[]{:S(2)}) collective-permute-start(bf16[16,253]{1,0:T(8,128)(2,1)S(1)} %split.25), channel_id=1, source_target_pairs={{0,128},{8,136},{16,144},{24,152},{32,160},{40,168},{48,176},{56,1... | collective-permute-start | bytes 24296 | tf_op jit(solution)/shard_map/ppermute | solution.py:41
  4.7 9.7 %collective-permute-start.29 = (bf16[16,254]{1,0:T(8,128)(2,1)S(1)}, bf16[16,254]{1,0:T(8,128)(2,1)S(1)}, u32[]{:S(2)}, u32[]{:S(2)}) collective-permute-start(bf16[16,254]{1,0:T(8,128)(2,1)S(1)} %split.24), channel_id=1, source_target_pairs={{0,32},{8,40},{16,48},{24,56},{32,0},{40,8},{48,16},{56,24},{64,96... | collective-permute-start | bytes 24392 | tf_op jit(solution)/shard_map/ppermute | solution.py:41
  12.1 5.3 %collective-permute-start.37 = (bf16[2,16,253]{2,1,0:T(8,128)(2,1)S(1)}, bf16[2,16,253]{2,1,0:T(8,128)(2,1)S(1)}, u32[]{:S(2)}, u32[]{:S(2)}) collective-permute-start(bf16[2,16,253]{2,1,0:T(8,128)(2,1)S(1)} %pad_maximum_fusion.16), channel_id=1, source_target_pairs={{0,2},{1,3},{2,0},{3,1},{4,6},{5,7},{6,4},{7,5},{8,10},{9,11},{10,... | collective-permute-start | bytes 48584 | tf_op jit(solution)/shard_map/ppermute | solution.py:41
  14.5 5.7 %collective-permute-start.30 = (bf16[2,16,254]{2,1,0:T(8,128)(2,1)S(1)}, bf16[2,16,254]{2,1,0:T(8,128)(2,1)S(1)}, u32[]{:S(2)}, u32[]{:S(2)}) collective-permute-start(bf16[2,16,254]{2,1,0:T(8,128)(2,1)S(1)} %pad_maximum_fusion.15), channel_id=1, source_target_pairs={{0,128},{8,136},{16,144},{24,152},{32,160},{40,168},{48,176},{56,1... | collective-permute-start | bytes 48776 | tf_op jit(solution)/shard_map/ppermute | solution.py:41
  17.4 8.1 %collective-permute-start.38 = (bf16[2,2,16,253]{3,2,1,0:T(8,128)(2,1)S(1)}, bf16[2,2,16,253]{3,2,1,0:T(8,128)(2,1)S(1)}, u32[]{:S(2)}, u32[]{:S(2)}) collective-permute-start(bf16[2,2,16,253]{3,2,1,0:T(8,128)(2,1)S(1)} %pad_maximum_fusion.14), channel_id=1, source_target_pairs={{0,32},{8,40},{16,48},{24,56},{32,0},{40,8},{48,16},{56,24},{64,96... | collective-permute-start | bytes 97160 | tf_op jit(solution)/shard_map/ppermute | solution.py:41
  20.2 6.8 %collective-permute-start.31 = (bf16[2,2,16,254]{3,2,1,0:T(8,128)(2,1)S(1)}, bf16[2,2,16,254]{3,2,1,0:T(8,128)(2,1)S(1)}, u32[]{:S(2)}, u32[]{:S(2)}) collective-permute-start(bf16[2,2,16,254]{3,2,1,0:T(8,128)(2,1)S(1)} %pad_maximum_fusion.13), channel_id=1, source_target_pairs={{0,16},{8,24},{16,0},{24,8},{32,48},{40,56},{48,32},{56,40},{64,80... | collective-permute-start | bytes 97544 | tf_op jit(solution)/shard_map/ppermute | solution.py:41
  25.6 6.0 %collective-permute-start.39 = (bf16[2,2,2,16,253]{4,3,2,1,0:T(8,128)(2,1)S(1)}, bf16[2,2,2,16,253]{4,3,2,1,0:T(8,128)(2,1)S(1)}, u32[]{:S(2)}, u32[]{:S(2)}) collective-permute-start(bf16[2,2,2,16,253]{4,3,2,1,0:T(8,128)(2,1)S(1)} %pad_maximum_fusion.12), channel_id=1, source_target_pairs={{0,16},{8,24},{16,0},{24,8},{32,48},{40,56},{48,32},{56,40},{64,80... | collective-permute-start | bytes 194312 | tf_op jit(solution)/shard_map/ppermute | solution.py:41
  27.1 6.3 %collective-permute-start.32 = (bf16[2,2,2,16,254]{4,3,2,1,0:T(8,128)(2,1)S(1)}, bf16[2,2,2,16,254]{4,3,2,1,0:T(8,128)(2,1)S(1)}, u32[]{:S(2)}, u32[]{:S(2)}) collective-permute-start(bf16[2,2,2,16,254]{4,3,2,1,0:T(8,128)(2,1)S(1)} %pad_maximum_fusion.11), channel_id=1, source_target_pairs={{0,2},{1,3},{2,0},{3,1},{4,6},{5,7},{6,4},{7,5},{8,10},{9,11},{10,... | collective-permute-start | bytes 195080 | tf_op jit(solution)/shard_map/ppermute | solution.py:41
  31.6 5.1 %collective-permute-start.40 = (bf16[2,2,2,2,16,253]{5,4,3,2,1,0:T(8,128)(2,1)S(1)}, bf16[2,2,2,2,16,253]{5,4,3,2,1,0:T(8,128)(2,1)S(1)}, u32[]{:S(2)}, u32[]{:S(2)}) collective-permute-start(bf16[2,2,2,2,16,253]{5,4,3,2,1,0:T(8,128)(2,1)S(1)} %pad_maximum_fusion.10), channel_id=1, source_target_pairs={{0,1},{1,0},{2,3},{3,2},{4,5},{5,4},{6,7},{7,6},{8,9},{9,8},{10,11... | collective-permute-start | bytes 388616 | tf_op jit(solution)/shard_map/ppermute | solution.py:41
  33.5 6.4 %collective-permute-start.33 = (bf16[2,2,2,2,16,254]{5,4,3,2,1,0:T(8,128)(2,1)S(1)}, bf16[2,2,2,2,16,254]{5,4,3,2,1,0:T(8,128)(2,1)S(1)}, u32[]{:S(2)}, u32[]{:S(2)}) collective-permute-start(bf16[2,2,2,2,16,254]{5,4,3,2,1,0:T(8,128)(2,1)S(1)} %pad_maximum_fusion.9), channel_id=1, source_target_pairs={{0,64},{8,72},{16,80},{24,88},{32,96},{40,104},{48,112},{56,120},{... | collective-permute-start | bytes 390152 | tf_op jit(solution)/shard_map/ppermute | solution.py:41
  36.8 6.6 %collective-permute-start.41 = (bf16[2,2,2,2,2,16,253]{6,5,4,3,2,1,0:T(8,128)(2,1)S(1)}, bf16[2,2,2,2,2,16,253]{6,5,4,3,2,1,0:T(8,128)(2,1)S(1)}, u32[]{:S(2)}, u32[]{:S(2)}) collective-permute-start(bf16[2,2,2,2,2,16,253]{6,5,4,3,2,1,0:T(8,128)(2,1)S(1)} %pad_maximum_fusion.8), channel_id=1, source_target_pairs={{0,64},{8,72},{16,80},{24,88},{32,96},{40,104},{48,112},{56,120},{... | collective-permute-start | bytes 777224 | tf_op jit(solution)/shard_map/ppermute | solution.py:41
  40.0 9.3 %collective-permute-start.34 = (bf16[2,2,2,2,2,16,254]{6,5,4,3,2,1,0:T(8,128)(2,1)S(1)}, bf16[2,2,2,2,2,16,254]{6,5,4,3,2,1,0:T(8,128)(2,1)S(1)}, u32[]{:S(2)}, u32[]{:S(2)}) collective-permute-start(bf16[2,2,2,2,2,16,254]{6,5,4,3,2,1,0:T(8,128)(2,1)S(1)} %pad_maximum_fusion.7), channel_id=1, source_target_pairs={{0,8},{8,0},{16,24},{24,16},{32,40},{40,32},{48,56},{56,48},{64,72... | collective-permute-start | bytes 780296 | tf_op jit(solution)/shard_map/ppermute | solution.py:41
  43.5 29.5 %collective-permute-start.42 = (bf16[2,2,2,2,2,2,16,253]{7,6,5,4,3,2,1,0:T(8,128)(2,1)S(1)}, bf16[2,2,2,2,2,2,16,253]{7,6,5,4,3,2,1,0:T(8,128)(2,1)}, u32[]{:S(2)}, u32[]{:S(2)}) collective-permute-start(bf16[2,2,2,2,2,2,16,253]{7,6,5,4,3,2,1,0:T(8,128)(2,1)S(1)} %pad_maximum_fusion.6), channel_id=1, source_target_pairs={{0,8},{8,0},{16,24},{24,16},{32,40},{40,32},{48,56},{56,48},{64,72... | collective-permute-start | bytes 1554440 | tf_op jit(solution)/shard_map/ppermute | solution.py:41
  49.3 8.2 %copy-start.15 = (bf16[416,384]{1,0:T(8,128)(2,1)S(1)}, bf16[416,384]{1,0:T(8,128)(2,1)}, u32[]{:S(2)}) copy-start(bf16[416,384]{1,0:T(8,128)(2,1)} %param.31) | copy-start | bytes 958468
  49.4 8.2 %copy-start.18 = (bf16[1,4,32,384]{3,2,1,0:T(8,128)(2,1)S(1)}, bf16[1,4,32,384]{3,2,1,0:T(8,128)(2,1)}, u32[]{:S(2)}) copy-start(bf16[1,4,32,384]{3,2,1,0:T(8,128)(2,1)} %param.28) | copy-start | bytes 294916
  49.4 8.2 %copy-start.20 = (bf16[1,2,16,384]{3,2,1,0:T(8,128)(2,1)S(1)}, bf16[1,2,16,384]{3,2,1,0:T(8,128)(2,1)}, u32[]{:S(2)}) copy-start(bf16[1,2,16,384]{3,2,1,0:T(8,128)(2,1)} %param.29) | copy-start | bytes 73732
  49.4 8.2 %copy-start.21 = (bf16[1,1,8,384]{3,2,1,0:T(8,128)(2,1)S(1)}, bf16[1,1,8,384]{3,2,1,0:T(8,128)(2,1)}, u32[]{:S(2)}) copy-start(bf16[1,1,8,384]{3,2,1,0:T(8,128)(2,1)} %param.30) | copy-start | bytes 18436
  50.3 24.3 %collective-permute-start.35 = (bf16[2,2,2,2,2,2,16,254]{7,6,5,4,3,2,1,0:T(8,128)(2,1)}, bf16[2,2,2,2,2,2,16,254]{7,6,5,4,3,2,1,0:T(8,128)(2,1)}, u32[]{:S(2)}, u32[]{:S(2)}) collective-permute-start(bf16[2,2,2,2,2,2,16,254]{7,6,5,4,3,2,1,0:T(8,128)(2,1)} %pad_maximum_fusion.5), channel_id=1, source_target_pairs={{0,1},{1,0},{2,3},{3,2},{4,5},{5,4},{6,7},{7,6},{8,9},{9,8},{10,11... | collective-permute-start | bytes 1560584 | tf_op jit(solution)/shard_map/ppermute | solution.py:41
  51.5 39.4 %collective-permute-start.45 = (bf16[2,32,2496]{2,1,0:T(8,128)(2,1)}, bf16[2,32,2496]{2,1,0:T(8,128)(2,1)}, u32[]{:S(2)}, u32[]{:S(2)}) collective-permute-start(bf16[2,32,2496]{2,1,0:T(8,128)(2,1)} %get-tuple-element.228), channel_id=1, source_target_pairs={{1,0},{2,1},{3,2},{5,4},{6,5},{7,6},{9,8},{10,9},{11,10},{13,12},{... | collective-permute-start | bytes 958472 | tf_op jit(solution)/shard_map/ppermute | solution.py:15
  55.1 35.8 %collective-permute-start.44 = (bf16[2,32,2496]{2,1,0:T(8,128)(2,1)}, bf16[2,32,2496]{2,1,0:T(8,128)(2,1)}, u32[]{:S(2)}, u32[]{:S(2)}) collective-permute-start(bf16[2,32,2496]{2,1,0:T(8,128)(2,1)} %get-tuple-element.227), channel_id=1, source_target_pairs={{0,1},{1,2},{2,3},{4,5},{5,6},{6,7},{8,9},{9,10},{10,11},{12,13},{... | collective-permute-start | bytes 958472 | tf_op jit(solution)/shard_map/ppermute | solution.py:12
  86.7 8.3 %collective-permute-start.43 = (bf16[4,32,2496]{2,1,0:T(8,128)(2,1)}, bf16[4,32,2496]{2,1,0:T(8,128)(2,1)S(1)}, u32[]{:S(2)}, u32[]{:S(2)}) collective-permute-start(bf16[4,32,2496]{2,1,0:T(8,128)(2,1)} %bitcast.280), channel_id=1, source_target_pairs={{0,4},{1,5},{2,6},{3,7},{8,12},{9,13},{10,14},{11,15},{16,20},{17,... | collective-permute-start | bytes 1916936 | tf_op jit(solution)/shard_map/ppermute | solution.py:23
  88.1 6.9 %collective-permute-start.28 = (bf16[4,32,416]{2,1,0:T(8,128)(2,1)}, bf16[4,32,416]{2,1,0:T(8,128)(2,1)}, u32[]{:S(2)}, u32[]{:S(2)}) collective-permute-start(bf16[4,32,416]{2,1,0:T(8,128)(2,1)} %copy-done.17), channel_id=1, source_target_pairs={{0,4},{1,5},{2,6},{3,7},{8,12},{9,13},{10,14},{11,15},{16,20},{17,... | collective-permute-start | bytes 319496 | tf_op jit(solution)/shard_map/ppermute | solution.py:23
  92.6 83.3 %collective-permute-start.46 = (f32[1,2496]{1,0:T(1,128)S(1)}, f32[1,2496]{1,0:T(1,128)S(1)}, u32[]{:S(2)}, u32[]{:S(2)}) collective-permute-start(f32[1,2496]{1,0:T(1,128)S(1)} %get-tuple-element.133), channel_id=1, source_target_pairs={{0,1},{1,0},{2,3},{3,2},{4,5},{5,4},{6,7},{7,6},{8,9},{9,8},{10,11... | collective-permute-start | bytes 29960 | tf_op jit(solution)/shard_map/ppermute | solution.py:84
  99.5 73.7 %copy-start.9 = (f32[4,32,2496]{2,1,0:T(8,128)S(1)}, f32[4,32,2496]{2,1,0:T(8,128)}, u32[]{:S(2)}) copy-start(f32[4,32,2496]{2,1,0:T(8,128)} %copy-done.8) | copy-start | bytes 3833860
  116.4 9.5 %collective-permute-start.7 = (bf16[2,2,2,2,2,16,502]{6,5,4,3,2,1,0:T(8,128)(2,1)}, bf16[2,2,2,2,2,16,502]{6,5,4,3,2,1,0:T(8,128)(2,1)}, u32[]{:S(2)}, u32[]{:S(2)}) collective-permute-start(bf16[2,2,2,2,2,16,502]{6,5,4,3,2,1,0:T(8,128)(2,1)} %fusion.4), channel_id=1, source_target_pairs={{0,8},{8,0},{16,24},{24,16},{32,40},{40,32},{48,56},{56,48},{64,72... | collective-permute-start | bytes 1542152 | tf_op jit(solution)/shard_map/cond/branch_1_fun/ppermute | solution.py:69
  121.6 9.5 %collective-permute-start = (bf16[2,2,2,2,2,16,512]{6,5,4,3,2,1,0:T(8,128)(2,1)}, bf16[2,2,2,2,2,16,512]{6,5,4,3,2,1,0:T(8,128)(2,1)}, u32[]{:S(2)}, u32[]{:S(2)}) collective-permute-start(bf16[2,2,2,2,2,16,512]{6,5,4,3,2,1,0:T(8,128)(2,1)} %fusion.3), channel_id=1, source_target_pairs={{0,1},{1,0},{2,3},{3,2},{4,5},{5,4},{6,7},{7,6},{8,9},{9,8},{10,11... | collective-permute-start | bytes 1572872 | tf_op jit(solution)/shard_map/cond/branch_1_fun/ppermute | solution.py:69
  122.3 8.8 %copy-start.2 = (f32[128,8,512]{2,1,0:T(8,128)S(1)}, f32[128,8,512]{2,1,0:T(8,128)}, u32[]{:S(2)}) copy-start(f32[128,8,512]{2,1,0:T(8,128)} %split.20) | copy-start | bytes 6291460 | tf_op jit(solution)/shard_map/cond
  127.5 7.0 %collective-permute-start.8 = (bf16[2,2,2,2,16,502]{5,4,3,2,1,0:T(8,128)(2,1)S(1)}, bf16[2,2,2,2,16,502]{5,4,3,2,1,0:T(8,128)(2,1)S(1)}, u32[]{:S(2)}, u32[]{:S(2)}) collective-permute-start(bf16[2,2,2,2,16,502]{5,4,3,2,1,0:T(8,128)(2,1)S(1)} %fusion.6), channel_id=1, source_target_pairs={{0,64},{8,72},{16,80},{24,88},{32,96},{40,104},{48,112},{56,120},{... | collective-permute-start | bytes 771080 | tf_op jit(solution)/shard_map/cond/branch_1_fun/ppermute | solution.py:69
  132.4 6.5 %collective-permute-start.1 = (bf16[2,2,2,2,16,512]{5,4,3,2,1,0:T(8,128)(2,1)S(1)}, bf16[2,2,2,2,16,512]{5,4,3,2,1,0:T(8,128)(2,1)S(1)}, u32[]{:S(2)}, u32[]{:S(2)}) collective-permute-start(bf16[2,2,2,2,16,512]{5,4,3,2,1,0:T(8,128)(2,1)S(1)} %fusion.5), channel_id=1, source_target_pairs={{0,8},{8,0},{16,24},{24,16},{32,40},{40,32},{48,56},{56,48},{64,72... | collective-permute-start | bytes 786440 | tf_op jit(solution)/shard_map/cond/branch_1_fun/ppermute | solution.py:69
  134.7 6.5 %collective-permute-start.9 = (f32[2,2,2,2,8,502]{5,4,3,2,1,0:T(8,128)S(1)}, f32[2,2,2,2,8,502]{5,4,3,2,1,0:T(8,128)S(1)}, u32[]{:S(2)}, u32[]{:S(2)}) collective-permute-start(f32[2,2,2,2,8,502]{5,4,3,2,1,0:T(8,128)S(1)} %dynamic-slice_bitcast_fusion), channel_id=1, source_target_pairs={{0,1},{1,0},{2,3},{3,2},{4,5},{5,4},{6,7},{7,6},{8,9},{9,8},{10,11... | collective-permute-start | bytes 771080 | tf_op jit(solution)/shard_map/cond/branch_1_fun/ppermute | solution.py:69
  139.0 6.5 %collective-permute-start.2 = (f32[2,2,2,2,8,512]{5,4,3,2,1,0:T(8,128)S(1)}, f32[2,2,2,2,8,512]{5,4,3,2,1,0:T(8,128)S(1)}, u32[]{:S(2)}, u32[]{:S(2)}) collective-permute-start(f32[2,2,2,2,8,512]{5,4,3,2,1,0:T(8,128)S(1)} %dynamic-slice_bitcast_fusion.1), channel_id=1, source_target_pairs={{0,64},{8,72},{16,80},{24,88},{32,96},{40,104},{48,112},{56,120},{... | collective-permute-start | bytes 786440 | tf_op jit(solution)/shard_map/cond/branch_1_fun/ppermute | solution.py:69
  141.2 7.3 %collective-permute-start.10 = (f32[2,2,2,8,502]{4,3,2,1,0:T(8,128)S(1)}, f32[2,2,2,8,502]{4,3,2,1,0:T(8,128)S(1)}, u32[]{:S(2)}, u32[]{:S(2)}) collective-permute-start(f32[2,2,2,8,502]{4,3,2,1,0:T(8,128)S(1)} %dynamic-slice_bitcast_fusion.2), channel_id=1, source_target_pairs={{0,16},{8,24},{16,0},{24,8},{32,48},{40,56},{48,32},{56,40},{64,80... | collective-permute-start | bytes 385544 | tf_op jit(solution)/shard_map/cond/branch_1_fun/ppermute | solution.py:69
  145.5 6.6 %collective-permute-start.3 = (f32[2,2,2,8,512]{4,3,2,1,0:T(8,128)S(1)}, f32[2,2,2,8,512]{4,3,2,1,0:T(8,128)S(1)}, u32[]{:S(2)}, u32[]{:S(2)}) collective-permute-start(f32[2,2,2,8,512]{4,3,2,1,0:T(8,128)S(1)} %dynamic-slice_bitcast_fusion.3), channel_id=1, source_target_pairs={{0,2},{1,3},{2,0},{3,1},{4,6},{5,7},{6,4},{7,5},{8,10},{9,11},{10,... | collective-permute-start | bytes 393224 | tf_op jit(solution)/shard_map/cond/branch_1_fun/ppermute | solution.py:69
  148.6 8.4 %collective-permute-start.11 = (f32[2,2,8,502]{3,2,1,0:T(8,128)S(1)}, f32[2,2,8,502]{3,2,1,0:T(8,128)S(1)}, u32[]{:S(2)}, u32[]{:S(2)}) collective-permute-start(f32[2,2,8,502]{3,2,1,0:T(8,128)S(1)} %dynamic-slice_bitcast_fusion.4), channel_id=1, source_target_pairs={{0,32},{8,40},{16,48},{24,56},{32,0},{40,8},{48,16},{56,24},{64,96... | collective-permute-start | bytes 192776 | tf_op jit(solution)/shard_map/cond/branch_1_fun/ppermute | solution.py:69
  152.1 7.2 %collective-permute-start.4 = (f32[2,2,8,512]{3,2,1,0:T(8,128)S(1)}, f32[2,2,8,512]{3,2,1,0:T(8,128)S(1)}, u32[]{:S(2)}, u32[]{:S(2)}) collective-permute-start(f32[2,2,8,512]{3,2,1,0:T(8,128)S(1)} %dynamic-slice_bitcast_fusion.5), channel_id=1, source_target_pairs={{0,16},{8,24},{16,0},{24,8},{32,48},{40,56},{48,32},{56,40},{64,80... | collective-permute-start | bytes 196616 | tf_op jit(solution)/shard_map/cond/branch_1_fun/ppermute | solution.py:69
  157.0 5.5 %collective-permute-start.12 = (f32[2,8,502]{2,1,0:T(8,128)S(1)}, f32[2,8,502]{2,1,0:T(8,128)S(1)}, u32[]{:S(2)}, u32[]{:S(2)}) collective-permute-start(f32[2,8,502]{2,1,0:T(8,128)S(1)} %dynamic-slice_bitcast_fusion.6), channel_id=1, source_target_pairs={{0,2},{1,3},{2,0},{3,1},{4,6},{5,7},{6,4},{7,5},{8,10},{9,11},{10,... | collective-permute-start | bytes 96392 | tf_op jit(solution)/shard_map/cond/branch_1_fun/ppermute | solution.py:69
  159.4 5.5 %collective-permute-start.5 = (f32[2,8,512]{2,1,0:T(8,128)S(1)}, f32[2,8,512]{2,1,0:T(8,128)S(1)}, u32[]{:S(2)}, u32[]{:S(2)}) collective-permute-start(f32[2,8,512]{2,1,0:T(8,128)S(1)} %dynamic-slice_bitcast_fusion.7), channel_id=1, source_target_pairs={{0,128},{8,136},{16,144},{24,152},{32,160},{40,168},{48,176},{56,1... | collective-permute-start | bytes 98312 | tf_op jit(solution)/shard_map/cond/branch_1_fun/ppermute | solution.py:69
  162.5 5.4 %collective-permute-start.13 = (f32[8,502]{1,0:T(8,128)S(1)}, f32[8,502]{1,0:T(8,128)S(1)}, u32[]{:S(2)}, u32[]{:S(2)}) collective-permute-start(f32[8,502]{1,0:T(8,128)S(1)} %dynamic-slice_bitcast_fusion.8), channel_id=1, source_target_pairs={{0,128},{8,136},{16,144},{24,152},{32,160},{40,168},{48,176},{56,1... | collective-permute-start | bytes 48200 | tf_op jit(solution)/shard_map/cond/branch_1_fun/ppermute | solution.py:69
  164.9 7.7 %collective-permute-start.6 = (f32[8,512]{1,0:T(8,128)S(1)}, f32[8,512]{1,0:T(8,128)S(1)}, u32[]{:S(2)}, u32[]{:S(2)}) collective-permute-start(f32[8,512]{1,0:T(8,128)S(1)} %dynamic-slice_bitcast_fusion.9), channel_id=1, source_target_pairs={{0,32},{8,40},{16,48},{24,56},{32,0},{40,8},{48,16},{56,24},{64,96... | collective-permute-start | bytes 49160 | tf_op jit(solution)/shard_map/cond/branch_1_fun/ppermute | solution.py:69
  173.1 8.7 %copy-start.19 = (f32[8112]{0:T(1024)}, f32[8112]{0:T(1024)S(1)}, u32[]{:S(2)}) copy-start(f32[8112]{0:T(1024)S(1)} %get-tuple-element.271) | copy-start | bytes 97348
  174.4 3.8 %collective-permute-start.48 = (f32[1,2496]{1,0:T(1,128)S(1)}, f32[1,2496]{1,0:T(1,128)S(1)}, u32[]{:S(2)}, u32[]{:S(2)}) collective-permute-start(f32[1,2496]{1,0:T(1,128)S(1)} %stack.178), channel_id=1, source_target_pairs={{0,1},{1,0},{2,3},{3,2},{4,5},{5,4},{6,7},{7,6},{8,9},{9,8},{10,11... | collective-permute-start | bytes 29960 | tf_op jit(solution)/shard_map/ppermute | solution.py:84
  176.0 8.2 %collective-permute-start.47 = (f32[1,2496]{1,0:T(1,128)S(1)}, f32[1,2496]{1,0:T(1,128)S(1)}, u32[]{:S(2)}, u32[]{:S(2)}) collective-permute-start(f32[1,2496]{1,0:T(1,128)S(1)} %add.434), channel_id=1, source_target_pairs={{0,2},{1,3},{2,0},{3,1},{4,6},{5,7},{6,4},{7,5},{8,10},{9,11},{10,... | collective-permute-start | bytes 29960 | tf_op jit(solution)/shard_map/ppermute | solution.py:84
  178.2 6.0 %collective-permute-start.49 = (f32[1,2496]{1,0:T(1,128)S(1)}, f32[1,2496]{1,0:T(1,128)S(1)}, u32[]{:S(2)}, u32[]{:S(2)}) collective-permute-start(f32[1,2496]{1,0:T(1,128)S(1)} %reshape_add_fusion), channel_id=1, source_target_pairs={{0,2},{1,3},{2,0},{3,1},{4,6},{5,7},{6,4},{7,5},{8,10},{9,11},{10,... | collective-permute-start | bytes 29960 | tf_op jit(solution)/shard_map/ppermute | solution.py:84
  184.3 9.0 %collective-permute-start.51 = (bf16[2,32,2496]{2,1,0:T(8,128)(2,1)S(1)}, bf16[2,32,2496]{2,1,0:T(8,128)(2,1)S(1)}, u32[]{:S(2)}, u32[]{:S(2)}) collective-permute-start(bf16[2,32,2496]{2,1,0:T(8,128)(2,1)S(1)} %get-tuple-element.226), channel_id=1, source_target_pairs={{1,0},{2,1},{3,2},{5,4},{6,5},{7,6},{9,8},{10,9},{11,10},{13,12},{... | collective-permute-start | bytes 958472 | tf_op jit(solution)/shard_map/ppermute | solution.py:15
  187.5 9.0 %collective-permute-start.50 = (bf16[2,32,2496]{2,1,0:T(8,128)(2,1)S(1)}, bf16[2,32,2496]{2,1,0:T(8,128)(2,1)S(1)}, u32[]{:S(2)}, u32[]{:S(2)}) collective-permute-start(bf16[2,32,2496]{2,1,0:T(8,128)(2,1)S(1)} %get-tuple-element.225), channel_id=1, source_target_pairs={{0,1},{1,2},{2,3},{4,5},{5,6},{6,7},{8,9},{9,10},{10,11},{12,13},{... | collective-permute-start | bytes 958472 | tf_op jit(solution)/shard_map/ppermute | solution.py:12
  190.2 7.5 %copy-start.4 = (bf16[1,1,4,32,2496]{4,3,2,1,0:T(8,128)(2,1)S(1)}, bf16[1,1,4,32,2496]{4,3,2,1,0:T(8,128)(2,1)}, u32[]{:S(2)}) copy-start(bf16[1,1,4,32,2496]{4,3,2,1,0:T(8,128)(2,1)} %param.27) | copy-start | bytes 1916932
  190.2 7.5 %copy-start.13 = (f32[25,2496]{1,0:T(8,128)S(1)}, f32[25,2496]{1,0:T(8,128)}, u32[]{:S(2)}) copy-start(f32[25,2496]{1,0:T(8,128)} %copy-done.12) | copy-start | bytes 748804
  190.2 7.5 %copy-start.16 = (bf16[1,4,32,416]{3,2,1,0:T(8,128)(2,1)S(1)}, bf16[1,4,32,416]{3,2,1,0:T(8,128)(2,1)}, u32[]{:S(2)}) copy-start(bf16[1,4,32,416]{3,2,1,0:T(8,128)(2,1)} %param.26) | copy-start | bytes 319492
  (8 other events, 18.2 us)

commit v7 on v4

--- a/solution.py
+++ b/solution.py
@@ -232,8 +232,9 @@
     head_share, sent_top, sent_mid, act = lax.optimization_barrier(
         (head_share, sent_top, sent_mid, act)
     )
+    (pool_total,) = rows_sum((pool_part,))
     grad_part = jnp.sum(sent_mid.astype(jnp.float32) * act, axis=(0, 1))
-    pool_total, grad_total = rows_sum((pool_part, grad_part))
+    (grad_total,) = rows_sum((grad_part,))
 
     def gate_branch():
         gate, dpool = squeeze_gate(pool_total, grad_total, cells, reduce_w, expand_w)

time: 203 us -> 203 us (level)
    ppermute x2 -> x4, starting transfers between devices: 3.99 us -> 7.21 us  [rows_sum(): total = total + lax.ppermute(total, 'rows', swap_pairs('rows', j))]
  transfers between devices with their start and end apart: 36 -> 38, of which waited for: 22 -> 22; matrix products, arithmetic and copies ran while one was open for 15% -> 27% of each run, Pallas kernels for 0% -> 0%
where the time goes in v7:
time: 203 us; the launch traced here: 201 us
  starting transfers between devices  66.9 us (33%)
  waiting for transfers between devices  59.7 us (29%)
  local copies, waits for them, and re-layouts  28.6 us (14%)
  other arithmetic  22.2 us (11%)
  loops' own time  14.8 us (7%)
  matrix products  6.54 us (3%)
  between operations  2.28 us (1%)
    ppermute x14, waiting for transfers between devices, scatter_chunks(): moved = lax.ppermute(other, axis, swap_pairs(axis, j))  29.6 us
    ppermute x14, starting transfers between devices, gather_chunks(): recv = lax.ppermute(buf, axis, swap_pairs(axis, j))  24 us
    ppermute x14, waiting for transfers between devices, gather_chunks(): recv = lax.ppermute(buf, axis, swap_pairs(axis, j))  23.1 us
    ppermute x14, starting transfers between devices, scatter_chunks(): moved = lax.ppermute(other, axis, swap_pairs(axis, j))  20.6 us
    another operation x1, loops' own time, body(): grad_out = lax.cond(segment == 0, lead_branch, lead_still)  13.3 us
    ppermute x4, starting transfers between devices, rows_sum(): total = total + lax.ppermute(total, 'rows', swap_pairs('rows', j))  7.21 us
    reshape x1, local copies, waits for them, and re-layouts, spread(): flat_term = (term / images).reshape(shards, len(SCATTER_ORDERS), 8, -1)  7.13 us
    ppermute x2, starting transfers between devices, extended_2(): lax.ppermute(lax.slice_in_dim(block, 0, width, axis=dim), axis, backward)  6.19 us
  transfers between devices with their start and end apart: 38, of which 22 were waited for; matrix products, arithmetic and copies ran while one was open for 27% of the time, Pallas kernels for 0%

profile of v7, /device:TPU:8, one launch (start us, length us, event | category | flops | bytes accessed | tf_op | source)
XLA Modules:
  0.0 201.0 jit_solution(1723246207410789376)
XLA Ops:
  1.7 3.0 %collective-permute-start.36 = (bf16[16,253]{1,0:T(8,128)(2,1)S(1)}, bf16[16,253]{1,0:T(8,128)(2,1)S(1)}, u32[]{:S(2)}, u32[]{:S(2)}) collective-permute-start(bf16[16,253]{1,0:T(8,128)(2,1)S(1)} %split.9), channel_id=1, source_target_pairs={{0,128},{8,136},{16,144},{24,152},{32,160},{40,168},{48,176},{56,1... | collective-permute-start | bytes 24296 | tf_op jit(solution)/shard_map/ppermute | solution.py:41
  4.7 7.2 %collective-permute-start.29 = (bf16[16,254]{1,0:T(8,128)(2,1)S(1)}, bf16[16,254]{1,0:T(8,128)(2,1)S(1)}, u32[]{:S(2)}, u32[]{:S(2)}) collective-permute-start(bf16[16,254]{1,0:T(8,128)(2,1)S(1)} %split.8), channel_id=1, source_target_pairs={{0,32},{8,40},{16,48},{24,56},{32,0},{40,8},{48,16},{56,24},{64,96... | collective-permute-start | bytes 24392 | tf_op jit(solution)/shard_map/ppermute | solution.py:41
  12.1 2.4 %collective-permute-start.37 = (bf16[2,16,253]{2,1,0:T(8,128)(2,1)S(1)}, bf16[2,16,253]{2,1,0:T(8,128)(2,1)S(1)}, u32[]{:S(2)}, u32[]{:S(2)}) collective-permute-start(bf16[2,16,253]{2,1,0:T(8,128)(2,1)S(1)} %pad_maximum_fusion.16), channel_id=1, source_target_pairs={{0,2},{1,3},{2,0},{3,1},{4,6},{5,7},{6,4},{7,5},{8,10},{9,11},{10,... | collective-permute-start | bytes 48584 | tf_op jit(solution)/shard_map/ppermute | solution.py:41
  15.1 2.3 %collective-permute-done.37 = bf16[2,16,253]{2,1,0:T(8,128)(2,1)S(1)} collective-permute-done((bf16[2,16,253]{2,1,0:T(8,128)(2,1)S(1)}, bf16[2,16,253]{2,1,0:T(8,128)(2,1)S(1)}, u32[]{:S(2)}, u32[]{:S(2)}) %collective-permute-start.37) | collective-permute-done | bytes 16224 | tf_op jit(solution)/shard_map/ppermute | solution.py:41
  17.4 2.8 %collective-permute-start.38 = (bf16[2,2,16,253]{3,2,1,0:T(8,128)(2,1)S(1)}, bf16[2,2,16,253]{3,2,1,0:T(8,128)(2,1)S(1)}, u32[]{:S(2)}, u32[]{:S(2)}) collective-permute-start(bf16[2,2,16,253]{3,2,1,0:T(8,128)(2,1)S(1)} %pad_maximum_fusion.14), channel_id=1, source_target_pairs={{0,32},{8,40},{16,48},{24,56},{32,0},{40,8},{48,16},{56,24},{64,96... | collective-permute-start | bytes 97160 | tf_op jit(solution)/shard_map/ppermute | solution.py:41
  21.8 3.8 %collective-permute-done.38 = bf16[2,2,16,253]{3,2,1,0:T(8,128)(2,1)S(1)} collective-permute-done((bf16[2,2,16,253]{3,2,1,0:T(8,128)(2,1)S(1)}, bf16[2,2,16,253]{3,2,1,0:T(8,128)(2,1)S(1)}, u32[]{:S(2)}, u32[]{:S(2)}) %collective-permute-start.38) | collective-permute-done | bytes 32416 | tf_op jit(solution)/shard_map/ppermute | solution.py:41
  27.1 2.4 %collective-permute-start.32 = (bf16[2,2,2,16,254]{4,3,2,1,0:T(8,128)(2,1)S(1)}, bf16[2,2,2,16,254]{4,3,2,1,0:T(8,128)(2,1)S(1)}, u32[]{:S(2)}, u32[]{:S(2)}) collective-permute-start(bf16[2,2,2,16,254]{4,3,2,1,0:T(8,128)(2,1)S(1)} %pad_maximum_fusion.11), channel_id=1, source_target_pairs={{0,2},{1,3},{2,0},{3,1},{4,6},{5,7},{6,4},{7,5},{8,10},{9,11},{10,... | collective-permute-start | bytes 195080 | tf_op jit(solution)/shard_map/ppermute | solution.py:41
  29.5 2.1 %collective-permute-done.39 = bf16[2,2,2,16,253]{4,3,2,1,0:T(8,128)(2,1)S(1)} collective-permute-done((bf16[2,2,2,16,253]{4,3,2,1,0:T(8,128)(2,1)S(1)}, bf16[2,2,2,16,253]{4,3,2,1,0:T(8,128)(2,1)S(1)}, u32[]{:S(2)}, u32[]{:S(2)}) %collective-permute-start.39) | collective-permute-done | bytes 64800 | tf_op jit(solution)/shard_map/ppermute | solution.py:41
  34.1 2.5 %collective-permute-done.40 = bf16[2,2,2,2,16,253]{5,4,3,2,1,0:T(8,128)(2,1)S(1)} collective-permute-done((bf16[2,2,2,2,16,253]{5,4,3,2,1,0:T(8,128)(2,1)S(1)}, bf16[2,2,2,2,16,253]{5,4,3,2,1,0:T(8,128)(2,1)S(1)}, u32[]{:S(2)}, u32[]{:S(2)}) %collective-permute-start.40) | collective-permute-done | bytes 129568 | tf_op jit(solution)/shard_map/ppermute | solution.py:41
  37.4 2.5 %collective-permute-done.33 = bf16[2,2,2,2,16,254]{5,4,3,2,1,0:T(8,128)(2,1)S(1)} collective-permute-done((bf16[2,2,2,2,16,254]{5,4,3,2,1,0:T(8,128)(2,1)S(1)}, bf16[2,2,2,2,16,254]{5,4,3,2,1,0:T(8,128)(2,1)S(1)}, u32[]{:S(2)}, u32[]{:S(2)}) %collective-permute-start.33) | collective-permute-done | bytes 130080 | tf_op jit(solution)/shard_map/ppermute | solution.py:41
  40.1 3.2 %collective-permute-done.41 = bf16[2,2,2,2,2,16,253]{6,5,4,3,2,1,0:T(8,128)(2,1)S(1)} collective-permute-done((bf16[2,2,2,2,2,16,253]{6,5,4,3,2,1,0:T(8,128)(2,1)S(1)}, bf16[2,2,2,2,2,16,253]{6,5,4,3,2,1,0:T(8,128)(2,1)S(1)}, u32[]{:S(2)}, u32[]{:S(2)}) %collective-permute-start.41) | collective-permute-done | bytes 259104 | tf_op jit(solution)/shard_map/ppermute | solution.py:41
  43.8 5.5 %collective-permute-done.34 = bf16[2,2,2,2,2,16,254]{6,5,4,3,2,1,0:T(8,128)(2,1)S(1)} collective-permute-done((bf16[2,2,2,2,2,16,254]{6,5,4,3,2,1,0:T(8,128)(2,1)S(1)}, bf16[2,2,2,2,2,16,254]{6,5,4,3,2,1,0:T(8,128)(2,1)S(1)}, u32[]{:S(2)}, u32[]{:S(2)}) %collective-permute-start.34) | collective-permute-done | bytes 260128 | tf_op jit(solution)/shard_map/ppermute | solution.py:41
  51.5 3.6 %collective-permute-start.45 = (bf16[2,32,2496]{2,1,0:T(8,128)(2,1)}, bf16[2,32,2496]{2,1,0:T(8,128)(2,1)}, u32[]{:S(2)}, u32[]{:S(2)}) collective-permute-start(bf16[2,32,2496]{2,1,0:T(8,128)(2,1)} %get-tuple-element.232), channel_id=1, source_target_pairs={{1,0},{2,1},{3,2},{5,4},{6,5},{7,6},{9,8},{10,9},{11,10},{13,12},{... | collective-permute-start | bytes 958472 | tf_op jit(solution)/shard_map/ppermute | solution.py:15
  55.1 2.4 %collective-permute-start.44 = (bf16[2,32,2496]{2,1,0:T(8,128)(2,1)}, bf16[2,32,2496]{2,1,0:T(8,128)(2,1)}, u32[]{:S(2)}, u32[]{:S(2)}) collective-permute-start(bf16[2,32,2496]{2,1,0:T(8,128)(2,1)} %get-tuple-element.231), channel_id=1, source_target_pairs={{0,1},{1,2},{2,3},{4,5},{5,6},{6,7},{8,9},{9,10},{10,11},{12,13},{... | collective-permute-start | bytes 958472 | tf_op jit(solution)/shard_map/ppermute | solution.py:12
  57.6 15.5 %conditional.8 = (bf16[128,416]{0,1:T(8,128)(2,1)}, bf16[4,32,416]{2,1,0:T(8,128)(2,1)S(1)}) conditional(s32[]{:T(128)} %convert_element_type.291, () %tuple.71, (bf16[1,4,32,384]{3,2,1,0:T(8,128)(2,1)S(1)}, bf16[1,2,16,384]{3,2,1,0:T(8,128)(2,1)S(1)}, bf16[1,1,8,384]{3,2,1,0:T(8,128)(2,1)S(1)}, bf16[416,384]{1,0:T(8,128)(2,1)S(1)}) %tuple.195), branch_computations={%region_0.1_spmd, %region_1.2_spmd} | conditional | flops 41138176 | bytes 1972240 | solution.py:199
  76.2 2.2 %pad_maximum_fusion.2 = bf16[128,16,507]{2,1,0:T(8,128)(2,1)} fusion(bf16[128,16,253]{2,1,0:T(8,128)(2,1)S(1)} %bitcast.294, bf16[128,16,254]{2,1,0:T(8,128)(2,1)S(1)} %bitcast.295), kind=kLoop, calls=%fused_computation.212 | loop fusion | flops 4153344 | bytes 4153344 | tf_op jit(solution)/shard_map/concatenate | solution.py:53
  78.4 5.2 %reshape_reshape.3 = bf16[416,2496]{1,0:T(8,128)(2,1)S(1)} reshape(bf16[128,16,507]{2,1,0:T(8,128)(2,1)} %pad_maximum_fusion.2) | data formatting | bytes 4153344 | tf_op jit(solution)/shard_map/reshape;reshape | solution.py:158
  83.7 2.0 %conditional.9 = (bf16[128,2496]{0,1:T(8,128)(2,1)S(1)}) conditional(s32[]{:T(128)} %convert_element_type.291, () %tuple.75, (bf16[128,416]{0,1:T(8,128)(2,1)}, bf16[416,2496]{1,0:T(8,128)(2,1)S(1)}) %tuple.76), branch_computations={%region_2.3_spmd, %region_3.4_spmd} | conditional | flops 266133504 | bytes 2822152 | solution.py:207
  83.7 2.0 %convolution_convert_fusion.1 = bf16[128,2496]{0,1:T(8,128)(2,1)S(1)} fusion(bf16[128,416]{0,1:T(8,128)(2,1)} %get-tuple-element.162, bf16[416,2496]{1,0:T(8,128)(2,1)S(1)} %get-tuple-element.89), kind=kOutput, calls=%fused_computation.6 | convolution fusion | flops 266133504 | bytes 2822144 | tf_op jit(solution)/shard_map/cond/branch_1_fun/dot_general | solution.py:202
  88.1 2.0 collective-permute-start.28
  92.7 2.4 %collective-permute-start.46 = (f32[1,2496]{1,0:T(1,128)S(1)}, f32[1,2496]{1,0:T(1,128)S(1)}, u32[]{:S(2)}, u32[]{:S(2)}) collective-permute-start(f32[1,2496]{1,0:T(1,128)S(1)} %get-tuple-element.133), channel_id=1, source_target_pairs={{0,1},{1,0},{2,3},{3,2},{4,5},{5,4},{6,7},{7,6},{8,9},{9,8},{10,11... | collective-permute-start | bytes 29960 | tf_op jit(solution)/shard_map/ppermute | solution.py:83
  96.0 3.6 %conditional.10 = (f32[416,2496]{1,0:T(8,128)}) conditional(s32[]{:T(128)} %convert_element_type.291, () %tuple.74, (bf16[1,1,4,32,2496]{4,3,2,1,0:T(8,128)(2,1)S(1)}, bf16[128,416]{0,1:T(8,128)(2,1)}) %tuple.184), branch_computations={%region_4.5_spmd, %region_5.6_spmd} | conditional | flops 265814016 | bytes 4898824 | solution.py:230
  96.0 3.6 %fusion.48 = f32[416,2496]{1,0:T(8,128)} fusion(bf16[128,416]{0,1:T(8,128)(2,1)} %get-tuple-element.165, bf16[128,2496]{1,0:T(8,128)(2,1)S(1)} %bitcast.291), kind=kOutput, calls=%fused_computation.263 | convolution fusion | flops 265814016 | bytes 4898816 | tf_op jit(solution)/shard_map/cond/branch_1_fun/dot_general | solution.py:223
  99.6 74.7 %conditional.11 = (f32[8112]{0:T(1024)S(1)}) conditional(s32[]{:T(128)} %convert_element_type.291, () %tuple.73, f32[416,2496]{1,0:T(8,128)} %get-tuple-element.274), branch_computations={%region_6.7_spmd, %region_7.8_spmd} | conditional | flops 2855492 | bytes 59543540 | solution.py:231
  99.6 4.6 %broadcast_multiply_fusion = f32[416,2496]{1,0:T(8,128)} fusion(f32[416,2496]{1,0:T(8,128)} %param.7), kind=kLoop, calls=%fused_computation.7 | loop fusion | flops 1038336 | bytes 8306688 | tf_op jit(solution)/shard_map/cond/branch_1_fun/div | solution.py:213
  104.1 7.1 %reshape.168 = f32[128,2,8,507]{3,2,1,0:T(8,128)} reshape(f32[416,2496]{1,0:T(8,128)} %broadcast_multiply_fusion) | data formatting | bytes 8306688 | tf_op jit(solution)/shard_map/cond/branch_1_fun/reshape | solution.py:213
  111.3 4.6 %fusion.44 = (f32[128,1,8,507]{3,2,1,0:T(8,128)}, f32[128,1,8,507]{3,2,1,0:T(8,128)}) fusion(f32[128,2,8,507]{3,2,1,0:T(8,128)} %reshape.168), kind=kLoop, calls=%fused_computation.259 | loop fusion | bytes 8306688 | tf_op jit(solution)/shard_map/cond/branch_1_fun/slice | solution.py:76
  115.9 2.1 %fusion.4 = bf16[2,2,2,2,2,16,507]{6,5,4,3,2,1,0:T(8,128)(2,1)} fusion(f32[2,2,2,2,2,2,2,8,507]{8,7,6,5,4,3,2,1,0:T(8,128)} %bitcast.287, s32[]{:T(128)S(6)} %select_n.226), kind=kLoop, calls=%fused_computation.13 | loop fusion | bytes 1038340 | tf_op jit(solution)/shard_map/cond/branch_1_fun/convert_element_type | solution.py:68
  118.0 2.1 %fusion.3 = bf16[2,2,2,2,2,16,507]{6,5,4,3,2,1,0:T(8,128)(2,1)} fusion(f32[2,2,2,2,2,2,2,8,507]{8,7,6,5,4,3,2,1,0:T(8,128)} %bitcast.283, s32[]{:T(128)S(6)} %select_n.224), kind=kLoop, calls=%fused_computation.12 | loop fusion | bytes 1038340 | tf_op jit(solution)/shard_map/cond/branch_1_fun/convert_element_type | solution.py:68
  120.8 6.7 %collective-permute-done.7 = bf16[2,2,2,2,2,16,507]{6,5,4,3,2,1,0:T(8,128)(2,1)} collective-permute-done((bf16[2,2,2,2,2,16,507]{6,5,4,3,2,1,0:T(8,128)(2,1)}, bf16[2,2,2,2,2,16,507]{6,5,4,3,2,1,0:T(8,128)(2,1)}, u32[]{:S(2)}, u32[]{:S(2)}) %collective-permute-start.7) | collective-permute-done | bytes 519200 | tf_op jit(solution)/shard_map/cond/branch_1_fun/ppermute | solution.py:69
  131.0 2.0 collective-permute-start.1
  133.0 2.5 %collective-permute-done.8 = bf16[2,2,2,2,16,507]{5,4,3,2,1,0:T(8,128)(2,1)S(1)} collective-permute-done((bf16[2,2,2,2,16,507]{5,4,3,2,1,0:T(8,128)(2,1)S(1)}, bf16[2,2,2,2,16,507]{5,4,3,2,1,0:T(8,128)(2,1)S(1)}, u32[]{:S(2)}, u32[]{:S(2)}) %collective-permute-start.8) | collective-permute-done | bytes 259616 | tf_op jit(solution)/shard_map/cond/branch_1_fun/ppermute | solution.py:69
  139.1 3.0 %collective-permute-done.9 = f32[2,2,2,2,8,507]{5,4,3,2,1,0:T(8,128)S(1)} collective-permute-done((f32[2,2,2,2,8,507]{5,4,3,2,1,0:T(8,128)S(1)}, f32[2,2,2,2,8,507]{5,4,3,2,1,0:T(8,128)S(1)}, u32[]{:S(2)}, u32[]{:S(2)}) %collective-permute-start.9) | collective-permute-done | bytes 259616 | tf_op jit(solution)/shard_map/cond/branch_1_fun/ppermute | solution.py:69
  144.1 2.6 %collective-permute-start.3 = (f32[2,2,2,8,507]{4,3,2,1,0:T(8,128)S(1)}, f32[2,2,2,8,507]{4,3,2,1,0:T(8,128)S(1)}, u32[]{:S(2)}, u32[]{:S(2)}) collective-permute-start(f32[2,2,2,8,507]{4,3,2,1,0:T(8,128)S(1)} %dynamic-slice_bitcast_fusion.3), channel_id=1, source_target_pairs={{0,2},{1,3},{2,0},{3,1},{4,6},{5,7},{6,4},{7,5},{8,10},{9,11},{10,... | collective-permute-start | bytes 389384 | tf_op jit(solution)/shard_map/cond/branch_1_fun/ppermute | solution.py:69
  146.7 2.3 %collective-permute-done.10 = f32[2,2,2,8,507]{4,3,2,1,0:T(8,128)S(1)} collective-permute-done((f32[2,2,2,8,507]{4,3,2,1,0:T(8,128)S(1)}, f32[2,2,2,8,507]{4,3,2,1,0:T(8,128)S(1)}, u32[]{:S(2)}, u32[]{:S(2)}) %collective-permute-start.10) | collective-permute-done | bytes 129824 | tf_op jit(solution)/shard_map/cond/branch_1_fun/ppermute | solution.py:69
  149.0 2.1 %collective-permute-start.11 = (f32[2,2,8,507]{3,2,1,0:T(8,128)S(1)}, f32[2,2,8,507]{3,2,1,0:T(8,128)S(1)}, u32[]{:S(2)}, u32[]{:S(2)}) collective-permute-start(f32[2,2,8,507]{3,2,1,0:T(8,128)S(1)} %dynamic-slice_bitcast_fusion.4), channel_id=1, source_target_pairs={{0,32},{8,40},{16,48},{24,56},{32,0},{40,8},{48,16},{56,24},{64,96... | collective-permute-start | bytes 194696 | tf_op jit(solution)/shard_map/cond/branch_1_fun/ppermute | solution.py:69
  151.2 1.9 collective-permute-start.4
  153.1 5.6 %collective-permute-done.11 = f32[2,2,8,507]{3,2,1,0:T(8,128)S(1)} collective-permute-done((f32[2,2,8,507]{3,2,1,0:T(8,128)S(1)}, f32[2,2,8,507]{3,2,1,0:T(8,128)S(1)}, u32[]{:S(2)}, u32[]{:S(2)}) %collective-permute-start.11) | collective-permute-done | bytes 64928 | tf_op jit(solution)/shard_map/cond/branch_1_fun/ppermute | solution.py:69
  158.7 1.8 collective-permute-start.12
  161.9 2.3 %collective-permute-done.12 = f32[2,8,507]{2,1,0:T(8,128)S(1)} collective-permute-done((f32[2,8,507]{2,1,0:T(8,128)S(1)}, f32[2,8,507]{2,1,0:T(8,128)S(1)}, u32[]{:S(2)}, u32[]{:S(2)}) %collective-permute-start.12) | collective-permute-done | bytes 32480 | tf_op jit(solution)/shard_map/cond/branch_1_fun/ppermute | solution.py:69
  166.0 3.1 %collective-permute-start.6 = (f32[8,507]{1,0:T(8,128)S(1)}, f32[8,507]{1,0:T(8,128)S(1)}, u32[]{:S(2)}, u32[]{:S(2)}) collective-permute-start(f32[8,507]{1,0:T(8,128)S(1)} %dynamic-slice_bitcast_fusion.9), channel_id=1, source_target_pairs={{0,32},{8,40},{16,48},{24,56},{32,0},{40,8},{48,16},{56,24},{64,96... | collective-permute-start | bytes 48680 | tf_op jit(solution)/shard_map/cond/branch_1_fun/ppermute | solution.py:69
  169.6 4.2 %collective-permute-done.6 = f32[8,507]{1,0:T(8,128)S(1)} collective-permute-done((f32[8,507]{1,0:T(8,128)S(1)}, f32[8,507]{1,0:T(8,128)S(1)}, u32[]{:S(2)}, u32[]{:S(2)}) %collective-permute-start.6) | collective-permute-done | bytes 16256 | tf_op jit(solution)/shard_map/cond/branch_1_fun/ppermute | solution.py:69
  179.4 2.3 %collective-permute-start.49 = (f32[1,2496]{1,0:T(1,128)S(1)}, f32[1,2496]{1,0:T(1,128)S(1)}, u32[]{:S(2)}, u32[]{:S(2)}) collective-permute-start(f32[1,2496]{1,0:T(1,128)S(1)} %reshape_add_fusion), channel_id=1, source_target_pairs={{0,2},{1,3},{2,0},{3,1},{4,6},{5,7},{6,4},{7,5},{8,10},{9,11},{10,... | collective-permute-start | bytes 29960 | tf_op jit(solution)/shard_map/ppermute | solution.py:83
  181.7 2.1 %copy.60 = bf16[2496,104]{1,0:T(8,128)(2,1)} copy(bf16[2496,104]{0,1:T(8,128)(2,1)} %param.34) | data formatting | bytes 1038336 | tf_op args[8]
  186.3 2.6 %collective-permute-start.51 = (bf16[2,32,2496]{2,1,0:T(8,128)(2,1)S(1)}, bf16[2,32,2496]{2,1,0:T(8,128)(2,1)S(1)}, u32[]{:S(2)}, u32[]{:S(2)}) collective-permute-start(bf16[2,32,2496]{2,1,0:T(8,128)(2,1)S(1)} %get-tuple-element.230), channel_id=1, source_target_pairs={{1,0},{2,1},{3,2},{5,4},{6,5},{7,6},{9,8},{10,9},{11,10},{13,12},{... | collective-permute-start | bytes 958472 | tf_op jit(solution)/shard_map/ppermute | solution.py:15
  188.9 3.3 %collective-permute-start.50 = (bf16[2,32,2496]{2,1,0:T(8,128)(2,1)S(1)}, bf16[2,32,2496]{2,1,0:T(8,128)(2,1)S(1)}, u32[]{:S(2)}, u32[]{:S(2)}) collective-permute-start(bf16[2,32,2496]{2,1,0:T(8,128)(2,1)S(1)} %get-tuple-element.229), channel_id=1, source_target_pairs={{0,1},{1,2},{2,3},{4,5},{5,6},{6,7},{8,9},{9,10},{10,11},{12,13},{... | collective-permute-start | bytes 958472 | tf_op jit(solution)/shard_map/ppermute | solution.py:12
  192.2 3.1 %collective-permute-done.51 = bf16[2,32,2496]{2,1,0:T(8,128)(2,1)S(1)} collective-permute-done((bf16[2,32,2496]{2,1,0:T(8,128)(2,1)S(1)}, bf16[2,32,2496]{2,1,0:T(8,128)(2,1)S(1)}, u32[]{:S(2)}, u32[]{:S(2)}) %collective-permute-start.51) | collective-permute-done | bytes 319520 | tf_op jit(solution)/shard_map/ppermute | solution.py:15
  195.3 2.6 %collective-permute-done.50 = bf16[2,32,2496]{2,1,0:T(8,128)(2,1)S(1)} collective-permute-done((bf16[2,32,2496]{2,1,0:T(8,128)(2,1)S(1)}, bf16[2,32,2496]{2,1,0:T(8,128)(2,1)S(1)}, u32[]{:S(2)}, u32[]{:S(2)}) %collective-permute-start.50) | collective-permute-done | bytes 319520 | tf_op jit(solution)/shard_map/ppermute | solution.py:12
  (170 shorter events, 45.8 us)
Async XLA Ops:
  1.7 10.3 %collective-permute-start.36 = (bf16[16,253]{1,0:T(8,128)(2,1)S(1)}, bf16[16,253]{1,0:T(8,128)(2,1)S(1)}, u32[]{:S(2)}, u32[]{:S(2)}) collective-permute-start(bf16[16,253]{1,0:T(8,128)(2,1)S(1)} %split.9), channel_id=1, source_target_pairs={{0,128},{8,136},{16,144},{24,152},{32,160},{40,168},{48,176},{56,1... | collective-permute-start | bytes 24296 | tf_op jit(solution)/shard_map/ppermute | solution.py:41
  4.7 9.7 %collective-permute-start.29 = (bf16[16,254]{1,0:T(8,128)(2,1)S(1)}, bf16[16,254]{1,0:T(8,128)(2,1)S(1)}, u32[]{:S(2)}, u32[]{:S(2)}) collective-permute-start(bf16[16,254]{1,0:T(8,128)(2,1)S(1)} %split.8), channel_id=1, source_target_pairs={{0,32},{8,40},{16,48},{24,56},{32,0},{40,8},{48,16},{56,24},{64,96... | collective-permute-start | bytes 24392 | tf_op jit(solution)/shard_map/ppermute | solution.py:41
  12.1 5.3 %collective-permute-start.37 = (bf16[2,16,253]{2,1,0:T(8,128)(2,1)S(1)}, bf16[2,16,253]{2,1,0:T(8,128)(2,1)S(1)}, u32[]{:S(2)}, u32[]{:S(2)}) collective-permute-start(bf16[2,16,253]{2,1,0:T(8,128)(2,1)S(1)} %pad_maximum_fusion.16), channel_id=1, source_target_pairs={{0,2},{1,3},{2,0},{3,1},{4,6},{5,7},{6,4},{7,5},{8,10},{9,11},{10,... | collective-permute-start | bytes 48584 | tf_op jit(solution)/shard_map/ppermute | solution.py:41
  14.5 5.7 %collective-permute-start.30 = (bf16[2,16,254]{2,1,0:T(8,128)(2,1)S(1)}, bf16[2,16,254]{2,1,0:T(8,128)(2,1)S(1)}, u32[]{:S(2)}, u32[]{:S(2)}) collective-permute-start(bf16[2,16,254]{2,1,0:T(8,128)(2,1)S(1)} %pad_maximum_fusion.15), channel_id=1, source_target_pairs={{0,128},{8,136},{16,144},{24,152},{32,160},{40,168},{48,176},{56,1... | collective-permute-start | bytes 48776 | tf_op jit(solution)/shard_map/ppermute | solution.py:41
  17.4 8.1 %collective-permute-start.38 = (bf16[2,2,16,253]{3,2,1,0:T(8,128)(2,1)S(1)}, bf16[2,2,16,253]{3,2,1,0:T(8,128)(2,1)S(1)}, u32[]{:S(2)}, u32[]{:S(2)}) collective-permute-start(bf16[2,2,16,253]{3,2,1,0:T(8,128)(2,1)S(1)} %pad_maximum_fusion.14), channel_id=1, source_target_pairs={{0,32},{8,40},{16,48},{24,56},{32,0},{40,8},{48,16},{56,24},{64,96... | collective-permute-start | bytes 97160 | tf_op jit(solution)/shard_map/ppermute | solution.py:41
  20.2 6.8 %collective-permute-start.31 = (bf16[2,2,16,254]{3,2,1,0:T(8,128)(2,1)S(1)}, bf16[2,2,16,254]{3,2,1,0:T(8,128)(2,1)S(1)}, u32[]{:S(2)}, u32[]{:S(2)}) collective-permute-start(bf16[2,2,16,254]{3,2,1,0:T(8,128)(2,1)S(1)} %pad_maximum_fusion.13), channel_id=1, source_target_pairs={{0,16},{8,24},{16,0},{24,8},{32,48},{40,56},{48,32},{56,40},{64,80... | collective-permute-start | bytes 97544 | tf_op jit(solution)/shard_map/ppermute | solution.py:41
  25.6 6.0 %collective-permute-start.39 = (bf16[2,2,2,16,253]{4,3,2,1,0:T(8,128)(2,1)S(1)}, bf16[2,2,2,16,253]{4,3,2,1,0:T(8,128)(2,1)S(1)}, u32[]{:S(2)}, u32[]{:S(2)}) collective-permute-start(bf16[2,2,2,16,253]{4,3,2,1,0:T(8,128)(2,1)S(1)} %pad_maximum_fusion.12), channel_id=1, source_target_pairs={{0,16},{8,24},{16,0},{24,8},{32,48},{40,56},{48,32},{56,40},{64,80... | collective-permute-start | bytes 194312 | tf_op jit(solution)/shard_map/ppermute | solution.py:41
  27.1 6.3 %collective-permute-start.32 = (bf16[2,2,2,16,254]{4,3,2,1,0:T(8,128)(2,1)S(1)}, bf16[2,2,2,16,254]{4,3,2,1,0:T(8,128)(2,1)S(1)}, u32[]{:S(2)}, u32[]{:S(2)}) collective-permute-start(bf16[2,2,2,16,254]{4,3,2,1,0:T(8,128)(2,1)S(1)} %pad_maximum_fusion.11), channel_id=1, source_target_pairs={{0,2},{1,3},{2,0},{3,1},{4,6},{5,7},{6,4},{7,5},{8,10},{9,11},{10,... | collective-permute-start | bytes 195080 | tf_op jit(solution)/shard_map/ppermute | solution.py:41
  31.6 5.1 %collective-permute-start.40 = (bf16[2,2,2,2,16,253]{5,4,3,2,1,0:T(8,128)(2,1)S(1)}, bf16[2,2,2,2,16,253]{5,4,3,2,1,0:T(8,128)(2,1)S(1)}, u32[]{:S(2)}, u32[]{:S(2)}) collective-permute-start(bf16[2,2,2,2,16,253]{5,4,3,2,1,0:T(8,128)(2,1)S(1)} %pad_maximum_fusion.10), channel_id=1, source_target_pairs={{0,1},{1,0},{2,3},{3,2},{4,5},{5,4},{6,7},{7,6},{8,9},{9,8},{10,11... | collective-permute-start | bytes 388616 | tf_op jit(solution)/shard_map/ppermute | solution.py:41
  33.5 6.4 %collective-permute-start.33 = (bf16[2,2,2,2,16,254]{5,4,3,2,1,0:T(8,128)(2,1)S(1)}, bf16[2,2,2,2,16,254]{5,4,3,2,1,0:T(8,128)(2,1)S(1)}, u32[]{:S(2)}, u32[]{:S(2)}) collective-permute-start(bf16[2,2,2,2,16,254]{5,4,3,2,1,0:T(8,128)(2,1)S(1)} %pad_maximum_fusion.9), channel_id=1, source_target_pairs={{0,64},{8,72},{16,80},{24,88},{32,96},{40,104},{48,112},{56,120},{... | collective-permute-start | bytes 390152 | tf_op jit(solution)/shard_map/ppermute | solution.py:41
  36.8 6.6 %collective-permute-start.41 = (bf16[2,2,2,2,2,16,253]{6,5,4,3,2,1,0:T(8,128)(2,1)S(1)}, bf16[2,2,2,2,2,16,253]{6,5,4,3,2,1,0:T(8,128)(2,1)S(1)}, u32[]{:S(2)}, u32[]{:S(2)}) collective-permute-start(bf16[2,2,2,2,2,16,253]{6,5,4,3,2,1,0:T(8,128)(2,1)S(1)} %pad_maximum_fusion.8), channel_id=1, source_target_pairs={{0,64},{8,72},{16,80},{24,88},{32,96},{40,104},{48,112},{56,120},{... | collective-permute-start | bytes 777224 | tf_op jit(solution)/shard_map/ppermute | solution.py:41
  40.0 9.3 %collective-permute-start.34 = (bf16[2,2,2,2,2,16,254]{6,5,4,3,2,1,0:T(8,128)(2,1)S(1)}, bf16[2,2,2,2,2,16,254]{6,5,4,3,2,1,0:T(8,128)(2,1)S(1)}, u32[]{:S(2)}, u32[]{:S(2)}) collective-permute-start(bf16[2,2,2,2,2,16,254]{6,5,4,3,2,1,0:T(8,128)(2,1)S(1)} %pad_maximum_fusion.7), channel_id=1, source_target_pairs={{0,8},{8,0},{16,24},{24,16},{32,40},{40,32},{48,56},{56,48},{64,72... | collective-permute-start | bytes 780296 | tf_op jit(solution)/shard_map/ppermute | solution.py:41
  43.5 29.6 %collective-permute-start.42 = (bf16[2,2,2,2,2,2,16,253]{7,6,5,4,3,2,1,0:T(8,128)(2,1)S(1)}, bf16[2,2,2,2,2,2,16,253]{7,6,5,4,3,2,1,0:T(8,128)(2,1)}, u32[]{:S(2)}, u32[]{:S(2)}) collective-permute-start(bf16[2,2,2,2,2,2,16,253]{7,6,5,4,3,2,1,0:T(8,128)(2,1)S(1)} %pad_maximum_fusion.6), channel_id=1, source_target_pairs={{0,8},{8,0},{16,24},{24,16},{32,40},{40,32},{48,56},{56,48},{64,72... | collective-permute-start | bytes 1554440 | tf_op jit(solution)/shard_map/ppermute | solution.py:41
  49.3 8.2 %copy-start.15 = (bf16[416,384]{1,0:T(8,128)(2,1)S(1)}, bf16[416,384]{1,0:T(8,128)(2,1)}, u32[]{:S(2)}) copy-start(bf16[416,384]{1,0:T(8,128)(2,1)} %param.31) | copy-start | bytes 958468
  49.4 8.2 %copy-start.18 = (bf16[1,4,32,384]{3,2,1,0:T(8,128)(2,1)S(1)}, bf16[1,4,32,384]{3,2,1,0:T(8,128)(2,1)}, u32[]{:S(2)}) copy-start(bf16[1,4,32,384]{3,2,1,0:T(8,128)(2,1)} %param.28) | copy-start | bytes 294916
  49.4 8.2 %copy-start.20 = (bf16[1,2,16,384]{3,2,1,0:T(8,128)(2,1)S(1)}, bf16[1,2,16,384]{3,2,1,0:T(8,128)(2,1)}, u32[]{:S(2)}) copy-start(bf16[1,2,16,384]{3,2,1,0:T(8,128)(2,1)} %param.29) | copy-start | bytes 73732
  49.4 8.2 %copy-start.21 = (bf16[1,1,8,384]{3,2,1,0:T(8,128)(2,1)S(1)}, bf16[1,1,8,384]{3,2,1,0:T(8,128)(2,1)}, u32[]{:S(2)}) copy-start(bf16[1,1,8,384]{3,2,1,0:T(8,128)(2,1)} %param.30) | copy-start | bytes 18436
  50.3 24.4 %collective-permute-start.35 = (bf16[2,2,2,2,2,2,16,254]{7,6,5,4,3,2,1,0:T(8,128)(2,1)}, bf16[2,2,2,2,2,2,16,254]{7,6,5,4,3,2,1,0:T(8,128)(2,1)}, u32[]{:S(2)}, u32[]{:S(2)}) collective-permute-start(bf16[2,2,2,2,2,2,16,254]{7,6,5,4,3,2,1,0:T(8,128)(2,1)} %pad_maximum_fusion.5), channel_id=1, source_target_pairs={{0,1},{1,0},{2,3},{3,2},{4,5},{5,4},{6,7},{7,6},{8,9},{9,8},{10,11... | collective-permute-start | bytes 1560584 | tf_op jit(solution)/shard_map/ppermute | solution.py:41
  51.5 39.5 %collective-permute-start.45 = (bf16[2,32,2496]{2,1,0:T(8,128)(2,1)}, bf16[2,32,2496]{2,1,0:T(8,128)(2,1)}, u32[]{:S(2)}, u32[]{:S(2)}) collective-permute-start(bf16[2,32,2496]{2,1,0:T(8,128)(2,1)} %get-tuple-element.232), channel_id=1, source_target_pairs={{1,0},{2,1},{3,2},{5,4},{6,5},{7,6},{9,8},{10,9},{11,10},{13,12},{... | collective-permute-start | bytes 958472 | tf_op jit(solution)/shard_map/ppermute | solution.py:15
  55.1 35.9 %collective-permute-start.44 = (bf16[2,32,2496]{2,1,0:T(8,128)(2,1)}, bf16[2,32,2496]{2,1,0:T(8,128)(2,1)}, u32[]{:S(2)}, u32[]{:S(2)}) collective-permute-start(bf16[2,32,2496]{2,1,0:T(8,128)(2,1)} %get-tuple-element.231), channel_id=1, source_target_pairs={{0,1},{1,2},{2,3},{4,5},{5,6},{6,7},{8,9},{9,10},{10,11},{12,13},{... | collective-permute-start | bytes 958472 | tf_op jit(solution)/shard_map/ppermute | solution.py:12
  86.8 8.3 %collective-permute-start.43 = (bf16[4,32,2496]{2,1,0:T(8,128)(2,1)}, bf16[4,32,2496]{2,1,0:T(8,128)(2,1)S(1)}, u32[]{:S(2)}, u32[]{:S(2)}) collective-permute-start(bf16[4,32,2496]{2,1,0:T(8,128)(2,1)} %bitcast.296), channel_id=1, source_target_pairs={{0,4},{1,5},{2,6},{3,7},{8,12},{9,13},{10,14},{11,15},{16,20},{17,... | collective-permute-start | bytes 1916936 | tf_op jit(solution)/shard_map/ppermute | solution.py:23
  88.1 7.0 %collective-permute-start.28 = (bf16[4,32,416]{2,1,0:T(8,128)(2,1)}, bf16[4,32,416]{2,1,0:T(8,128)(2,1)}, u32[]{:S(2)}, u32[]{:S(2)}) collective-permute-start(bf16[4,32,416]{2,1,0:T(8,128)(2,1)} %copy-done.17), channel_id=1, source_target_pairs={{0,4},{1,5},{2,6},{3,7},{8,12},{9,13},{10,14},{11,15},{16,20},{17,... | collective-permute-start | bytes 319496 | tf_op jit(solution)/shard_map/ppermute | solution.py:23
  92.7 84.2 %collective-permute-start.46 = (f32[1,2496]{1,0:T(1,128)S(1)}, f32[1,2496]{1,0:T(1,128)S(1)}, u32[]{:S(2)}, u32[]{:S(2)}) collective-permute-start(f32[1,2496]{1,0:T(1,128)S(1)} %get-tuple-element.133), channel_id=1, source_target_pairs={{0,1},{1,0},{2,3},{3,2},{4,5},{5,4},{6,7},{7,6},{8,9},{9,8},{10,11... | collective-permute-start | bytes 29960 | tf_op jit(solution)/shard_map/ppermute | solution.py:83
  99.6 74.7 %copy-start.9 = (f32[4,32,2496]{2,1,0:T(8,128)S(1)}, f32[4,32,2496]{2,1,0:T(8,128)}, u32[]{:S(2)}) copy-start(f32[4,32,2496]{2,1,0:T(8,128)} %copy-done.8) | copy-start | bytes 3833860
  117.9 9.5 %collective-permute-start.7 = (bf16[2,2,2,2,2,16,507]{6,5,4,3,2,1,0:T(8,128)(2,1)}, bf16[2,2,2,2,2,16,507]{6,5,4,3,2,1,0:T(8,128)(2,1)}, u32[]{:S(2)}, u32[]{:S(2)}) collective-permute-start(bf16[2,2,2,2,2,16,507]{6,5,4,3,2,1,0:T(8,128)(2,1)} %fusion.4), channel_id=1, source_target_pairs={{0,8},{8,0},{16,24},{24,16},{32,40},{40,32},{48,56},{56,48},{64,72... | collective-permute-start | bytes 1557512 | tf_op jit(solution)/shard_map/cond/branch_1_fun/ppermute | solution.py:69
  120.1 9.6 %collective-permute-start = (bf16[2,2,2,2,2,16,507]{6,5,4,3,2,1,0:T(8,128)(2,1)}, bf16[2,2,2,2,2,16,507]{6,5,4,3,2,1,0:T(8,128)(2,1)}, u32[]{:S(2)}, u32[]{:S(2)}) collective-permute-start(bf16[2,2,2,2,2,16,507]{6,5,4,3,2,1,0:T(8,128)(2,1)} %fusion.3), channel_id=1, source_target_pairs={{0,1},{1,0},{2,3},{3,2},{4,5},{5,4},{6,7},{7,6},{8,9},{9,8},{10,11... | collective-permute-start | bytes 1557512 | tf_op jit(solution)/shard_map/cond/branch_1_fun/ppermute | solution.py:69
  120.8 8.9 %copy-start.2 = (f32[128,1,8,507]{3,2,1,0:T(8,128)S(1)}, f32[128,1,8,507]{3,2,1,0:T(8,128)}, u32[]{:S(2)}) copy-start(f32[128,1,8,507]{3,2,1,0:T(8,128)} %get-tuple-element.219) | copy-start | bytes 6230020 | tf_op jit(solution)/shard_map/cond
  129.0 6.5 %collective-permute-start.8 = (bf16[2,2,2,2,16,507]{5,4,3,2,1,0:T(8,128)(2,1)S(1)}, bf16[2,2,2,2,16,507]{5,4,3,2,1,0:T(8,128)(2,1)S(1)}, u32[]{:S(2)}, u32[]{:S(2)}) collective-permute-start(bf16[2,2,2,2,16,507]{5,4,3,2,1,0:T(8,128)(2,1)S(1)} %fusion.6), channel_id=1, source_target_pairs={{0,64},{8,72},{16,80},{24,88},{32,96},{40,104},{48,112},{56,120},{... | collective-permute-start | bytes 778760 | tf_op jit(solution)/shard_map/cond/branch_1_fun/ppermute | solution.py:69
  131.0 6.5 %collective-permute-start.1 = (bf16[2,2,2,2,16,507]{5,4,3,2,1,0:T(8,128)(2,1)S(1)}, bf16[2,2,2,2,16,507]{5,4,3,2,1,0:T(8,128)(2,1)S(1)}, u32[]{:S(2)}, u32[]{:S(2)}) collective-permute-start(bf16[2,2,2,2,16,507]{5,4,3,2,1,0:T(8,128)(2,1)S(1)} %fusion.5), channel_id=1, source_target_pairs={{0,8},{8,0},{16,24},{24,16},{32,40},{40,32},{48,56},{56,48},{64,72... | collective-permute-start | bytes 778760 | tf_op jit(solution)/shard_map/cond/branch_1_fun/ppermute | solution.py:69
  135.6 6.5 %collective-permute-start.9 = (f32[2,2,2,2,8,507]{5,4,3,2,1,0:T(8,128)S(1)}, f32[2,2,2,2,8,507]{5,4,3,2,1,0:T(8,128)S(1)}, u32[]{:S(2)}, u32[]{:S(2)}) collective-permute-start(f32[2,2,2,2,8,507]{5,4,3,2,1,0:T(8,128)S(1)} %dynamic-slice_bitcast_fusion), channel_id=1, source_target_pairs={{0,1},{1,0},{2,3},{3,2},{4,5},{5,4},{6,7},{7,6},{8,9},{9,8},{10,11... | collective-permute-start | bytes 778760 | tf_op jit(solution)/shard_map/cond/branch_1_fun/ppermute | solution.py:69
  137.6 6.5 %collective-permute-start.2 = (f32[2,2,2,2,8,507]{5,4,3,2,1,0:T(8,128)S(1)}, f32[2,2,2,2,8,507]{5,4,3,2,1,0:T(8,128)S(1)}, u32[]{:S(2)}, u32[]{:S(2)}) collective-permute-start(f32[2,2,2,2,8,507]{5,4,3,2,1,0:T(8,128)S(1)} %dynamic-slice_bitcast_fusion.1), channel_id=1, source_target_pairs={{0,64},{8,72},{16,80},{24,88},{32,96},{40,104},{48,112},{56,120},{... | collective-permute-start | bytes 778760 | tf_op jit(solution)/shard_map/cond/branch_1_fun/ppermute | solution.py:69
  142.1 6.8 %collective-permute-start.10 = (f32[2,2,2,8,507]{4,3,2,1,0:T(8,128)S(1)}, f32[2,2,2,8,507]{4,3,2,1,0:T(8,128)S(1)}, u32[]{:S(2)}, u32[]{:S(2)}) collective-permute-start(f32[2,2,2,8,507]{4,3,2,1,0:T(8,128)S(1)} %dynamic-slice_bitcast_fusion.2), channel_id=1, source_target_pairs={{0,16},{8,24},{16,0},{24,8},{32,48},{40,56},{48,32},{56,40},{64,80... | collective-permute-start | bytes 389384 | tf_op jit(solution)/shard_map/cond/branch_1_fun/ppermute | solution.py:69
  144.1 7.0 %collective-permute-start.3 = (f32[2,2,2,8,507]{4,3,2,1,0:T(8,128)S(1)}, f32[2,2,2,8,507]{4,3,2,1,0:T(8,128)S(1)}, u32[]{:S(2)}, u32[]{:S(2)}) collective-permute-start(f32[2,2,2,8,507]{4,3,2,1,0:T(8,128)S(1)} %dynamic-slice_bitcast_fusion.3), channel_id=1, source_target_pairs={{0,2},{1,3},{2,0},{3,1},{4,6},{5,7},{6,4},{7,5},{8,10},{9,11},{10,... | collective-permute-start | bytes 389384 | tf_op jit(solution)/shard_map/cond/branch_1_fun/ppermute | solution.py:69
  149.0 9.7 %collective-permute-start.11 = (f32[2,2,8,507]{3,2,1,0:T(8,128)S(1)}, f32[2,2,8,507]{3,2,1,0:T(8,128)S(1)}, u32[]{:S(2)}, u32[]{:S(2)}) collective-permute-start(f32[2,2,8,507]{3,2,1,0:T(8,128)S(1)} %dynamic-slice_bitcast_fusion.4), channel_id=1, source_target_pairs={{0,32},{8,40},{16,48},{24,56},{32,0},{40,8},{48,16},{56,24},{64,96... | collective-permute-start | bytes 194696 | tf_op jit(solution)/shard_map/cond/branch_1_fun/ppermute | solution.py:69
  151.2 9.3 %collective-permute-start.4 = (f32[2,2,8,507]{3,2,1,0:T(8,128)S(1)}, f32[2,2,8,507]{3,2,1,0:T(8,128)S(1)}, u32[]{:S(2)}, u32[]{:S(2)}) collective-permute-start(f32[2,2,8,507]{3,2,1,0:T(8,128)S(1)} %dynamic-slice_bitcast_fusion.5), channel_id=1, source_target_pairs={{0,16},{8,24},{16,0},{24,8},{32,48},{40,56},{48,32},{56,40},{64,80... | collective-permute-start | bytes 194696 | tf_op jit(solution)/shard_map/cond/branch_1_fun/ppermute | solution.py:69
  158.7 5.5 %collective-permute-start.12 = (f32[2,8,507]{2,1,0:T(8,128)S(1)}, f32[2,8,507]{2,1,0:T(8,128)S(1)}, u32[]{:S(2)}, u32[]{:S(2)}) collective-permute-start(f32[2,8,507]{2,1,0:T(8,128)S(1)} %dynamic-slice_bitcast_fusion.6), channel_id=1, source_target_pairs={{0,2},{1,3},{2,0},{3,1},{4,6},{5,7},{6,4},{7,5},{8,10},{9,11},{10,... | collective-permute-start | bytes 97352 | tf_op jit(solution)/shard_map/cond/branch_1_fun/ppermute | solution.py:69
  160.5 5.5 %collective-permute-start.5 = (f32[2,8,507]{2,1,0:T(8,128)S(1)}, f32[2,8,507]{2,1,0:T(8,128)S(1)}, u32[]{:S(2)}, u32[]{:S(2)}) collective-permute-start(f32[2,8,507]{2,1,0:T(8,128)S(1)} %dynamic-slice_bitcast_fusion.7), channel_id=1, source_target_pairs={{0,128},{8,136},{16,144},{24,152},{32,160},{40,168},{48,176},{56,1... | collective-permute-start | bytes 97352 | tf_op jit(solution)/shard_map/cond/branch_1_fun/ppermute | solution.py:69
  164.2 5.3 %collective-permute-start.13 = (f32[8,507]{1,0:T(8,128)S(1)}, f32[8,507]{1,0:T(8,128)S(1)}, u32[]{:S(2)}, u32[]{:S(2)}) collective-permute-start(f32[8,507]{1,0:T(8,128)S(1)} %dynamic-slice_bitcast_fusion.8), channel_id=1, source_target_pairs={{0,128},{8,136},{16,144},{24,152},{32,160},{40,168},{48,176},{56,1... | collective-permute-start | bytes 48680 | tf_op jit(solution)/shard_map/cond/branch_1_fun/ppermute | solution.py:69
  166.0 7.7 %collective-permute-start.6 = (f32[8,507]{1,0:T(8,128)S(1)}, f32[8,507]{1,0:T(8,128)S(1)}, u32[]{:S(2)}, u32[]{:S(2)}) collective-permute-start(f32[8,507]{1,0:T(8,128)S(1)} %dynamic-slice_bitcast_fusion.9), channel_id=1, source_target_pairs={{0,32},{8,40},{16,48},{24,56},{32,0},{40,8},{48,16},{56,24},{64,96... | collective-permute-start | bytes 48680 | tf_op jit(solution)/shard_map/cond/branch_1_fun/ppermute | solution.py:69
  174.3 9.5 %copy-start.19 = (f32[8112]{0:T(1024)}, f32[8112]{0:T(1024)S(1)}, u32[]{:S(2)}) copy-start(f32[8112]{0:T(1024)S(1)} %get-tuple-element.275) | copy-start | bytes 97348
  175.6 3.8 %collective-permute-start.48 = (f32[1,2496]{1,0:T(1,128)S(1)}, f32[1,2496]{1,0:T(1,128)S(1)}, u32[]{:S(2)}, u32[]{:S(2)}) collective-permute-start(f32[1,2496]{1,0:T(1,128)S(1)} %stack.196), channel_id=1, source_target_pairs={{0,1},{1,0},{2,3},{3,2},{4,5},{5,4},{6,7},{7,6},{8,9},{9,8},{10,11... | collective-permute-start | bytes 29960 | tf_op jit(solution)/shard_map/ppermute | solution.py:83
  177.0 9.2 %collective-permute-start.47 = (f32[1,2496]{1,0:T(1,128)S(1)}, f32[1,2496]{1,0:T(1,128)S(1)}, u32[]{:S(2)}, u32[]{:S(2)}) collective-permute-start(f32[1,2496]{1,0:T(1,128)S(1)} %add.433), channel_id=1, source_target_pairs={{0,2},{1,3},{2,0},{3,1},{4,6},{5,7},{6,4},{7,5},{8,10},{9,11},{10,... | collective-permute-start | bytes 29960 | tf_op jit(solution)/shard_map/ppermute | solution.py:83
  179.4 6.8 %collective-permute-start.49 = (f32[1,2496]{1,0:T(1,128)S(1)}, f32[1,2496]{1,0:T(1,128)S(1)}, u32[]{:S(2)}, u32[]{:S(2)}) collective-permute-start(f32[1,2496]{1,0:T(1,128)S(1)} %reshape_add_fusion), channel_id=1, source_target_pairs={{0,2},{1,3},{2,0},{3,1},{4,6},{5,7},{6,4},{7,5},{8,10},{9,11},{10,... | collective-permute-start | bytes 29960 | tf_op jit(solution)/shard_map/ppermute | solution.py:83
  186.3 9.0 %collective-permute-start.51 = (bf16[2,32,2496]{2,1,0:T(8,128)(2,1)S(1)}, bf16[2,32,2496]{2,1,0:T(8,128)(2,1)S(1)}, u32[]{:S(2)}, u32[]{:S(2)}) collective-permute-start(bf16[2,32,2496]{2,1,0:T(8,128)(2,1)S(1)} %get-tuple-element.230), channel_id=1, source_target_pairs={{1,0},{2,1},{3,2},{5,4},{6,5},{7,6},{9,8},{10,9},{11,10},{13,12},{... | collective-permute-start | bytes 958472 | tf_op jit(solution)/shard_map/ppermute | solution.py:15
  188.9 9.0 %collective-permute-start.50 = (bf16[2,32,2496]{2,1,0:T(8,128)(2,1)S(1)}, bf16[2,32,2496]{2,1,0:T(8,128)(2,1)S(1)}, u32[]{:S(2)}, u32[]{:S(2)}) collective-permute-start(bf16[2,32,2496]{2,1,0:T(8,128)(2,1)S(1)} %get-tuple-element.229), channel_id=1, source_target_pairs={{0,1},{1,2},{2,3},{4,5},{5,6},{6,7},{8,9},{9,10},{10,11},{12,13},{... | collective-permute-start | bytes 958472 | tf_op jit(solution)/shard_map/ppermute | solution.py:12
  192.2 6.9 %copy-start.4 = (bf16[1,1,4,32,2496]{4,3,2,1,0:T(8,128)(2,1)S(1)}, bf16[1,1,4,32,2496]{4,3,2,1,0:T(8,128)(2,1)}, u32[]{:S(2)}) copy-start(bf16[1,1,4,32,2496]{4,3,2,1,0:T(8,128)(2,1)} %param.27) | copy-start | bytes 1916932
  192.2 6.9 %copy-start.13 = (f32[25,2496]{1,0:T(8,128)S(1)}, f32[25,2496]{1,0:T(8,128)}, u32[]{:S(2)}) copy-start(f32[25,2496]{1,0:T(8,128)} %copy-done.12) | copy-start | bytes 748804
  192.2 6.9 %copy-start.16 = (bf16[1,4,32,416]{3,2,1,0:T(8,128)(2,1)S(1)}, bf16[1,4,32,416]{3,2,1,0:T(8,128)(2,1)}, u32[]{:S(2)}) copy-start(bf16[1,4,32,416]{3,2,1,0:T(8,128)(2,1)} %param.26) | copy-start | bytes 319492
  (8 other events, 18.2 us)

commit v8 on v6

--- a/solution.py
+++ b/solution.py
@@ -53,7 +53,7 @@
     return jnp.concatenate(done, axis=-1).reshape(-1)
 
 
-def scatter_chunks(full, order, narrow=2):
+def scatter_chunks(full, order, narrow=3):
     bits = flat_bits()
     count = len(bits)
     buf = full.reshape((2,) * count + full.shape[1:])

time: 201 us -> 201 us (level)
  waiting for transfers between devices: 56.8 us -> 53 us
  starting transfers between devices: 66.8 us -> 70.2 us
    ppermute x14, waiting for transfers between devices: 25.8 us -> 22.3 us  [scatter_chunks(): moved = lax.ppermute(other, axis, swap_pairs(axis, j))]
    ppermute x14, starting transfers between devices: 21.7 us -> 24.5 us  [scatter_chunks(): moved = lax.ppermute(other, axis, swap_pairs(axis, j))]
    convert_element_type x4 -> x6, local copies, waits for them, and re-layouts: 4.35 us -> 4.4 us  [scatter_chunks(): other = other.reshape(shape[:-3] + (-1, shape[-1])).astype(jnp.bfloat16)]
  transfers between devices with their start and end apart: 38 -> 38, of which waited for: 22 -> 21; matrix products, arithmetic and copies ran while one was open for 28% -> 28% of each run, Pallas kernels for 0% -> 0%
where the time goes in v8:
time: 201 us; the launch traced here: 199 us
  starting transfers between devices  70.2 us (35%)
  waiting for transfers between devices  53 us (26%)
  local copies, waits for them, and re-layouts  30.3 us (15%)
  other arithmetic  22.2 us (11%)
  loops' own time  14.7 us (7%)
  matrix products  6.54 us (3%)
  between operations  2.28 us (1%)
    ppermute x14, starting transfers between devices, scatter_chunks(): moved = lax.ppermute(other, axis, swap_pairs(axis, j))  24.5 us
    ppermute x14, starting transfers between devices, gather_chunks(): recv = lax.ppermute(buf, axis, swap_pairs(axis, j))  24 us
    ppermute x14, waiting for transfers between devices, gather_chunks(): recv = lax.ppermute(buf, axis, swap_pairs(axis, j))  23.1 us
    ppermute x14, waiting for transfers between devices, scatter_chunks(): moved = lax.ppermute(other, axis, swap_pairs(axis, j))  22.3 us
    another operation x1, loops' own time, body(): grad_out = lax.cond(segment == 0, lead_branch, lead_still)  13.2 us
    reshape x1, local copies, waits for them, and re-layouts, spread(): flat_term = (term / images).reshape(shards, 8, -1)  7.15 us
    ppermute x2, starting transfers between devices, extended_2(): lax.ppermute(lax.slice_in_dim(block, 0, width, axis=dim), axis, backward)  6.84 us
    ppermute x4, starting transfers between devices, rows_sum(): total = total + lax.ppermute(total, 'rows', swap_pairs('rows', j))  6.58 us
  transfers between devices with their start and end apart: 38, of which 21 were waited for; matrix products, arithmetic and copies ran while one was open for 28% of the time, Pallas kernels for 0%

profile of v8, /device:TPU:8, one launch (start us, length us, event | category | flops | bytes accessed | tf_op | source)
XLA Modules:
  0.0 199.1 jit_solution(12092446237608594546)
XLA Ops:
  1.7 3.0 %collective-permute-start.36 = (bf16[16,253]{1,0:T(8,128)(2,1)S(1)}, bf16[16,253]{1,0:T(8,128)(2,1)S(1)}, u32[]{:S(2)}, u32[]{:S(2)}) collective-permute-start(bf16[16,253]{1,0:T(8,128)(2,1)S(1)} %split.25), channel_id=1, source_target_pairs={{0,128},{8,136},{16,144},{24,152},{32,160},{40,168},{48,176},{56,1... | collective-permute-start | bytes 24296 | tf_op jit(solution)/shard_map/ppermute | solution.py:41
  4.7 7.2 %collective-permute-start.29 = (bf16[16,254]{1,0:T(8,128)(2,1)S(1)}, bf16[16,254]{1,0:T(8,128)(2,1)S(1)}, u32[]{:S(2)}, u32[]{:S(2)}) collective-permute-start(bf16[16,254]{1,0:T(8,128)(2,1)S(1)} %split.24), channel_id=1, source_target_pairs={{0,32},{8,40},{16,48},{24,56},{32,0},{40,8},{48,16},{56,24},{64,96... | collective-permute-start | bytes 24392 | tf_op jit(solution)/shard_map/ppermute | solution.py:41
  12.1 2.4 %collective-permute-start.37 = (bf16[2,16,253]{2,1,0:T(8,128)(2,1)S(1)}, bf16[2,16,253]{2,1,0:T(8,128)(2,1)S(1)}, u32[]{:S(2)}, u32[]{:S(2)}) collective-permute-start(bf16[2,16,253]{2,1,0:T(8,128)(2,1)S(1)} %pad_maximum_fusion.16), channel_id=1, source_target_pairs={{0,2},{1,3},{2,0},{3,1},{4,6},{5,7},{6,4},{7,5},{8,10},{9,11},{10,... | collective-permute-start | bytes 48584 | tf_op jit(solution)/shard_map/ppermute | solution.py:41
  15.1 2.3 %collective-permute-done.37 = bf16[2,16,253]{2,1,0:T(8,128)(2,1)S(1)} collective-permute-done((bf16[2,16,253]{2,1,0:T(8,128)(2,1)S(1)}, bf16[2,16,253]{2,1,0:T(8,128)(2,1)S(1)}, u32[]{:S(2)}, u32[]{:S(2)}) %collective-permute-start.37) | collective-permute-done | bytes 16224 | tf_op jit(solution)/shard_map/ppermute | solution.py:41
  17.4 2.8 %collective-permute-start.38 = (bf16[2,2,16,253]{3,2,1,0:T(8,128)(2,1)S(1)}, bf16[2,2,16,253]{3,2,1,0:T(8,128)(2,1)S(1)}, u32[]{:S(2)}, u32[]{:S(2)}) collective-permute-start(bf16[2,2,16,253]{3,2,1,0:T(8,128)(2,1)S(1)} %pad_maximum_fusion.14), channel_id=1, source_target_pairs={{0,32},{8,40},{16,48},{24,56},{32,0},{40,8},{48,16},{56,24},{64,96... | collective-permute-start | bytes 97160 | tf_op jit(solution)/shard_map/ppermute | solution.py:41
  21.8 3.8 %collective-permute-done.38 = bf16[2,2,16,253]{3,2,1,0:T(8,128)(2,1)S(1)} collective-permute-done((bf16[2,2,16,253]{3,2,1,0:T(8,128)(2,1)S(1)}, bf16[2,2,16,253]{3,2,1,0:T(8,128)(2,1)S(1)}, u32[]{:S(2)}, u32[]{:S(2)}) %collective-permute-start.38) | collective-permute-done | bytes 32416 | tf_op jit(solution)/shard_map/ppermute | solution.py:41
  27.1 2.4 %collective-permute-start.32 = (bf16[2,2,2,16,254]{4,3,2,1,0:T(8,128)(2,1)S(1)}, bf16[2,2,2,16,254]{4,3,2,1,0:T(8,128)(2,1)S(1)}, u32[]{:S(2)}, u32[]{:S(2)}) collective-permute-start(bf16[2,2,2,16,254]{4,3,2,1,0:T(8,128)(2,1)S(1)} %pad_maximum_fusion.11), channel_id=1, source_target_pairs={{0,2},{1,3},{2,0},{3,1},{4,6},{5,7},{6,4},{7,5},{8,10},{9,11},{10,... | collective-permute-start | bytes 195080 | tf_op jit(solution)/shard_map/ppermute | solution.py:41
  29.5 2.1 %collective-permute-done.39 = bf16[2,2,2,16,253]{4,3,2,1,0:T(8,128)(2,1)S(1)} collective-permute-done((bf16[2,2,2,16,253]{4,3,2,1,0:T(8,128)(2,1)S(1)}, bf16[2,2,2,16,253]{4,3,2,1,0:T(8,128)(2,1)S(1)}, u32[]{:S(2)}, u32[]{:S(2)}) %collective-permute-start.39) | collective-permute-done | bytes 64800 | tf_op jit(solution)/shard_map/ppermute | solution.py:41
  34.1 2.5 %collective-permute-done.40 = bf16[2,2,2,2,16,253]{5,4,3,2,1,0:T(8,128)(2,1)S(1)} collective-permute-done((bf16[2,2,2,2,16,253]{5,4,3,2,1,0:T(8,128)(2,1)S(1)}, bf16[2,2,2,2,16,253]{5,4,3,2,1,0:T(8,128)(2,1)S(1)}, u32[]{:S(2)}, u32[]{:S(2)}) %collective-permute-start.40) | collective-permute-done | bytes 129568 | tf_op jit(solution)/shard_map/ppermute | solution.py:41
  37.4 2.5 %collective-permute-done.33 = bf16[2,2,2,2,16,254]{5,4,3,2,1,0:T(8,128)(2,1)S(1)} collective-permute-done((bf16[2,2,2,2,16,254]{5,4,3,2,1,0:T(8,128)(2,1)S(1)}, bf16[2,2,2,2,16,254]{5,4,3,2,1,0:T(8,128)(2,1)S(1)}, u32[]{:S(2)}, u32[]{:S(2)}) %collective-permute-start.33) | collective-permute-done | bytes 130080 | tf_op jit(solution)/shard_map/ppermute | solution.py:41
  40.1 3.2 %collective-permute-done.41 = bf16[2,2,2,2,2,16,253]{6,5,4,3,2,1,0:T(8,128)(2,1)S(1)} collective-permute-done((bf16[2,2,2,2,2,16,253]{6,5,4,3,2,1,0:T(8,128)(2,1)S(1)}, bf16[2,2,2,2,2,16,253]{6,5,4,3,2,1,0:T(8,128)(2,1)S(1)}, u32[]{:S(2)}, u32[]{:S(2)}) %collective-permute-start.41) | collective-permute-done | bytes 259104 | tf_op jit(solution)/shard_map/ppermute | solution.py:41
  43.8 5.5 %collective-permute-done.34 = bf16[2,2,2,2,2,16,254]{6,5,4,3,2,1,0:T(8,128)(2,1)S(1)} collective-permute-done((bf16[2,2,2,2,2,16,254]{6,5,4,3,2,1,0:T(8,128)(2,1)S(1)}, bf16[2,2,2,2,2,16,254]{6,5,4,3,2,1,0:T(8,128)(2,1)S(1)}, u32[]{:S(2)}, u32[]{:S(2)}) %collective-permute-start.34) | collective-permute-done | bytes 260128 | tf_op jit(solution)/shard_map/ppermute | solution.py:41
  51.5 3.6 %collective-permute-start.45 = (bf16[2,32,2496]{2,1,0:T(8,128)(2,1)}, bf16[2,32,2496]{2,1,0:T(8,128)(2,1)}, u32[]{:S(2)}, u32[]{:S(2)}) collective-permute-start(bf16[2,32,2496]{2,1,0:T(8,128)(2,1)} %get-tuple-element.228), channel_id=1, source_target_pairs={{1,0},{2,1},{3,2},{5,4},{6,5},{7,6},{9,8},{10,9},{11,10},{13,12},{... | collective-permute-start | bytes 958472 | tf_op jit(solution)/shard_map/ppermute | solution.py:15
  55.1 2.4 %collective-permute-start.44 = (bf16[2,32,2496]{2,1,0:T(8,128)(2,1)}, bf16[2,32,2496]{2,1,0:T(8,128)(2,1)}, u32[]{:S(2)}, u32[]{:S(2)}) collective-permute-start(bf16[2,32,2496]{2,1,0:T(8,128)(2,1)} %get-tuple-element.227), channel_id=1, source_target_pairs={{0,1},{1,2},{2,3},{4,5},{5,6},{6,7},{8,9},{9,10},{10,11},{12,13},{... | collective-permute-start | bytes 958472 | tf_op jit(solution)/shard_map/ppermute | solution.py:12
  57.6 15.4 %conditional.8 = (bf16[128,416]{0,1:T(8,128)(2,1)}, bf16[4,32,416]{2,1,0:T(8,128)(2,1)S(1)}) conditional(s32[]{:T(128)} %convert_element_type.319, () %tuple.71, (bf16[1,4,32,384]{3,2,1,0:T(8,128)(2,1)S(1)}, bf16[1,2,16,384]{3,2,1,0:T(8,128)(2,1)S(1)}, bf16[1,1,8,384]{3,2,1,0:T(8,128)(2,1)S(1)}, bf16[416,384]{1,0:T(8,128)(2,1)S(1)}) %tuple.193), branch_computations={%region_0.1_spmd, %region_1.2_spmd} | conditional | flops 41138176 | bytes 1972240 | solution.py:200
  76.1 2.2 %pad_maximum_fusion.2 = bf16[128,16,507]{2,1,0:T(8,128)(2,1)} fusion(bf16[128,16,253]{2,1,0:T(8,128)(2,1)S(1)} %bitcast.290, bf16[128,16,254]{2,1,0:T(8,128)(2,1)S(1)} %bitcast.291), kind=kLoop, calls=%fused_computation.212 | loop fusion | flops 4153344 | bytes 4153344 | tf_op jit(solution)/shard_map/concatenate | solution.py:53
  78.4 5.2 %reshape_reshape.3 = bf16[416,2496]{1,0:T(8,128)(2,1)S(1)} reshape(bf16[128,16,507]{2,1,0:T(8,128)(2,1)} %pad_maximum_fusion.2) | data formatting | bytes 4153344 | tf_op jit(solution)/shard_map/reshape;reshape | solution.py:159
  83.6 2.0 %conditional.9 = (bf16[128,2496]{0,1:T(8,128)(2,1)S(1)}) conditional(s32[]{:T(128)} %convert_element_type.319, () %tuple.75, (bf16[128,416]{0,1:T(8,128)(2,1)}, bf16[416,2496]{1,0:T(8,128)(2,1)S(1)}) %tuple.76), branch_computations={%region_2.3_spmd, %region_3.4_spmd} | conditional | flops 266133504 | bytes 2822152 | solution.py:208
  83.6 2.0 %convolution_convert_fusion.1 = bf16[128,2496]{0,1:T(8,128)(2,1)S(1)} fusion(bf16[128,416]{0,1:T(8,128)(2,1)} %get-tuple-element.162, bf16[416,2496]{1,0:T(8,128)(2,1)S(1)} %get-tuple-element.89), kind=kOutput, calls=%fused_computation.6 | convolution fusion | flops 266133504 | bytes 2822144 | tf_op jit(solution)/shard_map/cond/branch_1_fun/dot_general | solution.py:203
  88.1 1.9 collective-permute-start.28
  92.6 2.4 %collective-permute-start.46 = (f32[1,2496]{1,0:T(1,128)S(1)}, f32[1,2496]{1,0:T(1,128)S(1)}, u32[]{:S(2)}, u32[]{:S(2)}) collective-permute-start(f32[1,2496]{1,0:T(1,128)S(1)} %get-tuple-element.133), channel_id=1, source_target_pairs={{0,1},{1,0},{2,3},{3,2},{4,5},{5,4},{6,7},{7,6},{8,9},{9,8},{10,11... | collective-permute-start | bytes 29960 | tf_op jit(solution)/shard_map/ppermute | solution.py:84
  95.9 3.6 %conditional.10 = (f32[416,2496]{1,0:T(8,128)}) conditional(s32[]{:T(128)} %convert_element_type.319, () %tuple.74, (bf16[1,1,4,32,2496]{4,3,2,1,0:T(8,128)(2,1)S(1)}, bf16[128,416]{0,1:T(8,128)(2,1)}) %tuple.182), branch_computations={%region_4.5_spmd, %region_5.6_spmd} | conditional | flops 265814016 | bytes 4898824 | solution.py:231
  95.9 3.6 %fusion.46 = f32[416,2496]{1,0:T(8,128)} fusion(bf16[128,416]{0,1:T(8,128)(2,1)} %get-tuple-element.165, bf16[128,2496]{1,0:T(8,128)(2,1)S(1)} %bitcast.287), kind=kOutput, calls=%fused_computation.261 | convolution fusion | flops 265814016 | bytes 4898816 | tf_op jit(solution)/shard_map/cond/branch_1_fun/dot_general | solution.py:224
  99.5 72.9 %conditional.11 = (f32[8112]{0:T(1024)S(1)}) conditional(s32[]{:T(128)} %convert_element_type.319, () %tuple.73, f32[416,2496]{1,0:T(8,128)} %get-tuple-element.270), branch_computations={%region_6.7_spmd, %region_7.8_spmd} | conditional | flops 2985284 | bytes 57808372 | solution.py:232
  99.5 4.6 %broadcast_multiply_fusion = f32[416,2496]{1,0:T(8,128)} fusion(f32[416,2496]{1,0:T(8,128)} %param.7), kind=kLoop, calls=%fused_computation.7 | loop fusion | flops 1038336 | bytes 8306688 | tf_op jit(solution)/shard_map/cond/branch_1_fun/div | solution.py:214
  104.0 7.2 %reshape.204 = f32[128,8,1014]{2,1,0:T(8,128)} reshape(f32[416,2496]{1,0:T(8,128)} %broadcast_multiply_fusion) | data formatting | bytes 8306688 | tf_op jit(solution)/shard_map/cond/branch_1_fun/reshape | solution.py:214
  111.2 3.1 %split.21 = f32[128,8,502]{2,1,0:T(8,128)} slice(f32[128,8,1014]{2,1,0:T(8,128)} %reshape.204), slice={[0:128], [0:8], [512:1014]} | slice | bytes 4112384 | tf_op jit(solution)/shard_map/cond/branch_1_fun/split | solution.py:76
  114.3 2.1 %fusion.4 = bf16[2,2,2,2,2,16,502]{6,5,4,3,2,1,0:T(8,128)(2,1)} fusion(f32[2,2,2,2,2,2,2,8,502]{8,7,6,5,4,3,2,1,0:T(8,128)} %bitcast.279, s32[]{:T(128)S(6)} %select_n.227), kind=kLoop, calls=%fused_computation.13 | loop fusion | bytes 1028100 | tf_op jit(solution)/shard_map/cond/branch_1_fun/convert_element_type | solution.py:68
  116.4 3.1 %split.20 = f32[128,8,512]{2,1,0:T(8,128)} slice(f32[128,8,1014]{2,1,0:T(8,128)} %reshape.204), slice={[0:128], [0:8], [0:512]} | slice | bytes 4194304 | tf_op jit(solution)/shard_map/cond/branch_1_fun/split | solution.py:76
  119.5 2.1 %fusion.3 = bf16[2,2,2,2,2,16,512]{6,5,4,3,2,1,0:T(8,128)(2,1)} fusion(f32[2,2,2,2,2,2,2,8,512]{8,7,6,5,4,3,2,1,0:T(8,128)} %bitcast.283, s32[]{:T(128)S(6)} %select_n.225), kind=kLoop, calls=%fused_computation.12 | loop fusion | bytes 1048580 | tf_op jit(solution)/shard_map/cond/branch_1_fun/convert_element_type | solution.py:68
  122.3 3.6 %collective-permute-done.7 = bf16[2,2,2,2,2,16,502]{6,5,4,3,2,1,0:T(8,128)(2,1)} collective-permute-done((bf16[2,2,2,2,2,16,502]{6,5,4,3,2,1,0:T(8,128)(2,1)}, bf16[2,2,2,2,2,16,502]{6,5,4,3,2,1,0:T(8,128)(2,1)}, u32[]{:S(2)}, u32[]{:S(2)}) %collective-permute-start.7) | collective-permute-done | bytes 514080 | tf_op jit(solution)/shard_map/cond/branch_1_fun/ppermute | solution.py:69
  128.1 3.0 %collective-permute-done = bf16[2,2,2,2,2,16,512]{6,5,4,3,2,1,0:T(8,128)(2,1)} collective-permute-done((bf16[2,2,2,2,2,16,512]{6,5,4,3,2,1,0:T(8,128)(2,1)}, bf16[2,2,2,2,2,16,512]{6,5,4,3,2,1,0:T(8,128)(2,1)}, u32[]{:S(2)}, u32[]{:S(2)}) %collective-permute-start) | collective-permute-done | bytes 524320 | tf_op jit(solution)/shard_map/cond/branch_1_fun/ppermute | solution.py:69
  132.4 2.1 %collective-permute-start.1 = (bf16[2,2,2,2,16,512]{5,4,3,2,1,0:T(8,128)(2,1)S(1)}, bf16[2,2,2,2,16,512]{5,4,3,2,1,0:T(8,128)(2,1)S(1)}, u32[]{:S(2)}, u32[]{:S(2)}) collective-permute-start(bf16[2,2,2,2,16,512]{5,4,3,2,1,0:T(8,128)(2,1)S(1)} %fusion.5), channel_id=1, source_target_pairs={{0,8},{8,0},{16,24},{24,16},{32,40},{40,32},{48,56},{56,48},{64,72... | collective-permute-start | bytes 786440 | tf_op jit(solution)/shard_map/cond/branch_1_fun/ppermute | solution.py:69
  135.5 3.4 %collective-permute-done.1 = bf16[2,2,2,2,16,512]{5,4,3,2,1,0:T(8,128)(2,1)S(1)} collective-permute-done((bf16[2,2,2,2,16,512]{5,4,3,2,1,0:T(8,128)(2,1)S(1)}, bf16[2,2,2,2,16,512]{5,4,3,2,1,0:T(8,128)(2,1)S(1)}, u32[]{:S(2)}, u32[]{:S(2)}) %collective-permute-start.1) | collective-permute-done | bytes 262176 | tf_op jit(solution)/shard_map/cond/branch_1_fun/ppermute | solution.py:69
  139.8 2.5 %collective-permute-start.10 = (f32[2,2,2,8,502]{4,3,2,1,0:T(8,128)S(1)}, f32[2,2,2,8,502]{4,3,2,1,0:T(8,128)S(1)}, u32[]{:S(2)}, u32[]{:S(2)}) collective-permute-start(f32[2,2,2,8,502]{4,3,2,1,0:T(8,128)S(1)} %dynamic-slice_bitcast_fusion), channel_id=1, source_target_pairs={{0,16},{8,24},{16,0},{24,8},{32,48},{40,56},{48,32},{56,40},{64,80... | collective-permute-start | bytes 385544 | tf_op jit(solution)/shard_map/cond/branch_1_fun/ppermute | solution.py:69
  144.1 2.7 %collective-permute-start.3 = (f32[2,2,2,8,512]{4,3,2,1,0:T(8,128)S(1)}, f32[2,2,2,8,512]{4,3,2,1,0:T(8,128)S(1)}, u32[]{:S(2)}, u32[]{:S(2)}) collective-permute-start(f32[2,2,2,8,512]{4,3,2,1,0:T(8,128)S(1)} %dynamic-slice_bitcast_fusion.1), channel_id=1, source_target_pairs={{0,2},{1,3},{2,0},{3,1},{4,6},{5,7},{6,4},{7,5},{8,10},{9,11},{10,... | collective-permute-start | bytes 393224 | tf_op jit(solution)/shard_map/cond/branch_1_fun/ppermute | solution.py:69
  146.9 3.1 %collective-permute-start.11 = (f32[2,2,8,502]{3,2,1,0:T(8,128)S(1)}, f32[2,2,8,502]{3,2,1,0:T(8,128)S(1)}, u32[]{:S(2)}, u32[]{:S(2)}) collective-permute-start(f32[2,2,8,502]{3,2,1,0:T(8,128)S(1)} %dynamic-slice_bitcast_fusion.2), channel_id=1, source_target_pairs={{0,32},{8,40},{16,48},{24,56},{32,0},{40,8},{48,16},{56,24},{64,96... | collective-permute-start | bytes 192776 | tf_op jit(solution)/shard_map/cond/branch_1_fun/ppermute | solution.py:69
  150.7 2.5 %collective-permute-start.4 = (f32[2,2,8,512]{3,2,1,0:T(8,128)S(1)}, f32[2,2,8,512]{3,2,1,0:T(8,128)S(1)}, u32[]{:S(2)}, u32[]{:S(2)}) collective-permute-start(f32[2,2,8,512]{3,2,1,0:T(8,128)S(1)} %dynamic-slice_bitcast_fusion.3), channel_id=1, source_target_pairs={{0,16},{8,24},{16,0},{24,8},{32,48},{40,56},{48,32},{56,40},{64,80... | collective-permute-start | bytes 196616 | tf_op jit(solution)/shard_map/cond/branch_1_fun/ppermute | solution.py:69
  153.2 2.8 %collective-permute-done.11 = f32[2,2,8,502]{3,2,1,0:T(8,128)S(1)} collective-permute-done((f32[2,2,8,502]{3,2,1,0:T(8,128)S(1)}, f32[2,2,8,502]{3,2,1,0:T(8,128)S(1)}, u32[]{:S(2)}, u32[]{:S(2)}) %collective-permute-start.11) | collective-permute-done | bytes 64288 | tf_op jit(solution)/shard_map/cond/branch_1_fun/ppermute | solution.py:69
  156.0 2.1 %collective-permute-start.12 = (f32[2,8,502]{2,1,0:T(8,128)S(1)}, f32[2,8,502]{2,1,0:T(8,128)S(1)}, u32[]{:S(2)}, u32[]{:S(2)}) collective-permute-start(f32[2,8,502]{2,1,0:T(8,128)S(1)} %dynamic-slice_bitcast_fusion.4), channel_id=1, source_target_pairs={{0,2},{1,3},{2,0},{3,1},{4,6},{5,7},{6,4},{7,5},{8,10},{9,11},{10,... | collective-permute-start | bytes 96392 | tf_op jit(solution)/shard_map/cond/branch_1_fun/ppermute | solution.py:69
  158.2 2.0 %collective-permute-start.5 = (f32[2,8,512]{2,1,0:T(8,128)S(1)}, f32[2,8,512]{2,1,0:T(8,128)S(1)}, u32[]{:S(2)}, u32[]{:S(2)}) collective-permute-start(f32[2,8,512]{2,1,0:T(8,128)S(1)} %dynamic-slice_bitcast_fusion.5), channel_id=1, source_target_pairs={{0,128},{8,136},{16,144},{24,152},{32,160},{40,168},{48,176},{56,1... | collective-permute-start | bytes 98312 | tf_op jit(solution)/shard_map/cond/branch_1_fun/ppermute | solution.py:69
  164.1 3.2 %collective-permute-start.6 = (f32[8,512]{1,0:T(8,128)S(1)}, f32[8,512]{1,0:T(8,128)S(1)}, u32[]{:S(2)}, u32[]{:S(2)}) collective-permute-start(f32[8,512]{1,0:T(8,128)S(1)} %dynamic-slice_bitcast_fusion.7), channel_id=1, source_target_pairs={{0,32},{8,40},{16,48},{24,56},{32,0},{40,8},{48,16},{56,24},{64,96... | collective-permute-start | bytes 49160 | tf_op jit(solution)/shard_map/cond/branch_1_fun/ppermute | solution.py:69
  167.4 4.5 %collective-permute-done.6 = f32[8,512]{1,0:T(8,128)S(1)} collective-permute-done((f32[8,512]{1,0:T(8,128)S(1)}, f32[8,512]{1,0:T(8,128)S(1)}, u32[]{:S(2)}, u32[]{:S(2)}) %collective-permute-start.6) | collective-permute-done | bytes 16416 | tf_op jit(solution)/shard_map/cond/branch_1_fun/ppermute | solution.py:69
  179.2 2.1 %copy.60 = bf16[2496,104]{1,0:T(8,128)(2,1)} copy(bf16[2496,104]{0,1:T(8,128)(2,1)} %param.34) | data formatting | bytes 1038336 | tf_op args[8]
  183.7 3.2 %collective-permute-start.51 = (bf16[2,32,2496]{2,1,0:T(8,128)(2,1)S(1)}, bf16[2,32,2496]{2,1,0:T(8,128)(2,1)S(1)}, u32[]{:S(2)}, u32[]{:S(2)}) collective-permute-start(bf16[2,32,2496]{2,1,0:T(8,128)(2,1)S(1)} %get-tuple-element.226), channel_id=1, source_target_pairs={{1,0},{2,1},{3,2},{5,4},{6,5},{7,6},{9,8},{10,9},{11,10},{13,12},{... | collective-permute-start | bytes 958472 | tf_op jit(solution)/shard_map/ppermute | solution.py:15
  187.0 2.6 %collective-permute-start.50 = (bf16[2,32,2496]{2,1,0:T(8,128)(2,1)S(1)}, bf16[2,32,2496]{2,1,0:T(8,128)(2,1)S(1)}, u32[]{:S(2)}, u32[]{:S(2)}) collective-permute-start(bf16[2,32,2496]{2,1,0:T(8,128)(2,1)S(1)} %get-tuple-element.225), channel_id=1, source_target_pairs={{0,1},{1,2},{2,3},{4,5},{5,6},{6,7},{8,9},{9,10},{10,11},{12,13},{... | collective-permute-start | bytes 958472 | tf_op jit(solution)/shard_map/ppermute | solution.py:12
  189.6 3.1 %collective-permute-done.51 = bf16[2,32,2496]{2,1,0:T(8,128)(2,1)S(1)} collective-permute-done((bf16[2,32,2496]{2,1,0:T(8,128)(2,1)S(1)}, bf16[2,32,2496]{2,1,0:T(8,128)(2,1)S(1)}, u32[]{:S(2)}, u32[]{:S(2)}) %collective-permute-start.51) | collective-permute-done | bytes 319520 | tf_op jit(solution)/shard_map/ppermute | solution.py:15
  192.7 3.2 %collective-permute-done.50 = bf16[2,32,2496]{2,1,0:T(8,128)(2,1)S(1)} collective-permute-done((bf16[2,32,2496]{2,1,0:T(8,128)(2,1)S(1)}, bf16[2,32,2496]{2,1,0:T(8,128)(2,1)S(1)}, u32[]{:S(2)}, u32[]{:S(2)}) %collective-permute-start.50) | collective-permute-done | bytes 319520 | tf_op jit(solution)/shard_map/ppermute | solution.py:12
  (171 shorter events, 46.5 us)
Async XLA Ops:
  1.7 10.3 %collective-permute-start.36 = (bf16[16,253]{1,0:T(8,128)(2,1)S(1)}, bf16[16,253]{1,0:T(8,128)(2,1)S(1)}, u32[]{:S(2)}, u32[]{:S(2)}) collective-permute-start(bf16[16,253]{1,0:T(8,128)(2,1)S(1)} %split.25), channel_id=1, source_target_pairs={{0,128},{8,136},{16,144},{24,152},{32,160},{40,168},{48,176},{56,1... | collective-permute-start | bytes 24296 | tf_op jit(solution)/shard_map/ppermute | solution.py:41
  4.7 9.7 %collective-permute-start.29 = (bf16[16,254]{1,0:T(8,128)(2,1)S(1)}, bf16[16,254]{1,0:T(8,128)(2,1)S(1)}, u32[]{:S(2)}, u32[]{:S(2)}) collective-permute-start(bf16[16,254]{1,0:T(8,128)(2,1)S(1)} %split.24), channel_id=1, source_target_pairs={{0,32},{8,40},{16,48},{24,56},{32,0},{40,8},{48,16},{56,24},{64,96... | collective-permute-start | bytes 24392 | tf_op jit(solution)/shard_map/ppermute | solution.py:41
  12.1 5.3 %collective-permute-start.37 = (bf16[2,16,253]{2,1,0:T(8,128)(2,1)S(1)}, bf16[2,16,253]{2,1,0:T(8,128)(2,1)S(1)}, u32[]{:S(2)}, u32[]{:S(2)}) collective-permute-start(bf16[2,16,253]{2,1,0:T(8,128)(2,1)S(1)} %pad_maximum_fusion.16), channel_id=1, source_target_pairs={{0,2},{1,3},{2,0},{3,1},{4,6},{5,7},{6,4},{7,5},{8,10},{9,11},{10,... | collective-permute-start | bytes 48584 | tf_op jit(solution)/shard_map/ppermute | solution.py:41
  14.5 5.7 %collective-permute-start.30 = (bf16[2,16,254]{2,1,0:T(8,128)(2,1)S(1)}, bf16[2,16,254]{2,1,0:T(8,128)(2,1)S(1)}, u32[]{:S(2)}, u32[]{:S(2)}) collective-permute-start(bf16[2,16,254]{2,1,0:T(8,128)(2,1)S(1)} %pad_maximum_fusion.15), channel_id=1, source_target_pairs={{0,128},{8,136},{16,144},{24,152},{32,160},{40,168},{48,176},{56,1... | collective-permute-start | bytes 48776 | tf_op jit(solution)/shard_map/ppermute | solution.py:41
  17.4 8.1 %collective-permute-start.38 = (bf16[2,2,16,253]{3,2,1,0:T(8,128)(2,1)S(1)}, bf16[2,2,16,253]{3,2,1,0:T(8,128)(2,1)S(1)}, u32[]{:S(2)}, u32[]{:S(2)}) collective-permute-start(bf16[2,2,16,253]{3,2,1,0:T(8,128)(2,1)S(1)} %pad_maximum_fusion.14), channel_id=1, source_target_pairs={{0,32},{8,40},{16,48},{24,56},{32,0},{40,8},{48,16},{56,24},{64,96... | collective-permute-start | bytes 97160 | tf_op jit(solution)/shard_map/ppermute | solution.py:41
  20.2 6.8 %collective-permute-start.31 = (bf16[2,2,16,254]{3,2,1,0:T(8,128)(2,1)S(1)}, bf16[2,2,16,254]{3,2,1,0:T(8,128)(2,1)S(1)}, u32[]{:S(2)}, u32[]{:S(2)}) collective-permute-start(bf16[2,2,16,254]{3,2,1,0:T(8,128)(2,1)S(1)} %pad_maximum_fusion.13), channel_id=1, source_target_pairs={{0,16},{8,24},{16,0},{24,8},{32,48},{40,56},{48,32},{56,40},{64,80... | collective-permute-start | bytes 97544 | tf_op jit(solution)/shard_map/ppermute | solution.py:41
  25.6 6.0 %collective-permute-start.39 = (bf16[2,2,2,16,253]{4,3,2,1,0:T(8,128)(2,1)S(1)}, bf16[2,2,2,16,253]{4,3,2,1,0:T(8,128)(2,1)S(1)}, u32[]{:S(2)}, u32[]{:S(2)}) collective-permute-start(bf16[2,2,2,16,253]{4,3,2,1,0:T(8,128)(2,1)S(1)} %pad_maximum_fusion.12), channel_id=1, source_target_pairs={{0,16},{8,24},{16,0},{24,8},{32,48},{40,56},{48,32},{56,40},{64,80... | collective-permute-start | bytes 194312 | tf_op jit(solution)/shard_map/ppermute | solution.py:41
  27.1 6.3 %collective-permute-start.32 = (bf16[2,2,2,16,254]{4,3,2,1,0:T(8,128)(2,1)S(1)}, bf16[2,2,2,16,254]{4,3,2,1,0:T(8,128)(2,1)S(1)}, u32[]{:S(2)}, u32[]{:S(2)}) collective-permute-start(bf16[2,2,2,16,254]{4,3,2,1,0:T(8,128)(2,1)S(1)} %pad_maximum_fusion.11), channel_id=1, source_target_pairs={{0,2},{1,3},{2,0},{3,1},{4,6},{5,7},{6,4},{7,5},{8,10},{9,11},{10,... | collective-permute-start | bytes 195080 | tf_op jit(solution)/shard_map/ppermute | solution.py:41
  31.6 5.1 %collective-permute-start.40 = (bf16[2,2,2,2,16,253]{5,4,3,2,1,0:T(8,128)(2,1)S(1)}, bf16[2,2,2,2,16,253]{5,4,3,2,1,0:T(8,128)(2,1)S(1)}, u32[]{:S(2)}, u32[]{:S(2)}) collective-permute-start(bf16[2,2,2,2,16,253]{5,4,3,2,1,0:T(8,128)(2,1)S(1)} %pad_maximum_fusion.10), channel_id=1, source_target_pairs={{0,1},{1,0},{2,3},{3,2},{4,5},{5,4},{6,7},{7,6},{8,9},{9,8},{10,11... | collective-permute-start | bytes 388616 | tf_op jit(solution)/shard_map/ppermute | solution.py:41
  33.5 6.4 %collective-permute-start.33 = (bf16[2,2,2,2,16,254]{5,4,3,2,1,0:T(8,128)(2,1)S(1)}, bf16[2,2,2,2,16,254]{5,4,3,2,1,0:T(8,128)(2,1)S(1)}, u32[]{:S(2)}, u32[]{:S(2)}) collective-permute-start(bf16[2,2,2,2,16,254]{5,4,3,2,1,0:T(8,128)(2,1)S(1)} %pad_maximum_fusion.9), channel_id=1, source_target_pairs={{0,64},{8,72},{16,80},{24,88},{32,96},{40,104},{48,112},{56,120},{... | collective-permute-start | bytes 390152 | tf_op jit(solution)/shard_map/ppermute | solution.py:41
  36.8 6.6 %collective-permute-start.41 = (bf16[2,2,2,2,2,16,253]{6,5,4,3,2,1,0:T(8,128)(2,1)S(1)}, bf16[2,2,2,2,2,16,253]{6,5,4,3,2,1,0:T(8,128)(2,1)S(1)}, u32[]{:S(2)}, u32[]{:S(2)}) collective-permute-start(bf16[2,2,2,2,2,16,253]{6,5,4,3,2,1,0:T(8,128)(2,1)S(1)} %pad_maximum_fusion.8), channel_id=1, source_target_pairs={{0,64},{8,72},{16,80},{24,88},{32,96},{40,104},{48,112},{56,120},{... | collective-permute-start | bytes 777224 | tf_op jit(solution)/shard_map/ppermute | solution.py:41
  40.0 9.3 %collective-permute-start.34 = (bf16[2,2,2,2,2,16,254]{6,5,4,3,2,1,0:T(8,128)(2,1)S(1)}, bf16[2,2,2,2,2,16,254]{6,5,4,3,2,1,0:T(8,128)(2,1)S(1)}, u32[]{:S(2)}, u32[]{:S(2)}) collective-permute-start(bf16[2,2,2,2,2,16,254]{6,5,4,3,2,1,0:T(8,128)(2,1)S(1)} %pad_maximum_fusion.7), channel_id=1, source_target_pairs={{0,8},{8,0},{16,24},{24,16},{32,40},{40,32},{48,56},{56,48},{64,72... | collective-permute-start | bytes 780296 | tf_op jit(solution)/shard_map/ppermute | solution.py:41
  43.5 29.5 %collective-permute-start.42 = (bf16[2,2,2,2,2,2,16,253]{7,6,5,4,3,2,1,0:T(8,128)(2,1)S(1)}, bf16[2,2,2,2,2,2,16,253]{7,6,5,4,3,2,1,0:T(8,128)(2,1)}, u32[]{:S(2)}, u32[]{:S(2)}) collective-permute-start(bf16[2,2,2,2,2,2,16,253]{7,6,5,4,3,2,1,0:T(8,128)(2,1)S(1)} %pad_maximum_fusion.6), channel_id=1, source_target_pairs={{0,8},{8,0},{16,24},{24,16},{32,40},{40,32},{48,56},{56,48},{64,72... | collective-permute-start | bytes 1554440 | tf_op jit(solution)/shard_map/ppermute | solution.py:41
  49.3 8.2 %copy-start.15 = (bf16[416,384]{1,0:T(8,128)(2,1)S(1)}, bf16[416,384]{1,0:T(8,128)(2,1)}, u32[]{:S(2)}) copy-start(bf16[416,384]{1,0:T(8,128)(2,1)} %param.31) | copy-start | bytes 958468
  49.4 8.2 %copy-start.18 = (bf16[1,4,32,384]{3,2,1,0:T(8,128)(2,1)S(1)}, bf16[1,4,32,384]{3,2,1,0:T(8,128)(2,1)}, u32[]{:S(2)}) copy-start(bf16[1,4,32,384]{3,2,1,0:T(8,128)(2,1)} %param.28) | copy-start | bytes 294916
  49.4 8.2 %copy-start.20 = (bf16[1,2,16,384]{3,2,1,0:T(8,128)(2,1)S(1)}, bf16[1,2,16,384]{3,2,1,0:T(8,128)(2,1)}, u32[]{:S(2)}) copy-start(bf16[1,2,16,384]{3,2,1,0:T(8,128)(2,1)} %param.29) | copy-start | bytes 73732
  49.4 8.2 %copy-start.21 = (bf16[1,1,8,384]{3,2,1,0:T(8,128)(2,1)S(1)}, bf16[1,1,8,384]{3,2,1,0:T(8,128)(2,1)}, u32[]{:S(2)}) copy-start(bf16[1,1,8,384]{3,2,1,0:T(8,128)(2,1)} %param.30) | copy-start | bytes 18436
  50.3 24.3 %collective-permute-start.35 = (bf16[2,2,2,2,2,2,16,254]{7,6,5,4,3,2,1,0:T(8,128)(2,1)}, bf16[2,2,2,2,2,2,16,254]{7,6,5,4,3,2,1,0:T(8,128)(2,1)}, u32[]{:S(2)}, u32[]{:S(2)}) collective-permute-start(bf16[2,2,2,2,2,2,16,254]{7,6,5,4,3,2,1,0:T(8,128)(2,1)} %pad_maximum_fusion.5), channel_id=1, source_target_pairs={{0,1},{1,0},{2,3},{3,2},{4,5},{5,4},{6,7},{7,6},{8,9},{9,8},{10,11... | collective-permute-start | bytes 1560584 | tf_op jit(solution)/shard_map/ppermute | solution.py:41
  51.5 39.4 %collective-permute-start.45 = (bf16[2,32,2496]{2,1,0:T(8,128)(2,1)}, bf16[2,32,2496]{2,1,0:T(8,128)(2,1)}, u32[]{:S(2)}, u32[]{:S(2)}) collective-permute-start(bf16[2,32,2496]{2,1,0:T(8,128)(2,1)} %get-tuple-element.228), channel_id=1, source_target_pairs={{1,0},{2,1},{3,2},{5,4},{6,5},{7,6},{9,8},{10,9},{11,10},{13,12},{... | collective-permute-start | bytes 958472 | tf_op jit(solution)/shard_map/ppermute | solution.py:15
  55.1 35.8 %collective-permute-start.44 = (bf16[2,32,2496]{2,1,0:T(8,128)(2,1)}, bf16[2,32,2496]{2,1,0:T(8,128)(2,1)}, u32[]{:S(2)}, u32[]{:S(2)}) collective-permute-start(bf16[2,32,2496]{2,1,0:T(8,128)(2,1)} %get-tuple-element.227), channel_id=1, source_target_pairs={{0,1},{1,2},{2,3},{4,5},{5,6},{6,7},{8,9},{9,10},{10,11},{12,13},{... | collective-permute-start | bytes 958472 | tf_op jit(solution)/shard_map/ppermute | solution.py:12
  86.7 8.3 %collective-permute-start.43 = (bf16[4,32,2496]{2,1,0:T(8,128)(2,1)}, bf16[4,32,2496]{2,1,0:T(8,128)(2,1)S(1)}, u32[]{:S(2)}, u32[]{:S(2)}) collective-permute-start(bf16[4,32,2496]{2,1,0:T(8,128)(2,1)} %bitcast.292), channel_id=1, source_target_pairs={{0,4},{1,5},{2,6},{3,7},{8,12},{9,13},{10,14},{11,15},{16,20},{17,... | collective-permute-start | bytes 1916936 | tf_op jit(solution)/shard_map/ppermute | solution.py:23
  88.1 6.9 %collective-permute-start.28 = (bf16[4,32,416]{2,1,0:T(8,128)(2,1)}, bf16[4,32,416]{2,1,0:T(8,128)(2,1)}, u32[]{:S(2)}, u32[]{:S(2)}) collective-permute-start(bf16[4,32,416]{2,1,0:T(8,128)(2,1)} %copy-done.17), channel_id=1, source_target_pairs={{0,4},{1,5},{2,6},{3,7},{8,12},{9,13},{10,14},{11,15},{16,20},{17,... | collective-permute-start | bytes 319496 | tf_op jit(solution)/shard_map/ppermute | solution.py:23
  92.6 82.1 %collective-permute-start.46 = (f32[1,2496]{1,0:T(1,128)S(1)}, f32[1,2496]{1,0:T(1,128)S(1)}, u32[]{:S(2)}, u32[]{:S(2)}) collective-permute-start(f32[1,2496]{1,0:T(1,128)S(1)} %get-tuple-element.133), channel_id=1, source_target_pairs={{0,1},{1,0},{2,3},{3,2},{4,5},{5,4},{6,7},{7,6},{8,9},{9,8},{10,11... | collective-permute-start | bytes 29960 | tf_op jit(solution)/shard_map/ppermute | solution.py:84
  99.5 72.9 %copy-start.9 = (f32[4,32,2496]{2,1,0:T(8,128)S(1)}, f32[4,32,2496]{2,1,0:T(8,128)}, u32[]{:S(2)}) copy-start(f32[4,32,2496]{2,1,0:T(8,128)} %copy-done.8) | copy-start | bytes 3833860
  116.4 9.5 %collective-permute-start.7 = (bf16[2,2,2,2,2,16,502]{6,5,4,3,2,1,0:T(8,128)(2,1)}, bf16[2,2,2,2,2,16,502]{6,5,4,3,2,1,0:T(8,128)(2,1)}, u32[]{:S(2)}, u32[]{:S(2)}) collective-permute-start(bf16[2,2,2,2,2,16,502]{6,5,4,3,2,1,0:T(8,128)(2,1)} %fusion.4), channel_id=1, source_target_pairs={{0,8},{8,0},{16,24},{24,16},{32,40},{40,32},{48,56},{56,48},{64,72... | collective-permute-start | bytes 1542152 | tf_op jit(solution)/shard_map/cond/branch_1_fun/ppermute | solution.py:69
  121.6 9.5 %collective-permute-start = (bf16[2,2,2,2,2,16,512]{6,5,4,3,2,1,0:T(8,128)(2,1)}, bf16[2,2,2,2,2,16,512]{6,5,4,3,2,1,0:T(8,128)(2,1)}, u32[]{:S(2)}, u32[]{:S(2)}) collective-permute-start(bf16[2,2,2,2,2,16,512]{6,5,4,3,2,1,0:T(8,128)(2,1)} %fusion.3), channel_id=1, source_target_pairs={{0,1},{1,0},{2,3},{3,2},{4,5},{5,4},{6,7},{7,6},{8,9},{9,8},{10,11... | collective-permute-start | bytes 1572872 | tf_op jit(solution)/shard_map/cond/branch_1_fun/ppermute | solution.py:69
  122.3 8.8 %copy-start.2 = (f32[128,8,512]{2,1,0:T(8,128)S(1)}, f32[128,8,512]{2,1,0:T(8,128)}, u32[]{:S(2)}) copy-start(f32[128,8,512]{2,1,0:T(8,128)} %split.20) | copy-start | bytes 6291460 | tf_op jit(solution)/shard_map/cond
  127.5 7.0 %collective-permute-start.8 = (bf16[2,2,2,2,16,502]{5,4,3,2,1,0:T(8,128)(2,1)S(1)}, bf16[2,2,2,2,16,502]{5,4,3,2,1,0:T(8,128)(2,1)S(1)}, u32[]{:S(2)}, u32[]{:S(2)}) collective-permute-start(bf16[2,2,2,2,16,502]{5,4,3,2,1,0:T(8,128)(2,1)S(1)} %fusion.6), channel_id=1, source_target_pairs={{0,64},{8,72},{16,80},{24,88},{32,96},{40,104},{48,112},{56,120},{... | collective-permute-start | bytes 771080 | tf_op jit(solution)/shard_map/cond/branch_1_fun/ppermute | solution.py:69
  132.4 6.5 %collective-permute-start.1 = (bf16[2,2,2,2,16,512]{5,4,3,2,1,0:T(8,128)(2,1)S(1)}, bf16[2,2,2,2,16,512]{5,4,3,2,1,0:T(8,128)(2,1)S(1)}, u32[]{:S(2)}, u32[]{:S(2)}) collective-permute-start(bf16[2,2,2,2,16,512]{5,4,3,2,1,0:T(8,128)(2,1)S(1)} %fusion.5), channel_id=1, source_target_pairs={{0,8},{8,0},{16,24},{24,16},{32,40},{40,32},{48,56},{56,48},{64,72... | collective-permute-start | bytes 786440 | tf_op jit(solution)/shard_map/cond/branch_1_fun/ppermute | solution.py:69
  134.6 5.1 %collective-permute-start.9 = (bf16[2,2,2,16,502]{4,3,2,1,0:T(8,128)(2,1)S(1)}, bf16[2,2,2,16,502]{4,3,2,1,0:T(8,128)(2,1)S(1)}, u32[]{:S(2)}, u32[]{:S(2)}) collective-permute-start(bf16[2,2,2,16,502]{4,3,2,1,0:T(8,128)(2,1)S(1)} %fusion.8), channel_id=1, source_target_pairs={{0,1},{1,0},{2,3},{3,2},{4,5},{5,4},{6,7},{7,6},{8,9},{9,8},{10,11... | collective-permute-start | bytes 385544 | tf_op jit(solution)/shard_map/cond/branch_1_fun/ppermute | solution.py:69
  139.0 5.1 %collective-permute-start.2 = (bf16[2,2,2,16,512]{4,3,2,1,0:T(8,128)(2,1)S(1)}, bf16[2,2,2,16,512]{4,3,2,1,0:T(8,128)(2,1)S(1)}, u32[]{:S(2)}, u32[]{:S(2)}) collective-permute-start(bf16[2,2,2,16,512]{4,3,2,1,0:T(8,128)(2,1)S(1)} %fusion.7), channel_id=1, source_target_pairs={{0,64},{8,72},{16,80},{24,88},{32,96},{40,104},{48,112},{56,120},{... | collective-permute-start | bytes 393224 | tf_op jit(solution)/shard_map/cond/branch_1_fun/ppermute | solution.py:69
  139.8 7.1 %collective-permute-start.10 = (f32[2,2,2,8,502]{4,3,2,1,0:T(8,128)S(1)}, f32[2,2,2,8,502]{4,3,2,1,0:T(8,128)S(1)}, u32[]{:S(2)}, u32[]{:S(2)}) collective-permute-start(f32[2,2,2,8,502]{4,3,2,1,0:T(8,128)S(1)} %dynamic-slice_bitcast_fusion), channel_id=1, source_target_pairs={{0,16},{8,24},{16,0},{24,8},{32,48},{40,56},{48,32},{56,40},{64,80... | collective-permute-start | bytes 385544 | tf_op jit(solution)/shard_map/cond/branch_1_fun/ppermute | solution.py:69
  144.1 6.6 %collective-permute-start.3 = (f32[2,2,2,8,512]{4,3,2,1,0:T(8,128)S(1)}, f32[2,2,2,8,512]{4,3,2,1,0:T(8,128)S(1)}, u32[]{:S(2)}, u32[]{:S(2)}) collective-permute-start(f32[2,2,2,8,512]{4,3,2,1,0:T(8,128)S(1)} %dynamic-slice_bitcast_fusion.1), channel_id=1, source_target_pairs={{0,2},{1,3},{2,0},{3,1},{4,6},{5,7},{6,4},{7,5},{8,10},{9,11},{10,... | collective-permute-start | bytes 393224 | tf_op jit(solution)/shard_map/cond/branch_1_fun/ppermute | solution.py:69
  146.9 9.1 %collective-permute-start.11 = (f32[2,2,8,502]{3,2,1,0:T(8,128)S(1)}, f32[2,2,8,502]{3,2,1,0:T(8,128)S(1)}, u32[]{:S(2)}, u32[]{:S(2)}) collective-permute-start(f32[2,2,8,502]{3,2,1,0:T(8,128)S(1)} %dynamic-slice_bitcast_fusion.2), channel_id=1, source_target_pairs={{0,32},{8,40},{16,48},{24,56},{32,0},{40,8},{48,16},{56,24},{64,96... | collective-permute-start | bytes 192776 | tf_op jit(solution)/shard_map/cond/branch_1_fun/ppermute | solution.py:69
  150.7 7.5 %collective-permute-start.4 = (f32[2,2,8,512]{3,2,1,0:T(8,128)S(1)}, f32[2,2,8,512]{3,2,1,0:T(8,128)S(1)}, u32[]{:S(2)}, u32[]{:S(2)}) collective-permute-start(f32[2,2,8,512]{3,2,1,0:T(8,128)S(1)} %dynamic-slice_bitcast_fusion.3), channel_id=1, source_target_pairs={{0,16},{8,24},{16,0},{24,8},{32,48},{40,56},{48,32},{56,40},{64,80... | collective-permute-start | bytes 196616 | tf_op jit(solution)/shard_map/cond/branch_1_fun/ppermute | solution.py:69
  156.0 5.5 %collective-permute-start.12 = (f32[2,8,502]{2,1,0:T(8,128)S(1)}, f32[2,8,502]{2,1,0:T(8,128)S(1)}, u32[]{:S(2)}, u32[]{:S(2)}) collective-permute-start(f32[2,8,502]{2,1,0:T(8,128)S(1)} %dynamic-slice_bitcast_fusion.4), channel_id=1, source_target_pairs={{0,2},{1,3},{2,0},{3,1},{4,6},{5,7},{6,4},{7,5},{8,10},{9,11},{10,... | collective-permute-start | bytes 96392 | tf_op jit(solution)/shard_map/cond/branch_1_fun/ppermute | solution.py:69
  158.2 5.9 %collective-permute-start.5 = (f32[2,8,512]{2,1,0:T(8,128)S(1)}, f32[2,8,512]{2,1,0:T(8,128)S(1)}, u32[]{:S(2)}, u32[]{:S(2)}) collective-permute-start(f32[2,8,512]{2,1,0:T(8,128)S(1)} %dynamic-slice_bitcast_fusion.5), channel_id=1, source_target_pairs={{0,128},{8,136},{16,144},{24,152},{32,160},{40,168},{48,176},{56,1... | collective-permute-start | bytes 98312 | tf_op jit(solution)/shard_map/cond/branch_1_fun/ppermute | solution.py:69
  161.5 5.8 %collective-permute-start.13 = (f32[8,502]{1,0:T(8,128)S(1)}, f32[8,502]{1,0:T(8,128)S(1)}, u32[]{:S(2)}, u32[]{:S(2)}) collective-permute-start(f32[8,502]{1,0:T(8,128)S(1)} %dynamic-slice_bitcast_fusion.6), channel_id=1, source_target_pairs={{0,128},{8,136},{16,144},{24,152},{32,160},{40,168},{48,176},{56,1... | collective-permute-start | bytes 48200 | tf_op jit(solution)/shard_map/cond/branch_1_fun/ppermute | solution.py:69
  164.1 7.7 %collective-permute-start.6 = (f32[8,512]{1,0:T(8,128)S(1)}, f32[8,512]{1,0:T(8,128)S(1)}, u32[]{:S(2)}, u32[]{:S(2)}) collective-permute-start(f32[8,512]{1,0:T(8,128)S(1)} %dynamic-slice_bitcast_fusion.7), channel_id=1, source_target_pairs={{0,32},{8,40},{16,48},{24,56},{32,0},{40,8},{48,16},{56,24},{64,96... | collective-permute-start | bytes 49160 | tf_op jit(solution)/shard_map/cond/branch_1_fun/ppermute | solution.py:69
  172.4 8.9 %copy-start.19 = (f32[8112]{0:T(1024)}, f32[8112]{0:T(1024)S(1)}, u32[]{:S(2)}) copy-start(f32[8112]{0:T(1024)S(1)} %get-tuple-element.271) | copy-start | bytes 97348
  173.7 3.8 %collective-permute-start.48 = (f32[1,2496]{1,0:T(1,128)S(1)}, f32[1,2496]{1,0:T(1,128)S(1)}, u32[]{:S(2)}, u32[]{:S(2)}) collective-permute-start(f32[1,2496]{1,0:T(1,128)S(1)} %stack.178), channel_id=1, source_target_pairs={{0,1},{1,0},{2,3},{3,2},{4,5},{5,4},{6,7},{7,6},{8,9},{9,8},{10,11... | collective-permute-start | bytes 29960 | tf_op jit(solution)/shard_map/ppermute | solution.py:84
  174.7 8.9 %collective-permute-start.47 = (f32[1,2496]{1,0:T(1,128)S(1)}, f32[1,2496]{1,0:T(1,128)S(1)}, u32[]{:S(2)}, u32[]{:S(2)}) collective-permute-start(f32[1,2496]{1,0:T(1,128)S(1)} %add.434), channel_id=1, source_target_pairs={{0,2},{1,3},{2,0},{3,1},{4,6},{5,7},{6,4},{7,5},{8,10},{9,11},{10,... | collective-permute-start | bytes 29960 | tf_op jit(solution)/shard_map/ppermute | solution.py:84
  177.4 6.2 %collective-permute-start.49 = (f32[1,2496]{1,0:T(1,128)S(1)}, f32[1,2496]{1,0:T(1,128)S(1)}, u32[]{:S(2)}, u32[]{:S(2)}) collective-permute-start(f32[1,2496]{1,0:T(1,128)S(1)} %reshape_add_fusion), channel_id=1, source_target_pairs={{0,2},{1,3},{2,0},{3,1},{4,6},{5,7},{6,4},{7,5},{8,10},{9,11},{10,... | collective-permute-start | bytes 29960 | tf_op jit(solution)/shard_map/ppermute | solution.py:84
  183.7 9.0 %collective-permute-start.51 = (bf16[2,32,2496]{2,1,0:T(8,128)(2,1)S(1)}, bf16[2,32,2496]{2,1,0:T(8,128)(2,1)S(1)}, u32[]{:S(2)}, u32[]{:S(2)}) collective-permute-start(bf16[2,32,2496]{2,1,0:T(8,128)(2,1)S(1)} %get-tuple-element.226), channel_id=1, source_target_pairs={{1,0},{2,1},{3,2},{5,4},{6,5},{7,6},{9,8},{10,9},{11,10},{13,12},{... | collective-permute-start | bytes 958472 | tf_op jit(solution)/shard_map/ppermute | solution.py:15
  187.0 9.0 %collective-permute-start.50 = (bf16[2,32,2496]{2,1,0:T(8,128)(2,1)S(1)}, bf16[2,32,2496]{2,1,0:T(8,128)(2,1)S(1)}, u32[]{:S(2)}, u32[]{:S(2)}) collective-permute-start(bf16[2,32,2496]{2,1,0:T(8,128)(2,1)S(1)} %get-tuple-element.225), channel_id=1, source_target_pairs={{0,1},{1,2},{2,3},{4,5},{5,6},{6,7},{8,9},{9,10},{10,11},{12,13},{... | collective-permute-start | bytes 958472 | tf_op jit(solution)/shard_map/ppermute | solution.py:12
  189.6 7.6 %copy-start.4 = (bf16[1,1,4,32,2496]{4,3,2,1,0:T(8,128)(2,1)S(1)}, bf16[1,1,4,32,2496]{4,3,2,1,0:T(8,128)(2,1)}, u32[]{:S(2)}) copy-start(bf16[1,1,4,32,2496]{4,3,2,1,0:T(8,128)(2,1)} %param.27) | copy-start | bytes 1916932
  189.6 7.6 %copy-start.13 = (f32[25,2496]{1,0:T(8,128)S(1)}, f32[25,2496]{1,0:T(8,128)}, u32[]{:S(2)}) copy-start(f32[25,2496]{1,0:T(8,128)} %copy-done.12) | copy-start | bytes 748804
  189.6 7.6 %copy-start.16 = (bf16[1,4,32,416]{3,2,1,0:T(8,128)(2,1)S(1)}, bf16[1,4,32,416]{3,2,1,0:T(8,128)(2,1)}, u32[]{:S(2)}) copy-start(bf16[1,4,32,416]{3,2,1,0:T(8,128)(2,1)} %param.26) | copy-start | bytes 319492
  (8 other events, 18.2 us)
